TPU v7x, 128 devices: a whole 4x4x4 slice. The times are simulated.
128 devices in a mesh: rec: 16 (over x, y), chan: 8 (over z, core).
Axes of the slice: x: 4, y: 4, z: 4, core: 2. Of those that a mesh axis runs over, the one named last changes fastest.
Arguments:
- signal: bfloat16 [4, 128, 614400], P(None, 'chan', 'rec'), may hold values from -6 to 6
- montage: int32 [4, 8, 16], P(None, 'chan'), may hold values from 0 to 15, each once within a row
- channels: int32 [4], replicated, may hold values from 19 to 128
- lengths: int32 [4], replicated, may hold values from 1537 to 3072
- boundary: int32 [4, 3072], P(None, 'rec'), may hold values 0 or 1
- conv_in: bfloat16 [16, 8, 5, 200, 128], P('rec', 'chan'), may hold values from -0.1875 to 0.1875
- conv_hid: bfloat16 [16, 8, 2, 5, 128, 128], P('rec', 'chan'), may hold values from -0.25 to 0.25
- mix_weight: bfloat16 [16, 8, 128, 512], P(None, 'chan'), may hold values from -0.046875 to 0.046875
- norm_gain: float32 [512], replicated, may hold values from 0.1 to 1.9
- emit_weight: float32 [512, 5], replicated, may hold values from -1 to 1
- trans_within: float32 [5, 5], replicated, may hold values from -3 to 3
- trans_between: float32 [5, 5], replicated, may hold values from -2 to 102
- initial: float32 [5], replicated, may hold values from -6 to 6
Outputs:
- filtered: float32 [4, 5, 3072], P(None, None, 'rec')
- log_rate: float32 [4], replicated
All inputs are finite; a program needn't handle non-finite values. No bound on the sum of `boundary` on one device may be relied on, other than what follows from the above.
Results may differ from a plain program's by a relative error of at most 0.011.
Values may be sent and summed in bfloat16 or wider, within the bound.
No kernel may reach another device: no remote copies, remote signals or barrier semaphores. Data moves between devices by JAX's collectives and lax.ppermute only.
A program may use at most 128 MiB of HBM per device.

v0:
```python
import functools

import jax
import jax.numpy as jnp
from jax import lax
from jax.experimental import pallas as pl
from jax.sharding import PartitionSpec as P

SAMP = 200
EMB = 128
STATES = 5


EPSILON = 1e-05
NEGATIVE = -1e30


def log_sum_exp(values, along):
    peak_value = jnp.max(values, axis=along, keepdims=True)
    return jnp.squeeze(peak_value, along) + jnp.log(
        jnp.sum(jnp.exp(values - peak_value), axis=along)
    )


LANES = 128


def forward_step(state, matrices, extra):
    terms = [state[i : i + 1, :] + matrices[i] for i in range(len(matrices))]
    peak = functools.reduce(jnp.maximum, terms)
    total = functools.reduce(lambda x, y: x + y, [jnp.exp(t - peak) for t in terms])
    moved = peak + jnp.log(total)
    if extra is not None:
        moved = moved + extra
    top = jnp.max(moved, axis=0, keepdims=True)
    level = top + jnp.log(jnp.sum(jnp.exp(moved - top), axis=0, keepdims=True))
    return moved - level, level


def prefix_kernel(within_ref, between_ref, start_ref, emit_ref, cross_ref, valid_ref, prefix_ref, offset_ref):
    patches = emit_ref.shape[0]
    within = [within_ref[i] for i in range(STATES)]
    between = [between_ref[i] for i in range(STATES)]

    def body(p, carry):
        state, offset = carry
        crossing = cross_ref[p] > 0.5
        counted = valid_ref[p] > 0.5
        matrices = [jnp.where(crossing, between[i], within[i]) for i in range(STATES)]
        moved, level = forward_step(state, matrices, emit_ref[p])
        state = jnp.where(counted, moved, state)
        offset = offset + jnp.where(counted, level, 0.0)
        prefix_ref[p] = state
        offset_ref[p] = offset
        return state, offset

    lax.fori_loop(0, patches, body, (start_ref[...], jnp.zeros((1, LANES), jnp.float32)))


def chain_kernel(prior_ref, mats_ref, incoming_ref, total_ref):
    count = mats_ref.shape[0]

    def body(k, carry):
        state, total = carry
        incoming_ref[k] = state
        matrices = [mats_ref[k, j] for j in range(STATES)]
        moved, level = forward_step(state, matrices, None)
        return moved, total + level

    _, total = lax.fori_loop(0, count, body, (prior_ref[...], jnp.zeros((1, LANES), jnp.float32)))
    total_ref[...] = total


def lanes_padded(values):
    pad = [(0, 0)] * (values.ndim - 1) + [(0, LANES - values.shape[-1])]
    return jnp.pad(values, pad)


def crf_forward(emission, cross, valid, trans_within, trans_between, initial, rec_index):
    recordings, patches, _ = emission.shape
    width = STATES * recordings
    emit_in = lanes_padded(jnp.tile(jnp.transpose(emission, (1, 2, 0)), (1, 1, STATES)))
    cross_in = lanes_padded(jnp.tile(cross.T.astype(jnp.float32), (1, STATES)))[:, None, :]
    valid_in = lanes_padded(jnp.tile(valid.T.astype(jnp.float32), (1, STATES)))[:, None, :]
    lane_start = jnp.arange(width, dtype=jnp.int32) // recordings
    basis = jnp.arange(STATES, dtype=jnp.int32)[:, None] == lane_start[None, :]
    start = lanes_padded(jnp.where(basis, 0.0, NEGATIVE).astype(jnp.float32))
    within_in = jnp.broadcast_to(trans_within[:, :, None], (STATES, STATES, LANES))
    between_in = jnp.broadcast_to(trans_between[:, :, None], (STATES, STATES, LANES))
    prefix, offset = pl.pallas_call(
        prefix_kernel,
        out_shape=(
            jax.ShapeDtypeStruct((patches, STATES, LANES), jnp.float32),
            jax.ShapeDtypeStruct((patches, 1, LANES), jnp.float32),
        ),
        cost_estimate=pl.CostEstimate(
            flops=patches * 80 * LANES * 8, transcendentals=patches * 8 * LANES * 8,
            bytes_accessed=patches * 14 * LANES * 4,
        ),
    )(within_in, between_in, start, emit_in, cross_in, valid_in)
    prefix_sj = prefix[:, :, :width].reshape(patches, STATES, STATES, recordings)
    offset_j = offset[:, 0, :width].reshape(patches, STATES, recordings)
    transfer = prefix_sj[patches - 1] + offset_j[patches - 1][None]
    transfer = jnp.transpose(transfer, (1, 0, 2))
    gathered = lax.all_gather(transfer, "rec")
    mats = lanes_padded(gathered)
    prior = initial - log_sum_exp(initial, 0)
    prior_in = lanes_padded(jnp.broadcast_to(prior[:, None], (STATES, recordings)))
    groups = gathered.shape[0]
    incoming, total = pl.pallas_call(
        chain_kernel,
        out_shape=(
            jax.ShapeDtypeStruct((groups, STATES, LANES), jnp.float32),
            jax.ShapeDtypeStruct((1, LANES), jnp.float32),
        ),
    )(prior_in, mats)
    here = lax.dynamic_index_in_dim(incoming, rec_index, 0, keepdims=False)[:, :recordings]
    weights = here[None, None] + offset_j[:, None] + prefix_sj
    reached = log_sum_exp(weights, 2)
    totals = log_sum_exp(reached, 1)
    filtered = jnp.transpose(reached - totals[:, None], (2, 1, 0))
    return filtered, total[0, :recordings]


def neighbour_shift(block, axis, distance):
    devices = range(lax.axis_size(axis))
    route = [(i - distance, i) for i in devices if i - distance in devices]
    return lax.ppermute(block, axis, route)


def valid_temporal(rows, taps):
    length = rows.shape[2] - taps.shape[1] + 1
    accumulated = None
    for offset in range(taps.shape[1]):
        term = jnp.einsum(
            "mbqc,mce->mbqe", rows[:, :, offset : offset + length], taps[:, offset],
            preferred_element_type=jnp.float32,
        )
        accumulated = term if accumulated is None else accumulated + term
    return accumulated


def halo_conv_stack(patch_rows, first_taps, hidden_taps, rec_index):
    patches = patch_rows.shape[2]
    reach = first_taps.shape[1] // 2
    layers = hidden_taps.shape[1]
    halo = reach * (layers + 1)
    total = patches * lax.axis_size("rec")
    from_left = neighbour_shift(patch_rows[:, :, patches - halo :], "rec", 1)
    from_right = neighbour_shift(patch_rows[:, :, :halo], "rec", -1)
    extended = jnp.concatenate([from_left, patch_rows, from_right], axis=2)

    def masked(values, margin):
        spot = rec_index * patches - margin + jnp.arange(values.shape[2], dtype=jnp.int32)
        keep = (spot >= 0) & (spot < total)
        return jnp.where(keep[None, None, :, None], values, jnp.zeros((), values.dtype))

    margin = halo - reach
    current = masked(jax.nn.gelu(valid_temporal(extended, first_taps)).astype(jnp.bfloat16), margin)
    for depth_index in range(layers):
        update = jax.nn.gelu(valid_temporal(current, hidden_taps[:, depth_index]))
        margin = margin - reach
        current = (current[:, :, reach : current.shape[2] - reach].astype(jnp.float32) + update).astype(jnp.bfloat16)
        if margin > 0:
            current = masked(current, margin)
    return current


def local(
    signal,
    montage,
    channels,
    lengths,
    boundary,
    conv_in,
    conv_hid,
    mix_weight,
    norm_gain,
    emit_weight,
    trans_within,
    trans_between,
    initial,
):
    groups = lax.axis_size("rec")
    chan_index = lax.axis_index("chan")
    rec_index = lax.axis_index("rec")
    recordings = signal.shape[0]
    patches = signal.shape[2] // SAMP
    slot_ids = chan_index * groups + jnp.arange(groups, dtype=jnp.int32)
    live_slots = slot_ids[None, :] < channels[:, None]
    places = jnp.arange(groups, dtype=jnp.int32)
    pick = (montage[:, 0, None, :] == places[None, :, None]) & live_slots[:, None, :]
    rows = jnp.einsum(
        "bms,bst->mbt", pick.astype(jnp.bfloat16), signal, preferred_element_type=jnp.float32
    ).astype(jnp.bfloat16)
    patch_rows = rows.reshape(groups, recordings, patches, SAMP)
    first_taps = lax.all_gather(conv_in[:, 0], "rec", tiled=True)
    hidden_taps = lax.all_gather(conv_hid[:, 0], "rec", tiled=True)
    encoded = halo_conv_stack(patch_rows, first_taps, hidden_taps, rec_index)
    partial_value = jnp.einsum(
        "mbpe,meo->bpo", encoded, mix_weight[:, 0], preferred_element_type=jnp.float32
    )
    summed = lax.psum(partial_value, "chan")
    average = jnp.mean(summed, axis=-1, keepdims=True)
    centred = summed - average
    variance = jnp.mean(centred * centred, axis=-1, keepdims=True)
    activated = jax.nn.gelu(centred * lax.rsqrt(variance + EPSILON) * norm_gain)
    emission = jnp.einsum("bpo,os->bps", activated, emit_weight, precision=lax.Precision.HIGHEST)
    positions = rec_index * patches + jnp.arange(patches, dtype=jnp.int32)
    valid = positions[None, :] < lengths[:, None]
    cross = boundary == 1
    filtered, log_partition = crf_forward(
        emission, cross, valid, trans_within, trans_between, initial, rec_index
    )
    return (filtered, log_partition / lengths.astype(jnp.float32))


def solution(mesh):
    placed = (
        P(None, "chan", "rec"),
        P(None, "chan", None),
        P(),
        P(),
        P(None, "rec"),
        P("rec", "chan", None, None, None),
        P("rec", "chan", None, None, None, None),
        P(None, "chan", None, None),
        P(),
        P(),
        P(),
        P(),
        P(),
    )
    return jax.shard_map(
        local, mesh=mesh, in_specs=placed, out_specs=(P(None, None, "rec"), P()), check_vma=False
    )
```

profile of v0, /device:TPU:0, one launch (start us, length us, event | category | flops | bytes accessed | tf_op | source)
XLA Modules:
  0.0 320.4 jit_solution(16680105037313351057)
XLA Ops:
  7.2 0.7 all-gather.6.cloned.1.call-update
  8.0 0.7 all-gather.8.cloned.1.call-update
  8.7 0.7 broadcast_compare_fusion
  9.5 6.0 %fusion = bf16[16,4,38400]{2,0,1:T(8,128)(2,1)} fusion(bf16[4,16,38400]{2,1,0:T(8,128)(2,1)} %param.13, s32[4,16]{1,0:T(4,128)} %bitcast.165, pred[4,16]{1,0:T(4,128)(4,1)S(1)} %broadcast_compare_fusion), kind=kOutput, calls=%fused_computation.1 | convolution fusion | flops 81102848 | bytes 9830720 | tf_op jit(solution)/shard_map/bms,bst->mbt/dot_general | solution.py:193
  15.5 20.8 %reshape.145 = bf16[16,4,192,200]{3,2,0,1:T(8,128)(2,1)} reshape(bf16[16,4,38400]{2,0,1:T(8,128)(2,1)} %fusion) | data formatting | bytes 9830400 | tf_op jit(solution)/shard_map/reshape | solution.py:196
  36.3 1.1 fusion.111
  37.4 3.6 %collective-permute-start = (bf16[16,4,6,200]{3,2,1,0:T(8,128)(2,1)S(1)}, bf16[16,4,6,200]{3,2,1,0:T(8,128)(2,1)S(1)}, u32[]{:S(2)}, u32[]{:S(2)}) collective-permute-start(bf16[16,4,6,200]{3,2,1,0:T(8,128)(2,1)S(1)} %get-tuple-element.10), channel_id=1, source_target_pairs={{0,8},{8,16},{16,24},{24,32},{32,40},{40,48},{48,56},{56,64},{64,7... | collective-permute-start | bytes 460808 | tf_op jit(solution)/shard_map/ppermute | solution.py:128
  41.0 1.5 collective-permute-start.1
  42.7 8.1 %collective-permute-done = bf16[16,4,6,200]{3,2,1,0:T(8,128)(2,1)S(1)} collective-permute-done((bf16[16,4,6,200]{3,2,1,0:T(8,128)(2,1)S(1)}, bf16[16,4,6,200]{3,2,1,0:T(8,128)(2,1)S(1)}, u32[]{:S(2)}, u32[]{:S(2)}) %collective-permute-start) | collective-permute-done | bytes 153632 | tf_op jit(solution)/shard_map/ppermute | solution.py:128
  50.8 5.8 %collective-permute-done.1 = bf16[16,4,6,200]{3,2,1,0:T(8,128)(2,1)S(1)} collective-permute-done((bf16[16,4,6,200]{3,2,1,0:T(8,128)(2,1)S(1)}, bf16[16,4,6,200]{3,2,1,0:T(8,128)(2,1)S(1)}, u32[]{:S(2)}, u32[]{:S(2)}) %collective-permute-start.1) | collective-permute-done | bytes 153632 | tf_op jit(solution)/shard_map/ppermute | solution.py:128
  56.6 8.0 %pad_maximum_fusion = bf16[16,4,204,200]{3,2,1,0:T(8,128)(2,1)} fusion(bf16[16,4,6,200]{3,2,1,0:T(8,128)(2,1)S(1)} %collective-permute-done.1, bf16[16,4,6,200]{3,2,1,0:T(8,128)(2,1)S(1)} %collective-permute-done, bf16[16,4,192,200]{3,2,0,1:T(8,128)(2,1)} %reshape.145), kind=kLoop, calls=%fused_computation.5 | loop fusion | flops 15667200 | bytes 10444800 | tf_op jit(solution)/shard_map/concatenate | solution.py:151
  64.6 3.4 %all-gather.6.cloned.1.call-done = bf16[16,1,5,200,128]{4,3,0,2,1:T(8,128)(2,1)} async-done(((bf16[1,1,5,200,128]{4,3,0,2,1:T(8,128)(2,1)}), bf16[16,1,5,200,128]{4,3,0,2,1:T(8,128)(2,1)}) %all-gather.6.cloned.1.call-update) | async-done | bytes 4096016 | tf_op jit(solution)/shard_map/all_gather | solution.py:197
  68.0 7.7 %fusion.26 = f32[16,4,200,128]{3,2,1,0:T(8,128)} fusion(bf16[16,4,204,200]{3,2,1,0:T(8,128)(2,1)} %pad_maximum_fusion, bf16[16,5,200,128]{3,2,0,1:T(8,128)(2,1)} %bitcast.157), kind=kOutput, calls=%fused_computation.31 | convolution fusion | flops 655360000 | bytes 13926400 | tf_op jit(solution)/shard_map/mbqc,mce->mbqe/dot_general | solution.py:135
  75.8 4.7 %fusion.24 = f32[16,4,200,128]{3,2,1,0:T(8,128)} fusion(bf16[16,4,204,200]{3,2,1,0:T(8,128)(2,1)S(1)} %copy-done.3, bf16[16,5,200,128]{3,2,0,1:T(8,128)(2,1)S(1)} %bitcast.159), kind=kOutput, calls=%fused_computation.29 | convolution fusion | flops 655360000 | bytes 13926400 | tf_op jit(solution)/shard_map/mbqc,mce->mbqe/dot_general | solution.py:135
  80.5 4.7 %fusion.22 = f32[16,4,200,128]{3,2,1,0:T(8,128)} fusion(bf16[16,4,204,200]{3,2,1,0:T(8,128)(2,1)S(1)} %copy-done.3, bf16[16,5,200,128]{3,2,0,1:T(8,128)(2,1)S(1)} %bitcast.160), kind=kOutput, calls=%fused_computation.27 | convolution fusion | flops 655360000 | bytes 13926400 | tf_op jit(solution)/shard_map/mbqc,mce->mbqe/dot_general | solution.py:135
  85.2 4.7 %fusion.20 = f32[16,4,200,128]{3,2,1,0:T(8,128)} fusion(bf16[16,4,204,200]{3,2,1,0:T(8,128)(2,1)S(1)} %copy-done.3, bf16[16,5,200,128]{3,2,0,1:T(8,128)(2,1)S(1)} %bitcast.161), kind=kOutput, calls=%fused_computation.25 | convolution fusion | flops 655360000 | bytes 13926400 | tf_op jit(solution)/shard_map/mbqc,mce->mbqe/dot_general | solution.py:135
  89.9 13.2 %broadcast_select_fusion = bf16[16,4,200,128]{3,2,1,0:T(8,128)(2,1)} fusion(pred[200]{0:T(512)(128)(4,1)S(1)} %compare_and_fusion, f32[16,4,200,128]{3,2,1,0:T(8,128)} %fusion.20, f32[16,4,200,128]{3,2,1,0:T(8,128)} %fusion.22, f32[16,4,200,128]{3,2,1,0:T(8,128)} %fusion.26, f32[16,4,200,128]{3,2,1,0:T(8,128)} %fusion.24, ...), kind=kOutput, calls=%fused_computation.50 | convolution fusion | flops 678297600 | bytes 36864512 | tf_op jit(solution)/shard_map/mbqc,mce->mbqe/dot_general | solution.py:135
  103.1 24.4 %all-gather.8.cloned.1.call-done = bf16[16,1,2,5,128,128]{5,4,0,3,2,1:T(8,128)(2,1)} async-done(((bf16[1,1,2,5,128,128]{5,4,0,3,2,1:T(8,128)(2,1)}), bf16[16,1,2,5,128,128]{5,4,0,3,2,1:T(8,128)(2,1)}) %all-gather.8.cloned.1.call-update) | async-done | bytes 5242896 | tf_op jit(solution)/shard_map/all_gather | solution.py:198
  127.5 3.8 %slice_bitcast_fusion = (bf16[16,5,128,128]{3,2,0,1:T(8,128)(2,1)S(1)}, bf16[16,5,128,128]{3,2,0,1:T(8,128)(2,1)S(1)}) fusion(bf16[16,2,5,128,128]{4,3,0,2,1:T(8,128)(2,1)} %bitcast.152), kind=kLoop, calls=%fused_computation.66 | loop fusion | bytes 10485760 | tf_op jit(solution)/shard_map/squeeze | solution.py:161
  131.3 4.6 %fusion.37 = f32[16,4,196,128]{3,2,1,0:T(8,128)} fusion(bf16[16,4,200,128]{3,2,1,0:T(8,128)(2,1)S(1)} %copy-done.1, bf16[16,5,128,128]{3,2,0,1:T(8,128)(2,1)S(1)} %get-tuple-element.13), kind=kOutput, calls=%fused_computation.42 | convolution fusion | flops 411041792 | bytes 10223616 | tf_op jit(solution)/shard_map/mbqc,mce->mbqe/dot_general | solution.py:135
  135.9 4.6 %fusion.39 = f32[16,4,196,128]{3,2,1,0:T(8,128)} fusion(bf16[16,4,200,128]{3,2,1,0:T(8,128)(2,1)S(1)} %copy-done.1, bf16[16,5,128,128]{3,2,0,1:T(8,128)(2,1)S(1)} %get-tuple-element.13), kind=kOutput, calls=%fused_computation.44 | convolution fusion | flops 411041792 | bytes 10223616 | tf_op jit(solution)/shard_map/mbqc,mce->mbqe/dot_general | solution.py:135
  140.5 4.6 %fusion.41 = f32[16,4,196,128]{3,2,1,0:T(8,128)} fusion(bf16[16,4,200,128]{3,2,1,0:T(8,128)(2,1)S(1)} %copy-done.1, bf16[16,5,128,128]{3,2,0,1:T(8,128)(2,1)S(1)} %get-tuple-element.13), kind=kOutput, calls=%fused_computation.46 | convolution fusion | flops 411041792 | bytes 10223616 | tf_op jit(solution)/shard_map/mbqc,mce->mbqe/dot_general | solution.py:135
  145.1 4.6 %fusion.55 = f32[16,4,196,128]{3,2,1,0:T(8,128)} fusion(bf16[16,4,200,128]{3,2,1,0:T(8,128)(2,1)S(1)} %copy-done.1, bf16[16,5,128,128]{3,2,0,1:T(8,128)(2,1)S(1)} %get-tuple-element.13), kind=kOutput, calls=%fused_computation.61 | convolution fusion | flops 411041792 | bytes 10223616 | tf_op jit(solution)/shard_map/mbqc,mce->mbqe/dot_general | solution.py:135
  149.7 11.4 %broadcast_select_fusion.1 = bf16[16,4,196,128]{3,2,1,0:T(8,128)(2,1)S(1)} fusion(pred[196]{0:T(512)(128)(4,1)S(1)} %compare_and_fusion.1, f32[16,4,196,128]{3,2,1,0:T(8,128)} %fusion.37, f32[16,4,196,128]{3,2,1,0:T(8,128)} %fusion.39, f32[16,4,196,128]{3,2,1,0:T(8,128)} %fusion.55, f32[16,4,196,128]{3,2,1,0:T(8,128)} %fusion.41, ...), kind=kOutput, calls=%fused_computation.51 | convolution fusion | flops 436731904 | bytes 35979776 | tf_op jit(solution)/shard_map/mbqc,mce->mbqe/dot_general | solution.py:135
  161.1 3.7 %fusion.47 = f32[16,4,192,128]{3,2,1,0:T(8,128)} fusion(bf16[16,4,196,128]{3,2,1,0:T(8,128)(2,1)S(1)} %broadcast_select_fusion.1, bf16[16,5,128,128]{3,2,0,1:T(8,128)(2,1)S(1)} %get-tuple-element.12), kind=kOutput, calls=%fused_computation.54 | convolution fusion | flops 402653184 | bytes 9961472 | tf_op jit(solution)/shard_map/mbqc,mce->mbqe/dot_general | solution.py:135
  164.7 3.6 %fusion.49 = f32[16,4,192,128]{3,2,1,0:T(8,128)} fusion(bf16[16,4,196,128]{3,2,1,0:T(8,128)(2,1)S(1)} %broadcast_select_fusion.1, bf16[16,5,128,128]{3,2,0,1:T(8,128)(2,1)S(1)} %get-tuple-element.12), kind=kOutput, calls=%fused_computation.56 | convolution fusion | flops 402653184 | bytes 9961472 | tf_op jit(solution)/shard_map/mbqc,mce->mbqe/dot_general | solution.py:135
  168.4 3.6 %fusion.57 = f32[16,4,192,128]{3,2,1,0:T(8,128)} fusion(bf16[16,4,196,128]{3,2,1,0:T(8,128)(2,1)S(1)} %broadcast_select_fusion.1, bf16[16,5,128,128]{3,2,0,1:T(8,128)(2,1)S(1)} %get-tuple-element.12), kind=kOutput, calls=%fused_computation.63 | convolution fusion | flops 402653184 | bytes 9961472 | tf_op jit(solution)/shard_map/mbqc,mce->mbqe/dot_general | solution.py:135
  172.0 3.6 %fusion.45 = f32[16,4,192,128]{3,2,1,0:T(8,128)} fusion(bf16[16,4,196,128]{3,2,1,0:T(8,128)(2,1)S(1)} %broadcast_select_fusion.1, bf16[16,5,128,128]{3,2,0,1:T(8,128)(2,1)S(1)} %get-tuple-element.12), kind=kOutput, calls=%fused_computation.52 | convolution fusion | flops 402653184 | bytes 9961472 | tf_op jit(solution)/shard_map/mbqc,mce->mbqe/dot_general | solution.py:135
  175.6 15.5 %fusion.76 = f32[4,192,512]{2,1,0:T(8,128)} fusion(bf16[16,1,128,512]{3,2,1,0:T(8,128)(2,1)S(1)} %copy-done, f32[16,4,192,128]{3,2,1,0:T(8,128)} %fusion.45, f32[16,4,192,128]{3,2,1,0:T(8,128)} %fusion.47, f32[16,4,192,128]{3,2,1,0:T(8,128)} %fusion.57, f32[16,4,192,128]{3,2,1,0:T(8,128)} %fusion.49, bf16[16,4,196,128]{3,2,1,0:T(8,128)(2,1)} %copy-done.2, ...), kind=kOutput, calls=%fused_computation.79 | convolution fusion | flops 2036858880 | bytes 35651584 | tf_op jit(solution)/shard_map/mbpe,meo->bpo/dot_general | solution.py:200
  191.3 0.6 pad.27
  192.0 0.6 pad.26
  193.8 1.2 exponential_reduce_fusion.2
  197.1 58.2 %all-reduce.8.cloned.1.call-done = f32[4,192,512]{2,1,0:T(8,128)} async-done(((f32[4,192,512]{2,1,0:T(8,128)}), f32[4,192,512]{2,1,0:T(8,128)}) %all-reduce.8.cloned.1.call-update) | async-done | bytes 1572880 | tf_op jit(solution)/shard_map/psum | solution.py:203
  255.3 1.6 reduce_sum.46
  256.9 1.8 multiply_reduce_fusion
  258.7 3.5 %fusion.84 = f32[192,5,4]{0,1,2:T(8,128)S(1)} fusion(f32[4,192,512]{2,1,0:T(8,128)} %all-reduce.8.cloned.1.call-done, f32[512]{0:T(512)S(1)} %copy-done.11, f32[4,192]{1,0:T(4,128)S(1)} %add_rsqrt_fusion, f32[4,192]{1,0:T(4,128)S(1)} %broadcast_multiply_fusion, f32[512,5]{0,1:T(8,128)S(1)} %copy-done.10), kind=kOutput, calls=%fused_computation.81 | convolution fusion | flops 27918336 | bytes 1606656 | tf_op jit(solution)/shard_map/bpo,os->bps/dot_general | solution.py:208
  262.7 1.0 pad.25.emit_ref
  263.7 0.7 broadcast_in_dim.43.within_ref
  264.4 0.7 broadcast_in_dim.44.between_ref
  265.0 14.1 %shard_map.140 = (f32[192,5,128]{2,1,0:T(8,128)}, f32[192,1,128]{2,1,0:T(1,128)}) custom-call(f32[5,5,128]{2,1,0:T(8,128)} %broadcast_in_dim.43.within_ref, f32[5,5,128]{2,1,0:T(8,128)} %broadcast_in_dim.44.between_ref, f32[5,128]{1,0:T(8,128)} %pad.24.start_ref, f32[192,5,128]{2,1,0:T(8,128)} %pad.25.emit_ref, f32[192,1,128]{2,1,0:T(1,128)} %bitcast.163, ...), custom_call_target="tpu_custom_call" | custom-call | flops 15728640 | bytes 1376256 | tf_op jit(solution)/shard_map/pallas_call | solution.py:90
  279.2 0.7 slice.160
  280.8 23.7 %all-gather.2 = f32[80,5,4]{1,2,0:T(4,128)S(1)} all-gather(f32[5,5,4]{1,2,0:T(4,128)S(1)} %add_bitcast_fusion), channel_id=4, replica_groups=mesh['rec'=16,'chan'=8] {'rec'}, dimensions={0}, use_global_device_ids=true | all-gather | bytes 6800 | tf_op jit(solution)/shard_map/all_gather | solution.py:105
  305.1 0.8 pad.28.mats_ref
  305.9 1.0 copy.51
  306.9 1.4 copy.52
  308.3 2.5 shard_map.141
  310.8 0.7 dynamic-slice_bitcast_fusion
  312.3 1.1 bitcast_divide_fusion
  (70 shorter events, 5.3 us)
Async XLA Ops:
  7.2 168.5 %copy-start = (bf16[16,1,128,512]{3,2,1,0:T(8,128)(2,1)S(1)}, bf16[16,1,128,512]{3,2,1,0:T(8,128)(2,1)}, u32[]{:S(2)}) copy-start(bf16[16,1,128,512]{3,2,1,0:T(8,128)(2,1)} %param.20) | copy-start | bytes 6291460
  7.2 60.8 %all-gather.6.cloned.1.call-start = ((), (), s32[]{:S(2)}) async-start(), calls=%async_computation.1 | async-start | bytes 4352000 | tf_op jit(solution)/shard_map/all_gather | solution.py:197
  7.9 119.6 %all-gather.8.cloned.1.call-start = ((), (), s32[]{:S(2)}) async-start(), calls=%async_computation.2 | async-start | bytes 5570560 | tf_op jit(solution)/shard_map/all_gather | solution.py:198
  8.7 246.6 %all-reduce.8.cloned.1.call-start = ((), (), s32[]{:S(2)}) async-start(), calls=%async_computation | async-start | bytes 3145728 | tf_op jit(solution)/shard_map/psum | solution.py:203
  15.5 27.0 %copy-start.9 = (s32[4]{0:T(128)S(1)}, s32[4]{0:T(128)}, u32[]{:S(2)}) copy-start(s32[4]{0:T(128)} %param.16) | copy-start | bytes 52
  37.4 13.4 %collective-permute-start = (bf16[16,4,6,200]{3,2,1,0:T(8,128)(2,1)S(1)}, bf16[16,4,6,200]{3,2,1,0:T(8,128)(2,1)S(1)}, u32[]{:S(2)}, u32[]{:S(2)}) collective-permute-start(bf16[16,4,6,200]{3,2,1,0:T(8,128)(2,1)S(1)} %get-tuple-element.10), channel_id=1, source_target_pairs={{0,8},{8,16},{16,24},{24,32},{32,40},{40,48},{48,56},{56,64},{64,7... | collective-permute-start | bytes 460808 | tf_op jit(solution)/shard_map/ppermute | solution.py:128
  41.0 15.6 %collective-permute-start.1 = (bf16[16,4,6,200]{3,2,1,0:T(8,128)(2,1)S(1)}, bf16[16,4,6,200]{3,2,1,0:T(8,128)(2,1)S(1)}, u32[]{:S(2)}, u32[]{:S(2)}) collective-permute-start(bf16[16,4,6,200]{3,2,1,0:T(8,128)(2,1)S(1)} %get-tuple-element.11), channel_id=1, source_target_pairs={{8,0},{16,8},{24,16},{32,24},{40,32},{48,40},{56,48},{64,56},{72,6... | collective-permute-start | bytes 460808 | tf_op jit(solution)/shard_map/ppermute | solution.py:128
  68.0 7.7 %copy-start.3 = (bf16[16,4,204,200]{3,2,1,0:T(8,128)(2,1)S(1)}, bf16[16,4,204,200]{3,2,1,0:T(8,128)(2,1)}, u32[]{:S(2)}) copy-start(bf16[16,4,204,200]{3,2,1,0:T(8,128)(2,1)} %pad_maximum_fusion) | copy-start | bytes 15667204
  68.0 7.7 %copy-start.5 = (bf16[16,1,5,200,128]{4,3,0,2,1:T(8,128)(2,1)S(1)}, bf16[16,1,5,200,128]{4,3,0,2,1:T(8,128)(2,1)}, u32[]{:S(2)}) copy-start(bf16[16,1,5,200,128]{4,3,0,2,1:T(8,128)(2,1)} %all-gather.6.cloned.1.call-done) | copy-start | bytes 12288004
  127.5 3.8 %copy-start.1 = (bf16[16,4,200,128]{3,2,1,0:T(8,128)(2,1)S(1)}, bf16[16,4,200,128]{3,2,1,0:T(8,128)(2,1)}, u32[]{:S(2)}) copy-start(bf16[16,4,200,128]{3,2,1,0:T(8,128)(2,1)} %broadcast_select_fusion) | copy-start | bytes 9830404
  131.3 40.7 %copy-start.4 = (bf16[16,5,128,128]{3,2,0,1:T(8,128)(2,1)}, bf16[16,5,128,128]{3,2,0,1:T(8,128)(2,1)S(1)}, u32[]{:S(2)}) copy-start(bf16[16,5,128,128]{3,2,0,1:T(8,128)(2,1)S(1)} %get-tuple-element.12) | copy-start | bytes 7864324
  161.1 10.9 %copy-start.2 = (bf16[16,4,196,128]{3,2,1,0:T(8,128)(2,1)}, bf16[16,4,196,128]{3,2,1,0:T(8,128)(2,1)S(1)}, u32[]{:S(2)}) copy-start(bf16[16,4,196,128]{3,2,1,0:T(8,128)(2,1)S(1)} %broadcast_select_fusion.1) | copy-start | bytes 9633796
  175.6 15.5 %copy-start.6 = (s32[4,192]{1,0:T(4,128)S(1)}, s32[4,192]{1,0:T(4,128)}, u32[]{:S(2)}) copy-start(s32[4,192]{1,0:T(4,128)} %param.17) | copy-start | bytes 9220
  175.6 17.6 %copy-start.12 = (f32[5]{0:T(128)S(1)}, f32[5]{0:T(128)}, u32[]{:S(2)}) copy-start(f32[5]{0:T(128)} %param.25) | copy-start | bytes 64
  175.6 83.1 %copy-start.10 = (f32[512,5]{0,1:T(8,128)S(1)}, f32[512,5]{0,1:T(8,128)}, u32[]{:S(2)}) copy-start(f32[512,5]{0,1:T(8,128)} %param.22) | copy-start | bytes 30724
  175.6 83.1 %copy-start.11 = (f32[512]{0:T(512)S(1)}, f32[512]{0:T(512)}, u32[]{:S(2)}) copy-start(f32[512]{0:T(512)} %param.21) | copy-start | bytes 6148
  191.2 72.5 %copy-start.7 = (f32[5,5]{1,0:T(8,128)S(1)}, f32[5,5]{1,0:T(8,128)}, u32[]{:S(2)}) copy-start(f32[5,5]{1,0:T(8,128)} %param.23) | copy-start | bytes 304
  191.2 73.1 %copy-start.8 = (f32[5,5]{1,0:T(8,128)S(1)}, f32[5,5]{1,0:T(8,128)}, u32[]{:S(2)}) copy-start(f32[5,5]{1,0:T(8,128)} %param.24) | copy-start | bytes 304
Sparse Core Ops, SparseCore 0:
  10.2 57.7 all-gather.5
  70.2 57.2 all-gather.7
  191.3 63.9 all-reduce.7
where the time goes:
time: 324 us; the launch traced here: 320 us
  matrix products  104 us (32%)
  waiting for transfers between devices  101 us (31%)
  local copies, waits for them, and re-layouts  37.3 us (12%)
  blocking collectives  23.7 us (7%)
  Pallas kernels  16.6 us (5%)
  other arithmetic  16.2 us (5%)
  between operations  15.8 us (5%)
  starting transfers between devices  5.15 us (2%)
    dot_general x14, matrix products, valid_temporal(): jnp.einsum('mbqc,mce->mbqe', rows[:, :, offset:offset + length], taps[:,...  79.4 us
    psum x1, waiting for transfers between devices, local(): summed = lax.psum(partial_value, 'chan')  58.2 us
    all_gather x1, waiting for transfers between devices, local(): hidden_taps = lax.all_gather(conv_hid[:, 0], 'rec', tiled=True)  24.4 us
    all_gather x1, blocking collectives, crf_forward(): gathered = lax.all_gather(transfer, 'rec')  23.7 us
    reshape x1, local copies, waits for them, and re-layouts, local(): patch_rows = rows.reshape(groups, recordings, patches, SAMP)  20.8 us
    dot_general x1, matrix products, local(): jnp.einsum('mbpe,meo->bpo', encoded, mix_weight[:, 0], preferred_element_...  15.5 us
    pallas_call x1, Pallas kernels, crf_forward(): pl.pallas_call(prefix_kernel, out_shape=(jax.ShapeDtypeStruct((patches, S...  14.1 us
    ppermute x2, waiting for transfers between devices, neighbour_shift(): return lax.ppermute(block, axis, route)  13.9 us
  transfers between devices with their start and end apart: 5, of which 5 were waited for; matrix products, arithmetic and copies ran while one was open for 24% of the time, Pallas kernels for 0%

commit v1 on v0

--- a/solution.py
+++ b/solution.py
@@ -4,6 +4,7 @@
 import jax.numpy as jnp
 from jax import lax
 from jax.experimental import pallas as pl
+from jax.experimental.pallas import tpu as pltpu
 from jax.sharding import PartitionSpec as P
 
 SAMP = 200
@@ -128,42 +129,83 @@
     return lax.ppermute(block, axis, route)
 
 
-def valid_temporal(rows, taps):
-    length = rows.shape[2] - taps.shape[1] + 1
-    accumulated = None
-    for offset in range(taps.shape[1]):
-        term = jnp.einsum(
-            "mbqc,mce->mbqe", rows[:, :, offset : offset + length], taps[:, offset],
-            preferred_element_type=jnp.float32,
-        )
-        accumulated = term if accumulated is None else accumulated + term
-    return accumulated
-
-
-def halo_conv_stack(patch_rows, first_taps, hidden_taps, rec_index):
+def halo_rows(patch_rows):
     patches = patch_rows.shape[2]
-    reach = first_taps.shape[1] // 2
-    layers = hidden_taps.shape[1]
-    halo = reach * (layers + 1)
-    total = patches * lax.axis_size("rec")
+    halo = 6
     from_left = neighbour_shift(patch_rows[:, :, patches - halo :], "rec", 1)
     from_right = neighbour_shift(patch_rows[:, :, :halo], "rec", -1)
-    extended = jnp.concatenate([from_left, patch_rows, from_right], axis=2)
-
-    def masked(values, margin):
-        spot = rec_index * patches - margin + jnp.arange(values.shape[2], dtype=jnp.int32)
-        keep = (spot >= 0) & (spot < total)
-        return jnp.where(keep[None, None, :, None], values, jnp.zeros((), values.dtype))
-
-    margin = halo - reach
-    current = masked(jax.nn.gelu(valid_temporal(extended, first_taps)).astype(jnp.bfloat16), margin)
+    return jnp.concatenate([from_left, patch_rows, from_right], axis=2)
+
+def tap_sum(rows, weight_of, taps, length):
+    accumulated = None
+    for offset in range(taps):
+        product = jnp.dot(rows, weight_of(offset), preferred_element_type=jnp.float32)
+        product = product[offset : offset + length]
+        accumulated = product if accumulated is None else accumulated + product
+    return accumulated
+
+
+def conv_mix_kernel(rows_ref, first_ref, hidden_ref, mix_ref, keep_a_ref, keep_b_ref, out_ref):
+    @pl.when(pl.program_id(0) == 0)
+    def _():
+        out_ref[...] = jnp.zeros_like(out_ref)
+
+    taps = first_ref.shape[1]
+    reach = taps // 2
+    layers = hidden_ref.shape[1]
+    keeps = [keep_a_ref[...] > 0.5, keep_b_ref[...] > 0.5]
+    for item in range(rows_ref.shape[1]):
+        rows = rows_ref[0, item]
+        length = rows.shape[0] - 2 * reach
+        current = jax.nn.gelu(
+            tap_sum(rows, lambda k: first_ref[0, k], taps, length)
+        ).astype(jnp.bfloat16)
+        current = jnp.where(keeps[0], current, jnp.zeros((), jnp.bfloat16))
+        for depth_index in range(layers):
+            length = length - 2 * reach
+            update = jax.nn.gelu(
+                tap_sum(current, lambda k: hidden_ref[0, depth_index, k], taps, length)
+            )
+            current = (current[reach : reach + length].astype(jnp.float32) + update).astype(jnp.bfloat16)
+            if depth_index + 1 < len(keeps):
+                current = jnp.where(keeps[depth_index + 1], current, jnp.zeros((), jnp.bfloat16))
+        out_ref[item] += jnp.dot(current, mix_ref[0], preferred_element_type=jnp.float32)
+
+
+def conv_mix(extended, first_taps, hidden_taps, mix, rec_index, patches):
+    types, recordings, span, width = extended.shape
+    taps = first_taps.shape[1]
+    reach = taps // 2
+    layers = hidden_taps.shape[1]
+    total = patches * lax.axis_size("rec")
+    keeps = []
     for depth_index in range(layers):
-        update = jax.nn.gelu(valid_temporal(current, hidden_taps[:, depth_index]))
-        margin = margin - reach
-        current = (current[:, :, reach : current.shape[2] - reach].astype(jnp.float32) + update).astype(jnp.bfloat16)
-        if margin > 0:
-            current = masked(current, margin)
-    return current
+        margin = reach * (layers - depth_index)
+        length = span - 2 * reach * (depth_index + 1)
+        spot = rec_index * patches - margin + jnp.arange(length, dtype=jnp.int32)
+        keep = ((spot >= 0) & (spot < total)).astype(jnp.float32)
+        keeps.append(jnp.broadcast_to(keep[:, None], (length, EMB)))
+    mix_width = mix.shape[-1]
+    flops = 2 * types * recordings * (span * width * EMB * taps + 2 * span * EMB * EMB * taps + patches * EMB * mix_width)
+    return pl.pallas_call(
+        conv_mix_kernel,
+        grid=(types,),
+        in_specs=[
+            pl.BlockSpec((1, recordings, span, width), lambda m: (m, 0, 0, 0)),
+            pl.BlockSpec((1,) + first_taps.shape[1:], lambda m: (m, 0, 0, 0)),
+            pl.BlockSpec((1,) + hidden_taps.shape[1:], lambda m: (m, 0, 0, 0, 0)),
+            pl.BlockSpec((1,) + mix.shape[1:], lambda m: (m, 0, 0)),
+            pl.BlockSpec(keeps[0].shape, lambda m: (0, 0)),
+            pl.BlockSpec(keeps[1].shape, lambda m: (0, 0)),
+        ],
+        out_specs=pl.BlockSpec((recordings, patches, mix_width), lambda m: (0, 0, 0)),
+        out_shape=jax.ShapeDtypeStruct((recordings, patches, mix_width), jnp.float32),
+        compiler_params=pltpu.CompilerParams(dimension_semantics=("arbitrary",)),
+        cost_estimate=pl.CostEstimate(
+            flops=flops, transcendentals=types * recordings * span * EMB * (layers + 1),
+            bytes_accessed=extended.size * 2 + first_taps.size * 2 + hidden_taps.size * 2 + mix.size * 2 + recordings * patches * mix_width * 4,
+        ),
+    )(extended, first_taps, hidden_taps, mix, keeps[0], keeps[1])
 
 
 def local(
@@ -196,10 +238,8 @@
     patch_rows = rows.reshape(groups, recordings, patches, SAMP)
     first_taps = lax.all_gather(conv_in[:, 0], "rec", tiled=True)
     hidden_taps = lax.all_gather(conv_hid[:, 0], "rec", tiled=True)
-    encoded = halo_conv_stack(patch_rows, first_taps, hidden_taps, rec_index)
-    partial_value = jnp.einsum(
-        "mbpe,meo->bpo", encoded, mix_weight[:, 0], preferred_element_type=jnp.float32
-    )
+    extended = halo_rows(patch_rows)
+    partial_value = conv_mix(extended, first_taps, hidden_taps, mix_weight[:, 0], rec_index, patches)
     summed = lax.psum(partial_value, "chan")
     average = jnp.mean(summed, axis=-1, keepdims=True)
     centred = summed - average

time: 324 us -> 318 us (0.981)
  matrix products: 104 us -> 5.93 us
  Pallas kernels: 16.6 us -> 79.5 us
  waiting for transfers between devices: 101 us -> 133 us
    dot_general x15 -> x0, matrix products: 94.9 us -> none  [the longest x14 79.4 us: valid_temporal(): jnp.einsum('mbqc,mce->mbqe', rows[:, :, offset:offset + length], taps[:,...]
    pallas_call x0 -> x1, Pallas kernels: none -> 62.8 us  [conv_mix(): pl.pallas_call(conv_mix_kernel, grid=(types,), in_specs=[pl.BlockSpec((1,...]
    all_gather x1, waiting for transfers between devices: 24.4 us -> 58.2 us  [local(): hidden_taps = lax.all_gather(conv_hid[:, 0], 'rec', tiled=True)]
    convert_element_type x0 -> x1, local copies, waits for them, and re-layouts: none -> 5.99 us  [local(): rows = jnp.einsum('bms,bst->mbt', pick.astype(jnp.bfloat16), signal, pref...]
    squeeze x1 -> x0, local copies, waits for them, and re-layouts: 3.78 us -> none  [halo_conv_stack(): update = jax.nn.gelu(valid_temporal(current, hidden_taps[:, depth_index]))]
  transfers between devices with their start and end apart: 5 -> 5, of which waited for: 5 -> 5; matrix products, arithmetic and copies ran while one was open for 24% -> 14% of each run, Pallas kernels for 0% -> 0%
where the time goes in v1:
time: 318 us; the launch traced here: 317 us
  waiting for transfers between devices  133 us (42%)
  Pallas kernels  79.5 us (25%)
  local copies, waits for them, and re-layouts  40.1 us (13%)
  blocking collectives  23.7 us (7%)
  between operations  15.3 us (5%)
  other arithmetic  14.5 us (5%)
  matrix products  5.93 us (2%)
  starting transfers between devices  5.17 us (2%)
    pallas_call x1, Pallas kernels, conv_mix(): pl.pallas_call(conv_mix_kernel, grid=(types,), in_specs=[pl.BlockSpec((1,...  62.8 us
    all_gather x1, waiting for transfers between devices, local(): hidden_taps = lax.all_gather(conv_hid[:, 0], 'rec', tiled=True)  58.2 us
    psum x1, waiting for transfers between devices, local(): summed = lax.psum(partial_value, 'chan')  57.7 us
    all_gather x1, blocking collectives, crf_forward(): gathered = lax.all_gather(transfer, 'rec')  23.7 us
    reshape x1, local copies, waits for them, and re-layouts, local(): patch_rows = rows.reshape(groups, recordings, patches, SAMP)  20.3 us
    ppermute x2, waiting for transfers between devices, neighbour_shift(): return lax.ppermute(block, axis, route)  14.5 us
    pallas_call x1, Pallas kernels, crf_forward(): pl.pallas_call(prefix_kernel, out_shape=(jax.ShapeDtypeStruct((patches, S...  14.2 us
    concatenate x1, other arithmetic, halo_rows(): return jnp.concatenate([from_left, patch_rows, from_right], axis=2)  7.54 us
  transfers between devices with their start and end apart: 5, of which 5 were waited for; matrix products, arithmetic and copies ran while one was open for 14% of the time, Pallas kernels for 0%

profile of v1, /device:TPU:0, one launch (start us, length us, event | category | flops | bytes accessed | tf_op | source)
XLA Modules:
  0.0 317.2 jit_solution(2088914892987645217)
XLA Ops:
  7.2 0.7 all-gather.6.cloned.1.call-update
  8.0 0.7 all-gather.8.cloned.1.call-update
  8.7 0.7 broadcast_compare_fusion
  9.5 3.8 %fusion = bf16[16,4,38400]{2,0,1:T(8,128)(2,1)S(1)} fusion(bf16[4,16,38400]{2,1,0:T(8,128)(2,1)} %param.13, s32[4,16]{1,0:T(4,128)} %bitcast.47, pred[4,16]{1,0:T(4,128)(4,1)S(1)} %broadcast_compare_fusion), kind=kOutput, calls=%fused_computation.1 | convolution fusion | flops 81102848 | bytes 9830720 | tf_op jit(solution)/shard_map/bms,bst->mbt/dot_general | solution.py:235
  13.3 6.0 %copy.34 = bf16[16,4,38400]{2,1,0:T(4,128)(2,1)} copy(bf16[16,4,38400]{2,0,1:T(8,128)(2,1)S(1)} %fusion) | data formatting | bytes 9830400 | tf_op jit(solution)/shard_map/convert_element_type | solution.py:237
  19.3 20.3 %reshape.147 = bf16[16,4,192,200]{3,2,1,0:T(8,128)(2,1)} reshape(bf16[16,4,38400]{2,1,0:T(4,128)(2,1)} %copy.34) | data formatting | bytes 9830400 | tf_op jit(solution)/shard_map/reshape | solution.py:238
  39.5 1.1 fusion.32
  40.6 3.6 %collective-permute-start = (bf16[16,4,6,200]{3,2,1,0:T(8,128)(2,1)S(1)}, bf16[16,4,6,200]{3,2,1,0:T(8,128)(2,1)S(1)}, u32[]{:S(2)}, u32[]{:S(2)}) collective-permute-start(bf16[16,4,6,200]{3,2,1,0:T(8,128)(2,1)S(1)} %get-tuple-element.10), channel_id=1, source_target_pairs={{0,8},{8,16},{16,24},{24,32},{32,40},{40,48},{48,56},{56,64},{64,7... | collective-permute-start | bytes 460808 | tf_op jit(solution)/shard_map/ppermute | solution.py:129
  44.2 1.5 collective-permute-start.1
  45.9 0.1 copy.38
  46.0 10.0 %collective-permute-done = bf16[16,4,6,200]{3,2,1,0:T(8,128)(2,1)S(1)} collective-permute-done((bf16[16,4,6,200]{3,2,1,0:T(8,128)(2,1)S(1)}, bf16[16,4,6,200]{3,2,1,0:T(8,128)(2,1)S(1)}, u32[]{:S(2)}, u32[]{:S(2)}) %collective-permute-start) | collective-permute-done | bytes 153632 | tf_op jit(solution)/shard_map/ppermute | solution.py:129
  56.0 4.5 %collective-permute-done.1 = bf16[16,4,6,200]{3,2,1,0:T(8,128)(2,1)S(1)} collective-permute-done((bf16[16,4,6,200]{3,2,1,0:T(8,128)(2,1)S(1)}, bf16[16,4,6,200]{3,2,1,0:T(8,128)(2,1)S(1)}, u32[]{:S(2)}, u32[]{:S(2)}) %collective-permute-start.1) | collective-permute-done | bytes 153632 | tf_op jit(solution)/shard_map/ppermute | solution.py:129
  60.4 7.5 %pad_maximum_fusion.rows_ref = bf16[16,4,204,200]{3,2,1,0:T(8,128)(2,1)} fusion(bf16[16,4,6,200]{3,2,1,0:T(8,128)(2,1)S(1)} %collective-permute-done.1, bf16[16,4,192,200]{3,2,1,0:T(8,128)(2,1)} %reshape.147, bf16[16,4,6,200]{3,2,1,0:T(8,128)(2,1)S(1)} %collective-permute-done), kind=kLoop, calls=%fused_computation.2 | loop fusion | flops 15667200 | bytes 10444800 | tf_op jit(solution)/shard_map/concatenate | solution.py:137
  68.0 1.3 all-gather.6.cloned.1.call-done
  69.3 58.2 %all-gather.8.cloned.1.call-done = bf16[16,1,2,5,128,128]{5,4,3,2,1,0:T(8,128)(2,1)} async-done(((bf16[1,1,2,5,128,128]{5,4,3,2,1,0:T(8,128)(2,1)}), bf16[16,1,2,5,128,128]{5,4,3,2,1,0:T(8,128)(2,1)}) %all-gather.8.cloned.1.call-update) | async-done | bytes 5242896 | tf_op jit(solution)/shard_map/all_gather | solution.py:240
  127.5 0.7 broadcast_in_dim.27.keep_a_ref
  128.2 0.7 broadcast_in_dim.28.keep_b_ref
  128.9 62.8 %shard_map.140 = f32[4,192,512]{2,1,0:T(8,128)} custom-call(bf16[16,4,204,200]{3,2,1,0:T(8,128)(2,1)} %pad_maximum_fusion.rows_ref, bf16[16,5,200,128]{3,2,1,0:T(8,128)(2,1)} %bitcast.50, bf16[16,2,5,128,128]{4,3,2,1,0:T(8,128)(2,1)} %bitcast.49, bf16[16,128,512]{2,1,0:T(8,128)(2,1)} %bitcast.51, f32[200,128]{1,0:T(8,128)} %broadcast_in_dim.27.keep_a_ref, ...), custom_call_target="tpu_custom_call" | custom-call | flops 9231138816 | bytes 18231296 | tf_op jit(solution)/shard_map/pallas_call | solution.py:190
  191.8 0.7 copy-done.3
  192.5 0.1 copy.37
  192.6 0.6 pad.27
  193.3 0.6 pad.26
  193.9 0.6 pad.24.start_ref
  194.5 0.6 reduce_max.27
  195.1 1.2 exponential_reduce_fusion.2
  197.8 0.6 pad.23.prior_ref
  198.4 57.7 %all-reduce.8.cloned.1.call-done = f32[4,192,512]{2,1,0:T(8,128)} async-done(((f32[4,192,512]{2,1,0:T(8,128)}), f32[4,192,512]{2,1,0:T(8,128)}) %all-reduce.8.cloned.1.call-update) | async-done | bytes 1572880 | tf_op jit(solution)/shard_map/psum | solution.py:243
  256.0 1.7 reduce_sum.46
  257.8 0.1 copy-done.1
  257.9 0.4 multiply_reduce_fusion
  258.3 2.1 fusion.11
  260.6 0.3 copy.36
  260.9 1.0 pad.25.emit_ref
  261.9 0.7 broadcast_in_dim.21.within_ref
  262.6 0.7 broadcast_in_dim.22.between_ref
  263.2 14.2 %shard_map.141 = (f32[192,5,128]{2,1,0:T(8,128)}, f32[192,1,128]{2,1,0:T(1,128)}) custom-call(f32[5,5,128]{2,1,0:T(8,128)} %broadcast_in_dim.21.within_ref, f32[5,5,128]{2,1,0:T(8,128)} %broadcast_in_dim.22.between_ref, f32[5,128]{1,0:T(8,128)} %pad.24.start_ref, f32[192,5,128]{2,1,0:T(8,128)} %pad.25.emit_ref, f32[192,1,128]{2,1,0:T(1,128)} %bitcast.45, ...), custom_call_target="tpu_custom_call" | custom-call | flops 15728640 | bytes 1376256 | tf_op jit(solution)/shard_map/pallas_call | solution.py:91
  277.4 0.7 slice.30
  278.1 0.1 copy.39
  278.2 0.6 slice_reduce_fusion
  279.0 23.7 %all-gather.2 = f32[80,5,4]{1,2,0:T(4,128)S(1)} all-gather(f32[5,5,4]{1,2,0:T(4,128)S(1)} %add_bitcast_fusion), channel_id=4, replica_groups=mesh['rec'=16,'chan'=8] {'rec'}, dimensions={0}, use_global_device_ids=true | all-gather | bytes 6800 | tf_op jit(solution)/shard_map/all_gather | solution.py:106
  302.8 0.6 copy.40
  303.4 0.7 pad.28.mats_ref
  304.1 1.0 copy.41
  305.1 0.3 copy.42
  305.4 2.5 shard_map.142
  307.9 0.7 dynamic-slice_bitcast_fusion
  308.9 0.6 bitcast_subtract_fusion
  309.5 1.2 bitcast_divide_fusion
  (50 shorter events, 0.9 us)
Async XLA Ops:
  7.2 251.2 %copy-start = (f32[512,5]{0,1:T(8,128)S(1)}, f32[512,5]{0,1:T(8,128)}, u32[]{:S(2)}) copy-start(f32[512,5]{0,1:T(8,128)} %param.22) | copy-start | bytes 30724
  7.2 62.1 %all-gather.6.cloned.1.call-start = ((), (), s32[]{:S(2)}) async-start(), calls=%async_computation.1 | async-start | bytes 4352000 | tf_op jit(solution)/shard_map/all_gather | solution.py:239
  7.9 119.6 %all-gather.8.cloned.1.call-start = ((), (), s32[]{:S(2)}) async-start(), calls=%async_computation.2 | async-start | bytes 5570560 | tf_op jit(solution)/shard_map/all_gather | solution.py:240
  8.7 247.4 %all-reduce.8.cloned.1.call-start = ((), (), s32[]{:S(2)}) async-start(), calls=%async_computation | async-start | bytes 3145728 | tf_op jit(solution)/shard_map/psum | solution.py:243
  19.3 26.5 %copy-start.6 = (s32[4]{0:T(128)S(1)}, s32[4]{0:T(128)}, u32[]{:S(2)}) copy-start(s32[4]{0:T(128)} %param.16) | copy-start | bytes 52
  40.6 15.3 %collective-permute-start = (bf16[16,4,6,200]{3,2,1,0:T(8,128)(2,1)S(1)}, bf16[16,4,6,200]{3,2,1,0:T(8,128)(2,1)S(1)}, u32[]{:S(2)}, u32[]{:S(2)}) collective-permute-start(bf16[16,4,6,200]{3,2,1,0:T(8,128)(2,1)S(1)} %get-tuple-element.10), channel_id=1, source_target_pairs={{0,8},{8,16},{16,24},{24,32},{32,40},{40,48},{48,56},{56,64},{64,7... | collective-permute-start | bytes 460808 | tf_op jit(solution)/shard_map/ppermute | solution.py:129
  44.2 16.2 %collective-permute-start.1 = (bf16[16,4,6,200]{3,2,1,0:T(8,128)(2,1)S(1)}, bf16[16,4,6,200]{3,2,1,0:T(8,128)(2,1)S(1)}, u32[]{:S(2)}, u32[]{:S(2)}) collective-permute-start(bf16[16,4,6,200]{3,2,1,0:T(8,128)(2,1)S(1)} %get-tuple-element.11), channel_id=1, source_target_pairs={{8,0},{16,8},{24,16},{32,24},{40,32},{48,40},{56,48},{64,56},{72,6... | collective-permute-start | bytes 460808 | tf_op jit(solution)/shard_map/ppermute | solution.py:129
  191.8 0.7 copy-start.3
  191.8 2.7 copy-start.8
  198.4 60.0 %copy-start.7 = (f32[512]{0:T(512)S(1)}, f32[512]{0:T(512)}, u32[]{:S(2)}) copy-start(f32[512]{0:T(512)} %param.21) | copy-start | bytes 6148
  256.0 1.9 copy-start.1
  260.5 1.4 copy-start.4
  260.5 2.1 copy-start.5
  277.4 27.7 %copy-start.2 = (f32[192,5,128]{2,1,0:T(8,128)S(1)}, f32[192,5,128]{2,1,0:T(8,128)}, u32[]{:S(2)}) copy-start(f32[192,5,128]{2,1,0:T(8,128)} %get-tuple-element.6) | copy-start | bytes 1474564
Sparse Core Ops, SparseCore 0:
  10.2 59.0 all-gather.5
  71.5 55.9 all-gather.7
  191.9 64.0 all-reduce.7

commit v2 on v1

--- a/solution.py
+++ b/solution.py
@@ -145,67 +145,100 @@
     return accumulated
 
 
-def conv_mix_kernel(rows_ref, first_ref, hidden_ref, mix_ref, keep_a_ref, keep_b_ref, out_ref):
+def first_kernel(rows_ref, taps_ref, keep_ref, out_ref):
+    taps = taps_ref.shape[1]
+    keep = keep_ref[...] > 0.5
+    for item in range(rows_ref.shape[1]):
+        rows = rows_ref[0, item]
+        length = rows.shape[0] - 2 * (taps // 2)
+        value = jax.nn.gelu(tap_sum(rows, lambda k: taps_ref[0, k], taps, length)).astype(jnp.bfloat16)
+        out_ref[0, item] = jnp.where(keep, value, jnp.zeros((), jnp.bfloat16))
+
+
+def residual_layer(current, taps_ref, taps):
+    reach = taps // 2
+    length = current.shape[0] - 2 * reach
+    update = jax.nn.gelu(tap_sum(current, lambda k: taps_ref[0, k], taps, length))
+    return (current[reach : reach + length].astype(jnp.float32) + update).astype(jnp.bfloat16)
+
+
+def hidden_kernel(rows_ref, taps_ref, keep_ref, out_ref):
+    taps = taps_ref.shape[1]
+    keep = keep_ref[...] > 0.5
+    for item in range(rows_ref.shape[1]):
+        value = residual_layer(rows_ref[0, item], taps_ref, taps)
+        out_ref[0, item] = jnp.where(keep, value, jnp.zeros((), jnp.bfloat16))
+
+
+def last_kernel(rows_ref, taps_ref, mix_ref, out_ref):
     @pl.when(pl.program_id(0) == 0)
     def _():
         out_ref[...] = jnp.zeros_like(out_ref)
 
-    taps = first_ref.shape[1]
-    reach = taps // 2
-    layers = hidden_ref.shape[1]
-    keeps = [keep_a_ref[...] > 0.5, keep_b_ref[...] > 0.5]
+    taps = taps_ref.shape[1]
     for item in range(rows_ref.shape[1]):
-        rows = rows_ref[0, item]
-        length = rows.shape[0] - 2 * reach
-        current = jax.nn.gelu(
-            tap_sum(rows, lambda k: first_ref[0, k], taps, length)
-        ).astype(jnp.bfloat16)
-        current = jnp.where(keeps[0], current, jnp.zeros((), jnp.bfloat16))
-        for depth_index in range(layers):
-            length = length - 2 * reach
-            update = jax.nn.gelu(
-                tap_sum(current, lambda k: hidden_ref[0, depth_index, k], taps, length)
-            )
-            current = (current[reach : reach + length].astype(jnp.float32) + update).astype(jnp.bfloat16)
-            if depth_index + 1 < len(keeps):
-                current = jnp.where(keeps[depth_index + 1], current, jnp.zeros((), jnp.bfloat16))
-        out_ref[item] += jnp.dot(current, mix_ref[0], preferred_element_type=jnp.float32)
-
-
-def conv_mix(extended, first_taps, hidden_taps, mix, rec_index, patches):
+        value = residual_layer(rows_ref[0, item], taps_ref, taps)
+        out_ref[item] += jnp.dot(value, mix_ref[0], preferred_element_type=jnp.float32)
+
+
+def edge_keep(length, margin, rec_index, patches):
+    total = patches * lax.axis_size("rec")
+    spot = rec_index * patches - margin + jnp.arange(length, dtype=jnp.int32)
+    keep = ((spot >= 0) & (spot < total)).astype(jnp.float32)
+    return jnp.broadcast_to(keep[:, None], (length, EMB))
+
+
+def per_type_call(kernel, rows, taps, side, out_block, out_shape, out_map, flops):
+    types, recordings = rows.shape[:2]
+    side_spec = (
+        pl.BlockSpec((1,) + side.shape[1:], lambda m: (m, 0, 0))
+        if side.ndim == 3 and side.shape[0] == types and kernel is last_kernel
+        else pl.BlockSpec(side.shape, lambda m: (0, 0))
+    )
+    return pl.pallas_call(
+        kernel,
+        grid=(types,),
+        in_specs=[
+            pl.BlockSpec((1,) + rows.shape[1:], lambda m: (m, 0, 0, 0)),
+            pl.BlockSpec((1,) + taps.shape[1:], lambda m: (m, 0, 0, 0)),
+            side_spec,
+        ],
+        out_specs=pl.BlockSpec(out_block, out_map),
+        out_shape=out_shape,
+        compiler_params=pltpu.CompilerParams(dimension_semantics=("arbitrary",)),
+        cost_estimate=pl.CostEstimate(
+            flops=flops, transcendentals=rows.shape[0] * rows.shape[1] * rows.shape[2] * EMB,
+            bytes_accessed=rows.size * 2 + taps.size * 2 + side.size * 2 + out_shape.size * 4,
+        ),
+    )(rows, taps, side)
+
+
+def conv_mix(extended, first_taps, hidden_list, mix, rec_index, patches):
     types, recordings, span, width = extended.shape
     taps = first_taps.shape[1]
     reach = taps // 2
-    layers = hidden_taps.shape[1]
-    total = patches * lax.axis_size("rec")
-    keeps = []
-    for depth_index in range(layers):
-        margin = reach * (layers - depth_index)
-        length = span - 2 * reach * (depth_index + 1)
-        spot = rec_index * patches - margin + jnp.arange(length, dtype=jnp.int32)
-        keep = ((spot >= 0) & (spot < total)).astype(jnp.float32)
-        keeps.append(jnp.broadcast_to(keep[:, None], (length, EMB)))
+    layers = len(hidden_list)
+    length = span - 2 * reach
+    margin = reach * layers
+    current = per_type_call(
+        first_kernel, extended, first_taps, edge_keep(length, margin, rec_index, patches),
+        (1, recordings, length, EMB), jax.ShapeDtypeStruct((types, recordings, length, EMB), jnp.bfloat16),
+        lambda m: (m, 0, 0, 0), 2 * types * recordings * span * width * EMB * taps,
+    )
+    for depth_index in range(layers - 1):
+        length = length - 2 * reach
+        margin = margin - reach
+        current = per_type_call(
+            hidden_kernel, current, hidden_list[depth_index], edge_keep(length, margin, rec_index, patches),
+            (1, recordings, length, EMB), jax.ShapeDtypeStruct((types, recordings, length, EMB), jnp.bfloat16),
+            lambda m: (m, 0, 0, 0), 2 * types * recordings * span * EMB * EMB * taps,
+        )
     mix_width = mix.shape[-1]
-    flops = 2 * types * recordings * (span * width * EMB * taps + 2 * span * EMB * EMB * taps + patches * EMB * mix_width)
-    return pl.pallas_call(
-        conv_mix_kernel,
-        grid=(types,),
-        in_specs=[
-            pl.BlockSpec((1, recordings, span, width), lambda m: (m, 0, 0, 0)),
-            pl.BlockSpec((1,) + first_taps.shape[1:], lambda m: (m, 0, 0, 0)),
-            pl.BlockSpec((1,) + hidden_taps.shape[1:], lambda m: (m, 0, 0, 0, 0)),
-            pl.BlockSpec((1,) + mix.shape[1:], lambda m: (m, 0, 0)),
-            pl.BlockSpec(keeps[0].shape, lambda m: (0, 0)),
-            pl.BlockSpec(keeps[1].shape, lambda m: (0, 0)),
-        ],
-        out_specs=pl.BlockSpec((recordings, patches, mix_width), lambda m: (0, 0, 0)),
-        out_shape=jax.ShapeDtypeStruct((recordings, patches, mix_width), jnp.float32),
-        compiler_params=pltpu.CompilerParams(dimension_semantics=("arbitrary",)),
-        cost_estimate=pl.CostEstimate(
-            flops=flops, transcendentals=types * recordings * span * EMB * (layers + 1),
-            bytes_accessed=extended.size * 2 + first_taps.size * 2 + hidden_taps.size * 2 + mix.size * 2 + recordings * patches * mix_width * 4,
-        ),
-    )(extended, first_taps, hidden_taps, mix, keeps[0], keeps[1])
+    return per_type_call(
+        last_kernel, current, hidden_list[layers - 1], mix,
+        (recordings, patches, mix_width), jax.ShapeDtypeStruct((recordings, patches, mix_width), jnp.float32),
+        lambda m: (0, 0, 0), 2 * types * recordings * span * EMB * (EMB * taps + mix_width),
+    )
 
 
 def local(
@@ -237,9 +270,12 @@
     ).astype(jnp.bfloat16)
     patch_rows = rows.reshape(groups, recordings, patches, SAMP)
     first_taps = lax.all_gather(conv_in[:, 0], "rec", tiled=True)
-    hidden_taps = lax.all_gather(conv_hid[:, 0], "rec", tiled=True)
+    hidden_list = [
+        lax.all_gather(conv_hid[:, 0, depth_index], "rec", tiled=True)
+        for depth_index in range(conv_hid.shape[2])
+    ]
     extended = halo_rows(patch_rows)
-    partial_value = conv_mix(extended, first_taps, hidden_taps, mix_weight[:, 0], rec_index, patches)
+    partial_value = conv_mix(extended, first_taps, hidden_list, mix_weight[:, 0], rec_index, patches)
     summed = lax.psum(partial_value, "chan")
     average = jnp.mean(summed, axis=-1, keepdims=True)
     centred = summed - average

time: 318 us -> 317 us (level)
  Pallas kernels: 79.5 us -> 76.3 us
    pallas_call x1 -> x3, Pallas kernels: 62.8 us -> 59.6 us  [per_type_call(): pl.pallas_call(kernel, grid=(types,), in_specs=[pl.BlockSpec((1,) + rows....]
    all_gather x1 -> x2, waiting for transfers between devices: 58.2 us -> 60.2 us  [local(): lax.all_gather(conv_hid[:, 0, depth_index], 'rec', tiled=True)]
  transfers between devices with their start and end apart: 5 -> 6, of which waited for: 5 -> 5; matrix products, arithmetic and copies ran while one was open for 14% -> 15% of each run, Pallas kernels for 0% -> 11%
where the time goes in v2:
time: 317 us; the launch traced here: 316 us
  waiting for transfers between devices  133 us (42%)
  Pallas kernels  76.3 us (24%)
  local copies, waits for them, and re-layouts  41.8 us (13%)
  blocking collectives  23.7 us (7%)
  between operations  15.3 us (5%)
  other arithmetic  14.5 us (5%)
  matrix products  5.94 us (2%)
  starting transfers between devices  5.21 us (2%)
    all_gather x2, waiting for transfers between devices, local(): lax.all_gather(conv_hid[:, 0, depth_index], 'rec', tiled=True)  60.2 us
    pallas_call x3, Pallas kernels, per_type_call(): pl.pallas_call(kernel, grid=(types,), in_specs=[pl.BlockSpec((1,) + rows....  59.6 us
    psum x1, waiting for transfers between devices, local(): summed = lax.psum(partial_value, 'chan')  57.3 us
    all_gather x1, blocking collectives, crf_forward(): gathered = lax.all_gather(transfer, 'rec')  23.7 us
    reshape x1, local copies, waits for them, and re-layouts, local(): patch_rows = rows.reshape(groups, recordings, patches, SAMP)  20.3 us
    ppermute x2, waiting for transfers between devices, neighbour_shift(): return lax.ppermute(block, axis, route)  14.4 us
    pallas_call x1, Pallas kernels, crf_forward(): pl.pallas_call(prefix_kernel, out_shape=(jax.ShapeDtypeStruct((patches, S...  14.2 us
    concatenate x1, other arithmetic, halo_rows(): return jnp.concatenate([from_left, patch_rows, from_right], axis=2)  7.55 us
  transfers between devices with their start and end apart: 6, of which 5 were waited for; matrix products, arithmetic and copies ran while one was open for 15% of the time, Pallas kernels for 11%

profile of v2, /device:TPU:0, one launch (start us, length us, event | category | flops | bytes accessed | tf_op | source)
XLA Modules:
  0.0 316.1 jit_solution(12618263315235399780)
XLA Ops:
  7.2 0.7 all-gather.8.cloned.1.call-update
  8.0 1.8 fusion.33
  9.8 0.7 all-gather.12.cloned.1.call-update
  10.5 0.7 broadcast_compare_fusion
  11.3 3.8 %fusion = bf16[16,4,38400]{2,0,1:T(8,128)(2,1)S(1)} fusion(bf16[4,16,38400]{2,1,0:T(8,128)(2,1)} %param.13, s32[4,16]{1,0:T(4,128)} %bitcast.50, pred[4,16]{1,0:T(4,128)(4,1)S(1)} %broadcast_compare_fusion), kind=kOutput, calls=%fused_computation.1 | convolution fusion | flops 81102848 | bytes 9830720 | tf_op jit(solution)/shard_map/bms,bst->mbt/dot_general | solution.py:268
  15.1 6.0 %copy.36 = bf16[16,4,38400]{2,1,0:T(4,128)(2,1)} copy(bf16[16,4,38400]{2,0,1:T(8,128)(2,1)S(1)} %fusion) | data formatting | bytes 9830400 | tf_op jit(solution)/shard_map/convert_element_type | solution.py:270
  21.1 20.3 %reshape.147 = bf16[16,4,192,200]{3,2,1,0:T(8,128)(2,1)} reshape(bf16[16,4,38400]{2,1,0:T(4,128)(2,1)} %copy.36) | data formatting | bytes 9830400 | tf_op jit(solution)/shard_map/reshape | solution.py:271
  41.4 1.1 fusion.32
  42.5 3.6 %collective-permute-start = (bf16[16,4,6,200]{3,2,1,0:T(8,128)(2,1)S(1)}, bf16[16,4,6,200]{3,2,1,0:T(8,128)(2,1)S(1)}, u32[]{:S(2)}, u32[]{:S(2)}) collective-permute-start(bf16[16,4,6,200]{3,2,1,0:T(8,128)(2,1)S(1)} %get-tuple-element.10), channel_id=1, source_target_pairs={{0,8},{8,16},{16,24},{24,32},{32,40},{40,48},{48,56},{56,64},{64,7... | collective-permute-start | bytes 460808 | tf_op jit(solution)/shard_map/ppermute | solution.py:129
  46.1 1.5 collective-permute-start.1
  47.8 10.1 %collective-permute-done = bf16[16,4,6,200]{3,2,1,0:T(8,128)(2,1)S(1)} collective-permute-done((bf16[16,4,6,200]{3,2,1,0:T(8,128)(2,1)S(1)}, bf16[16,4,6,200]{3,2,1,0:T(8,128)(2,1)S(1)}, u32[]{:S(2)}, u32[]{:S(2)}) %collective-permute-start) | collective-permute-done | bytes 153632 | tf_op jit(solution)/shard_map/ppermute | solution.py:129
  57.9 4.3 %collective-permute-done.1 = bf16[16,4,6,200]{3,2,1,0:T(8,128)(2,1)S(1)} collective-permute-done((bf16[16,4,6,200]{3,2,1,0:T(8,128)(2,1)S(1)}, bf16[16,4,6,200]{3,2,1,0:T(8,128)(2,1)S(1)}, u32[]{:S(2)}, u32[]{:S(2)}) %collective-permute-start.1) | collective-permute-done | bytes 153632 | tf_op jit(solution)/shard_map/ppermute | solution.py:129
  62.3 7.5 %pad_maximum_fusion.rows_ref = bf16[16,4,204,200]{3,2,1,0:T(8,128)(2,1)} fusion(bf16[16,4,6,200]{3,2,1,0:T(8,128)(2,1)S(1)} %collective-permute-done.1, bf16[16,4,192,200]{3,2,1,0:T(8,128)(2,1)} %reshape.147, bf16[16,4,6,200]{3,2,1,0:T(8,128)(2,1)S(1)} %collective-permute-done), kind=kLoop, calls=%fused_computation.2 | loop fusion | flops 15667200 | bytes 10444800 | tf_op jit(solution)/shard_map/concatenate | solution.py:137
  69.8 0.7 broadcast_in_dim.27.keep_ref
  70.5 17.1 %shard_map.140.rows_ref = bf16[16,4,200,128]{3,2,1,0:T(8,128)(2,1)} custom-call(bf16[16,4,204,200]{3,2,1,0:T(8,128)(2,1)} %pad_maximum_fusion.rows_ref, bf16[16,5,200,128]{3,2,1,0:T(8,128)(2,1)} %bitcast.43, f32[200,128]{1,0:T(8,128)} %broadcast_in_dim.27.keep_ref), custom_call_target="tpu_custom_call" | custom-call | flops 3342336000 | bytes 15923200 | tf_op jit(solution)/shard_map/pallas_call | solution.py:198
  87.7 29.7 %all-gather.10.cloned.1.call-done = bf16[16,1,1,5,128,128]{5,4,3,2,1,0:T(8,128)(2,1)} async-done(((bf16[1,1,1,5,128,128]{5,4,3,2,1,0:T(8,128)(2,1)}), bf16[16,1,1,5,128,128]{5,4,3,2,1,0:T(8,128)(2,1)}) %all-gather.10.cloned.1.call-update) | async-done | bytes 2621456 | tf_op jit(solution)/shard_map/all_gather | solution.py:274
  117.4 0.7 broadcast_in_dim.28.keep_ref
  118.1 16.5 %shard_map.141.rows_ref = bf16[16,4,196,128]{3,2,1,0:T(8,128)(2,1)} custom-call(bf16[16,4,200,128]{3,2,1,0:T(8,128)(2,1)} %shard_map.140.rows_ref, bf16[16,5,128,128]{3,2,1,0:T(8,128)(2,1)} %bitcast.44, f32[196,128]{1,0:T(8,128)} %broadcast_in_dim.28.keep_ref), custom_call_target="tpu_custom_call" | custom-call | flops 2139095040 | bytes 12370944 | tf_op jit(solution)/shard_map/pallas_call | solution.py:198
  134.6 30.5 %all-gather.12.cloned.1.call-done = bf16[16,1,1,5,128,128]{5,4,3,2,1,0:T(8,128)(2,1)} async-done(((bf16[1,1,1,5,128,128]{5,4,3,2,1,0:T(8,128)(2,1)}), bf16[16,1,1,5,128,128]{5,4,3,2,1,0:T(8,128)(2,1)}) %all-gather.12.cloned.1.call-update) | async-done | bytes 2621456 | tf_op jit(solution)/shard_map/all_gather | solution.py:274
  165.1 26.0 %shard_map.142 = f32[4,192,512]{2,1,0:T(8,128)} custom-call(bf16[16,4,196,128]{3,2,1,0:T(8,128)(2,1)} %shard_map.141.rows_ref, bf16[16,5,128,128]{3,2,1,0:T(8,128)(2,1)} %bitcast.52, bf16[16,128,512]{2,1,0:T(8,128)(2,1)} %bitcast.53), custom_call_target="tpu_custom_call" | custom-call | flops 3850371072 | bytes 9502720 | tf_op jit(solution)/shard_map/pallas_call | solution.py:198
  191.2 0.7 copy-done.3
  192.0 0.6 pad.27
  192.6 0.6 pad.26
  193.2 0.6 pad.24.start_ref
  193.8 0.6 reduce_max.27
  194.4 1.2 exponential_reduce_fusion.2
  197.1 0.6 pad.23.prior_ref
  197.7 57.3 %all-reduce.8.cloned.1.call-done = f32[4,192,512]{2,1,0:T(8,128)} async-done(((f32[4,192,512]{2,1,0:T(8,128)}), f32[4,192,512]{2,1,0:T(8,128)}) %all-reduce.8.cloned.1.call-update) | async-done | bytes 1572880 | tf_op jit(solution)/shard_map/psum | solution.py:279
  255.0 1.7 reduce_sum.46
  256.8 0.1 copy-done.1
  256.9 0.4 multiply_reduce_fusion
  257.3 2.1 fusion.11
  259.5 0.3 copy.38
  259.9 1.0 pad.25.emit_ref
  260.8 0.7 broadcast_in_dim.21.within_ref
  261.5 0.7 broadcast_in_dim.22.between_ref
  262.2 14.2 %shard_map.143 = (f32[192,5,128]{2,1,0:T(8,128)}, f32[192,1,128]{2,1,0:T(1,128)}) custom-call(f32[5,5,128]{2,1,0:T(8,128)} %broadcast_in_dim.21.within_ref, f32[5,5,128]{2,1,0:T(8,128)} %broadcast_in_dim.22.between_ref, f32[5,128]{1,0:T(8,128)} %pad.24.start_ref, f32[192,5,128]{2,1,0:T(8,128)} %pad.25.emit_ref, f32[192,1,128]{2,1,0:T(1,128)} %bitcast.48, ...), custom_call_target="tpu_custom_call" | custom-call | flops 15728640 | bytes 1376256 | tf_op jit(solution)/shard_map/pallas_call | solution.py:91
  276.3 0.7 slice.38
  277.2 0.6 slice_reduce_fusion
  278.0 23.7 %all-gather.3 = f32[80,5,4]{1,2,0:T(4,128)S(1)} all-gather(f32[5,5,4]{1,2,0:T(4,128)S(1)} %add_bitcast_fusion), channel_id=5, replica_groups=mesh['rec'=16,'chan'=8] {'rec'}, dimensions={0}, use_global_device_ids=true | all-gather | bytes 6800 | tf_op jit(solution)/shard_map/all_gather | solution.py:106
  301.7 0.6 copy.42
  302.3 0.7 pad.28.mats_ref
  303.1 1.0 copy.43
  304.1 0.3 copy.44
  304.4 2.5 shard_map.144
  306.9 0.7 dynamic-slice_bitcast_fusion
  307.8 0.6 bitcast_subtract_fusion
  308.4 1.2 bitcast_divide_fusion
  (56 shorter events, 1.3 us)
Async XLA Ops:
  7.2 250.1 %copy-start = (f32[512,5]{0,1:T(8,128)S(1)}, f32[512,5]{0,1:T(8,128)}, u32[]{:S(2)}) copy-start(f32[512,5]{0,1:T(8,128)} %param.22) | copy-start | bytes 30724
  7.2 62.6 %all-gather.8.cloned.1.call-start = ((), (), s32[]{:S(2)}) async-start(), calls=%async_computation.1 | async-start | bytes 4352000 | tf_op jit(solution)/shard_map/all_gather | solution.py:272
  7.9 109.5 %all-gather.10.cloned.1.call-start = ((), (), s32[]{:S(2)}) async-start(), calls=%async_computation.2 | async-start | bytes 2785280 | tf_op jit(solution)/shard_map/all_gather | solution.py:274
  9.7 155.4 %all-gather.12.cloned.1.call-start = ((), (), s32[]{:S(2)}) async-start(), calls=%async_computation.3 | async-start | bytes 2785280 | tf_op jit(solution)/shard_map/all_gather | solution.py:274
  10.5 244.5 %all-reduce.8.cloned.1.call-start = ((), (), s32[]{:S(2)}) async-start(), calls=%async_computation | async-start | bytes 3145728 | tf_op jit(solution)/shard_map/psum | solution.py:279
  21.1 26.5 %copy-start.6 = (s32[4]{0:T(128)S(1)}, s32[4]{0:T(128)}, u32[]{:S(2)}) copy-start(s32[4]{0:T(128)} %param.16) | copy-start | bytes 52
  42.5 15.4 %collective-permute-start = (bf16[16,4,6,200]{3,2,1,0:T(8,128)(2,1)S(1)}, bf16[16,4,6,200]{3,2,1,0:T(8,128)(2,1)S(1)}, u32[]{:S(2)}, u32[]{:S(2)}) collective-permute-start(bf16[16,4,6,200]{3,2,1,0:T(8,128)(2,1)S(1)} %get-tuple-element.10), channel_id=1, source_target_pairs={{0,8},{8,16},{16,24},{24,32},{32,40},{40,48},{48,56},{56,64},{64,7... | collective-permute-start | bytes 460808 | tf_op jit(solution)/shard_map/ppermute | solution.py:129
  46.1 16.2 %collective-permute-start.1 = (bf16[16,4,6,200]{3,2,1,0:T(8,128)(2,1)S(1)}, bf16[16,4,6,200]{3,2,1,0:T(8,128)(2,1)S(1)}, u32[]{:S(2)}, u32[]{:S(2)}) collective-permute-start(bf16[16,4,6,200]{3,2,1,0:T(8,128)(2,1)S(1)} %get-tuple-element.11), channel_id=1, source_target_pairs={{8,0},{16,8},{24,16},{32,24},{40,32},{48,40},{56,48},{64,56},{72,6... | collective-permute-start | bytes 460808 | tf_op jit(solution)/shard_map/ppermute | solution.py:129
  191.1 0.7 copy-start.3
  191.1 2.7 copy-start.8
  197.7 59.6 %copy-start.7 = (f32[512]{0:T(512)S(1)}, f32[512]{0:T(512)}, u32[]{:S(2)}) copy-start(f32[512]{0:T(512)} %param.21) | copy-start | bytes 6148
  255.0 1.9 copy-start.1
  259.4 1.4 copy-start.4
  259.4 2.1 copy-start.5
  276.3 27.7 %copy-start.2 = (f32[192,5,128]{2,1,0:T(8,128)S(1)}, f32[192,5,128]{2,1,0:T(8,128)}, u32[]{:S(2)}) copy-start(f32[192,5,128]{2,1,0:T(8,128)} %get-tuple-element.6) | copy-start | bytes 1474564
Sparse Core Ops, SparseCore 0:
  10.2 59.0 all-gather.7
  71.5 45.8 all-gather.9
  119.6 45.4 all-gather.11
  191.3 63.6 all-reduce.7

commit v3 on v2

--- a/solution.py
+++ b/solution.py
@@ -270,10 +270,8 @@
     ).astype(jnp.bfloat16)
     patch_rows = rows.reshape(groups, recordings, patches, SAMP)
     first_taps = lax.all_gather(conv_in[:, 0], "rec", tiled=True)
-    hidden_list = [
-        lax.all_gather(conv_hid[:, 0, depth_index], "rec", tiled=True)
-        for depth_index in range(conv_hid.shape[2])
-    ]
+    hidden_taps = lax.all_gather(jnp.swapaxes(conv_hid[:, 0], 0, 1), "rec", axis=1, tiled=True)
+    hidden_list = [hidden_taps[depth_index] for depth_index in range(hidden_taps.shape[0])]
     extended = halo_rows(patch_rows)
     partial_value = conv_mix(extended, first_taps, hidden_list, mix_weight[:, 0], rec_index, patches)
     summed = lax.psum(partial_value, "chan")

time: 317 us -> 305 us (0.962)
  waiting for transfers between devices: 133 us -> 116 us
  local copies, waits for them, and re-layouts: 41.8 us -> 47.4 us
    all_gather x2 -> x1, waiting for transfers between devices: 60.2 us -> 40.3 us  [local(): lax.all_gather(jnp.swapaxes(conv_hid[:, 0], 0, 1), 'rec', axis=1, tiled=T...]
    slice x1, local copies, waits for them, and re-layouts: 1.76 us -> 6.96 us  [local(): hidden_taps[depth_index]]
  transfers between devices with their start and end apart: 6 -> 5, of which waited for: 5 -> 5; matrix products, arithmetic and copies ran while one was open for 15% -> 15% of each run, Pallas kernels for 11% -> 6%
where the time goes in v3:
time: 305 us; the launch traced here: 304 us
  waiting for transfers between devices  116 us (38%)
  Pallas kernels  76.3 us (25%)
  local copies, waits for them, and re-layouts  47.4 us (16%)
  blocking collectives  23.7 us (8%)
  between operations  15.3 us (5%)
  other arithmetic  14.5 us (5%)
  matrix products  5.93 us (2%)
  starting transfers between devices  5.17 us (2%)
    pallas_call x3, Pallas kernels, per_type_call(): pl.pallas_call(kernel, grid=(types,), in_specs=[pl.BlockSpec((1,) + rows....  59.6 us
    psum x1, waiting for transfers between devices, local(): summed = lax.psum(partial_value, 'chan')  58.3 us
    all_gather x1, waiting for transfers between devices, local(): lax.all_gather(jnp.swapaxes(conv_hid[:, 0], 0, 1), 'rec', axis=1, tiled=T...  40.3 us
    all_gather x1, blocking collectives, crf_forward(): gathered = lax.all_gather(transfer, 'rec')  23.7 us
    reshape x1, local copies, waits for them, and re-layouts, local(): patch_rows = rows.reshape(groups, recordings, patches, SAMP)  20.3 us
    ppermute x2, waiting for transfers between devices, neighbour_shift(): return lax.ppermute(block, axis, route)  14.5 us
    pallas_call x1, Pallas kernels, crf_forward(): pl.pallas_call(prefix_kernel, out_shape=(jax.ShapeDtypeStruct((patches, S...  14.2 us
    concatenate x1, other arithmetic, halo_rows(): return jnp.concatenate([from_left, patch_rows, from_right], axis=2)  7.54 us
  transfers between devices with their start and end apart: 5, of which 5 were waited for; matrix products, arithmetic and copies ran while one was open for 15% of the time, Pallas kernels for 6%

profile of v3, /device:TPU:0, one launch (start us, length us, event | category | flops | bytes accessed | tf_op | source)
XLA Modules:
  0.0 304.0 jit_solution(5156064006758212717)
XLA Ops:
  7.2 0.7 all-gather.6.cloned.1.call-update
  8.0 0.7 all-gather.8.cloned.1.call-update
  8.7 0.7 broadcast_compare_fusion
  9.5 3.8 %fusion = bf16[16,4,38400]{2,0,1:T(8,128)(2,1)S(1)} fusion(bf16[4,16,38400]{2,1,0:T(8,128)(2,1)} %param.13, s32[4,16]{1,0:T(4,128)} %bitcast.51, pred[4,16]{1,0:T(4,128)(4,1)S(1)} %broadcast_compare_fusion), kind=kOutput, calls=%fused_computation.1 | convolution fusion | flops 81102848 | bytes 9830720 | tf_op jit(solution)/shard_map/bms,bst->mbt/dot_general | solution.py:268
  13.3 6.0 %copy.32 = bf16[16,4,38400]{2,1,0:T(4,128)(2,1)} copy(bf16[16,4,38400]{2,0,1:T(8,128)(2,1)S(1)} %fusion) | data formatting | bytes 9830400 | tf_op jit(solution)/shard_map/convert_element_type | solution.py:270
  19.3 20.3 %reshape.147 = bf16[16,4,192,200]{3,2,1,0:T(8,128)(2,1)} reshape(bf16[16,4,38400]{2,1,0:T(4,128)(2,1)} %copy.32) | data formatting | bytes 9830400 | tf_op jit(solution)/shard_map/reshape | solution.py:271
  39.5 1.1 fusion.32
  40.6 3.6 %collective-permute-start = (bf16[16,4,6,200]{3,2,1,0:T(8,128)(2,1)S(1)}, bf16[16,4,6,200]{3,2,1,0:T(8,128)(2,1)S(1)}, u32[]{:S(2)}, u32[]{:S(2)}) collective-permute-start(bf16[16,4,6,200]{3,2,1,0:T(8,128)(2,1)S(1)} %get-tuple-element.10), channel_id=1, source_target_pairs={{0,8},{8,16},{16,24},{24,32},{32,40},{40,48},{48,56},{56,64},{64,7... | collective-permute-start | bytes 460808 | tf_op jit(solution)/shard_map/ppermute | solution.py:129
  44.2 1.5 collective-permute-start.1
  45.9 0.1 copy.36
  46.0 10.0 %collective-permute-done = bf16[16,4,6,200]{3,2,1,0:T(8,128)(2,1)S(1)} collective-permute-done((bf16[16,4,6,200]{3,2,1,0:T(8,128)(2,1)S(1)}, bf16[16,4,6,200]{3,2,1,0:T(8,128)(2,1)S(1)}, u32[]{:S(2)}, u32[]{:S(2)}) %collective-permute-start) | collective-permute-done | bytes 153632 | tf_op jit(solution)/shard_map/ppermute | solution.py:129
  56.0 4.5 %collective-permute-done.1 = bf16[16,4,6,200]{3,2,1,0:T(8,128)(2,1)S(1)} collective-permute-done((bf16[16,4,6,200]{3,2,1,0:T(8,128)(2,1)S(1)}, bf16[16,4,6,200]{3,2,1,0:T(8,128)(2,1)S(1)}, u32[]{:S(2)}, u32[]{:S(2)}) %collective-permute-start.1) | collective-permute-done | bytes 153632 | tf_op jit(solution)/shard_map/ppermute | solution.py:129
  60.4 7.5 %pad_maximum_fusion.rows_ref = bf16[16,4,204,200]{3,2,1,0:T(8,128)(2,1)} fusion(bf16[16,4,6,200]{3,2,1,0:T(8,128)(2,1)S(1)} %collective-permute-done.1, bf16[16,4,192,200]{3,2,1,0:T(8,128)(2,1)} %reshape.147, bf16[16,4,6,200]{3,2,1,0:T(8,128)(2,1)S(1)} %collective-permute-done), kind=kLoop, calls=%fused_computation.2 | loop fusion | flops 15667200 | bytes 10444800 | tf_op jit(solution)/shard_map/concatenate | solution.py:137
  68.0 1.3 all-gather.6.cloned.1.call-done
  69.3 0.7 broadcast_in_dim.27.keep_ref
  70.0 17.1 %shard_map.140.rows_ref = bf16[16,4,200,128]{3,2,1,0:T(8,128)(2,1)} custom-call(bf16[16,4,204,200]{3,2,1,0:T(8,128)(2,1)} %pad_maximum_fusion.rows_ref, bf16[16,5,200,128]{3,2,1,0:T(8,128)(2,1)} %bitcast.44, f32[200,128]{1,0:T(8,128)} %broadcast_in_dim.27.keep_ref), custom_call_target="tpu_custom_call" | custom-call | flops 3342336000 | bytes 15923200 | tf_op jit(solution)/shard_map/pallas_call | solution.py:198
  87.2 40.3 %all-gather.8.cloned.1.call-done = bf16[1,1,2,80,128,128]{5,4,3,2,1,0:T(8,128)(2,1)} async-done(((bf16[1,1,2,5,128,128]{5,4,3,2,1,0:T(8,128)(2,1)}), bf16[1,1,2,80,128,128]{5,4,3,2,1,0:T(8,128)(2,1)}) %all-gather.8.cloned.1.call-update) | async-done | bytes 5242896 | tf_op jit(solution)/shard_map/all_gather | solution.py:273
  127.4 7.0 %fusion.33 = (bf16[1,1,1,80,128,128]{5,4,3,2,1,0:T(8,128)(2,1)}, bf16[1,1,1,80,128,128]{5,4,3,2,1,0:T(8,128)(2,1)}) fusion(bf16[1,1,2,80,128,128]{5,4,3,2,1,0:T(8,128)(2,1)} %all-gather.8.cloned.1.call-done), kind=kLoop, calls=%fused_computation.61 | loop fusion | bytes 10485760 | tf_op jit(solution)/shard_map/slice | solution.py:274
  134.4 0.7 broadcast_in_dim.28.keep_ref
  135.1 16.4 %shard_map.141.rows_ref = bf16[16,4,196,128]{3,2,1,0:T(8,128)(2,1)} custom-call(bf16[16,4,200,128]{3,2,1,0:T(8,128)(2,1)} %shard_map.140.rows_ref, bf16[16,5,128,128]{3,2,1,0:T(8,128)(2,1)} %bitcast.43, f32[196,128]{1,0:T(8,128)} %broadcast_in_dim.28.keep_ref), custom_call_target="tpu_custom_call" | custom-call | flops 2139095040 | bytes 12370944 | tf_op jit(solution)/shard_map/pallas_call | solution.py:198
  151.6 26.0 %shard_map.142 = f32[4,192,512]{2,1,0:T(8,128)} custom-call(bf16[16,4,196,128]{3,2,1,0:T(8,128)(2,1)} %shard_map.141.rows_ref, bf16[16,5,128,128]{3,2,1,0:T(8,128)(2,1)} %bitcast.45, bf16[16,128,512]{2,1,0:T(8,128)(2,1)} %bitcast.53), custom_call_target="tpu_custom_call" | custom-call | flops 3850371072 | bytes 9502720 | tf_op jit(solution)/shard_map/pallas_call | solution.py:198
  177.8 0.6 pad.27
  178.4 0.6 pad.26
  179.1 0.6 pad.24.start_ref
  179.7 0.6 reduce_max.27
  180.3 1.2 exponential_reduce_fusion.2
  183.0 0.6 pad.23.prior_ref
  183.6 58.3 %all-reduce.8.cloned.1.call-done = f32[4,192,512]{2,1,0:T(8,128)} async-done(((f32[4,192,512]{2,1,0:T(8,128)}), f32[4,192,512]{2,1,0:T(8,128)}) %all-reduce.8.cloned.1.call-update) | async-done | bytes 1572880 | tf_op jit(solution)/shard_map/psum | solution.py:277
  241.9 1.7 reduce_sum.46
  243.6 0.1 copy-done.1
  243.8 0.4 multiply_reduce_fusion
  244.2 2.1 fusion.11
  246.4 0.3 copy.34
  246.7 1.0 pad.25.emit_ref
  247.7 0.7 broadcast_in_dim.21.within_ref
  248.4 0.7 broadcast_in_dim.22.between_ref
  249.1 14.2 %shard_map.143 = (f32[192,5,128]{2,1,0:T(8,128)}, f32[192,1,128]{2,1,0:T(1,128)}) custom-call(f32[5,5,128]{2,1,0:T(8,128)} %broadcast_in_dim.21.within_ref, f32[5,5,128]{2,1,0:T(8,128)} %broadcast_in_dim.22.between_ref, f32[5,128]{1,0:T(8,128)} %pad.24.start_ref, f32[192,5,128]{2,1,0:T(8,128)} %pad.25.emit_ref, f32[192,1,128]{2,1,0:T(1,128)} %bitcast.49, ...), custom_call_target="tpu_custom_call" | custom-call | flops 15728640 | bytes 1376256 | tf_op jit(solution)/shard_map/pallas_call | solution.py:91
  263.2 0.7 slice.38
  264.0 0.6 slice_reduce_fusion
  264.8 23.7 %all-gather.2 = f32[80,5,4]{1,2,0:T(4,128)S(1)} all-gather(f32[5,5,4]{1,2,0:T(4,128)S(1)} %add_bitcast_fusion), channel_id=4, replica_groups=mesh['rec'=16,'chan'=8] {'rec'}, dimensions={0}, use_global_device_ids=true | all-gather | bytes 6800 | tf_op jit(solution)/shard_map/all_gather | solution.py:106
  288.5 0.6 copy.38
  289.1 0.7 pad.28.mats_ref
  289.9 1.0 copy.39
  290.9 1.4 copy.40
  292.3 2.5 shard_map.144
  294.8 0.7 dynamic-slice_bitcast_fusion
  295.7 0.6 bitcast_subtract_fusion
  296.3 1.2 bitcast_divide_fusion
  (51 shorter events, 1.1 us)
Async XLA Ops:
  7.2 237.0 %copy-start = (f32[512,5]{0,1:T(8,128)S(1)}, f32[512,5]{0,1:T(8,128)}, u32[]{:S(2)}) copy-start(f32[512,5]{0,1:T(8,128)} %param.22) | copy-start | bytes 30724
  7.2 62.1 %all-gather.6.cloned.1.call-start = ((), (), s32[]{:S(2)}) async-start(), calls=%async_computation.1 | async-start | bytes 4352000 | tf_op jit(solution)/shard_map/all_gather | solution.py:272
  7.9 119.5 %all-gather.8.cloned.1.call-start = ((), (), s32[]{:S(2)}) async-start(), calls=%async_computation.2 | async-start | bytes 5570560 | tf_op jit(solution)/shard_map/all_gather | solution.py:273
  8.7 233.2 %all-reduce.8.cloned.1.call-start = ((), (), s32[]{:S(2)}) async-start(), calls=%async_computation | async-start | bytes 3145728 | tf_op jit(solution)/shard_map/psum | solution.py:277
  19.3 26.5 %copy-start.5 = (s32[4]{0:T(128)S(1)}, s32[4]{0:T(128)}, u32[]{:S(2)}) copy-start(s32[4]{0:T(128)} %param.16) | copy-start | bytes 52
  40.6 15.3 %collective-permute-start = (bf16[16,4,6,200]{3,2,1,0:T(8,128)(2,1)S(1)}, bf16[16,4,6,200]{3,2,1,0:T(8,128)(2,1)S(1)}, u32[]{:S(2)}, u32[]{:S(2)}) collective-permute-start(bf16[16,4,6,200]{3,2,1,0:T(8,128)(2,1)S(1)} %get-tuple-element.10), channel_id=1, source_target_pairs={{0,8},{8,16},{16,24},{24,32},{32,40},{40,48},{48,56},{56,64},{64,7... | collective-permute-start | bytes 460808 | tf_op jit(solution)/shard_map/ppermute | solution.py:129
  44.2 16.2 %collective-permute-start.1 = (bf16[16,4,6,200]{3,2,1,0:T(8,128)(2,1)S(1)}, bf16[16,4,6,200]{3,2,1,0:T(8,128)(2,1)S(1)}, u32[]{:S(2)}, u32[]{:S(2)}) collective-permute-start(bf16[16,4,6,200]{3,2,1,0:T(8,128)(2,1)S(1)} %get-tuple-element.11), channel_id=1, source_target_pairs={{8,0},{16,8},{24,16},{32,24},{40,32},{48,40},{56,48},{64,56},{72,6... | collective-permute-start | bytes 460808 | tf_op jit(solution)/shard_map/ppermute | solution.py:129
  151.6 26.1 %copy-start.2 = (s32[4,192]{1,0:T(4,128)S(1)}, s32[4,192]{1,0:T(4,128)}, u32[]{:S(2)}) copy-start(s32[4,192]{1,0:T(4,128)} %param.17) | copy-start | bytes 9220
  151.6 28.1 %copy-start.7 = (f32[5]{0:T(128)S(1)}, f32[5]{0:T(128)}, u32[]{:S(2)}) copy-start(f32[5]{0:T(128)} %param.25) | copy-start | bytes 64
  177.6 66.6 %copy-start.6 = (f32[512]{0:T(512)S(1)}, f32[512]{0:T(512)}, u32[]{:S(2)}) copy-start(f32[512]{0:T(512)} %param.21) | copy-start | bytes 6148
  241.9 1.9 copy-start.1
  246.3 1.4 copy-start.3
  246.3 2.1 copy-start.4
Sparse Core Ops, SparseCore 0:
  10.2 59.0 all-gather.5
  71.4 55.9 all-gather.7
  177.8 64.0 all-reduce.7

commit v4 on v3

--- a/solution.py
+++ b/solution.py
@@ -14,6 +14,7 @@
 
 EPSILON = 1e-05
 NEGATIVE = -1e30
+MESH_SIDE = 4
 
 
 def log_sum_exp(values, along):
@@ -158,12 +159,12 @@
 def residual_layer(current, taps_ref, taps):
     reach = taps // 2
     length = current.shape[0] - 2 * reach
-    update = jax.nn.gelu(tap_sum(current, lambda k: taps_ref[0, k], taps, length))
+    update = jax.nn.gelu(tap_sum(current, lambda k: taps_ref[0, 0, k], taps, length))
     return (current[reach : reach + length].astype(jnp.float32) + update).astype(jnp.bfloat16)
 
 
 def hidden_kernel(rows_ref, taps_ref, keep_ref, out_ref):
-    taps = taps_ref.shape[1]
+    taps = taps_ref.shape[2]
     keep = keep_ref[...] > 0.5
     for item in range(rows_ref.shape[1]):
         value = residual_layer(rows_ref[0, item], taps_ref, taps)
@@ -175,7 +176,7 @@
     def _():
         out_ref[...] = jnp.zeros_like(out_ref)
 
-    taps = taps_ref.shape[1]
+    taps = taps_ref.shape[2]
     for item in range(rows_ref.shape[1]):
         value = residual_layer(rows_ref[0, item], taps_ref, taps)
         out_ref[item] += jnp.dot(value, mix_ref[0], preferred_element_type=jnp.float32)
@@ -188,7 +189,7 @@
     return jnp.broadcast_to(keep[:, None], (length, EMB))
 
 
-def per_type_call(kernel, rows, taps, side, out_block, out_shape, out_map, flops):
+def per_type_call(kernel, rows, taps, side, out_block, out_shape, out_map, flops, layer=None):
     types, recordings = rows.shape[:2]
     side_spec = (
         pl.BlockSpec((1,) + side.shape[1:], lambda m: (m, 0, 0))
@@ -200,7 +201,9 @@
         grid=(types,),
         in_specs=[
             pl.BlockSpec((1,) + rows.shape[1:], lambda m: (m, 0, 0, 0)),
-            pl.BlockSpec((1,) + taps.shape[1:], lambda m: (m, 0, 0, 0)),
+            pl.BlockSpec((1,) + taps.shape[1:], lambda m: (m, 0, 0, 0))
+            if layer is None
+            else pl.BlockSpec((1, 1) + taps.shape[2:], lambda m: (m, layer, 0, 0, 0)),
             side_spec,
         ],
         out_specs=pl.BlockSpec(out_block, out_map),
@@ -208,16 +211,16 @@
         compiler_params=pltpu.CompilerParams(dimension_semantics=("arbitrary",)),
         cost_estimate=pl.CostEstimate(
             flops=flops, transcendentals=rows.shape[0] * rows.shape[1] * rows.shape[2] * EMB,
-            bytes_accessed=rows.size * 2 + taps.size * 2 + side.size * 2 + out_shape.size * 4,
+            bytes_accessed=rows.size * 2 + taps.size * 2 // (1 if layer is None else taps.shape[1]) + side.size * 2 + out_shape.size * 4,
         ),
     )(rows, taps, side)
 
 
-def conv_mix(extended, first_taps, hidden_list, mix, rec_index, patches):
+def conv_mix(extended, first_taps, hidden_taps, mix, rec_index, patches):
     types, recordings, span, width = extended.shape
     taps = first_taps.shape[1]
     reach = taps // 2
-    layers = len(hidden_list)
+    layers = hidden_taps.shape[1]
     length = span - 2 * reach
     margin = reach * layers
     current = per_type_call(
@@ -229,16 +232,39 @@
         length = length - 2 * reach
         margin = margin - reach
         current = per_type_call(
-            hidden_kernel, current, hidden_list[depth_index], edge_keep(length, margin, rec_index, patches),
+            hidden_kernel, current, hidden_taps, edge_keep(length, margin, rec_index, patches),
             (1, recordings, length, EMB), jax.ShapeDtypeStruct((types, recordings, length, EMB), jnp.bfloat16),
-            lambda m: (m, 0, 0, 0), 2 * types * recordings * span * EMB * EMB * taps,
+            lambda m: (m, 0, 0, 0), 2 * types * recordings * span * EMB * EMB * taps, depth_index,
         )
     mix_width = mix.shape[-1]
     return per_type_call(
-        last_kernel, current, hidden_list[layers - 1], mix,
+        last_kernel, current, hidden_taps, mix,
         (recordings, patches, mix_width), jax.ShapeDtypeStruct((recordings, patches, mix_width), jnp.float32),
-        lambda m: (0, 0, 0), 2 * types * recordings * span * EMB * (EMB * taps + mix_width),
-    )
+        lambda m: (0, 0, 0), 2 * types * recordings * span * EMB * (EMB * taps + mix_width), layers - 1,
+    )
+
+
+def torus_gather(block, rec_index, side):
+    inner = rec_index % side
+    outer = rec_index // side
+    devices = side * side
+
+    def shifted(values, step, stride):
+        route = []
+        for source in range(devices):
+            row, col = source // side, source % side
+            if stride == 1:
+                target = row * side + (col + step) % side
+            else:
+                target = ((row + step) % side) * side + col
+            route.append((source, target))
+        return lax.ppermute(values, "rec", route)
+
+    along = jnp.concatenate([block] + [shifted(block, step, 1) for step in range(1, side)], axis=0)
+    whole = jnp.concatenate([along] + [shifted(along, step, side) for step in range(1, side)], axis=0)
+    types = jnp.arange(devices, dtype=jnp.int32)
+    position = ((outer - types // side) % side) * side + (inner - types % side) % side
+    return jnp.take(whole, position, axis=0)
 
 
 def local(
@@ -257,6 +283,7 @@
     initial,
 ):
     groups = lax.axis_size("rec")
+    mesh_side = MESH_SIDE
     chan_index = lax.axis_index("chan")
     rec_index = lax.axis_index("rec")
     recordings = signal.shape[0]
@@ -270,10 +297,9 @@
     ).astype(jnp.bfloat16)
     patch_rows = rows.reshape(groups, recordings, patches, SAMP)
     first_taps = lax.all_gather(conv_in[:, 0], "rec", tiled=True)
-    hidden_taps = lax.all_gather(jnp.swapaxes(conv_hid[:, 0], 0, 1), "rec", axis=1, tiled=True)
-    hidden_list = [hidden_taps[depth_index] for depth_index in range(hidden_taps.shape[0])]
+    hidden_taps = torus_gather(conv_hid[:, 0], rec_index, mesh_side)
     extended = halo_rows(patch_rows)
-    partial_value = conv_mix(extended, first_taps, hidden_list, mix_weight[:, 0], rec_index, patches)
+    partial_value = conv_mix(extended, first_taps, hidden_taps, mix_weight[:, 0], rec_index, patches)
     summed = lax.psum(partial_value, "chan")
     average = jnp.mean(summed, axis=-1, keepdims=True)
     centred = summed - average

time: 305 us -> 332 us (1.089)
  starting transfers between devices: 5.17 us -> 17.9 us
  local copies, waits for them, and re-layouts: 47.4 us -> 55.6 us
  other arithmetic: 14.5 us -> 21.4 us
    ppermute x0 -> x6, waiting for transfers between devices: none -> 46.6 us  [shifted(): return lax.ppermute(values, 'rec', route)]
    all_gather x1 -> x0, waiting for transfers between devices: 40.3 us -> none  [local(): lax.all_gather(jnp.swapaxes(conv_hid[:, 0], 0, 1), 'rec', axis=1, tiled=T...]
    ppermute x0 -> x6, starting transfers between devices: none -> 11.2 us  [shifted(): return lax.ppermute(values, 'rec', route)]
    ppermute x2, waiting for transfers between devices: 14.5 us -> 4.23 us  [neighbour_shift(): return lax.ppermute(block, axis, route)]
    unnamed x16 -> x22, local copies, waits for them, and re-layouts: 0.16 us -> 8.13 us
    slice x1 -> x0, local copies, waits for them, and re-layouts: 6.96 us -> none  [local(): hidden_taps[depth_index]]
    gather x0 -> x1, local copies, waits for them, and re-layouts: none -> 6.06 us  [torus_gather(): return jnp.take(whole, position, axis=0)]
    select_n x0 -> x2, other arithmetic: none -> 5.42 us  [torus_gather(): return jnp.take(whole, position, axis=0)]
  transfers between devices with their start and end apart: 5 -> 10, of which waited for: 5 -> 6; matrix products, arithmetic and copies ran while one was open for 15% -> 20% of each run, Pallas kernels for 6% -> 0%
where the time goes in v4:
time: 332 us; the launch traced here: 331 us
  waiting for transfers between devices  113 us (34%)
  Pallas kernels  76.3 us (23%)
  local copies, waits for them, and re-layouts  55.6 us (17%)
  blocking collectives  23.7 us (7%)
  other arithmetic  21.4 us (6%)
  starting transfers between devices  17.9 us (5%)
  between operations  15.6 us (5%)
  matrix products  7.35 us (2%)
    psum x1, waiting for transfers between devices, local(): summed = lax.psum(partial_value, 'chan')  61.2 us
    pallas_call x3, Pallas kernels, per_type_call(): pl.pallas_call(kernel, grid=(types,), in_specs=[pl.BlockSpec((1,) + rows....  59.6 us
    ppermute x6, waiting for transfers between devices, shifted(): return lax.ppermute(values, 'rec', route)  46.6 us
    all_gather x1, blocking collectives, crf_forward(): gathered = lax.all_gather(transfer, 'rec')  23.7 us
    reshape x1, local copies, waits for them, and re-layouts, local(): patch_rows = rows.reshape(groups, recordings, patches, SAMP)  20.3 us
    pallas_call x1, Pallas kernels, crf_forward(): pl.pallas_call(prefix_kernel, out_shape=(jax.ShapeDtypeStruct((patches, S...  14.2 us
    ppermute x6, starting transfers between devices, shifted(): return lax.ppermute(values, 'rec', route)  11.2 us
    unnamed x22, local copies, waits for them, and re-layouts  8.13 us
  transfers between devices with their start and end apart: 10, of which 6 were waited for; matrix products, arithmetic and copies ran while one was open for 20% of the time, Pallas kernels for 0%

profile of v4, /device:TPU:0, one launch (start us, length us, event | category | flops | bytes accessed | tf_op | source)
XLA Modules:
  0.0 330.7 jit_solution(10308115964020825551)
XLA Ops:
  7.2 0.7 all-gather.4.cloned.1.call-update
  8.0 1.7 collective-permute-start.2
  9.7 2.9 collective-permute-start.3
  12.6 1.3 collective-permute-start.4
  13.9 0.7 broadcast_compare_fusion
  14.7 3.8 %fusion = bf16[16,4,38400]{2,0,1:T(8,128)(2,1)S(1)} fusion(bf16[4,16,38400]{2,1,0:T(8,128)(2,1)} %param.13, s32[4,16]{1,0:T(4,128)} %bitcast.55, pred[4,16]{1,0:T(4,128)(4,1)S(1)} %broadcast_compare_fusion), kind=kOutput, calls=%fused_computation.2 | convolution fusion | flops 81102848 | bytes 9830720 | tf_op jit(solution)/shard_map/bms,bst->mbt/dot_general | solution.py:295
  18.5 6.0 %copy.32 = bf16[16,4,38400]{2,1,0:T(4,128)(2,1)} copy(bf16[16,4,38400]{2,0,1:T(8,128)(2,1)S(1)} %fusion) | data formatting | bytes 9830400 | tf_op jit(solution)/shard_map/convert_element_type | solution.py:297
  24.5 20.3 %reshape.288 = bf16[16,4,192,200]{3,2,1,0:T(8,128)(2,1)} reshape(bf16[16,4,38400]{2,1,0:T(4,128)(2,1)} %copy.32) | data formatting | bytes 9830400 | tf_op jit(solution)/shard_map/reshape | solution.py:298
  44.8 1.1 fusion.45
  45.9 1.3 collective-permute-start.1
  47.2 5.3 %collective-permute-start = (bf16[16,4,6,200]{3,2,1,0:T(8,128)(2,1)S(1)}, bf16[16,4,6,200]{3,2,1,0:T(8,128)(2,1)}, u32[]{:S(2)}, u32[]{:S(2)}) collective-permute-start(bf16[16,4,6,200]{3,2,1,0:T(8,128)(2,1)S(1)} %get-tuple-element.10), channel_id=1, source_target_pairs={{0,8},{8,16},{16,24},{24,32},{32,40},{40,48},{48,56},{56,64},{64,7... | collective-permute-start | bytes 460808 | tf_op jit(solution)/shard_map/ppermute | solution.py:130
  52.6 0.8 constant_dynamic-update-slice_fusion.6
  53.6 0.9 collective-permute-start.5
  54.4 2.7 collective-permute-start.6
  57.3 1.7 collective-permute-start.7
  59.0 2.9 collective-permute-done.1
  61.9 1.3 collective-permute-done
  63.2 7.6 %pad_maximum_fusion.rows_ref = bf16[16,4,204,200]{3,2,1,0:T(8,128)(2,1)} fusion(bf16[16,4,6,200]{3,2,1,0:T(8,128)(2,1)S(1)} %collective-permute-done.1, bf16[16,4,192,200]{3,2,1,0:T(8,128)(2,1)} %reshape.288, bf16[16,4,6,200]{3,2,1,0:T(8,128)(2,1)} %collective-permute-done), kind=kLoop, calls=%fused_computation.3 | loop fusion | flops 15667200 | bytes 10444800 | tf_op jit(solution)/shard_map/concatenate | solution.py:138
  70.8 0.8 constant_dynamic-update-slice_fusion.5
  71.6 0.7 constant_dynamic-update-slice_fusion.4
  72.3 0.8 constant_dynamic-update-slice_fusion.3
  73.1 19.9 %collective-permute-done.5 = bf16[4,2,5,128,128]{4,3,2,1,0:T(8,128)(2,1)} collective-permute-done((bf16[4,2,5,128,128]{4,3,2,1,0:T(8,128)(2,1)S(1)}, bf16[4,2,5,128,128]{4,3,2,1,0:T(8,128)(2,1)}, u32[]{:S(2)}, u32[]{:S(2)}) %collective-permute-start.5) | collective-permute-done | bytes 1310752 | tf_op jit(solution)/shard_map/ppermute | solution.py:261
  93.0 2.5 constant_dynamic-update-slice_fusion.2
  95.5 25.2 %collective-permute-done.6 = bf16[4,2,5,128,128]{4,3,2,1,0:T(8,128)(2,1)} collective-permute-done((bf16[4,2,5,128,128]{4,3,2,1,0:T(8,128)(2,1)S(1)}, bf16[4,2,5,128,128]{4,3,2,1,0:T(8,128)(2,1)}, u32[]{:S(2)}, u32[]{:S(2)}) %collective-permute-start.6) | collective-permute-done | bytes 1310752 | tf_op jit(solution)/shard_map/ppermute | solution.py:261
  120.7 2.5 constant_dynamic-update-slice_fusion.1
  123.3 1.4 collective-permute-done.7
  124.7 1.2 constant_dynamic-update-slice_fusion
  125.8 6.1 %gather_fusion = bf16[16,2,5,128,128]{4,3,2,1,0:T(8,128)(2,1)} fusion(bf16[16,2,5,128,128]{4,3,2,1,0:T(8,128)(2,1)} %constant_dynamic-update-slice_fusion, s32[1024]{0:T(1024)S(1)} %pad_clamp_fusion), kind=kCustom, calls=%fused_computation | custom fusion | bytes 10485824 | tf_op jit(solution)/shard_map/jit(_take)/gather | solution.py:267
  131.9 5.4 %broadcast_select_fusion.taps_ref = bf16[16,2,5,128,128]{4,3,2,1,0:T(8,128)(2,1)} fusion(bf16[16,2,5,128,128]{4,3,2,1,0:T(8,128)(2,1)} %gather_fusion, pred[16]{0:T(512)(128)(4,1)S(1)} %compare_and_fusion), kind=kLoop, calls=%fused_computation.4 | loop fusion | flops 2621440 | bytes 10485776 | tf_op jit(solution)/shard_map/jit(_take)/select_n | solution.py:267
  137.3 0.7 broadcast_in_dim.37.keep_ref
  138.1 17.1 %shard_map.140.rows_ref = bf16[16,4,200,128]{3,2,1,0:T(8,128)(2,1)} custom-call(bf16[16,4,204,200]{3,2,1,0:T(8,128)(2,1)} %pad_maximum_fusion.rows_ref, bf16[16,5,200,128]{3,2,1,0:T(8,128)(2,1)} %bitcast.45, f32[200,128]{1,0:T(8,128)} %broadcast_in_dim.37.keep_ref), custom_call_target="tpu_custom_call" | custom-call | flops 3342336000 | bytes 15923200 | tf_op jit(solution)/shard_map/pallas_call | solution.py:199
  155.2 0.7 broadcast_in_dim.40.keep_ref
  155.9 16.4 %shard_map.141.rows_ref = bf16[16,4,196,128]{3,2,1,0:T(8,128)(2,1)} custom-call(bf16[16,4,200,128]{3,2,1,0:T(8,128)(2,1)} %shard_map.140.rows_ref, bf16[16,2,5,128,128]{4,3,2,1,0:T(8,128)(2,1)} %broadcast_select_fusion.taps_ref, f32[196,128]{1,0:T(8,128)} %broadcast_in_dim.40.keep_ref), custom_call_target="tpu_custom_call" | custom-call | flops 2139095040 | bytes 12370944 | tf_op jit(solution)/shard_map/pallas_call | solution.py:199
  172.3 26.0 %shard_map.142 = f32[4,192,512]{2,1,0:T(8,128)} custom-call(bf16[16,4,196,128]{3,2,1,0:T(8,128)(2,1)} %shard_map.141.rows_ref, bf16[16,2,5,128,128]{4,3,2,1,0:T(8,128)(2,1)} %broadcast_select_fusion.taps_ref, bf16[16,128,512]{2,1,0:T(8,128)(2,1)} %bitcast.57), custom_call_target="tpu_custom_call" | custom-call | flops 3850371072 | bytes 9502720 | tf_op jit(solution)/shard_map/pallas_call | solution.py:199
  201.1 1.2 exponential_reduce_fusion.2
  204.4 61.2 %all-reduce.8.cloned.1.call-done = f32[4,192,512]{2,1,0:T(8,128)} async-done(((f32[4,192,512]{2,1,0:T(8,128)}), f32[4,192,512]{2,1,0:T(8,128)}) %all-reduce.8.cloned.1.call-update) | async-done | bytes 1572880 | tf_op jit(solution)/shard_map/psum | solution.py:303
  265.6 1.6 reduce_sum.46
  267.3 1.8 multiply_reduce_fusion
  269.1 3.5 %fusion.11 = f32[192,5,4]{0,1,2:T(8,128)S(1)} fusion(f32[4,192,512]{2,1,0:T(8,128)} %all-reduce.8.cloned.1.call-done, f32[512]{0:T(512)S(1)} %copy-done.6, f32[4,192]{1,0:T(4,128)S(1)} %add_rsqrt_fusion, f32[4,192]{1,0:T(4,128)S(1)} %broadcast_multiply_fusion, f32[512,5]{0,1:T(8,128)S(1)} %copy-done), kind=kOutput, calls=%fused_computation.17 | convolution fusion | flops 27918336 | bytes 1606656 | tf_op jit(solution)/shard_map/bpo,os->bps/dot_general | solution.py:308
  273.1 0.9 pad.25.emit_ref
  275.4 14.2 %shard_map.143 = (f32[192,5,128]{2,1,0:T(8,128)}, f32[192,1,128]{2,1,0:T(1,128)}) custom-call(f32[5,5,128]{2,1,0:T(8,128)} %broadcast_in_dim.33.within_ref, f32[5,5,128]{2,1,0:T(8,128)} %broadcast_in_dim.34.between_ref, f32[5,128]{1,0:T(8,128)} %pad.24.start_ref, f32[192,5,128]{2,1,0:T(8,128)} %pad.25.emit_ref, f32[192,1,128]{2,1,0:T(1,128)} %bitcast.52, ...), custom_call_target="tpu_custom_call" | custom-call | flops 15728640 | bytes 1376256 | tf_op jit(solution)/shard_map/pallas_call | solution.py:92
  290.2 1.4 copy.40
  292.3 1.0 copy.39
  293.5 23.7 %all-gather.1 = f32[80,5,4]{1,2,0:T(4,128)S(1)} all-gather(f32[5,5,4]{1,2,0:T(4,128)S(1)} %add_bitcast_fusion), channel_id=3, replica_groups=mesh['rec'=16,'chan'=8] {'rec'}, dimensions={0}, use_global_device_ids=true | all-gather | bytes 6800 | tf_op jit(solution)/shard_map/all_gather | solution.py:107
  317.9 0.7 pad.28.mats_ref
  318.6 2.5 shard_map.144
  321.1 0.7 dynamic-slice_bitcast_fusion
  322.7 1.2 bitcast_divide_fusion
  (72 shorter events, 8.7 us)
Async XLA Ops:
  7.2 261.9 %copy-start = (f32[512,5]{0,1:T(8,128)S(1)}, f32[512,5]{0,1:T(8,128)}, u32[]{:S(2)}) copy-start(f32[512,5]{0,1:T(8,128)} %param.22) | copy-start | bytes 30724
  7.2 130.1 %all-gather.4.cloned.1.call-start = ((), (), s32[]{:S(2)}) async-start(), calls=%async_computation.1 | async-start | bytes 4352000 | tf_op jit(solution)/shard_map/all_gather | solution.py:299
  7.9 257.7 %all-reduce.8.cloned.1.call-start = ((), (), s32[]{:S(2)}) async-start(), calls=%async_computation | async-start | bytes 3145728 | tf_op jit(solution)/shard_map/psum | solution.py:303
  8.0 45.4 %collective-permute-start.2 = (bf16[1,2,5,128,128]{4,3,2,1,0:T(8,128)(2,1)}, bf16[1,2,5,128,128]{4,3,2,1,0:T(8,128)(2,1)S(1)}, u32[]{:S(2)}, u32[]{:S(2)}) collective-permute-start(bf16[1,2,5,128,128]{4,3,2,1,0:T(8,128)(2,1)} %bitcast.46), channel_id=1, source_target_pairs={{0,8},{8,16},{16,24},{24,0},{32,40},{40,48},{48,56},{56,32},{64,72... | collective-permute-start | bytes 983048 | tf_op jit(solution)/shard_map/ppermute | solution.py:261
  9.7 43.7 %collective-permute-start.3 = (bf16[1,2,5,128,128]{4,3,2,1,0:T(8,128)(2,1)}, bf16[1,2,5,128,128]{4,3,2,1,0:T(8,128)(2,1)S(1)}, u32[]{:S(2)}, u32[]{:S(2)}) collective-permute-start(bf16[1,2,5,128,128]{4,3,2,1,0:T(8,128)(2,1)} %bitcast.47), channel_id=1, source_target_pairs={{0,16},{8,24},{16,0},{24,8},{32,48},{40,56},{48,32},{56,40},{64,80... | collective-permute-start | bytes 983048 | tf_op jit(solution)/shard_map/ppermute | solution.py:261
  12.6 40.8 %collective-permute-start.4 = (bf16[1,2,5,128,128]{4,3,2,1,0:T(8,128)(2,1)}, bf16[1,2,5,128,128]{4,3,2,1,0:T(8,128)(2,1)S(1)}, u32[]{:S(2)}, u32[]{:S(2)}) collective-permute-start(bf16[1,2,5,128,128]{4,3,2,1,0:T(8,128)(2,1)} %bitcast.48), channel_id=1, source_target_pairs={{0,24},{8,0},{16,8},{24,16},{32,56},{40,32},{48,40},{56,48},{64,88... | collective-permute-start | bytes 983048 | tf_op jit(solution)/shard_map/ppermute | solution.py:261
  24.5 28.1 %copy-start.2 = (s32[4,192]{1,0:T(4,128)S(1)}, s32[4,192]{1,0:T(4,128)}, u32[]{:S(2)}) copy-start(s32[4,192]{1,0:T(4,128)} %param.17) | copy-start | bytes 9220
  24.5 28.1 %copy-start.1 = (bf16[1,1,2,5,128,128]{5,4,3,2,1,0:T(8,128)(2,1)S(1)}, bf16[1,1,2,5,128,128]{5,4,3,2,1,0:T(8,128)(2,1)}, u32[]{:S(2)}) copy-start(bf16[1,1,2,5,128,128]{5,4,3,2,1,0:T(8,128)(2,1)} %param.19) | copy-start | bytes 983044
  45.9 16.0 %collective-permute-start.1 = (bf16[16,4,6,200]{3,2,1,0:T(8,128)(2,1)S(1)}, bf16[16,4,6,200]{3,2,1,0:T(8,128)(2,1)S(1)}, u32[]{:S(2)}, u32[]{:S(2)}) collective-permute-start(bf16[16,4,6,200]{3,2,1,0:T(8,128)(2,1)S(1)} %get-tuple-element.11), channel_id=1, source_target_pairs={{8,0},{16,8},{24,16},{32,24},{40,32},{48,40},{56,48},{64,56},{72,6... | collective-permute-start | bytes 460808 | tf_op jit(solution)/shard_map/ppermute | solution.py:130
  47.2 16.0 %collective-permute-start = (bf16[16,4,6,200]{3,2,1,0:T(8,128)(2,1)S(1)}, bf16[16,4,6,200]{3,2,1,0:T(8,128)(2,1)}, u32[]{:S(2)}, u32[]{:S(2)}) collective-permute-start(bf16[16,4,6,200]{3,2,1,0:T(8,128)(2,1)S(1)} %get-tuple-element.10), channel_id=1, source_target_pairs={{0,8},{8,16},{16,24},{24,32},{32,40},{40,48},{48,56},{56,64},{64,7... | collective-permute-start | bytes 460808 | tf_op jit(solution)/shard_map/ppermute | solution.py:130
  53.6 39.5 %collective-permute-start.5 = (bf16[4,2,5,128,128]{4,3,2,1,0:T(8,128)(2,1)S(1)}, bf16[4,2,5,128,128]{4,3,2,1,0:T(8,128)(2,1)}, u32[]{:S(2)}, u32[]{:S(2)}) collective-permute-start(bf16[4,2,5,128,128]{4,3,2,1,0:T(8,128)(2,1)S(1)} %pad_maximum_fusion.1), channel_id=1, source_target_pairs={{0,32},{8,40},{16,48},{24,56},{32,64},{40,72},{48,80},{56,88},{64,... | collective-permute-start | bytes 3932168 | tf_op jit(solution)/shard_map/ppermute | solution.py:261
  54.4 66.3 %collective-permute-start.6 = (bf16[4,2,5,128,128]{4,3,2,1,0:T(8,128)(2,1)S(1)}, bf16[4,2,5,128,128]{4,3,2,1,0:T(8,128)(2,1)}, u32[]{:S(2)}, u32[]{:S(2)}) collective-permute-start(bf16[4,2,5,128,128]{4,3,2,1,0:T(8,128)(2,1)S(1)} %pad_maximum_fusion.1), channel_id=1, source_target_pairs={{0,64},{8,72},{16,80},{24,88},{32,96},{40,104},{48,112},{56,120},{... | collective-permute-start | bytes 3932168 | tf_op jit(solution)/shard_map/ppermute | solution.py:261
  57.3 67.4 %collective-permute-start.7 = (bf16[4,2,5,128,128]{4,3,2,1,0:T(8,128)(2,1)S(1)}, bf16[4,2,5,128,128]{4,3,2,1,0:T(8,128)(2,1)S(1)}, u32[]{:S(2)}, u32[]{:S(2)}) collective-permute-start(bf16[4,2,5,128,128]{4,3,2,1,0:T(8,128)(2,1)S(1)} %pad_maximum_fusion.1), channel_id=1, source_target_pairs={{0,96},{8,104},{16,112},{24,120},{32,0},{40,8},{48,16},{56,24},{64... | collective-permute-start | bytes 3932168 | tf_op jit(solution)/shard_map/ppermute | solution.py:261
  172.3 27.3 %copy-start.5 = (s32[4]{0:T(128)S(1)}, s32[4]{0:T(128)}, u32[]{:S(2)}) copy-start(s32[4]{0:T(128)} %param.16) | copy-start | bytes 52
  172.3 28.2 %copy-start.7 = (f32[5]{0:T(128)S(1)}, f32[5]{0:T(128)}, u32[]{:S(2)}) copy-start(f32[5]{0:T(128)} %param.25) | copy-start | bytes 64
  198.4 70.7 %copy-start.6 = (f32[512]{0:T(512)S(1)}, f32[512]{0:T(512)}, u32[]{:S(2)}) copy-start(f32[512]{0:T(512)} %param.21) | copy-start | bytes 6148
  267.3 6.8 %copy-start.3 = (f32[5,5]{1,0:T(8,128)S(1)}, f32[5,5]{1,0:T(8,128)}, u32[]{:S(2)}) copy-start(f32[5,5]{1,0:T(8,128)} %param.23) | copy-start | bytes 304
  267.3 7.4 %copy-start.4 = (f32[5,5]{1,0:T(8,128)S(1)}, f32[5,5]{1,0:T(8,128)}, u32[]{:S(2)}) copy-start(f32[5,5]{1,0:T(8,128)} %param.24) | copy-start | bytes 304
Sparse Core Ops, SparseCore 0:
  10.2 86.4 all-gather.3
  198.5 67.0 all-reduce.7

commit v5 on v4

--- a/solution.py
+++ b/solution.py
@@ -14,7 +14,6 @@
 
 EPSILON = 1e-05
 NEGATIVE = -1e30
-MESH_SIDE = 4
 
 
 def log_sum_exp(values, along):
@@ -203,7 +202,7 @@
             pl.BlockSpec((1,) + rows.shape[1:], lambda m: (m, 0, 0, 0)),
             pl.BlockSpec((1,) + taps.shape[1:], lambda m: (m, 0, 0, 0))
             if layer is None
-            else pl.BlockSpec((1, 1) + taps.shape[2:], lambda m: (m, layer, 0, 0, 0)),
+            else pl.BlockSpec((1, 1) + taps.shape[2:], lambda m: (layer, m, 0, 0, 0)),
             side_spec,
         ],
         out_specs=pl.BlockSpec(out_block, out_map),
@@ -220,7 +219,7 @@
     types, recordings, span, width = extended.shape
     taps = first_taps.shape[1]
     reach = taps // 2
-    layers = hidden_taps.shape[1]
+    layers = hidden_taps.shape[0]
     length = span - 2 * reach
     margin = reach * layers
     current = per_type_call(
@@ -242,29 +241,6 @@
         (recordings, patches, mix_width), jax.ShapeDtypeStruct((recordings, patches, mix_width), jnp.float32),
         lambda m: (0, 0, 0), 2 * types * recordings * span * EMB * (EMB * taps + mix_width), layers - 1,
     )
-
-
-def torus_gather(block, rec_index, side):
-    inner = rec_index % side
-    outer = rec_index // side
-    devices = side * side
-
-    def shifted(values, step, stride):
-        route = []
-        for source in range(devices):
-            row, col = source // side, source % side
-            if stride == 1:
-                target = row * side + (col + step) % side
-            else:
-                target = ((row + step) % side) * side + col
-            route.append((source, target))
-        return lax.ppermute(values, "rec", route)
-
-    along = jnp.concatenate([block] + [shifted(block, step, 1) for step in range(1, side)], axis=0)
-    whole = jnp.concatenate([along] + [shifted(along, step, side) for step in range(1, side)], axis=0)
-    types = jnp.arange(devices, dtype=jnp.int32)
-    position = ((outer - types // side) % side) * side + (inner - types % side) % side
-    return jnp.take(whole, position, axis=0)
 
 
 def local(
@@ -283,7 +259,6 @@
     initial,
 ):
     groups = lax.axis_size("rec")
-    mesh_side = MESH_SIDE
     chan_index = lax.axis_index("chan")
     rec_index = lax.axis_index("rec")
     recordings = signal.shape[0]
@@ -297,10 +272,10 @@
     ).astype(jnp.bfloat16)
     patch_rows = rows.reshape(groups, recordings, patches, SAMP)
     first_taps = lax.all_gather(conv_in[:, 0], "rec", tiled=True)
-    hidden_taps = torus_gather(conv_hid[:, 0], rec_index, mesh_side)
+    hidden_taps = lax.all_gather(jnp.swapaxes(conv_hid[:, 0], 0, 1), "rec", axis=1, tiled=True)
     extended = halo_rows(patch_rows)
     partial_value = conv_mix(extended, first_taps, hidden_taps, mix_weight[:, 0], rec_index, patches)
-    summed = lax.psum(partial_value, "chan")
+    summed = lax.psum(partial_value.astype(jnp.bfloat16), "chan").astype(jnp.float32)
     average = jnp.mean(summed, axis=-1, keepdims=True)
     centred = summed - average
     variance = jnp.mean(centred * centred, axis=-1, keepdims=True)

time: 332 us -> 298 us (0.90)
  local copies, waits for them, and re-layouts: 55.6 us -> 39.3 us
  starting transfers between devices: 17.9 us -> 5.17 us
  other arithmetic: 21.4 us -> 17.7 us
    ppermute x6 -> x0, waiting for transfers between devices: 46.6 us -> none  [shifted(): return lax.ppermute(values, 'rec', route)]
    all_gather x0 -> x1, waiting for transfers between devices: none -> 40.3 us  [local(): lax.all_gather(jnp.swapaxes(conv_hid[:, 0], 0, 1), 'rec', axis=1, tiled=T...]
    ppermute x6 -> x0, starting transfers between devices: 11.2 us -> none  [shifted(): return lax.ppermute(values, 'rec', route)]
    ppermute x2, waiting for transfers between devices: 4.23 us -> 14.6 us  [neighbour_shift(): return lax.ppermute(block, axis, route)]
    unnamed x22 -> x18, local copies, waits for them, and re-layouts: 8.13 us -> 0.04 us
    gather x1 -> x0, local copies, waits for them, and re-layouts: 6.06 us -> none  [torus_gather(): return jnp.take(whole, position, axis=0)]
    psum x1, waiting for transfers between devices: 61.2 us -> 55.8 us  [local(): lax.psum(partial_value.astype(jnp.bfloat16), 'chan').astype(jnp.float32)]
    select_n x2 -> x0, other arithmetic: 5.42 us -> none  [torus_gather(): return jnp.take(whole, position, axis=0)]
  transfers between devices with their start and end apart: 10 -> 5, of which waited for: 6 -> 5; matrix products, arithmetic and copies ran while one was open for 20% -> 15% of each run, Pallas kernels for 0% -> 6%
where the time goes in v5:
time: 298 us; the launch traced here: 297 us
  waiting for transfers between devices  113 us (38%)
  Pallas kernels  76.2 us (26%)
  local copies, waits for them, and re-layouts  39.3 us (13%)
  blocking collectives  23.7 us (8%)
  other arithmetic  17.7 us (6%)
  between operations  15.3 us (5%)
  matrix products  5.95 us (2%)
  starting transfers between devices  5.17 us (2%)
    pallas_call x3, Pallas kernels, per_type_call(): pl.pallas_call(kernel, grid=(types,), in_specs=[pl.BlockSpec((1,) + rows....  59.6 us
    psum x1, waiting for transfers between devices, local(): lax.psum(partial_value.astype(jnp.bfloat16), 'chan').astype(jnp.float32)  55.8 us
    all_gather x1, waiting for transfers between devices, local(): lax.all_gather(jnp.swapaxes(conv_hid[:, 0], 0, 1), 'rec', axis=1, tiled=T...  40.3 us
    all_gather x1, blocking collectives, crf_forward(): gathered = lax.all_gather(transfer, 'rec')  23.7 us
    reshape x1, local copies, waits for them, and re-layouts, local(): patch_rows = rows.reshape(groups, recordings, patches, SAMP)  20.3 us
    ppermute x2, waiting for transfers between devices, neighbour_shift(): return lax.ppermute(block, axis, route)  14.6 us
    pallas_call x1, Pallas kernels, crf_forward(): pl.pallas_call(prefix_kernel, out_shape=(jax.ShapeDtypeStruct((patches, S...  14.2 us
    concatenate x1, other arithmetic, halo_rows(): return jnp.concatenate([from_left, patch_rows, from_right], axis=2)  7.56 us
  transfers between devices with their start and end apart: 5, of which 5 were waited for; matrix products, arithmetic and copies ran while one was open for 15% of the time, Pallas kernels for 6%

profile of v5, /device:TPU:0, one launch (start us, length us, event | category | flops | bytes accessed | tf_op | source)
XLA Modules:
  0.0 296.7 jit_solution(17590609554053306704)
XLA Ops:
  7.2 0.7 all-gather.6.cloned.1.call-update
  8.0 0.7 all-gather.8.cloned.1.call-update
  8.7 0.7 broadcast_compare_fusion
  9.5 3.8 %fusion = bf16[16,4,38400]{2,0,1:T(8,128)(2,1)S(1)} fusion(bf16[4,16,38400]{2,1,0:T(8,128)(2,1)} %param.13, s32[4,16]{1,0:T(4,128)} %bitcast.50, pred[4,16]{1,0:T(4,128)(4,1)S(1)} %broadcast_compare_fusion), kind=kOutput, calls=%fused_computation.1 | convolution fusion | flops 81102848 | bytes 9830720 | tf_op jit(solution)/shard_map/bms,bst->mbt/dot_general | solution.py:270
  13.3 6.0 %copy.32 = bf16[16,4,38400]{2,1,0:T(4,128)(2,1)} copy(bf16[16,4,38400]{2,0,1:T(8,128)(2,1)S(1)} %fusion) | data formatting | bytes 9830400 | tf_op jit(solution)/shard_map/convert_element_type | solution.py:272
  19.3 20.3 %reshape.147 = bf16[16,4,192,200]{3,2,1,0:T(8,128)(2,1)} reshape(bf16[16,4,38400]{2,1,0:T(4,128)(2,1)} %copy.32) | data formatting | bytes 9830400 | tf_op jit(solution)/shard_map/reshape | solution.py:273
  39.5 1.1 fusion.37
  40.7 3.6 %collective-permute-start = (bf16[16,4,6,200]{3,2,1,0:T(8,128)(2,1)S(1)}, bf16[16,4,6,200]{3,2,1,0:T(8,128)(2,1)S(1)}, u32[]{:S(2)}, u32[]{:S(2)}) collective-permute-start(bf16[16,4,6,200]{3,2,1,0:T(8,128)(2,1)S(1)} %get-tuple-element.10), channel_id=1, source_target_pairs={{0,8},{8,16},{16,24},{24,32},{32,40},{40,48},{48,56},{56,64},{64,7... | collective-permute-start | bytes 460808 | tf_op jit(solution)/shard_map/ppermute | solution.py:129
  44.3 1.5 collective-permute-start.1
  45.9 10.1 %collective-permute-done = bf16[16,4,6,200]{3,2,1,0:T(8,128)(2,1)S(1)} collective-permute-done((bf16[16,4,6,200]{3,2,1,0:T(8,128)(2,1)S(1)}, bf16[16,4,6,200]{3,2,1,0:T(8,128)(2,1)S(1)}, u32[]{:S(2)}, u32[]{:S(2)}) %collective-permute-start) | collective-permute-done | bytes 153632 | tf_op jit(solution)/shard_map/ppermute | solution.py:129
  56.0 4.5 %collective-permute-done.1 = bf16[16,4,6,200]{3,2,1,0:T(8,128)(2,1)S(1)} collective-permute-done((bf16[16,4,6,200]{3,2,1,0:T(8,128)(2,1)S(1)}, bf16[16,4,6,200]{3,2,1,0:T(8,128)(2,1)S(1)}, u32[]{:S(2)}, u32[]{:S(2)}) %collective-permute-start.1) | collective-permute-done | bytes 153632 | tf_op jit(solution)/shard_map/ppermute | solution.py:129
  60.4 7.6 %pad_maximum_fusion.rows_ref = bf16[16,4,204,200]{3,2,1,0:T(8,128)(2,1)} fusion(bf16[16,4,6,200]{3,2,1,0:T(8,128)(2,1)S(1)} %collective-permute-done.1, bf16[16,4,192,200]{3,2,1,0:T(8,128)(2,1)} %reshape.147, bf16[16,4,6,200]{3,2,1,0:T(8,128)(2,1)S(1)} %collective-permute-done), kind=kLoop, calls=%fused_computation.2 | loop fusion | flops 15667200 | bytes 10444800 | tf_op jit(solution)/shard_map/concatenate | solution.py:137
  68.0 1.3 all-gather.6.cloned.1.call-done
  69.3 0.7 broadcast_in_dim.27.keep_ref
  70.0 17.1 %shard_map.140.rows_ref = bf16[16,4,200,128]{3,2,1,0:T(8,128)(2,1)} custom-call(bf16[16,4,204,200]{3,2,1,0:T(8,128)(2,1)} %pad_maximum_fusion.rows_ref, bf16[16,5,200,128]{3,2,1,0:T(8,128)(2,1)} %bitcast.44, f32[200,128]{1,0:T(8,128)} %broadcast_in_dim.27.keep_ref), custom_call_target="tpu_custom_call" | custom-call | flops 3342336000 | bytes 15923200 | tf_op jit(solution)/shard_map/pallas_call | solution.py:198
  87.2 40.3 %all-gather.8.cloned.1.call-done = bf16[1,1,2,80,128,128]{5,4,3,2,1,0:T(8,128)(2,1)} async-done(((bf16[1,1,2,5,128,128]{5,4,3,2,1,0:T(8,128)(2,1)}), bf16[1,1,2,80,128,128]{5,4,3,2,1,0:T(8,128)(2,1)}) %all-gather.8.cloned.1.call-update) | async-done | bytes 5242896 | tf_op jit(solution)/shard_map/all_gather | solution.py:275
  127.4 0.7 broadcast_in_dim.28.keep_ref
  128.2 16.4 %shard_map.141.rows_ref = bf16[16,4,196,128]{3,2,1,0:T(8,128)(2,1)} custom-call(bf16[16,4,200,128]{3,2,1,0:T(8,128)(2,1)} %shard_map.140.rows_ref, bf16[2,16,5,128,128]{4,3,2,1,0:T(8,128)(2,1)} %bitcast.42, f32[196,128]{1,0:T(8,128)} %broadcast_in_dim.28.keep_ref), custom_call_target="tpu_custom_call" | custom-call | flops 2139095040 | bytes 10077184 | tf_op jit(solution)/shard_map/pallas_call | solution.py:198
  144.6 26.0 %shard_map.142 = f32[4,192,512]{2,1,0:T(8,128)} custom-call(bf16[16,4,196,128]{3,2,1,0:T(8,128)(2,1)} %shard_map.141.rows_ref, bf16[2,16,5,128,128]{4,3,2,1,0:T(8,128)(2,1)} %bitcast.43, bf16[16,128,512]{2,1,0:T(8,128)(2,1)} %bitcast.52), custom_call_target="tpu_custom_call" | custom-call | flops 3850371072 | bytes 7208960 | tf_op jit(solution)/shard_map/pallas_call | solution.py:198
  170.6 2.4 convert_element_type.58
  173.1 0.1 copy.36
  173.2 0.1 copy.35
  173.3 0.6 pad.27
  174.0 0.6 pad.26
  174.6 0.6 pad.24.start_ref
  175.2 0.6 reduce_max.27
  175.8 1.2 exponential_reduce_fusion.2
  178.5 0.6 pad.23.prior_ref
  179.1 55.8 %all-reduce.8.cloned.1.call-done = bf16[4,192,512]{2,1,0:T(8,128)(2,1)} async-done(((bf16[4,192,512]{2,1,0:T(8,128)(2,1)}), bf16[4,192,512]{2,1,0:T(8,128)(2,1)}) %all-reduce.8.cloned.1.call-update) | async-done | bytes 786448 | tf_op jit(solution)/shard_map/psum | solution.py:278
  234.8 1.4 convert_reduce_fusion
  236.3 1.5 fusion.3
  237.9 2.1 fusion.16
  240.1 0.3 copy.34
  240.4 1.0 pad.25.emit_ref
  241.4 0.7 broadcast_in_dim.21.within_ref
  242.1 0.7 broadcast_in_dim.22.between_ref
  242.8 14.2 %shard_map.143 = (f32[192,5,128]{2,1,0:T(8,128)}, f32[192,1,128]{2,1,0:T(1,128)}) custom-call(f32[5,5,128]{2,1,0:T(8,128)} %broadcast_in_dim.21.within_ref, f32[5,5,128]{2,1,0:T(8,128)} %broadcast_in_dim.22.between_ref, f32[5,128]{1,0:T(8,128)} %pad.24.start_ref, f32[192,5,128]{2,1,0:T(8,128)} %pad.25.emit_ref, f32[192,1,128]{2,1,0:T(1,128)} %bitcast.48, ...), custom_call_target="tpu_custom_call" | custom-call | flops 15728640 | bytes 1376256 | tf_op jit(solution)/shard_map/pallas_call | solution.py:91
  256.9 0.7 slice.30
  257.8 0.6 slice_reduce_fusion
  258.5 23.7 %all-gather.2 = f32[80,5,4]{1,2,0:T(4,128)S(1)} all-gather(f32[5,5,4]{1,2,0:T(4,128)S(1)} %add_bitcast_fusion), channel_id=4, replica_groups=mesh['rec'=16,'chan'=8] {'rec'}, dimensions={0}, use_global_device_ids=true | all-gather | bytes 6800 | tf_op jit(solution)/shard_map/all_gather | solution.py:106
  282.3 0.6 copy.38
  282.9 0.7 pad.28.mats_ref
  283.6 1.0 copy.39
  284.6 0.3 copy.40
  284.9 2.5 shard_map.144
  287.4 0.7 dynamic-slice_bitcast_fusion
  288.4 0.6 bitcast_subtract_fusion
  289.0 1.2 bitcast_divide_fusion
  (53 shorter events, 1.0 us)
Async XLA Ops:
  7.2 230.7 %copy-start = (f32[512,5]{0,1:T(8,128)S(1)}, f32[512,5]{0,1:T(8,128)}, u32[]{:S(2)}) copy-start(f32[512,5]{0,1:T(8,128)} %param.22) | copy-start | bytes 30724
  7.2 62.1 %all-gather.6.cloned.1.call-start = ((), (), s32[]{:S(2)}) async-start(), calls=%async_computation.1 | async-start | bytes 4352000 | tf_op jit(solution)/shard_map/all_gather | solution.py:274
  7.9 119.5 %all-gather.8.cloned.1.call-start = ((), (), s32[]{:S(2)}) async-start(), calls=%async_computation.2 | async-start | bytes 5570560 | tf_op jit(solution)/shard_map/all_gather | solution.py:275
  8.7 226.2 %all-reduce.8.cloned.1.call-start = ((), (), s32[]{:S(2)}) async-start(), calls=%async_computation | async-start | bytes 1572864 | tf_op jit(solution)/shard_map/psum | solution.py:278
  19.3 26.5 %copy-start.6 = (s32[4]{0:T(128)S(1)}, s32[4]{0:T(128)}, u32[]{:S(2)}) copy-start(s32[4]{0:T(128)} %param.16) | copy-start | bytes 52
  19.3 26.6 %copy-start.3 = (s32[4,192]{1,0:T(4,128)S(1)}, s32[4,192]{1,0:T(4,128)}, u32[]{:S(2)}) copy-start(s32[4,192]{1,0:T(4,128)} %param.17) | copy-start | bytes 9220
  40.7 15.3 %collective-permute-start = (bf16[16,4,6,200]{3,2,1,0:T(8,128)(2,1)S(1)}, bf16[16,4,6,200]{3,2,1,0:T(8,128)(2,1)S(1)}, u32[]{:S(2)}, u32[]{:S(2)}) collective-permute-start(bf16[16,4,6,200]{3,2,1,0:T(8,128)(2,1)S(1)} %get-tuple-element.10), channel_id=1, source_target_pairs={{0,8},{8,16},{16,24},{24,32},{32,40},{40,48},{48,56},{56,64},{64,7... | collective-permute-start | bytes 460808 | tf_op jit(solution)/shard_map/ppermute | solution.py:129
  44.3 16.2 %collective-permute-start.1 = (bf16[16,4,6,200]{3,2,1,0:T(8,128)(2,1)S(1)}, bf16[16,4,6,200]{3,2,1,0:T(8,128)(2,1)S(1)}, u32[]{:S(2)}, u32[]{:S(2)}) collective-permute-start(bf16[16,4,6,200]{3,2,1,0:T(8,128)(2,1)S(1)} %get-tuple-element.11), channel_id=1, source_target_pairs={{8,0},{16,8},{24,16},{32,24},{40,32},{48,40},{56,48},{64,56},{72,6... | collective-permute-start | bytes 460808 | tf_op jit(solution)/shard_map/ppermute | solution.py:129
  170.6 4.6 %copy-start.8 = (f32[5]{0:T(128)S(1)}, f32[5]{0:T(128)}, u32[]{:S(2)}) copy-start(f32[5]{0:T(128)} %param.25) | copy-start | bytes 64
  173.0 64.8 %copy-start.7 = (f32[512]{0:T(512)S(1)}, f32[512]{0:T(512)}, u32[]{:S(2)}) copy-start(f32[512]{0:T(512)} %param.21) | copy-start | bytes 6148
  234.8 3.0 %copy-start.1 = (bf16[4,192,512]{2,1,0:T(8,128)(2,1)S(1)}, bf16[4,192,512]{2,1,0:T(8,128)(2,1)}, u32[]{:S(2)}) copy-start(bf16[4,192,512]{2,1,0:T(8,128)(2,1)} %all-reduce.8.cloned.1.call-done) | copy-start | bytes 2359300
  240.0 1.4 copy-start.4
  240.0 2.1 copy-start.5
  256.9 27.7 %copy-start.2 = (f32[192,5,128]{2,1,0:T(8,128)S(1)}, f32[192,5,128]{2,1,0:T(8,128)}, u32[]{:S(2)}) copy-start(f32[192,5,128]{2,1,0:T(8,128)} %get-tuple-element.6) | copy-start | bytes 1474564
Sparse Core Ops, SparseCore 0:
  10.2 59.0 all-gather.5
  71.4 55.9 all-gather.7
  173.2 61.6 all-reduce.7

commit v6 on v5

--- a/solution.py
+++ b/solution.py
@@ -14,6 +14,7 @@
 
 EPSILON = 1e-05
 NEGATIVE = -1e30
+HALO = 8
 
 
 def log_sum_exp(values, along):
@@ -129,45 +130,45 @@
     return lax.ppermute(block, axis, route)
 
 
-def halo_rows(patch_rows):
+def halo_rows(patch_rows, halo):
     patches = patch_rows.shape[2]
-    halo = 6
     from_left = neighbour_shift(patch_rows[:, :, patches - halo :], "rec", 1)
     from_right = neighbour_shift(patch_rows[:, :, :halo], "rec", -1)
     return jnp.concatenate([from_left, patch_rows, from_right], axis=2)
 
-def tap_sum(rows, weight_of, taps, length):
+def rolled_taps(rows, weight_of, taps):
+    reach = taps // 2
+    count = rows.shape[0]
     accumulated = None
     for offset in range(taps):
         product = jnp.dot(rows, weight_of(offset), preferred_element_type=jnp.float32)
-        product = product[offset : offset + length]
+        shift = (reach - offset) % count
+        if shift:
+            product = pltpu.roll(product, shift, 0)
         accumulated = product if accumulated is None else accumulated + product
     return accumulated
 
 
+def merged(ref):
+    shape = ref.shape
+    return ref[0].reshape(shape[1] * shape[2], shape[3])
+
+
 def first_kernel(rows_ref, taps_ref, keep_ref, out_ref):
-    taps = taps_ref.shape[1]
-    keep = keep_ref[...] > 0.5
-    for item in range(rows_ref.shape[1]):
-        rows = rows_ref[0, item]
-        length = rows.shape[0] - 2 * (taps // 2)
-        value = jax.nn.gelu(tap_sum(rows, lambda k: taps_ref[0, k], taps, length)).astype(jnp.bfloat16)
-        out_ref[0, item] = jnp.where(keep, value, jnp.zeros((), jnp.bfloat16))
-
-
-def residual_layer(current, taps_ref, taps):
-    reach = taps // 2
-    length = current.shape[0] - 2 * reach
-    update = jax.nn.gelu(tap_sum(current, lambda k: taps_ref[0, 0, k], taps, length))
-    return (current[reach : reach + length].astype(jnp.float32) + update).astype(jnp.bfloat16)
+    value = jax.nn.gelu(rolled_taps(merged(rows_ref), lambda k: taps_ref[0, k], taps_ref.shape[1]))
+    value = jnp.where(keep_ref[...] > 0.5, value.astype(jnp.bfloat16), jnp.zeros((), jnp.bfloat16))
+    out_ref[0] = value.reshape(out_ref.shape[1:])
+
+
+def residual_layer(current, taps_ref):
+    update = jax.nn.gelu(rolled_taps(current, lambda k: taps_ref[0, 0, k], taps_ref.shape[2]))
+    return (current.astype(jnp.float32) + update).astype(jnp.bfloat16)
 
 
 def hidden_kernel(rows_ref, taps_ref, keep_ref, out_ref):
-    taps = taps_ref.shape[2]
-    keep = keep_ref[...] > 0.5
-    for item in range(rows_ref.shape[1]):
-        value = residual_layer(rows_ref[0, item], taps_ref, taps)
-        out_ref[0, item] = jnp.where(keep, value, jnp.zeros((), jnp.bfloat16))
+    value = residual_layer(merged(rows_ref), taps_ref)
+    value = jnp.where(keep_ref[...] > 0.5, value, jnp.zeros((), jnp.bfloat16))
+    out_ref[0] = value.reshape(out_ref.shape[1:])
 
 
 def last_kernel(rows_ref, taps_ref, mix_ref, out_ref):
@@ -175,24 +176,28 @@
     def _():
         out_ref[...] = jnp.zeros_like(out_ref)
 
-    taps = taps_ref.shape[2]
-    for item in range(rows_ref.shape[1]):
-        value = residual_layer(rows_ref[0, item], taps_ref, taps)
-        out_ref[item] += jnp.dot(value, mix_ref[0], preferred_element_type=jnp.float32)
-
-
-def edge_keep(length, margin, rec_index, patches):
+    span = rows_ref.shape[2]
+    recordings, patches = out_ref.shape[:2]
+    margin = (span - patches) // 2
+    value = residual_layer(merged(rows_ref), taps_ref)
+    mixed = jnp.dot(value, mix_ref[0], preferred_element_type=jnp.float32)
+    for item in range(recordings):
+        start = item * span + margin
+        out_ref[item] += mixed[start : start + patches]
+
+
+def edge_keep(span, margin, rec_index, patches, recordings):
     total = patches * lax.axis_size("rec")
-    spot = rec_index * patches - margin + jnp.arange(length, dtype=jnp.int32)
+    spot = rec_index * patches - margin + jnp.arange(span, dtype=jnp.int32)
     keep = ((spot >= 0) & (spot < total)).astype(jnp.float32)
-    return jnp.broadcast_to(keep[:, None], (length, EMB))
+    return jnp.tile(jnp.broadcast_to(keep[:, None], (span, EMB)), (recordings, 1))
 
 
 def per_type_call(kernel, rows, taps, side, out_block, out_shape, out_map, flops, layer=None):
     types, recordings = rows.shape[:2]
     side_spec = (
         pl.BlockSpec((1,) + side.shape[1:], lambda m: (m, 0, 0))
-        if side.ndim == 3 and side.shape[0] == types and kernel is last_kernel
+        if kernel is last_kernel
         else pl.BlockSpec(side.shape, lambda m: (0, 0))
     )
     return pl.pallas_call(
@@ -210,7 +215,7 @@
         compiler_params=pltpu.CompilerParams(dimension_semantics=("arbitrary",)),
         cost_estimate=pl.CostEstimate(
             flops=flops, transcendentals=rows.shape[0] * rows.shape[1] * rows.shape[2] * EMB,
-            bytes_accessed=rows.size * 2 + taps.size * 2 // (1 if layer is None else taps.shape[1]) + side.size * 2 + out_shape.size * 4,
+            bytes_accessed=rows.size * 2 + taps.size * 2 // (1 if layer is None else taps.shape[0]) + side.size * 2 + out_shape.size * 4,
         ),
     )(rows, taps, side)
 
@@ -218,21 +223,18 @@
 def conv_mix(extended, first_taps, hidden_taps, mix, rec_index, patches):
     types, recordings, span, width = extended.shape
     taps = first_taps.shape[1]
-    reach = taps // 2
     layers = hidden_taps.shape[0]
-    length = span - 2 * reach
-    margin = reach * layers
+    margin = (span - patches) // 2
+    keep = edge_keep(span, margin, rec_index, patches, recordings)
+    block = (1, recordings, span, EMB)
+    inner = jax.ShapeDtypeStruct((types, recordings, span, EMB), jnp.bfloat16)
     current = per_type_call(
-        first_kernel, extended, first_taps, edge_keep(length, margin, rec_index, patches),
-        (1, recordings, length, EMB), jax.ShapeDtypeStruct((types, recordings, length, EMB), jnp.bfloat16),
+        first_kernel, extended, first_taps, keep, block, inner,
         lambda m: (m, 0, 0, 0), 2 * types * recordings * span * width * EMB * taps,
     )
     for depth_index in range(layers - 1):
-        length = length - 2 * reach
-        margin = margin - reach
         current = per_type_call(
-            hidden_kernel, current, hidden_taps, edge_keep(length, margin, rec_index, patches),
-            (1, recordings, length, EMB), jax.ShapeDtypeStruct((types, recordings, length, EMB), jnp.bfloat16),
+            hidden_kernel, current, hidden_taps, keep, block, inner,
             lambda m: (m, 0, 0, 0), 2 * types * recordings * span * EMB * EMB * taps, depth_index,
         )
     mix_width = mix.shape[-1]
@@ -273,9 +275,9 @@
     patch_rows = rows.reshape(groups, recordings, patches, SAMP)
     first_taps = lax.all_gather(conv_in[:, 0], "rec", tiled=True)
     hidden_taps = lax.all_gather(jnp.swapaxes(conv_hid[:, 0], 0, 1), "rec", axis=1, tiled=True)
-    extended = halo_rows(patch_rows)
+    extended = halo_rows(patch_rows, HALO)
     partial_value = conv_mix(extended, first_taps, hidden_taps, mix_weight[:, 0], rec_index, patches)
-    summed = lax.psum(partial_value.astype(jnp.bfloat16), "chan").astype(jnp.float32)
+    summed = lax.psum(partial_value, "chan")
     average = jnp.mean(summed, axis=-1, keepdims=True)
     centred = summed - average
     variance = jnp.mean(centred * centred, axis=-1, keepdims=True)

time: 298 us -> 286 us (0.960)
  Pallas kernels: 76.2 us -> 66.3 us
  other arithmetic: 17.7 us -> 13.3 us
  waiting for transfers between devices: 113 us -> 116 us
    pallas_call x3, Pallas kernels: 59.6 us -> 49.7 us  [per_type_call(): pl.pallas_call(kernel, grid=(types,), in_specs=[pl.BlockSpec((1,) + rows....]
where the time goes in v6:
time: 286 us; the launch traced here: 285 us
  waiting for transfers between devices  116 us (41%)
  Pallas kernels  66.3 us (23%)
  local copies, waits for them, and re-layouts  39.6 us (14%)
  blocking collectives  23.7 us (8%)
  between operations  15.3 us (5%)
  other arithmetic  13.3 us (5%)
  matrix products  5.93 us (2%)
  starting transfers between devices  5.17 us (2%)
    psum x1, waiting for transfers between devices, local(): summed = lax.psum(partial_value, 'chan')  57.7 us
    pallas_call x3, Pallas kernels, per_type_call(): pl.pallas_call(kernel, grid=(types,), in_specs=[pl.BlockSpec((1,) + rows....  49.7 us
    all_gather x1, waiting for transfers between devices, local(): lax.all_gather(jnp.swapaxes(conv_hid[:, 0], 0, 1), 'rec', axis=1, tiled=T...  39.7 us
    all_gather x1, blocking collectives, crf_forward(): gathered = lax.all_gather(transfer, 'rec')  23.7 us
    reshape x1, local copies, waits for them, and re-layouts, local(): patch_rows = rows.reshape(groups, recordings, patches, SAMP)  20.3 us
    ppermute x2, waiting for transfers between devices, neighbour_shift(): return lax.ppermute(block, axis, route)  14.4 us
    pallas_call x1, Pallas kernels, crf_forward(): pl.pallas_call(prefix_kernel, out_shape=(jax.ShapeDtypeStruct((patches, S...  14.2 us
    concatenate x1, other arithmetic, halo_rows(): return jnp.concatenate([from_left, patch_rows, from_right], axis=2)  6.4 us
  transfers between devices with their start and end apart: 5, of which 5 were waited for; matrix products, arithmetic and copies ran while one was open for 15% of the time, Pallas kernels for 6%

profile of v6, /device:TPU:0, one launch (start us, length us, event | category | flops | bytes accessed | tf_op | source)
XLA Modules:
  0.0 285.0 jit_solution(14703711125402599058)
XLA Ops:
  7.2 0.7 all-gather.6.cloned.1.call-update
  8.0 0.7 all-gather.8.cloned.1.call-update
  8.7 0.7 broadcast_compare_fusion
  9.5 3.8 %fusion = bf16[16,4,38400]{2,0,1:T(8,128)(2,1)S(1)} fusion(bf16[4,16,38400]{2,1,0:T(8,128)(2,1)} %param.13, s32[4,16]{1,0:T(4,128)} %bitcast.50, pred[4,16]{1,0:T(4,128)(4,1)S(1)} %broadcast_compare_fusion), kind=kOutput, calls=%fused_computation.1 | convolution fusion | flops 81102848 | bytes 9830720 | tf_op jit(solution)/shard_map/bms,bst->mbt/dot_general | solution.py:272
  13.3 6.0 %copy.32 = bf16[16,4,38400]{2,1,0:T(4,128)(2,1)} copy(bf16[16,4,38400]{2,0,1:T(8,128)(2,1)S(1)} %fusion) | data formatting | bytes 9830400 | tf_op jit(solution)/shard_map/convert_element_type | solution.py:274
  19.3 20.3 %reshape.142 = bf16[16,4,192,200]{3,2,1,0:T(8,128)(2,1)} reshape(bf16[16,4,38400]{2,1,0:T(4,128)(2,1)} %copy.32) | data formatting | bytes 9830400 | tf_op jit(solution)/shard_map/reshape | solution.py:275
  39.5 1.1 fusion.32
  40.6 3.6 %collective-permute-start = (bf16[16,4,8,200]{3,2,1,0:T(8,128)(2,1)S(1)}, bf16[16,4,8,200]{3,2,1,0:T(8,128)(2,1)S(1)}, u32[]{:S(2)}, u32[]{:S(2)}) collective-permute-start(bf16[16,4,8,200]{3,2,1,0:T(8,128)(2,1)S(1)} %get-tuple-element.10), channel_id=1, source_target_pairs={{0,8},{8,16},{16,24},{24,32},{32,40},{40,48},{48,56},{56,64},{64,7... | collective-permute-start | bytes 614408 | tf_op jit(solution)/shard_map/ppermute | solution.py:130
  44.2 1.5 collective-permute-start.1
  45.9 0.1 copy.36
  46.0 9.9 %collective-permute-done = bf16[16,4,8,200]{3,2,1,0:T(8,128)(2,1)S(1)} collective-permute-done((bf16[16,4,8,200]{3,2,1,0:T(8,128)(2,1)S(1)}, bf16[16,4,8,200]{3,2,1,0:T(8,128)(2,1)S(1)}, u32[]{:S(2)}, u32[]{:S(2)}) %collective-permute-start) | collective-permute-done | bytes 204832 | tf_op jit(solution)/shard_map/ppermute | solution.py:130
  55.9 4.5 %collective-permute-done.1 = bf16[16,4,8,200]{3,2,1,0:T(8,128)(2,1)S(1)} collective-permute-done((bf16[16,4,8,200]{3,2,1,0:T(8,128)(2,1)S(1)}, bf16[16,4,8,200]{3,2,1,0:T(8,128)(2,1)S(1)}, u32[]{:S(2)}, u32[]{:S(2)}) %collective-permute-start.1) | collective-permute-done | bytes 204832 | tf_op jit(solution)/shard_map/ppermute | solution.py:130
  60.4 6.4 %pad_maximum_fusion.rows_ref = bf16[16,4,208,200]{3,2,1,0:T(8,128)(2,1)} fusion(bf16[16,4,8,200]{3,2,1,0:T(8,128)(2,1)S(1)} %collective-permute-done.1, bf16[16,4,192,200]{3,2,1,0:T(8,128)(2,1)} %reshape.142, bf16[16,4,8,200]{3,2,1,0:T(8,128)(2,1)S(1)} %collective-permute-done), kind=kLoop, calls=%fused_computation.2 | loop fusion | flops 15974400 | bytes 10649600 | tf_op jit(solution)/shard_map/concatenate | solution.py:137
  66.8 2.5 all-gather.6.cloned.1.call-done
  69.3 0.9 tile.40.keep_ref
  70.2 17.5 %shard_map.140.rows_ref = bf16[16,4,208,128]{3,2,1,0:T(8,128)(2,1)} custom-call(bf16[16,4,208,200]{3,2,1,0:T(8,128)(2,1)} %pad_maximum_fusion.rows_ref, bf16[16,5,200,128]{3,2,1,0:T(8,128)(2,1)} %bitcast.44, f32[832,128]{1,0:T(8,128)} %tile.40.keep_ref), custom_call_target="tpu_custom_call" | custom-call | flops 3407872000 | bytes 16449536 | tf_op jit(solution)/shard_map/pallas_call | solution.py:203
  87.7 39.7 %all-gather.8.cloned.1.call-done = bf16[1,1,2,80,128,128]{5,4,3,2,1,0:T(8,128)(2,1)} async-done(((bf16[1,1,2,5,128,128]{5,4,3,2,1,0:T(8,128)(2,1)}), bf16[1,1,2,80,128,128]{5,4,3,2,1,0:T(8,128)(2,1)}) %all-gather.8.cloned.1.call-update) | async-done | bytes 5242896 | tf_op jit(solution)/shard_map/all_gather | solution.py:277
  127.4 15.4 %shard_map.141.rows_ref = bf16[16,4,208,128]{3,2,1,0:T(8,128)(2,1)} custom-call(bf16[16,4,208,128]{3,2,1,0:T(8,128)(2,1)} %shard_map.140.rows_ref, bf16[2,16,5,128,128]{4,3,2,1,0:T(8,128)(2,1)} %bitcast.42, f32[832,128]{1,0:T(8,128)} %tile.40.keep_ref), custom_call_target="tpu_custom_call" | custom-call | flops 2181038080 | bytes 13058048 | tf_op jit(solution)/shard_map/pallas_call | solution.py:203
  142.8 16.8 %shard_map.142 = f32[4,192,512]{2,1,0:T(8,128)} custom-call(bf16[16,4,208,128]{3,2,1,0:T(8,128)(2,1)} %shard_map.141.rows_ref, bf16[2,16,5,128,128]{4,3,2,1,0:T(8,128)(2,1)} %bitcast.43, bf16[16,128,512]{2,1,0:T(8,128)(2,1)} %bitcast.52), custom_call_target="tpu_custom_call" | custom-call | flops 3925868544 | bytes 9699328 | tf_op jit(solution)/shard_map/pallas_call | solution.py:203
  159.6 0.7 copy-done.3
  160.3 0.1 copy.35
  160.4 0.6 pad.27
  161.1 0.6 pad.26
  161.7 0.6 pad.24.start_ref
  162.3 0.6 reduce_max.27
  162.9 1.2 exponential_reduce_fusion.2
  165.6 0.6 pad.23.prior_ref
  166.2 57.7 %all-reduce.8.cloned.1.call-done = f32[4,192,512]{2,1,0:T(8,128)} async-done(((f32[4,192,512]{2,1,0:T(8,128)}), f32[4,192,512]{2,1,0:T(8,128)}) %all-reduce.8.cloned.1.call-update) | async-done | bytes 1572880 | tf_op jit(solution)/shard_map/psum | solution.py:280
  223.9 1.7 reduce_sum.46
  225.6 0.1 copy-done.1
  225.8 0.4 multiply_reduce_fusion
  226.2 2.1 fusion.11
  228.4 0.3 copy.34
  228.7 1.0 pad.25.emit_ref
  229.7 0.7 broadcast_in_dim.17.within_ref
  230.4 0.7 broadcast_in_dim.18.between_ref
  231.1 14.2 %shard_map.143 = (f32[192,5,128]{2,1,0:T(8,128)}, f32[192,1,128]{2,1,0:T(1,128)}) custom-call(f32[5,5,128]{2,1,0:T(8,128)} %broadcast_in_dim.17.within_ref, f32[5,5,128]{2,1,0:T(8,128)} %broadcast_in_dim.18.between_ref, f32[5,128]{1,0:T(8,128)} %pad.24.start_ref, f32[192,5,128]{2,1,0:T(8,128)} %pad.25.emit_ref, f32[192,1,128]{2,1,0:T(1,128)} %bitcast.48, ...), custom_call_target="tpu_custom_call" | custom-call | flops 15728640 | bytes 1376256 | tf_op jit(solution)/shard_map/pallas_call | solution.py:92
  245.2 0.7 slice.30
  246.1 0.6 slice_reduce_fusion
  246.8 23.7 %all-gather.2 = f32[80,5,4]{1,2,0:T(4,128)S(1)} all-gather(f32[5,5,4]{1,2,0:T(4,128)S(1)} %add_bitcast_fusion), channel_id=4, replica_groups=mesh['rec'=16,'chan'=8] {'rec'}, dimensions={0}, use_global_device_ids=true | all-gather | bytes 6800 | tf_op jit(solution)/shard_map/all_gather | solution.py:107
  270.6 0.6 copy.38
  271.2 0.7 pad.28.mats_ref
  271.9 1.0 copy.39
  272.9 0.3 copy.40
  273.3 2.5 shard_map.144
  275.7 0.7 dynamic-slice_bitcast_fusion
  276.7 0.6 bitcast_subtract_fusion
  277.3 1.2 bitcast_divide_fusion
  (52 shorter events, 1.1 us)
Async XLA Ops:
  7.2 219.0 %copy-start = (f32[512,5]{0,1:T(8,128)S(1)}, f32[512,5]{0,1:T(8,128)}, u32[]{:S(2)}) copy-start(f32[512,5]{0,1:T(8,128)} %param.22) | copy-start | bytes 30724
  7.2 62.1 %all-gather.6.cloned.1.call-start = ((), (), s32[]{:S(2)}) async-start(), calls=%async_computation.1 | async-start | bytes 4352000 | tf_op jit(solution)/shard_map/all_gather | solution.py:276
  7.9 119.5 %all-gather.8.cloned.1.call-start = ((), (), s32[]{:S(2)}) async-start(), calls=%async_computation.2 | async-start | bytes 5570560 | tf_op jit(solution)/shard_map/all_gather | solution.py:277
  8.7 215.2 %all-reduce.8.cloned.1.call-start = ((), (), s32[]{:S(2)}) async-start(), calls=%async_computation | async-start | bytes 3145728 | tf_op jit(solution)/shard_map/psum | solution.py:280
  19.3 26.5 %copy-start.6 = (s32[4]{0:T(128)S(1)}, s32[4]{0:T(128)}, u32[]{:S(2)}) copy-start(s32[4]{0:T(128)} %param.16) | copy-start | bytes 52
  40.6 15.3 %collective-permute-start = (bf16[16,4,8,200]{3,2,1,0:T(8,128)(2,1)S(1)}, bf16[16,4,8,200]{3,2,1,0:T(8,128)(2,1)S(1)}, u32[]{:S(2)}, u32[]{:S(2)}) collective-permute-start(bf16[16,4,8,200]{3,2,1,0:T(8,128)(2,1)S(1)} %get-tuple-element.10), channel_id=1, source_target_pairs={{0,8},{8,16},{16,24},{24,32},{32,40},{40,48},{48,56},{56,64},{64,7... | collective-permute-start | bytes 614408 | tf_op jit(solution)/shard_map/ppermute | solution.py:130
  44.2 16.2 %collective-permute-start.1 = (bf16[16,4,8,200]{3,2,1,0:T(8,128)(2,1)S(1)}, bf16[16,4,8,200]{3,2,1,0:T(8,128)(2,1)S(1)}, u32[]{:S(2)}, u32[]{:S(2)}) collective-permute-start(bf16[16,4,8,200]{3,2,1,0:T(8,128)(2,1)S(1)} %get-tuple-element.11), channel_id=1, source_target_pairs={{8,0},{16,8},{24,16},{32,24},{40,32},{48,40},{56,48},{64,56},{72,6... | collective-permute-start | bytes 614408 | tf_op jit(solution)/shard_map/ppermute | solution.py:130
  159.6 0.7 copy-start.3
  159.6 2.7 copy-start.8
  166.2 59.9 %copy-start.7 = (f32[512]{0:T(512)S(1)}, f32[512]{0:T(512)}, u32[]{:S(2)}) copy-start(f32[512]{0:T(512)} %param.21) | copy-start | bytes 6148
  223.9 1.9 copy-start.1
  228.3 1.4 copy-start.4
  228.3 2.1 copy-start.5
  245.2 27.7 %copy-start.2 = (f32[192,5,128]{2,1,0:T(8,128)S(1)}, f32[192,5,128]{2,1,0:T(8,128)}, u32[]{:S(2)}) copy-start(f32[192,5,128]{2,1,0:T(8,128)} %get-tuple-element.6) | copy-start | bytes 1474564
Sparse Core Ops, SparseCore 0:
  10.2 59.0 all-gather.5
  71.4 55.9 all-gather.7
  159.8 64.0 all-reduce.7

commit v7 on v6

--- a/solution.py
+++ b/solution.py
@@ -277,12 +277,17 @@
     hidden_taps = lax.all_gather(jnp.swapaxes(conv_hid[:, 0], 0, 1), "rec", axis=1, tiled=True)
     extended = halo_rows(patch_rows, HALO)
     partial_value = conv_mix(extended, first_taps, hidden_taps, mix_weight[:, 0], rec_index, patches)
-    summed = lax.psum(partial_value, "chan")
+    spread = lax.axis_size("chan")
+    pieces = partial_value.reshape(recordings, spread, patches // spread, partial_value.shape[-1])
+    pieces = lax.all_to_all(jnp.swapaxes(pieces, 0, 1), "chan", 0, 0, tiled=True)
+    summed = jnp.sum(pieces, axis=0)
     average = jnp.mean(summed, axis=-1, keepdims=True)
     centred = summed - average
     variance = jnp.mean(centred * centred, axis=-1, keepdims=True)
     activated = jax.nn.gelu(centred * lax.rsqrt(variance + EPSILON) * norm_gain)
     emission = jnp.einsum("bpo,os->bps", activated, emit_weight, precision=lax.Precision.HIGHEST)
+    shared = lax.all_to_all(jnp.broadcast_to(emission[None], (spread,) + emission.shape), "chan", 0, 0, tiled=True)
+    emission = jnp.swapaxes(shared, 0, 1).reshape(recordings, patches, STATES)
     positions = rec_index * patches + jnp.arange(patches, dtype=jnp.int32)
     valid = positions[None, :] < lengths[:, None]
     cross = boundary == 1

time: 286 us -> 260 us (0.909)
  waiting for transfers between devices: 116 us -> 79.1 us
  starting transfers between devices: 5.17 us -> 12.8 us
  local copies, waits for them, and re-layouts: 39.6 us -> 44 us
    psum x1 -> x0, waiting for transfers between devices: 57.7 us -> none  [local(): summed = lax.psum(partial_value, 'chan')]
    all_to_all x0 -> x2, waiting for transfers between devices: none -> 20.7 us  [the longest x1 18.3 us: local(): lax.all_to_all(jnp.swapaxes(pieces, 0, 1), 'chan', 0, 0, tiled=True)]
    all_to_all x0 -> x2, starting transfers between devices: none -> 7.89 us  [the longest x1 4.55 us: local(): lax.all_to_all(jnp.swapaxes(pieces, 0, 1), 'chan', 0, 0, tiled=True)]
  transfers between devices with their start and end apart: 5 -> 6, of which waited for: 5 -> 6; matrix products, arithmetic and copies ran while one was open for 15% -> 17% of each run, Pallas kernels for 6% -> 7%
where the time goes in v7:
time: 260 us; the launch traced here: 258 us
  waiting for transfers between devices  79.1 us (30%)
  Pallas kernels  66.3 us (26%)
  local copies, waits for them, and re-layouts  44 us (17%)
  blocking collectives  23.4 us (9%)
  between operations  15.7 us (6%)
  starting transfers between devices  12.8 us (5%)
  other arithmetic  12.2 us (5%)
  matrix products  4.54 us (2%)
    pallas_call x3, Pallas kernels, per_type_call(): pl.pallas_call(kernel, grid=(types,), in_specs=[pl.BlockSpec((1,) + rows....  49.7 us
    all_gather x1, waiting for transfers between devices, local(): lax.all_gather(jnp.swapaxes(conv_hid[:, 0], 0, 1), 'rec', axis=1, tiled=T...  39.7 us
    all_gather x1, blocking collectives, crf_forward(): gathered = lax.all_gather(transfer, 'rec')  23.4 us
    reshape x1, local copies, waits for them, and re-layouts, local(): patch_rows = rows.reshape(groups, recordings, patches, SAMP)  20.3 us
    all_to_all x1, waiting for transfers between devices, local(): lax.all_to_all(jnp.swapaxes(pieces, 0, 1), 'chan', 0, 0, tiled=True)  18.3 us
    ppermute x2, waiting for transfers between devices, neighbour_shift(): return lax.ppermute(block, axis, route)  14.8 us
    pallas_call x1, Pallas kernels, crf_forward(): pl.pallas_call(prefix_kernel, out_shape=(jax.ShapeDtypeStruct((patches, S...  14.2 us
    concatenate x1, other arithmetic, halo_rows(): return jnp.concatenate([from_left, patch_rows, from_right], axis=2)  6.4 us
  transfers between devices with their start and end apart: 6, of which 6 were waited for; matrix products, arithmetic and copies ran while one was open for 17% of the time, Pallas kernels for 7%

profile of v7, /device:TPU:0, one launch (start us, length us, event | category | flops | bytes accessed | tf_op | source)
XLA Modules:
  0.0 258.1 jit_solution(12626958631486898432)
XLA Ops:
  7.2 0.7 all-gather.6.cloned.1.call-update
  8.0 0.7 all-gather.8.cloned.1.call-update
  8.7 0.7 broadcast_compare_fusion
  9.4 3.8 %fusion = bf16[16,4,38400]{2,0,1:T(8,128)(2,1)S(1)} fusion(bf16[4,16,38400]{2,1,0:T(8,128)(2,1)} %param.13, s32[4,16]{1,0:T(4,128)} %bitcast.65, pred[4,16]{1,0:T(4,128)(4,1)S(1)} %broadcast_compare_fusion), kind=kOutput, calls=%fused_computation.1 | convolution fusion | flops 81102848 | bytes 9830720 | tf_op jit(solution)/shard_map/bms,bst->mbt/dot_general | solution.py:272
  13.2 6.0 %copy.42 = bf16[16,4,38400]{2,1,0:T(4,128)(2,1)} copy(bf16[16,4,38400]{2,0,1:T(8,128)(2,1)S(1)} %fusion) | data formatting | bytes 9830400 | tf_op jit(solution)/shard_map/convert_element_type | solution.py:274
  19.2 20.3 %reshape.149 = bf16[16,4,192,200]{3,2,1,0:T(8,128)(2,1)} reshape(bf16[16,4,38400]{2,1,0:T(4,128)(2,1)} %copy.42) | data formatting | bytes 9830400 | tf_op jit(solution)/shard_map/reshape | solution.py:275
  39.5 1.1 fusion.30
  40.5 3.6 %collective-permute-start = (bf16[16,4,8,200]{3,2,1,0:T(8,128)(2,1)S(1)}, bf16[16,4,8,200]{3,2,1,0:T(8,128)(2,1)S(1)}, u32[]{:S(2)}, u32[]{:S(2)}) collective-permute-start(bf16[16,4,8,200]{3,2,1,0:T(8,128)(2,1)S(1)} %get-tuple-element.12), channel_id=1, source_target_pairs={{0,8},{8,16},{16,24},{24,32},{32,40},{40,48},{48,56},{56,64},{64,7... | collective-permute-start | bytes 614408 | tf_op jit(solution)/shard_map/ppermute | solution.py:130
  44.1 1.3 collective-permute-start.1
  45.5 10.3 %collective-permute-done = bf16[16,4,8,200]{3,2,1,0:T(8,128)(2,1)S(1)} collective-permute-done((bf16[16,4,8,200]{3,2,1,0:T(8,128)(2,1)S(1)}, bf16[16,4,8,200]{3,2,1,0:T(8,128)(2,1)S(1)}, u32[]{:S(2)}, u32[]{:S(2)}) %collective-permute-start) | collective-permute-done | bytes 204832 | tf_op jit(solution)/shard_map/ppermute | solution.py:130
  55.8 4.5 %collective-permute-done.1 = bf16[16,4,8,200]{3,2,1,0:T(8,128)(2,1)S(1)} collective-permute-done((bf16[16,4,8,200]{3,2,1,0:T(8,128)(2,1)S(1)}, bf16[16,4,8,200]{3,2,1,0:T(8,128)(2,1)S(1)}, u32[]{:S(2)}, u32[]{:S(2)}) %collective-permute-start.1) | collective-permute-done | bytes 204832 | tf_op jit(solution)/shard_map/ppermute | solution.py:130
  60.3 6.4 %pad_maximum_fusion.rows_ref = bf16[16,4,208,200]{3,2,1,0:T(8,128)(2,1)} fusion(bf16[16,4,8,200]{3,2,1,0:T(8,128)(2,1)S(1)} %collective-permute-done.1, bf16[16,4,192,200]{3,2,1,0:T(8,128)(2,1)} %reshape.149, bf16[16,4,8,200]{3,2,1,0:T(8,128)(2,1)S(1)} %collective-permute-done), kind=kLoop, calls=%fused_computation.2 | loop fusion | flops 15974400 | bytes 10649600 | tf_op jit(solution)/shard_map/concatenate | solution.py:137
  66.7 2.6 all-gather.6.cloned.1.call-done
  69.3 0.9 tile.40.keep_ref
  70.2 17.5 %shard_map.140.rows_ref = bf16[16,4,208,128]{3,2,1,0:T(8,128)(2,1)} custom-call(bf16[16,4,208,200]{3,2,1,0:T(8,128)(2,1)} %pad_maximum_fusion.rows_ref, bf16[16,5,200,128]{3,2,1,0:T(8,128)(2,1)} %bitcast.57, f32[832,128]{1,0:T(8,128)} %tile.40.keep_ref), custom_call_target="tpu_custom_call" | custom-call | flops 3407872000 | bytes 16449536 | tf_op jit(solution)/shard_map/pallas_call | solution.py:203
  87.7 39.7 %all-gather.8.cloned.1.call-done = bf16[1,1,2,80,128,128]{5,4,3,2,1,0:T(8,128)(2,1)} async-done(((bf16[1,1,2,5,128,128]{5,4,3,2,1,0:T(8,128)(2,1)}), bf16[1,1,2,80,128,128]{5,4,3,2,1,0:T(8,128)(2,1)}) %all-gather.8.cloned.1.call-update) | async-done | bytes 5242896 | tf_op jit(solution)/shard_map/all_gather | solution.py:277
  127.4 15.4 %shard_map.141.rows_ref = bf16[16,4,208,128]{3,2,1,0:T(8,128)(2,1)} custom-call(bf16[16,4,208,128]{3,2,1,0:T(8,128)(2,1)} %shard_map.140.rows_ref, bf16[2,16,5,128,128]{4,3,2,1,0:T(8,128)(2,1)} %bitcast.55, f32[832,128]{1,0:T(8,128)} %tile.40.keep_ref), custom_call_target="tpu_custom_call" | custom-call | flops 2181038080 | bytes 13058048 | tf_op jit(solution)/shard_map/pallas_call | solution.py:203
  142.9 16.8 %shard_map.142 = f32[4,192,512]{2,1,0:T(8,128)} custom-call(bf16[16,4,208,128]{3,2,1,0:T(8,128)(2,1)} %shard_map.141.rows_ref, bf16[2,16,5,128,128]{4,3,2,1,0:T(8,128)(2,1)} %bitcast.56, bf16[16,128,512]{2,1,0:T(8,128)(2,1)} %bitcast.67), custom_call_target="tpu_custom_call" | custom-call | flops 3925868544 | bytes 9699328 | tf_op jit(solution)/shard_map/pallas_call | solution.py:203
  159.6 2.7 %copy.54 = f32[4,8,24,512]{3,2,0,1:T(8,128)} copy(f32[4,8,24,512]{3,2,1,0:T(8,128)} %bitcast.58) | data formatting | bytes 3145728 | tf_op jit(solution)/shard_map/reshape | solution.py:281
  162.4 4.6 %all-to-all-start = ((f32[8,4,24,512]{3,2,1,0:T(8,128)}), f32[8,4,24,512]{3,2,1,0:T(8,128)S(1)}, u32[]{:S(2)}, u32[]{:S(2)}) async-start(f32[8,4,24,512]{3,2,1,0:T(8,128)} %bitcast.51), calls=%async_computation | async-start | bytes 3145728 | tf_op jit(solution)/shard_map/all_to_all | solution.py:282
  167.0 0.6 reduce_max.27
  167.6 1.2 exponential_reduce_fusion.2
  170.3 18.3 %all-to-all-done = f32[8,4,24,512]{3,2,1,0:T(8,128)S(1)} async-done(((f32[8,4,24,512]{3,2,1,0:T(8,128)}), f32[8,4,24,512]{3,2,1,0:T(8,128)S(1)}, u32[]{:S(2)}, u32[]{:S(2)}) %all-to-all-start) | async-done | bytes 1572896 | tf_op jit(solution)/shard_map/all_to_all | solution.py:282
  188.9 0.7 fusion.8
  189.7 0.7 reshape.164
  190.4 3.3 %all-to-all-start.1 = ((f32[8,1,480]{2,1,0:T(1,128)}), f32[8,1,480]{2,1,0:T(1,128)S(1)}, u32[]{:S(2)}, u32[]{:S(2)}) async-start(f32[8,1,480]{2,1,0:T(1,128)} %reshape.164), calls=%async_computation.1 | async-start | bytes 32768 | tf_op jit(solution)/shard_map/all_to_all | solution.py:289
  194.1 0.6 pad.27
  194.7 0.6 pad.26
  195.4 0.6 pad.24.start_ref
  196.0 0.6 pad.23.prior_ref
  196.6 2.4 all-to-all-done.1
  199.1 0.5 broadcast.163
  199.6 0.7 reduce.5
  200.9 1.0 pad.25.emit_ref
  201.9 0.7 broadcast_in_dim.19.within_ref
  202.6 0.7 broadcast_in_dim.20.between_ref
  203.3 14.2 %shard_map.143 = (f32[192,5,128]{2,1,0:T(8,128)}, f32[192,1,128]{2,1,0:T(1,128)}) custom-call(f32[5,5,128]{2,1,0:T(8,128)} %broadcast_in_dim.19.within_ref, f32[5,5,128]{2,1,0:T(8,128)} %broadcast_in_dim.20.between_ref, f32[5,128]{1,0:T(8,128)} %pad.24.start_ref, f32[192,5,128]{2,1,0:T(8,128)} %pad.25.emit_ref, f32[192,1,128]{2,1,0:T(1,128)} %bitcast.62, ...), custom_call_target="tpu_custom_call" | custom-call | flops 15728640 | bytes 1376256 | tf_op jit(solution)/shard_map/pallas_call | solution.py:92
  217.4 0.7 slice.30
  218.2 0.6 slice_reduce_fusion
  219.0 23.4 %all-gather.2 = f32[80,5,4]{1,2,0:T(4,128)S(1)} all-gather(f32[5,5,4]{1,2,0:T(4,128)S(1)} %add_bitcast_fusion), channel_id=4, replica_groups=mesh['rec'=16,'chan'=8] {'rec'}, dimensions={0}, use_global_device_ids=true | all-gather | bytes 6800 | tf_op jit(solution)/shard_map/all_gather | solution.py:107
  242.3 0.6 copy.50
  242.9 0.7 pad.28.mats_ref
  243.7 1.0 copy.51
  244.7 1.4 copy.52
  246.1 2.5 shard_map.144
  248.6 0.7 dynamic-slice_bitcast_fusion
  249.5 0.6 bitcast_subtract_fusion
  250.1 1.2 bitcast_divide_fusion
  (58 shorter events, 2.2 us)
Async XLA Ops:
  7.2 181.8 %copy-start = (f32[512,5]{0,1:T(8,128)S(1)}, f32[512,5]{0,1:T(8,128)}, u32[]{:S(2)}) copy-start(f32[512,5]{0,1:T(8,128)} %param.22) | copy-start | bytes 30724
  7.2 62.1 %all-gather.6.cloned.1.call-start = ((), (), s32[]{:S(2)}) async-start(), calls=%async_computation.2 | async-start | bytes 4352000 | tf_op jit(solution)/shard_map/all_gather | solution.py:276
  7.9 119.5 %all-gather.8.cloned.1.call-start = ((), (), s32[]{:S(2)}) async-start(), calls=%async_computation.3 | async-start | bytes 5570560 | tf_op jit(solution)/shard_map/all_gather | solution.py:277
  40.5 15.3 %collective-permute-start = (bf16[16,4,8,200]{3,2,1,0:T(8,128)(2,1)S(1)}, bf16[16,4,8,200]{3,2,1,0:T(8,128)(2,1)S(1)}, u32[]{:S(2)}, u32[]{:S(2)}) collective-permute-start(bf16[16,4,8,200]{3,2,1,0:T(8,128)(2,1)S(1)} %get-tuple-element.12), channel_id=1, source_target_pairs={{0,8},{8,16},{16,24},{24,32},{32,40},{40,48},{48,56},{56,64},{64,7... | collective-permute-start | bytes 614408 | tf_op jit(solution)/shard_map/ppermute | solution.py:130
  44.1 16.2 %collective-permute-start.1 = (bf16[16,4,8,200]{3,2,1,0:T(8,128)(2,1)S(1)}, bf16[16,4,8,200]{3,2,1,0:T(8,128)(2,1)S(1)}, u32[]{:S(2)}, u32[]{:S(2)}) collective-permute-start(bf16[16,4,8,200]{3,2,1,0:T(8,128)(2,1)S(1)} %get-tuple-element.13), channel_id=1, source_target_pairs={{8,0},{16,8},{24,16},{32,24},{40,32},{48,40},{56,48},{64,56},{72,6... | collective-permute-start | bytes 614408 | tf_op jit(solution)/shard_map/ppermute | solution.py:130
  159.6 7.3 %copy-start.6 = (f32[5]{0:T(128)S(1)}, f32[5]{0:T(128)}, u32[]{:S(2)}) copy-start(f32[5]{0:T(128)} %param.25) | copy-start | bytes 64
  159.6 10.6 %copy-start.4 = (s32[4]{0:T(128)S(1)}, s32[4]{0:T(128)}, u32[]{:S(2)}) copy-start(s32[4]{0:T(128)} %param.16) | copy-start | bytes 52
  159.6 10.6 %copy-start.1 = (s32[4,192]{1,0:T(4,128)S(1)}, s32[4,192]{1,0:T(4,128)}, u32[]{:S(2)}) copy-start(s32[4,192]{1,0:T(4,128)} %param.17) | copy-start | bytes 9220
  159.6 29.3 %copy-start.5 = (f32[512]{0:T(512)S(1)}, f32[512]{0:T(512)}, u32[]{:S(2)}) copy-start(f32[512]{0:T(512)} %param.21) | copy-start | bytes 6148
  162.4 39.5 %copy-start.2 = (f32[5,5]{1,0:T(8,128)S(1)}, f32[5,5]{1,0:T(8,128)}, u32[]{:S(2)}) copy-start(f32[5,5]{1,0:T(8,128)} %param.23) | copy-start | bytes 304
  162.4 40.2 %copy-start.3 = (f32[5,5]{1,0:T(8,128)S(1)}, f32[5,5]{1,0:T(8,128)}, u32[]{:S(2)}) copy-start(f32[5,5]{1,0:T(8,128)} %param.24) | copy-start | bytes 304
  162.4 26.1 %all-to-all-start = ((f32[8,4,24,512]{3,2,1,0:T(8,128)}), f32[8,4,24,512]{3,2,1,0:T(8,128)S(1)}, u32[]{:S(2)}, u32[]{:S(2)}) async-start(f32[8,4,24,512]{3,2,1,0:T(8,128)} %bitcast.51), calls=%async_computation | async-start | bytes 3145728 | tf_op jit(solution)/shard_map/all_to_all | solution.py:282
  190.4 8.6 %all-to-all-start.1 = ((f32[8,1,480]{2,1,0:T(1,128)}), f32[8,1,480]{2,1,0:T(1,128)S(1)}, u32[]{:S(2)}, u32[]{:S(2)}) async-start(f32[8,1,480]{2,1,0:T(1,128)} %reshape.164), calls=%async_computation.1 | async-start | bytes 32768 | tf_op jit(solution)/shard_map/all_to_all | solution.py:289
Sparse Core Ops, SparseCore 0:
  10.2 59.0 all-gather.5
  71.4 55.9 all-gather.7

commit v8 on v7

--- a/solution.py
+++ b/solution.py
@@ -104,11 +104,11 @@
     offset_j = offset[:, 0, :width].reshape(patches, STATES, recordings)
     transfer = prefix_sj[patches - 1] + offset_j[patches - 1][None]
     transfer = jnp.transpose(transfer, (1, 0, 2))
-    gathered = lax.all_gather(transfer, "rec")
+    groups = lax.axis_size("rec")
+    gathered = lax.all_to_all(jnp.broadcast_to(transfer[None], (groups,) + transfer.shape), "rec", 0, 0, tiled=True)
     mats = lanes_padded(gathered)
     prior = initial - log_sum_exp(initial, 0)
     prior_in = lanes_padded(jnp.broadcast_to(prior[:, None], (STATES, recordings)))
-    groups = gathered.shape[0]
     incoming, total = pl.pallas_call(
         chain_kernel,
         out_shape=(
@@ -274,7 +274,10 @@
     ).astype(jnp.bfloat16)
     patch_rows = rows.reshape(groups, recordings, patches, SAMP)
     first_taps = lax.all_gather(conv_in[:, 0], "rec", tiled=True)
-    hidden_taps = lax.all_gather(jnp.swapaxes(conv_hid[:, 0], 0, 1), "rec", axis=1, tiled=True)
+    hidden_own = jnp.swapaxes(conv_hid[:, 0], 0, 1)
+    hidden_taps = lax.all_to_all(
+        jnp.broadcast_to(hidden_own, (hidden_own.shape[0], groups) + hidden_own.shape[2:]), "rec", 1, 1, tiled=True
+    )
     extended = halo_rows(patch_rows, HALO)
     partial_value = conv_mix(extended, first_taps, hidden_taps, mix_weight[:, 0], rec_index, patches)
     spread = lax.axis_size("chan")

time: 260 us -> 278 us (1.069)
  starting transfers between devices: 12.8 us -> 40.8 us
  blocking collectives: 23.4 us -> 0 us
  local copies, waits for them, and re-layouts: 44 us -> 56.6 us
    all_gather x1 -> x0, waiting for transfers between devices: 39.7 us -> none  [local(): lax.all_gather(jnp.swapaxes(conv_hid[:, 0], 0, 1), 'rec', axis=1, tiled=T...]
    all_to_all x0 -> x2, starting transfers between devices: none -> 27.4 us  [the longest x1 20.1 us: crf_forward(): lax.all_to_all(jnp.broadcast_to(transfer[None], (groups,) + transfer.shap...]
    all_gather x1 -> x0, blocking collectives: 23.4 us -> none  [crf_forward(): gathered = lax.all_gather(transfer, 'rec')]
    all_to_all x0 -> x2, waiting for transfers between devices: none -> 19.7 us  [the longest x1 14.8 us: local(): lax.all_to_all(jnp.broadcast_to(hidden_own, (hidden_own.shape[0], groups)...]
    all_gather x1, waiting for transfers between devices: 2.57 us -> 15.3 us  [local(): first_taps = lax.all_gather(conv_in[:, 0], 'rec', tiled=True)]
    ppermute x2, waiting for transfers between devices: 14.8 us -> 23.8 us  [neighbour_shift(): return lax.ppermute(block, axis, route)]
    all_to_all x0 -> x2, local copies, waits for them, and re-layouts: none -> 7.9 us  [the longest x1 7.3 us: local(): lax.all_to_all(jnp.broadcast_to(hidden_own, (hidden_own.shape[0], groups)...]
    broadcast_in_dim x0 -> x2, local copies, waits for them, and re-layouts: none -> 5.31 us  [the longest x1 4.61 us: local(): jnp.broadcast_to(hidden_own, (hidden_own.shape[0], groups) + hidden_own.s...]
  transfers between devices with their start and end apart: 6 -> 7, of which waited for: 6 -> 7; matrix products, arithmetic and copies ran while one was open for 17% -> 21% of each run, Pallas kernels for 7% -> 0%
where the time goes in v8:
time: 278 us; the launch traced here: 277 us
  waiting for transfers between devices  80.9 us (29%)
  Pallas kernels  66.3 us (24%)
  local copies, waits for them, and re-layouts  56.6 us (20%)
  starting transfers between devices  40.8 us (15%)
  between operations  15.7 us (6%)
  other arithmetic  11.6 us (4%)
  matrix products  4.58 us (2%)
    pallas_call x3, Pallas kernels, per_type_call(): pl.pallas_call(kernel, grid=(types,), in_specs=[pl.BlockSpec((1,) + rows....  49.7 us
    ppermute x2, waiting for transfers between devices, neighbour_shift(): return lax.ppermute(block, axis, route)  23.8 us
    all_to_all x1, waiting for transfers between devices, local(): lax.all_to_all(jnp.swapaxes(pieces, 0, 1), 'chan', 0, 0, tiled=True)  20.9 us
    reshape x1, local copies, waits for them, and re-layouts, local(): patch_rows = rows.reshape(groups, recordings, patches, SAMP)  20.3 us
    all_to_all x1, starting transfers between devices, crf_forward(): lax.all_to_all(jnp.broadcast_to(transfer[None], (groups,) + transfer.shap...  20.1 us
    all_gather x1, waiting for transfers between devices, local(): first_taps = lax.all_gather(conv_in[:, 0], 'rec', tiled=True)  15.3 us
    all_to_all x1, waiting for transfers between devices, local(): lax.all_to_all(jnp.broadcast_to(hidden_own, (hidden_own.shape[0], groups)...  14.8 us
    pallas_call x1, Pallas kernels, crf_forward(): pl.pallas_call(prefix_kernel, out_shape=(jax.ShapeDtypeStruct((patches, S...  14.2 us
  transfers between devices with their start and end apart: 7, of which 7 were waited for; matrix products, arithmetic and copies ran while one was open for 21% of the time, Pallas kernels for 0%

profile of v8, /device:TPU:0, one launch (start us, length us, event | category | flops | bytes accessed | tf_op | source)
XLA Modules:
  0.0 276.5 jit_solution(10122225130175347260)
XLA Ops:
  7.2 0.7 all-gather.3.cloned.1.call-update
  7.9 4.6 %broadcast_in_dim.32 = bf16[2,16,5,128,128]{4,3,2,0,1:T(8,128)(2,1)} broadcast(bf16[2,5,128,128]{3,2,1,0:T(8,128)(2,1)} %bitcast.57), dimensions={0,2,3,4} | broadcast | bytes 5570560 | tf_op jit(solution)/shard_map/broadcast_in_dim | solution.py:279
  12.5 7.3 %all-to-all-start = ((bf16[2,16,5,128,128]{4,3,2,0,1:T(8,128)(2,1)}), bf16[2,16,5,128,128]{4,3,2,0,1:T(8,128)(2,1)}, u32[]{:S(2)}, u32[]{:S(2)}) async-start(bf16[2,16,5,128,128]{4,3,2,0,1:T(8,128)(2,1)} %broadcast_in_dim.32), calls=%async_computation | async-start | bytes 10485760 | tf_op jit(solution)/shard_map/all_to_all | solution.py:278
  19.9 3.9 %fusion = bf16[16,4,38400]{2,0,1:T(8,128)(2,1)S(1)} fusion(bf16[4,16,38400]{2,1,0:T(8,128)(2,1)} %param.13, s32[4,16]{1,0:T(4,128)S(1)} %bitcast.62, pred[4,16]{1,0:T(4,128)(4,1)S(1)} %broadcast_compare_fusion), kind=kOutput, calls=%fused_computation.1 | convolution fusion | flops 81102848 | bytes 9830720 | tf_op jit(solution)/shard_map/bms,bst->mbt/dot_general | solution.py:272
  23.8 6.0 %copy.44 = bf16[16,4,38400]{2,1,0:T(4,128)(2,1)} copy(bf16[16,4,38400]{2,0,1:T(8,128)(2,1)S(1)} %fusion) | data formatting | bytes 9830400 | tf_op jit(solution)/shard_map/convert_element_type | solution.py:274
  29.8 20.3 %reshape.151 = bf16[16,4,192,200]{3,2,1,0:T(8,128)(2,1)} reshape(bf16[16,4,38400]{2,1,0:T(4,128)(2,1)} %copy.44) | data formatting | bytes 9830400 | tf_op jit(solution)/shard_map/reshape | solution.py:275
  50.0 1.1 fusion.30
  51.1 3.8 %collective-permute-start = (bf16[16,4,8,200]{3,2,1,0:T(8,128)(2,1)S(1)}, bf16[16,4,8,200]{3,2,1,0:T(8,128)(2,1)S(1)}, u32[]{:S(2)}, u32[]{:S(2)}) collective-permute-start(bf16[16,4,8,200]{3,2,1,0:T(8,128)(2,1)S(1)} %get-tuple-element.12), channel_id=1, source_target_pairs={{0,8},{8,16},{16,24},{24,32},{32,40},{40,48},{48,56},{56,64},{64,7... | collective-permute-start | bytes 614408 | tf_op jit(solution)/shard_map/ppermute | solution.py:130
  55.0 1.5 collective-permute-start.1
  56.5 15.5 %collective-permute-done = bf16[16,4,8,200]{3,2,1,0:T(8,128)(2,1)S(1)} collective-permute-done((bf16[16,4,8,200]{3,2,1,0:T(8,128)(2,1)S(1)}, bf16[16,4,8,200]{3,2,1,0:T(8,128)(2,1)S(1)}, u32[]{:S(2)}, u32[]{:S(2)}) %collective-permute-start) | collective-permute-done | bytes 204832 | tf_op jit(solution)/shard_map/ppermute | solution.py:130
  72.0 8.3 %collective-permute-done.1 = bf16[16,4,8,200]{3,2,1,0:T(8,128)(2,1)S(1)} collective-permute-done((bf16[16,4,8,200]{3,2,1,0:T(8,128)(2,1)S(1)}, bf16[16,4,8,200]{3,2,1,0:T(8,128)(2,1)S(1)}, u32[]{:S(2)}, u32[]{:S(2)}) %collective-permute-start.1) | collective-permute-done | bytes 204832 | tf_op jit(solution)/shard_map/ppermute | solution.py:130
  80.4 6.4 %pad_maximum_fusion.rows_ref = bf16[16,4,208,200]{3,2,1,0:T(8,128)(2,1)} fusion(bf16[16,4,8,200]{3,2,1,0:T(8,128)(2,1)S(1)} %collective-permute-done.1, bf16[16,4,192,200]{3,2,1,0:T(8,128)(2,1)} %reshape.151, bf16[16,4,8,200]{3,2,1,0:T(8,128)(2,1)S(1)} %collective-permute-done), kind=kLoop, calls=%fused_computation.2 | loop fusion | flops 15974400 | bytes 10649600 | tf_op jit(solution)/shard_map/concatenate | solution.py:137
  86.8 14.8 %all-to-all-done = bf16[2,16,5,128,128]{4,3,2,0,1:T(8,128)(2,1)} async-done(((bf16[2,16,5,128,128]{4,3,2,0,1:T(8,128)(2,1)}), bf16[2,16,5,128,128]{4,3,2,0,1:T(8,128)(2,1)}, u32[]{:S(2)}, u32[]{:S(2)}) %all-to-all-start) | async-done | bytes 5242912 | tf_op jit(solution)/shard_map/all_to_all | solution.py:278
  101.6 7.3 %copy.45.taps_ref = bf16[2,16,5,128,128]{4,3,2,1,0:T(8,128)(2,1)} copy(bf16[2,16,5,128,128]{4,3,2,0,1:T(8,128)(2,1)} %all-to-all-done) | data formatting | bytes 10485760 | tf_op jit(solution)/shard_map/all_to_all | solution.py:278
  108.9 15.3 %all-gather.3.cloned.1.call-done = bf16[16,1,5,200,128]{4,3,2,1,0:T(8,128)(2,1)} async-done(((bf16[1,1,5,200,128]{4,3,2,1,0:T(8,128)(2,1)}), bf16[16,1,5,200,128]{4,3,2,1,0:T(8,128)(2,1)}) %all-gather.3.cloned.1.call-update) | async-done | bytes 4096016 | tf_op jit(solution)/shard_map/all_gather | solution.py:276
  124.2 0.9 tile.40.keep_ref
  125.1 17.5 %shard_map.140.rows_ref = bf16[16,4,208,128]{3,2,1,0:T(8,128)(2,1)} custom-call(bf16[16,4,208,200]{3,2,1,0:T(8,128)(2,1)} %pad_maximum_fusion.rows_ref, bf16[16,5,200,128]{3,2,1,0:T(8,128)(2,1)} %bitcast.54, f32[832,128]{1,0:T(8,128)} %tile.40.keep_ref), custom_call_target="tpu_custom_call" | custom-call | flops 3407872000 | bytes 16449536 | tf_op jit(solution)/shard_map/pallas_call | solution.py:203
  142.6 15.4 %shard_map.141.rows_ref = bf16[16,4,208,128]{3,2,1,0:T(8,128)(2,1)} custom-call(bf16[16,4,208,128]{3,2,1,0:T(8,128)(2,1)} %shard_map.140.rows_ref, bf16[2,16,5,128,128]{4,3,2,1,0:T(8,128)(2,1)} %copy.45.taps_ref, f32[832,128]{1,0:T(8,128)} %tile.40.keep_ref), custom_call_target="tpu_custom_call" | custom-call | flops 2181038080 | bytes 13058048 | tf_op jit(solution)/shard_map/pallas_call | solution.py:203
  158.0 16.8 %shard_map.142 = f32[4,192,512]{2,1,0:T(8,128)} custom-call(bf16[16,4,208,128]{3,2,1,0:T(8,128)(2,1)} %shard_map.141.rows_ref, bf16[2,16,5,128,128]{4,3,2,1,0:T(8,128)(2,1)} %copy.45.taps_ref, bf16[16,128,512]{2,1,0:T(8,128)(2,1)} %bitcast.64), custom_call_target="tpu_custom_call" | custom-call | flops 3925868544 | bytes 9699328 | tf_op jit(solution)/shard_map/pallas_call | solution.py:203
  174.8 2.7 copy.58
  177.6 4.7 %all-to-all-start.1 = ((f32[8,4,24,512]{3,2,1,0:T(8,128)}), f32[8,4,24,512]{3,2,1,0:T(8,128)S(1)}, u32[]{:S(2)}, u32[]{:S(2)}) async-start(f32[8,4,24,512]{3,2,1,0:T(8,128)} %bitcast.50), calls=%async_computation.1 | async-start | bytes 3145728 | tf_op jit(solution)/shard_map/all_to_all | solution.py:285
  182.3 0.6 reduce_max.27
  183.0 20.9 %all-to-all-done.1 = f32[8,4,24,512]{3,2,1,0:T(8,128)S(1)} async-done(((f32[8,4,24,512]{3,2,1,0:T(8,128)}), f32[8,4,24,512]{3,2,1,0:T(8,128)S(1)}, u32[]{:S(2)}, u32[]{:S(2)}) %all-to-all-start.1) | async-done | bytes 1572896 | tf_op jit(solution)/shard_map/all_to_all | solution.py:285
  204.3 0.7 fusion.8
  205.1 0.7 reshape.164
  205.8 3.3 %all-to-all-start.2 = ((f32[8,1,480]{2,1,0:T(1,128)}), f32[8,1,480]{2,1,0:T(1,128)S(1)}, u32[]{:S(2)}, u32[]{:S(2)}) async-start(f32[8,1,480]{2,1,0:T(1,128)} %reshape.164), calls=%async_computation.2 | async-start | bytes 32768 | tf_op jit(solution)/shard_map/all_to_all | solution.py:292
  209.1 1.3 exponential_reduce_fusion.2
  210.7 0.6 pad.27
  211.3 0.6 pad.26
  214.9 0.7 reduce.5
  216.3 1.0 pad.25.emit_ref
  217.2 0.7 broadcast_in_dim.25.within_ref
  217.9 0.7 broadcast_in_dim.28.between_ref
  218.6 14.2 %shard_map.143 = (f32[192,5,128]{2,1,0:T(8,128)}, f32[192,1,128]{2,1,0:T(1,128)}) custom-call(f32[5,5,128]{2,1,0:T(8,128)} %broadcast_in_dim.25.within_ref, f32[5,5,128]{2,1,0:T(8,128)} %broadcast_in_dim.28.between_ref, f32[5,128]{1,0:T(8,128)} %pad.24.start_ref, f32[192,5,128]{2,1,0:T(8,128)} %pad.25.emit_ref, f32[192,1,128]{2,1,0:T(1,128)} %bitcast.59, ...), custom_call_target="tpu_custom_call" | custom-call | flops 15728640 | bytes 1376256 | tf_op jit(solution)/shard_map/pallas_call | solution.py:92
  232.8 0.7 slice.30
  233.5 0.6 slice_reduce_fusion
  234.3 0.7 broadcast_in_dim.36
  235.0 20.1 %all-to-all-start.3 = ((f32[16,5,5,4]{2,3,1,0:T(4,128)}), f32[16,5,5,4]{2,3,1,0:T(4,128)S(1)}, u32[]{:S(2)}, u32[]{:S(2)}) async-start(f32[16,5,5,4]{2,3,1,0:T(4,128)} %broadcast_in_dim.36), calls=%async_computation.3 | async-start | bytes 327680 | tf_op jit(solution)/shard_map/all_to_all | solution.py:108
  255.2 0.6 pad.23.prior_ref
  255.8 1.0 copy.55
  256.8 1.4 copy.56
  258.2 4.9 %all-to-all-done.3 = f32[16,5,5,4]{2,3,1,0:T(4,128)S(1)} async-done(((f32[16,5,5,4]{2,3,1,0:T(4,128)}), f32[16,5,5,4]{2,3,1,0:T(4,128)S(1)}, u32[]{:S(2)}, u32[]{:S(2)}) %all-to-all-start.3) | async-done | bytes 6432 | tf_op jit(solution)/shard_map/all_to_all | solution.py:108
  263.1 0.6 copy.54
  263.7 0.7 pad.28.mats_ref
  264.4 2.5 shard_map.144
  266.9 0.7 dynamic-slice_bitcast_fusion
  267.9 0.6 bitcast_subtract_fusion
  268.5 1.2 bitcast_divide_fusion
  (65 shorter events, 3.9 us)
Async XLA Ops:
  7.2 197.1 %copy-start = (f32[512,5]{0,1:T(8,128)S(1)}, f32[512,5]{0,1:T(8,128)}, u32[]{:S(2)}) copy-start(f32[512,5]{0,1:T(8,128)} %param.22) | copy-start | bytes 30724
  7.2 117.0 %all-gather.3.cloned.1.call-start = ((), (), s32[]{:S(2)}) async-start(), calls=%async_computation.4 | async-start | bytes 4352000 | tf_op jit(solution)/shard_map/all_gather | solution.py:276
  12.5 7.3 %copy-start.7 = (s32[4]{0:T(128)S(1)}, s32[4]{0:T(128)}, u32[]{:S(2)}) copy-start(s32[4]{0:T(128)} %param.15) | copy-start | bytes 52
  12.5 7.4 %copy-start.1 = (s32[4,1,16]{2,1,0:T(1,128)S(1)}, s32[4,1,16]{2,1,0:T(1,128)}, u32[]{:S(2)}) copy-start(s32[4,1,16]{2,1,0:T(1,128)} %param.14) | copy-start | bytes 772
  12.5 89.1 %all-to-all-start = ((bf16[2,16,5,128,128]{4,3,2,0,1:T(8,128)(2,1)}), bf16[2,16,5,128,128]{4,3,2,0,1:T(8,128)(2,1)}, u32[]{:S(2)}, u32[]{:S(2)}) async-start(bf16[2,16,5,128,128]{4,3,2,0,1:T(8,128)(2,1)} %broadcast_in_dim.32), calls=%async_computation | async-start | bytes 10485760 | tf_op jit(solution)/shard_map/all_to_all | solution.py:278
  51.1 20.9 %collective-permute-start = (bf16[16,4,8,200]{3,2,1,0:T(8,128)(2,1)S(1)}, bf16[16,4,8,200]{3,2,1,0:T(8,128)(2,1)S(1)}, u32[]{:S(2)}, u32[]{:S(2)}) collective-permute-start(bf16[16,4,8,200]{3,2,1,0:T(8,128)(2,1)S(1)} %get-tuple-element.12), channel_id=1, source_target_pairs={{0,8},{8,16},{16,24},{24,32},{32,40},{40,48},{48,56},{56,64},{64,7... | collective-permute-start | bytes 614408 | tf_op jit(solution)/shard_map/ppermute | solution.py:130
  55.0 25.4 %collective-permute-start.1 = (bf16[16,4,8,200]{3,2,1,0:T(8,128)(2,1)S(1)}, bf16[16,4,8,200]{3,2,1,0:T(8,128)(2,1)S(1)}, u32[]{:S(2)}, u32[]{:S(2)}) collective-permute-start(bf16[16,4,8,200]{3,2,1,0:T(8,128)(2,1)S(1)} %get-tuple-element.13), channel_id=1, source_target_pairs={{8,0},{16,8},{24,16},{32,24},{40,32},{48,40},{56,48},{64,56},{72,6... | collective-permute-start | bytes 614408 | tf_op jit(solution)/shard_map/ppermute | solution.py:130
  174.8 7.5 %copy-start.8 = (f32[5]{0:T(128)S(1)}, f32[5]{0:T(128)}, u32[]{:S(2)}) copy-start(f32[5]{0:T(128)} %param.25) | copy-start | bytes 64
  174.8 8.1 %copy-start.5 = (s32[4]{0:T(128)S(1)}, s32[4]{0:T(128)}, u32[]{:S(2)}) copy-start(s32[4]{0:T(128)} %param.16) | copy-start | bytes 52
  174.8 8.2 %copy-start.2 = (s32[4,192]{1,0:T(4,128)S(1)}, s32[4,192]{1,0:T(4,128)}, u32[]{:S(2)}) copy-start(s32[4,192]{1,0:T(4,128)} %param.17) | copy-start | bytes 9220
  174.8 29.5 %copy-start.6 = (f32[512]{0:T(512)S(1)}, f32[512]{0:T(512)}, u32[]{:S(2)}) copy-start(f32[512]{0:T(512)} %param.21) | copy-start | bytes 6148
  177.6 39.7 %copy-start.3 = (f32[5,5]{1,0:T(8,128)S(1)}, f32[5,5]{1,0:T(8,128)}, u32[]{:S(2)}) copy-start(f32[5,5]{1,0:T(8,128)} %param.23) | copy-start | bytes 304
  177.6 40.4 %copy-start.4 = (f32[5,5]{1,0:T(8,128)S(1)}, f32[5,5]{1,0:T(8,128)}, u32[]{:S(2)}) copy-start(f32[5,5]{1,0:T(8,128)} %param.24) | copy-start | bytes 304
  177.6 26.3 %all-to-all-start.1 = ((f32[8,4,24,512]{3,2,1,0:T(8,128)}), f32[8,4,24,512]{3,2,1,0:T(8,128)S(1)}, u32[]{:S(2)}, u32[]{:S(2)}) async-start(f32[8,4,24,512]{3,2,1,0:T(8,128)} %bitcast.50), calls=%async_computation.1 | async-start | bytes 3145728 | tf_op jit(solution)/shard_map/all_to_all | solution.py:285
  205.8 8.6 %all-to-all-start.2 = ((f32[8,1,480]{2,1,0:T(1,128)}), f32[8,1,480]{2,1,0:T(1,128)S(1)}, u32[]{:S(2)}, u32[]{:S(2)}) async-start(f32[8,1,480]{2,1,0:T(1,128)} %reshape.164), calls=%async_computation.2 | async-start | bytes 32768 | tf_op jit(solution)/shard_map/all_to_all | solution.py:292
  235.0 28.1 %all-to-all-start.3 = ((f32[16,5,5,4]{2,3,1,0:T(4,128)}), f32[16,5,5,4]{2,3,1,0:T(4,128)S(1)}, u32[]{:S(2)}, u32[]{:S(2)}) async-start(f32[16,5,5,4]{2,3,1,0:T(4,128)} %broadcast_in_dim.36), calls=%async_computation.3 | async-start | bytes 327680 | tf_op jit(solution)/shard_map/all_to_all | solution.py:108
Sparse Core Ops, SparseCore 0:
  10.2 113.9 all-gather.2

commit v9 on v7

--- a/solution.py
+++ b/solution.py
@@ -14,6 +14,7 @@
 
 EPSILON = 1e-05
 NEGATIVE = -1e30
+MESH_SIDE = 4
 HALO = 8
 
 
@@ -104,7 +105,7 @@
     offset_j = offset[:, 0, :width].reshape(patches, STATES, recordings)
     transfer = prefix_sj[patches - 1] + offset_j[patches - 1][None]
     transfer = jnp.transpose(transfer, (1, 0, 2))
-    gathered = lax.all_gather(transfer, "rec")
+    gathered = torus_gather(transfer[None], rec_index, MESH_SIDE)
     mats = lanes_padded(gathered)
     prior = initial - log_sum_exp(initial, 0)
     prior_in = lanes_padded(jnp.broadcast_to(prior[:, None], (STATES, recordings)))
@@ -243,6 +244,29 @@
         (recordings, patches, mix_width), jax.ShapeDtypeStruct((recordings, patches, mix_width), jnp.float32),
         lambda m: (0, 0, 0), 2 * types * recordings * span * EMB * (EMB * taps + mix_width), layers - 1,
     )
+
+
+def torus_gather(block, rec_index, side):
+    inner = rec_index % side
+    outer = rec_index // side
+    devices = side * side
+
+    def shifted(values, step, stride):
+        route = []
+        for source in range(devices):
+            row, col = source // side, source % side
+            if stride == 1:
+                target = row * side + (col + step) % side
+            else:
+                target = ((row + step) % side) * side + col
+            route.append((source, target))
+        return lax.ppermute(values, "rec", route)
+
+    along = jnp.concatenate([block] + [shifted(block, step, 1) for step in range(1, side)], axis=0)
+    whole = jnp.concatenate([along] + [shifted(along, step, side) for step in range(1, side)], axis=0)
+    types = jnp.arange(devices, dtype=jnp.int32)
+    position = ((outer - types // side) % side) * side + (inner - types % side) % side
+    return jnp.take(whole, position, axis=0)
 
 
 def local(

time: 260 us -> 250 us (0.962)
  blocking collectives: 23.4 us -> 0 us
  starting transfers between devices: 12.8 us -> 22.8 us
    all_gather x1 -> x0, blocking collectives: 23.4 us -> none  [crf_forward(): gathered = lax.all_gather(transfer, 'rec')]
    ppermute x0 -> x6, starting transfers between devices: none -> 9.78 us  [shifted(): return lax.ppermute(values, 'rec', route)]
  transfers between devices with their start and end apart: 6 -> 12, of which waited for: 6 -> 9; matrix products, arithmetic and copies ran while one was open for 17% -> 19% of each run, Pallas kernels for 7% -> 7%
where the time goes in v9:
time: 250 us; the launch traced here: 248 us
  waiting for transfers between devices  81.4 us (33%)
  Pallas kernels  66.3 us (27%)
  local copies, waits for them, and re-layouts  44.7 us (18%)
  starting transfers between devices  22.8 us (9%)
  between operations  15.7 us (6%)
  other arithmetic  12.4 us (5%)
  matrix products  4.54 us (2%)
    pallas_call x3, Pallas kernels, per_type_call(): pl.pallas_call(kernel, grid=(types,), in_specs=[pl.BlockSpec((1,) + rows....  49.7 us
    all_gather x1, waiting for transfers between devices, local(): lax.all_gather(jnp.swapaxes(conv_hid[:, 0], 0, 1), 'rec', axis=1, tiled=T...  39.7 us
    reshape x1, local copies, waits for them, and re-layouts, local(): patch_rows = rows.reshape(groups, recordings, patches, SAMP)  20.3 us
    all_to_all x1, waiting for transfers between devices, local(): lax.all_to_all(jnp.swapaxes(pieces, 0, 1), 'chan', 0, 0, tiled=True)  18.8 us
    pallas_call x1, Pallas kernels, crf_forward(): pl.pallas_call(prefix_kernel, out_shape=(jax.ShapeDtypeStruct((patches, S...  14.2 us
    ppermute x2, waiting for transfers between devices, neighbour_shift(): return lax.ppermute(block, axis, route)  14.2 us
    ppermute x6, starting transfers between devices, shifted(): return lax.ppermute(values, 'rec', route)  9.78 us
    concatenate x1, other arithmetic, halo_rows(): return jnp.concatenate([from_left, patch_rows, from_right], axis=2)  6.4 us
  transfers between devices with their start and end apart: 12, of which 9 were waited for; matrix products, arithmetic and copies ran while one was open for 19% of the time, Pallas kernels for 7%

profile of v9, /device:TPU:0, one launch (start us, length us, event | category | flops | bytes accessed | tf_op | source)
XLA Modules:
  0.0 247.9 jit_solution(15809329658479935847)
XLA Ops:
  7.2 0.7 all-gather.5.cloned.1.call-update
  8.0 0.7 all-gather.7.cloned.1.call-update
  8.7 0.7 broadcast_compare_fusion
  9.4 3.8 %fusion = bf16[16,4,38400]{2,0,1:T(8,128)(2,1)S(1)} fusion(bf16[4,16,38400]{2,1,0:T(8,128)(2,1)} %param.13, s32[4,16]{1,0:T(4,128)} %bitcast.68, pred[4,16]{1,0:T(4,128)(4,1)S(1)} %broadcast_compare_fusion), kind=kOutput, calls=%fused_computation.2 | convolution fusion | flops 81102848 | bytes 9830720 | tf_op jit(solution)/shard_map/bms,bst->mbt/dot_general | solution.py:296
  13.2 6.0 %copy.68 = bf16[16,4,38400]{2,1,0:T(4,128)(2,1)} copy(bf16[16,4,38400]{2,0,1:T(8,128)(2,1)S(1)} %fusion) | data formatting | bytes 9830400 | tf_op jit(solution)/shard_map/convert_element_type | solution.py:298
  19.2 20.3 %reshape.290 = bf16[16,4,192,200]{3,2,1,0:T(8,128)(2,1)} reshape(bf16[16,4,38400]{2,1,0:T(4,128)(2,1)} %copy.68) | data formatting | bytes 9830400 | tf_op jit(solution)/shard_map/reshape | solution.py:299
  39.5 1.1 fusion.43
  40.6 3.6 %collective-permute-start = (bf16[16,4,8,200]{3,2,1,0:T(8,128)(2,1)S(1)}, bf16[16,4,8,200]{3,2,1,0:T(8,128)(2,1)S(1)}, u32[]{:S(2)}, u32[]{:S(2)}) collective-permute-start(bf16[16,4,8,200]{3,2,1,0:T(8,128)(2,1)S(1)} %get-tuple-element.14), channel_id=1, source_target_pairs={{0,8},{8,16},{16,24},{24,32},{32,40},{40,48},{48,56},{56,64},{64,7... | collective-permute-start | bytes 614408 | tf_op jit(solution)/shard_map/ppermute | solution.py:131
  44.1 1.3 collective-permute-start.1
  46.2 9.7 %collective-permute-done = bf16[16,4,8,200]{3,2,1,0:T(8,128)(2,1)S(1)} collective-permute-done((bf16[16,4,8,200]{3,2,1,0:T(8,128)(2,1)S(1)}, bf16[16,4,8,200]{3,2,1,0:T(8,128)(2,1)S(1)}, u32[]{:S(2)}, u32[]{:S(2)}) %collective-permute-start) | collective-permute-done | bytes 204832 | tf_op jit(solution)/shard_map/ppermute | solution.py:131
  55.8 4.5 %collective-permute-done.1 = bf16[16,4,8,200]{3,2,1,0:T(8,128)(2,1)S(1)} collective-permute-done((bf16[16,4,8,200]{3,2,1,0:T(8,128)(2,1)S(1)}, bf16[16,4,8,200]{3,2,1,0:T(8,128)(2,1)S(1)}, u32[]{:S(2)}, u32[]{:S(2)}) %collective-permute-start.1) | collective-permute-done | bytes 204832 | tf_op jit(solution)/shard_map/ppermute | solution.py:131
  60.3 6.4 %pad_maximum_fusion.rows_ref = bf16[16,4,208,200]{3,2,1,0:T(8,128)(2,1)} fusion(bf16[16,4,8,200]{3,2,1,0:T(8,128)(2,1)S(1)} %collective-permute-done.1, bf16[16,4,192,200]{3,2,1,0:T(8,128)(2,1)} %reshape.290, bf16[16,4,8,200]{3,2,1,0:T(8,128)(2,1)S(1)} %collective-permute-done), kind=kLoop, calls=%fused_computation.3 | loop fusion | flops 15974400 | bytes 10649600 | tf_op jit(solution)/shard_map/concatenate | solution.py:138
  66.7 2.5 %all-gather.5.cloned.1.call-done = bf16[16,1,5,200,128]{4,3,2,1,0:T(8,128)(2,1)} async-done(((bf16[1,1,5,200,128]{4,3,2,1,0:T(8,128)(2,1)}), bf16[16,1,5,200,128]{4,3,2,1,0:T(8,128)(2,1)}) %all-gather.5.cloned.1.call-update) | async-done | bytes 4096016 | tf_op jit(solution)/shard_map/all_gather | solution.py:300
  69.3 0.9 tile.40.keep_ref
  70.2 17.5 %shard_map.140.rows_ref = bf16[16,4,208,128]{3,2,1,0:T(8,128)(2,1)} custom-call(bf16[16,4,208,200]{3,2,1,0:T(8,128)(2,1)} %pad_maximum_fusion.rows_ref, bf16[16,5,200,128]{3,2,1,0:T(8,128)(2,1)} %bitcast.61, f32[832,128]{1,0:T(8,128)} %tile.40.keep_ref), custom_call_target="tpu_custom_call" | custom-call | flops 3407872000 | bytes 16449536 | tf_op jit(solution)/shard_map/pallas_call | solution.py:204
  87.7 39.7 %all-gather.7.cloned.1.call-done = bf16[1,1,2,80,128,128]{5,4,3,2,1,0:T(8,128)(2,1)} async-done(((bf16[1,1,2,5,128,128]{5,4,3,2,1,0:T(8,128)(2,1)}), bf16[1,1,2,80,128,128]{5,4,3,2,1,0:T(8,128)(2,1)}) %all-gather.7.cloned.1.call-update) | async-done | bytes 5242896 | tf_op jit(solution)/shard_map/all_gather | solution.py:301
  127.4 15.4 %shard_map.141.rows_ref = bf16[16,4,208,128]{3,2,1,0:T(8,128)(2,1)} custom-call(bf16[16,4,208,128]{3,2,1,0:T(8,128)(2,1)} %shard_map.140.rows_ref, bf16[2,16,5,128,128]{4,3,2,1,0:T(8,128)(2,1)} %bitcast.59, f32[832,128]{1,0:T(8,128)} %tile.40.keep_ref), custom_call_target="tpu_custom_call" | custom-call | flops 2181038080 | bytes 13058048 | tf_op jit(solution)/shard_map/pallas_call | solution.py:204
  142.8 16.8 %shard_map.142 = f32[4,192,512]{2,1,0:T(8,128)} custom-call(bf16[16,4,208,128]{3,2,1,0:T(8,128)(2,1)} %shard_map.141.rows_ref, bf16[2,16,5,128,128]{4,3,2,1,0:T(8,128)(2,1)} %bitcast.60, bf16[16,128,512]{2,1,0:T(8,128)(2,1)} %bitcast.70), custom_call_target="tpu_custom_call" | custom-call | flops 3925868544 | bytes 9699328 | tf_op jit(solution)/shard_map/pallas_call | solution.py:204
  159.6 2.7 %copy.80 = f32[4,8,24,512]{3,2,0,1:T(8,128)} copy(f32[4,8,24,512]{3,2,1,0:T(8,128)} %bitcast.62) | data formatting | bytes 3145728 | tf_op jit(solution)/shard_map/reshape | solution.py:305
  162.4 4.6 %all-to-all-start = ((f32[8,4,24,512]{3,2,1,0:T(8,128)}), f32[8,4,24,512]{3,2,1,0:T(8,128)S(1)}, u32[]{:S(2)}, u32[]{:S(2)}) async-start(f32[8,4,24,512]{3,2,1,0:T(8,128)} %bitcast.55), calls=%async_computation | async-start | bytes 3145728 | tf_op jit(solution)/shard_map/all_to_all | solution.py:306
  166.9 1.2 exponential_reduce_fusion.2
  169.7 18.8 %all-to-all-done = f32[8,4,24,512]{3,2,1,0:T(8,128)S(1)} async-done(((f32[8,4,24,512]{3,2,1,0:T(8,128)}), f32[8,4,24,512]{3,2,1,0:T(8,128)S(1)}, u32[]{:S(2)}, u32[]{:S(2)}) %all-to-all-start) | async-done | bytes 1572896 | tf_op jit(solution)/shard_map/all_to_all | solution.py:306
  188.9 0.7 fusion.8
  189.7 0.7 reshape.312
  190.4 3.5 %all-to-all-start.1 = ((f32[8,1,480]{2,1,0:T(1,128)}), f32[8,1,480]{2,1,0:T(1,128)S(1)}, u32[]{:S(2)}, u32[]{:S(2)}) async-start(f32[8,1,480]{2,1,0:T(1,128)} %reshape.312), calls=%async_computation.1 | async-start | bytes 32768 | tf_op jit(solution)/shard_map/all_to_all | solution.py:313
  194.3 0.6 pad.27
  194.9 0.6 pad.26
  196.8 2.3 all-to-all-done.1
  199.6 0.7 reduce.5
  200.9 0.9 pad.25.emit_ref
  201.9 0.7 broadcast_in_dim.31.within_ref
  202.5 0.7 broadcast_in_dim.32.between_ref
  203.2 14.2 %shard_map.143 = (f32[192,5,128]{2,1,0:T(8,128)}, f32[192,1,128]{2,1,0:T(1,128)}) custom-call(f32[5,5,128]{2,1,0:T(8,128)} %broadcast_in_dim.31.within_ref, f32[5,5,128]{2,1,0:T(8,128)} %broadcast_in_dim.32.between_ref, f32[5,128]{1,0:T(8,128)} %pad.24.start_ref, f32[192,5,128]{2,1,0:T(8,128)} %pad.25.emit_ref, f32[192,1,128]{2,1,0:T(1,128)} %bitcast.65, ...), custom_call_target="tpu_custom_call" | custom-call | flops 15728640 | bytes 1376256 | tf_op jit(solution)/shard_map/pallas_call | solution.py:93
  217.4 0.7 slice.30
  219.0 1.4 collective-permute-start.2
  220.4 2.7 %collective-permute-start.3 = (f32[1,5,5,4]{2,3,1,0:T(4,128)S(1)}, f32[1,5,5,4]{2,3,1,0:T(4,128)S(1)}, u32[]{:S(2)}, u32[]{:S(2)}) collective-permute-start(f32[1,5,5,4]{2,3,1,0:T(4,128)S(1)} %get-tuple-element.13), channel_id=1, source_target_pairs={{0,16},{8,24},{16,0},{24,8},{32,48},{40,56},{48,32},{56,40},{64,80... | collective-permute-start | bytes 1208 | tf_op jit(solution)/shard_map/ppermute | solution.py:263
  223.1 1.4 collective-permute-start.4
  224.5 1.0 copy.77
  225.5 1.4 copy.78
  227.3 2.4 collective-permute-start.6
  229.7 1.5 collective-permute-start.7
  231.2 1.1 collective-permute-done.5
  232.8 0.9 collective-permute-done.7
  233.7 0.6 gather_fusion
  235.1 0.7 pad.28.mats_ref
  235.8 2.5 %shard_map.144 = (f32[16,5,128]{2,1,0:T(8,128)}, f32[1,128]{1,0:T(1,128)}) custom-call(f32[5,128]{1,0:T(8,128)} %pad.23.prior_ref, f32[16,5,5,128]{3,2,1,0:T(8,128)} %pad.28.mats_ref), custom_call_target="tpu_custom_call" | custom-call | tf_op jit(solution)/shard_map/pallas_call | solution.py:113
  238.3 0.7 dynamic-slice_bitcast_fusion
  239.9 1.2 bitcast_divide_fusion
  (81 shorter events, 7.4 us)
Async XLA Ops:
  7.2 181.7 %copy-start = (f32[512,5]{0,1:T(8,128)S(1)}, f32[512,5]{0,1:T(8,128)}, u32[]{:S(2)}) copy-start(f32[512,5]{0,1:T(8,128)} %param.22) | copy-start | bytes 30724
  7.2 62.1 %all-gather.5.cloned.1.call-start = ((), (), s32[]{:S(2)}) async-start(), calls=%async_computation.2 | async-start | bytes 4352000 | tf_op jit(solution)/shard_map/all_gather | solution.py:300
  7.9 119.5 %all-gather.7.cloned.1.call-start = ((), (), s32[]{:S(2)}) async-start(), calls=%async_computation.3 | async-start | bytes 5570560 | tf_op jit(solution)/shard_map/all_gather | solution.py:301
  19.2 26.3 %copy-start.6 = (f32[5]{0:T(128)S(1)}, f32[5]{0:T(128)}, u32[]{:S(2)}) copy-start(f32[5]{0:T(128)} %param.25) | copy-start | bytes 64
  40.6 15.3 %collective-permute-start = (bf16[16,4,8,200]{3,2,1,0:T(8,128)(2,1)S(1)}, bf16[16,4,8,200]{3,2,1,0:T(8,128)(2,1)S(1)}, u32[]{:S(2)}, u32[]{:S(2)}) collective-permute-start(bf16[16,4,8,200]{3,2,1,0:T(8,128)(2,1)S(1)} %get-tuple-element.14), channel_id=1, source_target_pairs={{0,8},{8,16},{16,24},{24,32},{32,40},{40,48},{48,56},{56,64},{64,7... | collective-permute-start | bytes 614408 | tf_op jit(solution)/shard_map/ppermute | solution.py:131
  44.1 16.2 %collective-permute-start.1 = (bf16[16,4,8,200]{3,2,1,0:T(8,128)(2,1)S(1)}, bf16[16,4,8,200]{3,2,1,0:T(8,128)(2,1)S(1)}, u32[]{:S(2)}, u32[]{:S(2)}) collective-permute-start(bf16[16,4,8,200]{3,2,1,0:T(8,128)(2,1)S(1)} %get-tuple-element.15), channel_id=1, source_target_pairs={{8,0},{16,8},{24,16},{32,24},{40,32},{48,40},{56,48},{64,56},{72,6... | collective-permute-start | bytes 614408 | tf_op jit(solution)/shard_map/ppermute | solution.py:131
  159.6 10.0 %copy-start.4 = (s32[4]{0:T(128)S(1)}, s32[4]{0:T(128)}, u32[]{:S(2)}) copy-start(s32[4]{0:T(128)} %param.16) | copy-start | bytes 52
  159.6 10.1 %copy-start.1 = (s32[4,192]{1,0:T(4,128)S(1)}, s32[4,192]{1,0:T(4,128)}, u32[]{:S(2)}) copy-start(s32[4,192]{1,0:T(4,128)} %param.17) | copy-start | bytes 9220
  159.6 29.3 %copy-start.5 = (f32[512]{0:T(512)S(1)}, f32[512]{0:T(512)}, u32[]{:S(2)}) copy-start(f32[512]{0:T(512)} %param.21) | copy-start | bytes 6148
  162.4 39.5 %copy-start.2 = (f32[5,5]{1,0:T(8,128)S(1)}, f32[5,5]{1,0:T(8,128)}, u32[]{:S(2)}) copy-start(f32[5,5]{1,0:T(8,128)} %param.23) | copy-start | bytes 304
  162.4 40.2 %copy-start.3 = (f32[5,5]{1,0:T(8,128)S(1)}, f32[5,5]{1,0:T(8,128)}, u32[]{:S(2)}) copy-start(f32[5,5]{1,0:T(8,128)} %param.24) | copy-start | bytes 304
  162.4 26.1 %all-to-all-start = ((f32[8,4,24,512]{3,2,1,0:T(8,128)}), f32[8,4,24,512]{3,2,1,0:T(8,128)S(1)}, u32[]{:S(2)}, u32[]{:S(2)}) async-start(f32[8,4,24,512]{3,2,1,0:T(8,128)} %bitcast.55), calls=%async_computation | async-start | bytes 3145728 | tf_op jit(solution)/shard_map/all_to_all | solution.py:306
  190.4 8.6 %all-to-all-start.1 = ((f32[8,1,480]{2,1,0:T(1,128)}), f32[8,1,480]{2,1,0:T(1,128)S(1)}, u32[]{:S(2)}, u32[]{:S(2)}) async-start(f32[8,1,480]{2,1,0:T(1,128)} %reshape.312), calls=%async_computation.1 | async-start | bytes 32768 | tf_op jit(solution)/shard_map/all_to_all | solution.py:313
  219.0 8.0 %collective-permute-start.2 = (f32[1,5,5,4]{2,3,1,0:T(4,128)S(1)}, f32[1,5,5,4]{2,3,1,0:T(4,128)S(1)}, u32[]{:S(2)}, u32[]{:S(2)}) collective-permute-start(f32[1,5,5,4]{2,3,1,0:T(4,128)S(1)} %get-tuple-element.13), channel_id=1, source_target_pairs={{0,8},{8,16},{16,24},{24,0},{32,40},{40,48},{48,56},{56,32},{64,72... | collective-permute-start | bytes 1208 | tf_op jit(solution)/shard_map/ppermute | solution.py:263
  220.4 6.6 %collective-permute-start.3 = (f32[1,5,5,4]{2,3,1,0:T(4,128)S(1)}, f32[1,5,5,4]{2,3,1,0:T(4,128)S(1)}, u32[]{:S(2)}, u32[]{:S(2)}) collective-permute-start(f32[1,5,5,4]{2,3,1,0:T(4,128)S(1)} %get-tuple-element.13), channel_id=1, source_target_pairs={{0,16},{8,24},{16,0},{24,8},{32,48},{40,56},{48,32},{56,40},{64,80... | collective-permute-start | bytes 1208 | tf_op jit(solution)/shard_map/ppermute | solution.py:263
  223.1 3.9 %collective-permute-start.4 = (f32[1,5,5,4]{2,3,1,0:T(4,128)S(1)}, f32[1,5,5,4]{2,3,1,0:T(4,128)S(1)}, u32[]{:S(2)}, u32[]{:S(2)}) collective-permute-start(f32[1,5,5,4]{2,3,1,0:T(4,128)S(1)} %get-tuple-element.13), channel_id=1, source_target_pairs={{0,24},{8,0},{16,8},{24,16},{32,56},{40,32},{48,40},{56,48},{64,88... | collective-permute-start | bytes 1208 | tf_op jit(solution)/shard_map/ppermute | solution.py:263
  227.0 5.3 %collective-permute-start.5 = (f32[4,5,5,4]{2,3,1,0:T(4,128)S(1)}, f32[4,5,5,4]{2,3,1,0:T(4,128)S(1)}, u32[]{:S(2)}, u32[]{:S(2)}) collective-permute-start(f32[4,5,5,4]{2,3,1,0:T(4,128)S(1)} %pad_maximum_fusion.1), channel_id=1, source_target_pairs={{0,32},{8,40},{16,48},{24,56},{32,64},{40,72},{48,80},{56,88},{64,... | collective-permute-start | bytes 4808 | tf_op jit(solution)/shard_map/ppermute | solution.py:263
  227.3 5.5 %collective-permute-start.6 = (f32[4,5,5,4]{2,3,1,0:T(4,128)S(1)}, f32[4,5,5,4]{2,3,1,0:T(4,128)S(1)}, u32[]{:S(2)}, u32[]{:S(2)}) collective-permute-start(f32[4,5,5,4]{2,3,1,0:T(4,128)S(1)} %pad_maximum_fusion.1), channel_id=1, source_target_pairs={{0,64},{8,72},{16,80},{24,88},{32,96},{40,104},{48,112},{56,120},{... | collective-permute-start | bytes 4808 | tf_op jit(solution)/shard_map/ppermute | solution.py:263
  229.7 4.0 %collective-permute-start.7 = (f32[4,5,5,4]{2,3,1,0:T(4,128)S(1)}, f32[4,5,5,4]{2,3,1,0:T(4,128)S(1)}, u32[]{:S(2)}, u32[]{:S(2)}) collective-permute-start(f32[4,5,5,4]{2,3,1,0:T(4,128)S(1)} %pad_maximum_fusion.1), channel_id=1, source_target_pairs={{0,96},{8,104},{16,112},{24,120},{32,0},{40,8},{48,16},{56,24},{64... | collective-permute-start | bytes 4808 | tf_op jit(solution)/shard_map/ppermute | solution.py:263
Sparse Core Ops, SparseCore 0:
  10.2 59.0 all-gather.4
  71.4 55.9 all-gather.6

commit v10 on v9

--- a/solution.py
+++ b/solution.py
@@ -194,8 +194,12 @@
     return jnp.tile(jnp.broadcast_to(keep[:, None], (span, EMB)), (recordings, 1))
 
 
-def per_type_call(kernel, rows, taps, side, out_block, out_shape, out_map, flops, layer=None):
+def per_type_call(kernel, rows, taps, side, out_block, out_shape, out_map, flops, layer=None, part=None):
     types, recordings = rows.shape[:2]
+    rows_spec = pl.BlockSpec((1,) + rows.shape[1:], lambda m: (m, 0, 0, 0))
+    if part is not None:
+        count = out_block[0]
+        rows_spec = pl.BlockSpec((1, count) + rows.shape[2:], lambda m: (m, part, 0, 0))
     side_spec = (
         pl.BlockSpec((1,) + side.shape[1:], lambda m: (m, 0, 0))
         if kernel is last_kernel
@@ -205,7 +209,7 @@
         kernel,
         grid=(types,),
         in_specs=[
-            pl.BlockSpec((1,) + rows.shape[1:], lambda m: (m, 0, 0, 0)),
+            rows_spec,
             pl.BlockSpec((1,) + taps.shape[1:], lambda m: (m, 0, 0, 0))
             if layer is None
             else pl.BlockSpec((1, 1) + taps.shape[2:], lambda m: (layer, m, 0, 0, 0)),
@@ -239,12 +243,16 @@
             lambda m: (m, 0, 0, 0), 2 * types * recordings * span * EMB * EMB * taps, depth_index,
         )
     mix_width = mix.shape[-1]
-    return per_type_call(
-        last_kernel, current, hidden_taps, mix,
-        (recordings, patches, mix_width), jax.ShapeDtypeStruct((recordings, patches, mix_width), jnp.float32),
-        lambda m: (0, 0, 0), 2 * types * recordings * span * EMB * (EMB * taps + mix_width), layers - 1,
-    )
-
+    halves = 2
+    count = recordings // halves
+    return [
+        per_type_call(
+            last_kernel, current, hidden_taps, mix,
+            (count, patches, mix_width), jax.ShapeDtypeStruct((count, patches, mix_width), jnp.float32),
+            lambda m: (0, 0, 0), 2 * types * count * span * EMB * (EMB * taps + mix_width), layers - 1, half,
+        )
+        for half in range(halves)
+    ]
 
 def torus_gather(block, rec_index, side):
     inner = rec_index % side
@@ -302,14 +310,18 @@
     extended = halo_rows(patch_rows, HALO)
     partial_value = conv_mix(extended, first_taps, hidden_taps, mix_weight[:, 0], rec_index, patches)
     spread = lax.axis_size("chan")
-    pieces = partial_value.reshape(recordings, spread, patches // spread, partial_value.shape[-1])
-    pieces = lax.all_to_all(jnp.swapaxes(pieces, 0, 1), "chan", 0, 0, tiled=True)
-    summed = jnp.sum(pieces, axis=0)
-    average = jnp.mean(summed, axis=-1, keepdims=True)
-    centred = summed - average
-    variance = jnp.mean(centred * centred, axis=-1, keepdims=True)
-    activated = jax.nn.gelu(centred * lax.rsqrt(variance + EPSILON) * norm_gain)
-    emission = jnp.einsum("bpo,os->bps", activated, emit_weight, precision=lax.Precision.HIGHEST)
+    emissions = []
+    for part_value in partial_value:
+        count = part_value.shape[0]
+        pieces = part_value.reshape(count, spread, patches // spread, part_value.shape[-1])
+        pieces = lax.all_to_all(jnp.swapaxes(pieces, 0, 1), "chan", 0, 0, tiled=True)
+        summed = jnp.sum(pieces, axis=0)
+        average = jnp.mean(summed, axis=-1, keepdims=True)
+        centred = summed - average
+        variance = jnp.mean(centred * centred, axis=-1, keepdims=True)
+        activated = jax.nn.gelu(centred * lax.rsqrt(variance + EPSILON) * norm_gain)
+        emissions.append(jnp.einsum("bpo,os->bps", activated, emit_weight, precision=lax.Precision.HIGHEST))
+    emission = jnp.concatenate(emissions, axis=0)
     shared = lax.all_to_all(jnp.broadcast_to(emission[None], (spread,) + emission.shape), "chan", 0, 0, tiled=True)
     emission = jnp.swapaxes(shared, 0, 1).reshape(recordings, patches, STATES)
     positions = rec_index * patches + jnp.arange(patches, dtype=jnp.int32)

time: 250 us -> 261 us (1.044)
  Pallas kernels: 66.3 us -> 78.1 us
  waiting for transfers between devices: 81.4 us -> 74.4 us
  starting transfers between devices: 22.8 us -> 27.5 us
    pallas_call x3 -> x4, Pallas kernels: 49.7 us -> 61.4 us  [per_type_call(): pl.pallas_call(kernel, grid=(types,), in_specs=[rows_spec, pl.BlockSpec((...]
    all_to_all x1 -> x2, waiting for transfers between devices: 18.8 us -> 13.1 us  [local(): lax.all_to_all(jnp.swapaxes(pieces, 0, 1), 'chan', 0, 0, tiled=True)]
    all_to_all x1 -> x2, starting transfers between devices: 4.56 us -> 9.23 us  [local(): lax.all_to_all(jnp.swapaxes(pieces, 0, 1), 'chan', 0, 0, tiled=True)]
  transfers between devices with their start and end apart: 12 -> 13, of which waited for: 9 -> 9; matrix products, arithmetic and copies ran while one was open for 19% -> 19% of each run, Pallas kernels for 7% -> 12%
where the time goes in v10:
time: 261 us; the launch traced here: 259 us
  Pallas kernels  78.1 us (30%)
  waiting for transfers between devices  74.4 us (29%)
  local copies, waits for them, and re-layouts  46.1 us (18%)
  starting transfers between devices  27.5 us (11%)
  between operations  15.8 us (6%)
  other arithmetic  12.6 us (5%)
  matrix products  4.69 us (2%)
    pallas_call x4, Pallas kernels, per_type_call(): pl.pallas_call(kernel, grid=(types,), in_specs=[rows_spec, pl.BlockSpec((...  61.4 us
    all_gather x1, waiting for transfers between devices, local(): lax.all_gather(jnp.swapaxes(conv_hid[:, 0], 0, 1), 'rec', axis=1, tiled=T...  39.7 us
    reshape x1, local copies, waits for them, and re-layouts, local(): patch_rows = rows.reshape(groups, recordings, patches, SAMP)  20.3 us
    pallas_call x1, Pallas kernels, crf_forward(): pl.pallas_call(prefix_kernel, out_shape=(jax.ShapeDtypeStruct((patches, S...  14.2 us
    all_to_all x2, waiting for transfers between devices, local(): lax.all_to_all(jnp.swapaxes(pieces, 0, 1), 'chan', 0, 0, tiled=True)  13.1 us
    ppermute x2, waiting for transfers between devices, neighbour_shift(): return lax.ppermute(block, axis, route)  12.9 us
    ppermute x6, starting transfers between devices, shifted(): return lax.ppermute(values, 'rec', route)  9.78 us
    all_to_all x2, starting transfers between devices, local(): lax.all_to_all(jnp.swapaxes(pieces, 0, 1), 'chan', 0, 0, tiled=True)  9.23 us
  transfers between devices with their start and end apart: 13, of which 9 were waited for; matrix products, arithmetic and copies ran while one was open for 19% of the time, Pallas kernels for 12%

profile of v10, /device:TPU:0, one launch (start us, length us, event | category | flops | bytes accessed | tf_op | source)
XLA Modules:
  0.0 259.2 jit_solution(16949856930887115071)
XLA Ops:
  7.2 0.7 all-gather.5.cloned.1.call-update
  8.0 0.7 all-gather.7.cloned.1.call-update
  8.7 0.7 broadcast_compare_fusion
  9.4 3.8 %fusion = bf16[16,4,38400]{2,0,1:T(8,128)(2,1)S(1)} fusion(bf16[4,16,38400]{2,1,0:T(8,128)(2,1)} %param.13, s32[4,16]{1,0:T(4,128)} %bitcast.78, pred[4,16]{1,0:T(4,128)(4,1)S(1)} %broadcast_compare_fusion), kind=kOutput, calls=%fused_computation.2 | convolution fusion | flops 81102848 | bytes 9830720 | tf_op jit(solution)/shard_map/bms,bst->mbt/dot_general | solution.py:304
  13.2 6.0 %copy.70 = bf16[16,4,38400]{2,1,0:T(4,128)(2,1)} copy(bf16[16,4,38400]{2,0,1:T(8,128)(2,1)S(1)} %fusion) | data formatting | bytes 9830400 | tf_op jit(solution)/shard_map/convert_element_type | solution.py:306
  19.2 20.3 %reshape.305 = bf16[16,4,192,200]{3,2,1,0:T(8,128)(2,1)} reshape(bf16[16,4,38400]{2,1,0:T(4,128)(2,1)} %copy.70) | data formatting | bytes 9830400 | tf_op jit(solution)/shard_map/reshape | solution.py:307
  39.5 1.1 fusion.66
  40.6 3.6 %collective-permute-start = (bf16[16,4,8,200]{3,2,1,0:T(8,128)(2,1)S(1)}, bf16[16,4,8,200]{3,2,1,0:T(8,128)(2,1)S(1)}, u32[]{:S(2)}, u32[]{:S(2)}) collective-permute-start(bf16[16,4,8,200]{3,2,1,0:T(8,128)(2,1)S(1)} %get-tuple-element.16), channel_id=1, source_target_pairs={{0,8},{8,16},{16,24},{24,32},{32,40},{40,48},{48,56},{56,64},{64,7... | collective-permute-start | bytes 614408 | tf_op jit(solution)/shard_map/ppermute | solution.py:131
  44.1 1.3 collective-permute-start.1
  46.2 1.2 exponential_reduce_fusion.2
  47.4 8.4 %collective-permute-done = bf16[16,4,8,200]{3,2,1,0:T(8,128)(2,1)S(1)} collective-permute-done((bf16[16,4,8,200]{3,2,1,0:T(8,128)(2,1)S(1)}, bf16[16,4,8,200]{3,2,1,0:T(8,128)(2,1)S(1)}, u32[]{:S(2)}, u32[]{:S(2)}) %collective-permute-start) | collective-permute-done | bytes 204832 | tf_op jit(solution)/shard_map/ppermute | solution.py:131
  55.8 4.5 %collective-permute-done.1 = bf16[16,4,8,200]{3,2,1,0:T(8,128)(2,1)S(1)} collective-permute-done((bf16[16,4,8,200]{3,2,1,0:T(8,128)(2,1)S(1)}, bf16[16,4,8,200]{3,2,1,0:T(8,128)(2,1)S(1)}, u32[]{:S(2)}, u32[]{:S(2)}) %collective-permute-start.1) | collective-permute-done | bytes 204832 | tf_op jit(solution)/shard_map/ppermute | solution.py:131
  60.3 6.4 %pad_maximum_fusion.rows_ref = bf16[16,4,208,200]{3,2,1,0:T(8,128)(2,1)} fusion(bf16[16,4,8,200]{3,2,1,0:T(8,128)(2,1)S(1)} %collective-permute-done.1, bf16[16,4,192,200]{3,2,1,0:T(8,128)(2,1)} %reshape.305, bf16[16,4,8,200]{3,2,1,0:T(8,128)(2,1)S(1)} %collective-permute-done), kind=kLoop, calls=%fused_computation.3 | loop fusion | flops 15974400 | bytes 10649600 | tf_op jit(solution)/shard_map/concatenate | solution.py:138
  66.7 2.5 all-gather.5.cloned.1.call-done
  69.3 0.9 tile.40.keep_ref
  70.2 17.5 %shard_map.140.rows_ref = bf16[16,4,208,128]{3,2,1,0:T(8,128)(2,1)} custom-call(bf16[16,4,208,200]{3,2,1,0:T(8,128)(2,1)} %pad_maximum_fusion.rows_ref, bf16[16,5,200,128]{3,2,1,0:T(8,128)(2,1)} %bitcast.70, f32[832,128]{1,0:T(8,128)} %tile.40.keep_ref), custom_call_target="tpu_custom_call" | custom-call | flops 3407872000 | bytes 16449536 | tf_op jit(solution)/shard_map/pallas_call | solution.py:208
  87.7 39.7 %all-gather.7.cloned.1.call-done = bf16[1,1,2,80,128,128]{5,4,3,2,1,0:T(8,128)(2,1)} async-done(((bf16[1,1,2,5,128,128]{5,4,3,2,1,0:T(8,128)(2,1)}), bf16[1,1,2,80,128,128]{5,4,3,2,1,0:T(8,128)(2,1)}) %all-gather.7.cloned.1.call-update) | async-done | bytes 5242896 | tf_op jit(solution)/shard_map/all_gather | solution.py:309
  127.4 15.4 %shard_map.141.rows_ref = bf16[16,4,208,128]{3,2,1,0:T(8,128)(2,1)} custom-call(bf16[16,4,208,128]{3,2,1,0:T(8,128)(2,1)} %shard_map.140.rows_ref, bf16[2,16,5,128,128]{4,3,2,1,0:T(8,128)(2,1)} %bitcast.65, f32[832,128]{1,0:T(8,128)} %tile.40.keep_ref), custom_call_target="tpu_custom_call" | custom-call | flops 2181038080 | bytes 13058048 | tf_op jit(solution)/shard_map/pallas_call | solution.py:208
  142.8 14.3 %shard_map.143 = f32[2,192,512]{2,1,0:T(8,128)} custom-call(bf16[16,4,208,128]{3,2,1,0:T(8,128)(2,1)} %shard_map.141.rows_ref, bf16[2,16,5,128,128]{4,3,2,1,0:T(8,128)(2,1)} %bitcast.66, bf16[16,128,512]{2,1,0:T(8,128)(2,1)} %bitcast.68), custom_call_target="tpu_custom_call" | custom-call | flops 1962934272 | bytes 8912896 | tf_op jit(solution)/shard_map/pallas_call | solution.py:208
  157.1 2.1 copy.84
  159.2 4.4 %all-to-all-start.1 = ((f32[8,2,24,512]{3,2,1,0:T(8,128)}), f32[8,2,24,512]{3,2,1,0:T(8,128)S(1)}, u32[]{:S(2)}, u32[]{:S(2)}) async-start(f32[8,2,24,512]{3,2,1,0:T(8,128)} %bitcast.60), calls=%async_computation.1 | async-start | bytes 1572864 | tf_op jit(solution)/shard_map/all_to_all | solution.py:317
  165.1 14.3 %shard_map.142 = f32[2,192,512]{2,1,0:T(8,128)} custom-call(bf16[16,4,208,128]{3,2,1,0:T(8,128)(2,1)} %shard_map.141.rows_ref, bf16[2,16,5,128,128]{4,3,2,1,0:T(8,128)(2,1)} %bitcast.67, bf16[16,128,512]{2,1,0:T(8,128)(2,1)} %bitcast.69), custom_call_target="tpu_custom_call" | custom-call | flops 1962934272 | bytes 8912896 | tf_op jit(solution)/shard_map/pallas_call | solution.py:208
  179.4 2.1 copy.85
  181.5 4.8 %all-to-all-start = ((f32[8,2,24,512]{3,2,1,0:T(8,128)}), f32[8,2,24,512]{3,2,1,0:T(8,128)S(1)}, u32[]{:S(2)}, u32[]{:S(2)}) async-start(f32[8,2,24,512]{3,2,1,0:T(8,128)} %bitcast.61), calls=%async_computation | async-start | bytes 1572864 | tf_op jit(solution)/shard_map/all_to_all | solution.py:317
  186.4 13.1 %all-to-all-done = f32[8,2,24,512]{3,2,1,0:T(8,128)S(1)} async-done(((f32[8,2,24,512]{3,2,1,0:T(8,128)}), f32[8,2,24,512]{3,2,1,0:T(8,128)S(1)}, u32[]{:S(2)}, u32[]{:S(2)}) %all-to-all-start) | async-done | bytes 786464 | tf_op jit(solution)/shard_map/all_to_all | solution.py:317
  201.0 0.7 reshape.328
  201.7 3.5 %all-to-all-start.2 = ((f32[8,1,480]{2,1,0:T(1,128)}), f32[8,1,480]{2,1,0:T(1,128)S(1)}, u32[]{:S(2)}, u32[]{:S(2)}) async-start(f32[8,1,480]{2,1,0:T(1,128)} %reshape.328), calls=%async_computation.2 | async-start | bytes 32768 | tf_op jit(solution)/shard_map/all_to_all | solution.py:325
  208.1 2.3 all-to-all-done.2
  210.8 0.7 reduce.6
  212.2 0.9 pad.25.emit_ref
  213.1 0.7 broadcast_in_dim.31.within_ref
  213.8 0.7 broadcast_in_dim.32.between_ref
  214.5 14.2 %shard_map.144 = (f32[192,5,128]{2,1,0:T(8,128)}, f32[192,1,128]{2,1,0:T(1,128)}) custom-call(f32[5,5,128]{2,1,0:T(8,128)} %broadcast_in_dim.31.within_ref, f32[5,5,128]{2,1,0:T(8,128)} %broadcast_in_dim.32.between_ref, f32[5,128]{1,0:T(8,128)} %pad.24.start_ref, f32[192,5,128]{2,1,0:T(8,128)} %pad.25.emit_ref, f32[192,1,128]{2,1,0:T(1,128)} %bitcast.75, ...), custom_call_target="tpu_custom_call" | custom-call | flops 15728640 | bytes 1376256 | tf_op jit(solution)/shard_map/pallas_call | solution.py:93
  228.6 0.7 slice.30
  230.2 1.4 collective-permute-start.2
  231.6 2.7 %collective-permute-start.3 = (f32[1,5,5,4]{2,3,1,0:T(4,128)S(1)}, f32[1,5,5,4]{2,3,1,0:T(4,128)S(1)}, u32[]{:S(2)}, u32[]{:S(2)}) collective-permute-start(f32[1,5,5,4]{2,3,1,0:T(4,128)S(1)} %get-tuple-element.15), channel_id=1, source_target_pairs={{0,16},{8,24},{16,0},{24,8},{32,48},{40,56},{48,32},{56,40},{64,80... | collective-permute-start | bytes 1208 | tf_op jit(solution)/shard_map/ppermute | solution.py:271
  234.4 1.4 collective-permute-start.4
  235.8 1.0 copy.80
  236.8 1.4 copy.81
  238.6 2.4 collective-permute-start.6
  241.0 1.5 collective-permute-start.7
  242.5 1.1 collective-permute-done.5
  244.1 0.9 collective-permute-done.7
  245.0 0.6 gather_fusion
  246.4 0.7 pad.28.mats_ref
  247.1 2.5 shard_map.145
  249.6 0.7 dynamic-slice_bitcast_fusion
  251.2 1.2 bitcast_divide_fusion
  (90 shorter events, 9.7 us)
Async XLA Ops:
  7.2 192.8 %copy-start = (f32[512,5]{0,1:T(8,128)S(1)}, f32[512,5]{0,1:T(8,128)}, u32[]{:S(2)}) copy-start(f32[512,5]{0,1:T(8,128)} %param.22) | copy-start | bytes 30724
  7.2 62.1 %all-gather.5.cloned.1.call-start = ((), (), s32[]{:S(2)}) async-start(), calls=%async_computation.3 | async-start | bytes 4352000 | tf_op jit(solution)/shard_map/all_gather | solution.py:308
  7.9 119.5 %all-gather.7.cloned.1.call-start = ((), (), s32[]{:S(2)}) async-start(), calls=%async_computation.4 | async-start | bytes 5570560 | tf_op jit(solution)/shard_map/all_gather | solution.py:309
  19.2 26.3 %copy-start.6 = (f32[5]{0:T(128)S(1)}, f32[5]{0:T(128)}, u32[]{:S(2)}) copy-start(f32[5]{0:T(128)} %param.25) | copy-start | bytes 64
  40.6 15.3 %collective-permute-start = (bf16[16,4,8,200]{3,2,1,0:T(8,128)(2,1)S(1)}, bf16[16,4,8,200]{3,2,1,0:T(8,128)(2,1)S(1)}, u32[]{:S(2)}, u32[]{:S(2)}) collective-permute-start(bf16[16,4,8,200]{3,2,1,0:T(8,128)(2,1)S(1)} %get-tuple-element.16), channel_id=1, source_target_pairs={{0,8},{8,16},{16,24},{24,32},{32,40},{40,48},{48,56},{56,64},{64,7... | collective-permute-start | bytes 614408 | tf_op jit(solution)/shard_map/ppermute | solution.py:131
  44.1 16.2 %collective-permute-start.1 = (bf16[16,4,8,200]{3,2,1,0:T(8,128)(2,1)S(1)}, bf16[16,4,8,200]{3,2,1,0:T(8,128)(2,1)S(1)}, u32[]{:S(2)}, u32[]{:S(2)}) collective-permute-start(bf16[16,4,8,200]{3,2,1,0:T(8,128)(2,1)S(1)} %get-tuple-element.17), channel_id=1, source_target_pairs={{8,0},{16,8},{24,16},{32,24},{40,32},{48,40},{56,48},{64,56},{72,6... | collective-permute-start | bytes 614408 | tf_op jit(solution)/shard_map/ppermute | solution.py:131
  159.2 22.2 %all-to-all-start.1 = ((f32[8,2,24,512]{3,2,1,0:T(8,128)}), f32[8,2,24,512]{3,2,1,0:T(8,128)S(1)}, u32[]{:S(2)}, u32[]{:S(2)}) async-start(f32[8,2,24,512]{3,2,1,0:T(8,128)} %bitcast.60), calls=%async_computation.1 | async-start | bytes 1572864 | tf_op jit(solution)/shard_map/all_to_all | solution.py:317
  165.1 21.2 %copy-start.4 = (s32[4]{0:T(128)S(1)}, s32[4]{0:T(128)}, u32[]{:S(2)}) copy-start(s32[4]{0:T(128)} %param.16) | copy-start | bytes 52
  165.1 21.3 %copy-start.1 = (s32[4,192]{1,0:T(4,128)S(1)}, s32[4,192]{1,0:T(4,128)}, u32[]{:S(2)}) copy-start(s32[4,192]{1,0:T(4,128)} %param.17) | copy-start | bytes 9220
  165.1 34.9 %copy-start.5 = (f32[512]{0:T(512)S(1)}, f32[512]{0:T(512)}, u32[]{:S(2)}) copy-start(f32[512]{0:T(512)} %param.21) | copy-start | bytes 6148
  179.4 33.8 %copy-start.2 = (f32[5,5]{1,0:T(8,128)S(1)}, f32[5,5]{1,0:T(8,128)}, u32[]{:S(2)}) copy-start(f32[5,5]{1,0:T(8,128)} %param.23) | copy-start | bytes 304
  179.4 34.4 %copy-start.3 = (f32[5,5]{1,0:T(8,128)S(1)}, f32[5,5]{1,0:T(8,128)}, u32[]{:S(2)}) copy-start(f32[5,5]{1,0:T(8,128)} %param.24) | copy-start | bytes 304
  181.5 18.0 %all-to-all-start = ((f32[8,2,24,512]{3,2,1,0:T(8,128)}), f32[8,2,24,512]{3,2,1,0:T(8,128)S(1)}, u32[]{:S(2)}, u32[]{:S(2)}) async-start(f32[8,2,24,512]{3,2,1,0:T(8,128)} %bitcast.61), calls=%async_computation | async-start | bytes 1572864 | tf_op jit(solution)/shard_map/all_to_all | solution.py:317
  201.7 8.6 %all-to-all-start.2 = ((f32[8,1,480]{2,1,0:T(1,128)}), f32[8,1,480]{2,1,0:T(1,128)S(1)}, u32[]{:S(2)}, u32[]{:S(2)}) async-start(f32[8,1,480]{2,1,0:T(1,128)} %reshape.328), calls=%async_computation.2 | async-start | bytes 32768 | tf_op jit(solution)/shard_map/all_to_all | solution.py:325
  230.2 8.0 %collective-permute-start.2 = (f32[1,5,5,4]{2,3,1,0:T(4,128)S(1)}, f32[1,5,5,4]{2,3,1,0:T(4,128)S(1)}, u32[]{:S(2)}, u32[]{:S(2)}) collective-permute-start(f32[1,5,5,4]{2,3,1,0:T(4,128)S(1)} %get-tuple-element.15), channel_id=1, source_target_pairs={{0,8},{8,16},{16,24},{24,0},{32,40},{40,48},{48,56},{56,32},{64,72... | collective-permute-start | bytes 1208 | tf_op jit(solution)/shard_map/ppermute | solution.py:271
  231.6 6.6 %collective-permute-start.3 = (f32[1,5,5,4]{2,3,1,0:T(4,128)S(1)}, f32[1,5,5,4]{2,3,1,0:T(4,128)S(1)}, u32[]{:S(2)}, u32[]{:S(2)}) collective-permute-start(f32[1,5,5,4]{2,3,1,0:T(4,128)S(1)} %get-tuple-element.15), channel_id=1, source_target_pairs={{0,16},{8,24},{16,0},{24,8},{32,48},{40,56},{48,32},{56,40},{64,80... | collective-permute-start | bytes 1208 | tf_op jit(solution)/shard_map/ppermute | solution.py:271
  234.4 3.9 %collective-permute-start.4 = (f32[1,5,5,4]{2,3,1,0:T(4,128)S(1)}, f32[1,5,5,4]{2,3,1,0:T(4,128)S(1)}, u32[]{:S(2)}, u32[]{:S(2)}) collective-permute-start(f32[1,5,5,4]{2,3,1,0:T(4,128)S(1)} %get-tuple-element.15), channel_id=1, source_target_pairs={{0,24},{8,0},{16,8},{24,16},{32,56},{40,32},{48,40},{56,48},{64,88... | collective-permute-start | bytes 1208 | tf_op jit(solution)/shard_map/ppermute | solution.py:271
  238.3 5.3 %collective-permute-start.5 = (f32[4,5,5,4]{2,3,1,0:T(4,128)S(1)}, f32[4,5,5,4]{2,3,1,0:T(4,128)S(1)}, u32[]{:S(2)}, u32[]{:S(2)}) collective-permute-start(f32[4,5,5,4]{2,3,1,0:T(4,128)S(1)} %pad_maximum_fusion.1), channel_id=1, source_target_pairs={{0,32},{8,40},{16,48},{24,56},{32,64},{40,72},{48,80},{56,88},{64,... | collective-permute-start | bytes 4808 | tf_op jit(solution)/shard_map/ppermute | solution.py:271
  238.6 5.5 %collective-permute-start.6 = (f32[4,5,5,4]{2,3,1,0:T(4,128)S(1)}, f32[4,5,5,4]{2,3,1,0:T(4,128)S(1)}, u32[]{:S(2)}, u32[]{:S(2)}) collective-permute-start(f32[4,5,5,4]{2,3,1,0:T(4,128)S(1)} %pad_maximum_fusion.1), channel_id=1, source_target_pairs={{0,64},{8,72},{16,80},{24,88},{32,96},{40,104},{48,112},{56,120},{... | collective-permute-start | bytes 4808 | tf_op jit(solution)/shard_map/ppermute | solution.py:271
  241.0 4.0 %collective-permute-start.7 = (f32[4,5,5,4]{2,3,1,0:T(4,128)S(1)}, f32[4,5,5,4]{2,3,1,0:T(4,128)S(1)}, u32[]{:S(2)}, u32[]{:S(2)}) collective-permute-start(f32[4,5,5,4]{2,3,1,0:T(4,128)S(1)} %pad_maximum_fusion.1), channel_id=1, source_target_pairs={{0,96},{8,104},{16,112},{24,120},{32,0},{40,8},{48,16},{56,24},{64... | collective-permute-start | bytes 4808 | tf_op jit(solution)/shard_map/ppermute | solution.py:271
Sparse Core Ops, SparseCore 0:
  10.2 59.0 all-gather.4
  71.4 55.9 all-gather.6

commit v11 on v9

--- a/solution.py
+++ b/solution.py
@@ -57,7 +57,7 @@
         offset_ref[p] = offset
         return state, offset
 
-    lax.fori_loop(0, patches, body, (start_ref[...], jnp.zeros((1, LANES), jnp.float32)))
+    lax.fori_loop(0, patches, body, (start_ref[...], jnp.zeros((1, LANES), jnp.float32)), unroll=8)
 
 
 def chain_kernel(prior_ref, mats_ref, incoming_ref, total_ref):

time: 250 us -> 249 us (level)
  no operation moved by 1% of the time
where the time goes in v11:
time: 249 us; the launch traced here: 247 us
  waiting for transfers between devices  81.4 us (33%)
  Pallas kernels  65.7 us (26%)
  local copies, waits for them, and re-layouts  44.7 us (18%)
  starting transfers between devices  22.8 us (9%)
  between operations  15.7 us (6%)
  other arithmetic  12.4 us (5%)
  matrix products  4.54 us (2%)
    pallas_call x3, Pallas kernels, per_type_call(): pl.pallas_call(kernel, grid=(types,), in_specs=[pl.BlockSpec((1,) + rows....  49.7 us
    all_gather x1, waiting for transfers between devices, local(): lax.all_gather(jnp.swapaxes(conv_hid[:, 0], 0, 1), 'rec', axis=1, tiled=T...  39.7 us
    reshape x1, local copies, waits for them, and re-layouts, local(): patch_rows = rows.reshape(groups, recordings, patches, SAMP)  20.3 us
    all_to_all x1, waiting for transfers between devices, local(): lax.all_to_all(jnp.swapaxes(pieces, 0, 1), 'chan', 0, 0, tiled=True)  18.8 us
    ppermute x2, waiting for transfers between devices, neighbour_shift(): return lax.ppermute(block, axis, route)  14.2 us
    pallas_call x1, Pallas kernels, crf_forward(): pl.pallas_call(prefix_kernel, out_shape=(jax.ShapeDtypeStruct((patches, S...  13.5 us
    ppermute x6, starting transfers between devices, shifted(): return lax.ppermute(values, 'rec', route)  9.78 us
    concatenate x1, other arithmetic, halo_rows(): return jnp.concatenate([from_left, patch_rows, from_right], axis=2)  6.4 us
  transfers between devices with their start and end apart: 12, of which 9 were waited for; matrix products, arithmetic and copies ran while one was open for 19% of the time, Pallas kernels for 7%

profile of v11, /device:TPU:0, one launch (start us, length us, event | category | flops | bytes accessed | tf_op | source)
XLA Modules:
  0.0 247.3 jit_solution(5024112116254126976)
XLA Ops:
  7.2 0.7 all-gather.5.cloned.1.call-update
  8.0 0.7 all-gather.7.cloned.1.call-update
  8.7 0.7 broadcast_compare_fusion
  9.4 3.8 %fusion = bf16[16,4,38400]{2,0,1:T(8,128)(2,1)S(1)} fusion(bf16[4,16,38400]{2,1,0:T(8,128)(2,1)} %param.13, s32[4,16]{1,0:T(4,128)} %bitcast.68, pred[4,16]{1,0:T(4,128)(4,1)S(1)} %broadcast_compare_fusion), kind=kOutput, calls=%fused_computation.2 | convolution fusion | flops 81102848 | bytes 9830720 | tf_op jit(solution)/shard_map/bms,bst->mbt/dot_general | solution.py:296
  13.2 6.0 %copy.68 = bf16[16,4,38400]{2,1,0:T(4,128)(2,1)} copy(bf16[16,4,38400]{2,0,1:T(8,128)(2,1)S(1)} %fusion) | data formatting | bytes 9830400 | tf_op jit(solution)/shard_map/convert_element_type | solution.py:298
  19.2 20.3 %reshape.290 = bf16[16,4,192,200]{3,2,1,0:T(8,128)(2,1)} reshape(bf16[16,4,38400]{2,1,0:T(4,128)(2,1)} %copy.68) | data formatting | bytes 9830400 | tf_op jit(solution)/shard_map/reshape | solution.py:299
  39.5 1.1 fusion.43
  40.6 3.6 %collective-permute-start = (bf16[16,4,8,200]{3,2,1,0:T(8,128)(2,1)S(1)}, bf16[16,4,8,200]{3,2,1,0:T(8,128)(2,1)S(1)}, u32[]{:S(2)}, u32[]{:S(2)}) collective-permute-start(bf16[16,4,8,200]{3,2,1,0:T(8,128)(2,1)S(1)} %get-tuple-element.14), channel_id=1, source_target_pairs={{0,8},{8,16},{16,24},{24,32},{32,40},{40,48},{48,56},{56,64},{64,7... | collective-permute-start | bytes 614408 | tf_op jit(solution)/shard_map/ppermute | solution.py:131
  44.1 1.3 collective-permute-start.1
  46.2 9.7 %collective-permute-done = bf16[16,4,8,200]{3,2,1,0:T(8,128)(2,1)S(1)} collective-permute-done((bf16[16,4,8,200]{3,2,1,0:T(8,128)(2,1)S(1)}, bf16[16,4,8,200]{3,2,1,0:T(8,128)(2,1)S(1)}, u32[]{:S(2)}, u32[]{:S(2)}) %collective-permute-start) | collective-permute-done | bytes 204832 | tf_op jit(solution)/shard_map/ppermute | solution.py:131
  55.8 4.5 %collective-permute-done.1 = bf16[16,4,8,200]{3,2,1,0:T(8,128)(2,1)S(1)} collective-permute-done((bf16[16,4,8,200]{3,2,1,0:T(8,128)(2,1)S(1)}, bf16[16,4,8,200]{3,2,1,0:T(8,128)(2,1)S(1)}, u32[]{:S(2)}, u32[]{:S(2)}) %collective-permute-start.1) | collective-permute-done | bytes 204832 | tf_op jit(solution)/shard_map/ppermute | solution.py:131
  60.3 6.4 %pad_maximum_fusion.rows_ref = bf16[16,4,208,200]{3,2,1,0:T(8,128)(2,1)} fusion(bf16[16,4,8,200]{3,2,1,0:T(8,128)(2,1)S(1)} %collective-permute-done.1, bf16[16,4,192,200]{3,2,1,0:T(8,128)(2,1)} %reshape.290, bf16[16,4,8,200]{3,2,1,0:T(8,128)(2,1)S(1)} %collective-permute-done), kind=kLoop, calls=%fused_computation.3 | loop fusion | flops 15974400 | bytes 10649600 | tf_op jit(solution)/shard_map/concatenate | solution.py:138
  66.7 2.5 %all-gather.5.cloned.1.call-done = bf16[16,1,5,200,128]{4,3,2,1,0:T(8,128)(2,1)} async-done(((bf16[1,1,5,200,128]{4,3,2,1,0:T(8,128)(2,1)}), bf16[16,1,5,200,128]{4,3,2,1,0:T(8,128)(2,1)}) %all-gather.5.cloned.1.call-update) | async-done | bytes 4096016 | tf_op jit(solution)/shard_map/all_gather | solution.py:300
  69.3 0.9 tile.40.keep_ref
  70.2 17.5 %shard_map.140.rows_ref = bf16[16,4,208,128]{3,2,1,0:T(8,128)(2,1)} custom-call(bf16[16,4,208,200]{3,2,1,0:T(8,128)(2,1)} %pad_maximum_fusion.rows_ref, bf16[16,5,200,128]{3,2,1,0:T(8,128)(2,1)} %bitcast.61, f32[832,128]{1,0:T(8,128)} %tile.40.keep_ref), custom_call_target="tpu_custom_call" | custom-call | flops 3407872000 | bytes 16449536 | tf_op jit(solution)/shard_map/pallas_call | solution.py:204
  87.7 39.7 %all-gather.7.cloned.1.call-done = bf16[1,1,2,80,128,128]{5,4,3,2,1,0:T(8,128)(2,1)} async-done(((bf16[1,1,2,5,128,128]{5,4,3,2,1,0:T(8,128)(2,1)}), bf16[1,1,2,80,128,128]{5,4,3,2,1,0:T(8,128)(2,1)}) %all-gather.7.cloned.1.call-update) | async-done | bytes 5242896 | tf_op jit(solution)/shard_map/all_gather | solution.py:301
  127.4 15.4 %shard_map.141.rows_ref = bf16[16,4,208,128]{3,2,1,0:T(8,128)(2,1)} custom-call(bf16[16,4,208,128]{3,2,1,0:T(8,128)(2,1)} %shard_map.140.rows_ref, bf16[2,16,5,128,128]{4,3,2,1,0:T(8,128)(2,1)} %bitcast.59, f32[832,128]{1,0:T(8,128)} %tile.40.keep_ref), custom_call_target="tpu_custom_call" | custom-call | flops 2181038080 | bytes 13058048 | tf_op jit(solution)/shard_map/pallas_call | solution.py:204
  142.8 16.8 %shard_map.142 = f32[4,192,512]{2,1,0:T(8,128)} custom-call(bf16[16,4,208,128]{3,2,1,0:T(8,128)(2,1)} %shard_map.141.rows_ref, bf16[2,16,5,128,128]{4,3,2,1,0:T(8,128)(2,1)} %bitcast.60, bf16[16,128,512]{2,1,0:T(8,128)(2,1)} %bitcast.70), custom_call_target="tpu_custom_call" | custom-call | flops 3925868544 | bytes 9699328 | tf_op jit(solution)/shard_map/pallas_call | solution.py:204
  159.6 2.7 %copy.80 = f32[4,8,24,512]{3,2,0,1:T(8,128)} copy(f32[4,8,24,512]{3,2,1,0:T(8,128)} %bitcast.62) | data formatting | bytes 3145728 | tf_op jit(solution)/shard_map/reshape | solution.py:305
  162.4 4.6 %all-to-all-start = ((f32[8,4,24,512]{3,2,1,0:T(8,128)}), f32[8,4,24,512]{3,2,1,0:T(8,128)S(1)}, u32[]{:S(2)}, u32[]{:S(2)}) async-start(f32[8,4,24,512]{3,2,1,0:T(8,128)} %bitcast.55), calls=%async_computation | async-start | bytes 3145728 | tf_op jit(solution)/shard_map/all_to_all | solution.py:306
  166.9 1.2 exponential_reduce_fusion.2
  169.7 18.8 %all-to-all-done = f32[8,4,24,512]{3,2,1,0:T(8,128)S(1)} async-done(((f32[8,4,24,512]{3,2,1,0:T(8,128)}), f32[8,4,24,512]{3,2,1,0:T(8,128)S(1)}, u32[]{:S(2)}, u32[]{:S(2)}) %all-to-all-start) | async-done | bytes 1572896 | tf_op jit(solution)/shard_map/all_to_all | solution.py:306
  188.9 0.7 fusion.8
  189.7 0.7 reshape.312
  190.4 3.5 %all-to-all-start.1 = ((f32[8,1,480]{2,1,0:T(1,128)}), f32[8,1,480]{2,1,0:T(1,128)S(1)}, u32[]{:S(2)}, u32[]{:S(2)}) async-start(f32[8,1,480]{2,1,0:T(1,128)} %reshape.312), calls=%async_computation.1 | async-start | bytes 32768 | tf_op jit(solution)/shard_map/all_to_all | solution.py:313
  194.3 0.6 pad.27
  194.9 0.6 pad.26
  196.8 2.3 all-to-all-done.1
  199.6 0.7 reduce.5
  200.9 0.9 pad.25.emit_ref
  201.9 0.7 broadcast_in_dim.31.within_ref
  202.5 0.7 broadcast_in_dim.32.between_ref
  203.2 13.5 %shard_map.143 = (f32[192,5,128]{2,1,0:T(8,128)}, f32[192,1,128]{2,1,0:T(1,128)}) custom-call(f32[5,5,128]{2,1,0:T(8,128)} %broadcast_in_dim.31.within_ref, f32[5,5,128]{2,1,0:T(8,128)} %broadcast_in_dim.32.between_ref, f32[5,128]{1,0:T(8,128)} %pad.24.start_ref, f32[192,5,128]{2,1,0:T(8,128)} %pad.25.emit_ref, f32[192,1,128]{2,1,0:T(1,128)} %bitcast.65, ...), custom_call_target="tpu_custom_call" | custom-call | flops 15728640 | bytes 1376256 | tf_op jit(solution)/shard_map/pallas_call | solution.py:93
  216.8 0.7 slice.30
  218.3 1.4 collective-permute-start.2
  219.8 2.7 %collective-permute-start.3 = (f32[1,5,5,4]{2,3,1,0:T(4,128)S(1)}, f32[1,5,5,4]{2,3,1,0:T(4,128)S(1)}, u32[]{:S(2)}, u32[]{:S(2)}) collective-permute-start(f32[1,5,5,4]{2,3,1,0:T(4,128)S(1)} %get-tuple-element.13), channel_id=1, source_target_pairs={{0,16},{8,24},{16,0},{24,8},{32,48},{40,56},{48,32},{56,40},{64,80... | collective-permute-start | bytes 1208 | tf_op jit(solution)/shard_map/ppermute | solution.py:263
  222.5 1.4 collective-permute-start.4
  223.9 1.0 copy.77
  224.9 1.4 copy.78
  226.7 2.4 collective-permute-start.6
  229.1 1.5 collective-permute-start.7
  230.6 1.1 collective-permute-done.5
  232.2 0.9 collective-permute-done.7
  233.1 0.6 gather_fusion
  234.5 0.7 pad.28.mats_ref
  235.2 2.5 %shard_map.144 = (f32[16,5,128]{2,1,0:T(8,128)}, f32[1,128]{1,0:T(1,128)}) custom-call(f32[5,128]{1,0:T(8,128)} %pad.23.prior_ref, f32[16,5,5,128]{3,2,1,0:T(8,128)} %pad.28.mats_ref), custom_call_target="tpu_custom_call" | custom-call | tf_op jit(solution)/shard_map/pallas_call | solution.py:113
  237.7 0.7 dynamic-slice_bitcast_fusion
  239.3 1.2 bitcast_divide_fusion
  (81 shorter events, 7.4 us)
Async XLA Ops:
  7.2 181.7 %copy-start = (f32[512,5]{0,1:T(8,128)S(1)}, f32[512,5]{0,1:T(8,128)}, u32[]{:S(2)}) copy-start(f32[512,5]{0,1:T(8,128)} %param.22) | copy-start | bytes 30724
  7.2 62.1 %all-gather.5.cloned.1.call-start = ((), (), s32[]{:S(2)}) async-start(), calls=%async_computation.2 | async-start | bytes 4352000 | tf_op jit(solution)/shard_map/all_gather | solution.py:300
  7.9 119.5 %all-gather.7.cloned.1.call-start = ((), (), s32[]{:S(2)}) async-start(), calls=%async_computation.3 | async-start | bytes 5570560 | tf_op jit(solution)/shard_map/all_gather | solution.py:301
  19.2 26.3 %copy-start.6 = (f32[5]{0:T(128)S(1)}, f32[5]{0:T(128)}, u32[]{:S(2)}) copy-start(f32[5]{0:T(128)} %param.25) | copy-start | bytes 64
  40.6 15.3 %collective-permute-start = (bf16[16,4,8,200]{3,2,1,0:T(8,128)(2,1)S(1)}, bf16[16,4,8,200]{3,2,1,0:T(8,128)(2,1)S(1)}, u32[]{:S(2)}, u32[]{:S(2)}) collective-permute-start(bf16[16,4,8,200]{3,2,1,0:T(8,128)(2,1)S(1)} %get-tuple-element.14), channel_id=1, source_target_pairs={{0,8},{8,16},{16,24},{24,32},{32,40},{40,48},{48,56},{56,64},{64,7... | collective-permute-start | bytes 614408 | tf_op jit(solution)/shard_map/ppermute | solution.py:131
  44.1 16.2 %collective-permute-start.1 = (bf16[16,4,8,200]{3,2,1,0:T(8,128)(2,1)S(1)}, bf16[16,4,8,200]{3,2,1,0:T(8,128)(2,1)S(1)}, u32[]{:S(2)}, u32[]{:S(2)}) collective-permute-start(bf16[16,4,8,200]{3,2,1,0:T(8,128)(2,1)S(1)} %get-tuple-element.15), channel_id=1, source_target_pairs={{8,0},{16,8},{24,16},{32,24},{40,32},{48,40},{56,48},{64,56},{72,6... | collective-permute-start | bytes 614408 | tf_op jit(solution)/shard_map/ppermute | solution.py:131
  159.6 10.0 %copy-start.4 = (s32[4]{0:T(128)S(1)}, s32[4]{0:T(128)}, u32[]{:S(2)}) copy-start(s32[4]{0:T(128)} %param.16) | copy-start | bytes 52
  159.6 10.1 %copy-start.1 = (s32[4,192]{1,0:T(4,128)S(1)}, s32[4,192]{1,0:T(4,128)}, u32[]{:S(2)}) copy-start(s32[4,192]{1,0:T(4,128)} %param.17) | copy-start | bytes 9220
  159.6 29.3 %copy-start.5 = (f32[512]{0:T(512)S(1)}, f32[512]{0:T(512)}, u32[]{:S(2)}) copy-start(f32[512]{0:T(512)} %param.21) | copy-start | bytes 6148
  162.4 39.5 %copy-start.2 = (f32[5,5]{1,0:T(8,128)S(1)}, f32[5,5]{1,0:T(8,128)}, u32[]{:S(2)}) copy-start(f32[5,5]{1,0:T(8,128)} %param.23) | copy-start | bytes 304
  162.4 40.2 %copy-start.3 = (f32[5,5]{1,0:T(8,128)S(1)}, f32[5,5]{1,0:T(8,128)}, u32[]{:S(2)}) copy-start(f32[5,5]{1,0:T(8,128)} %param.24) | copy-start | bytes 304
  162.4 26.1 %all-to-all-start = ((f32[8,4,24,512]{3,2,1,0:T(8,128)}), f32[8,4,24,512]{3,2,1,0:T(8,128)S(1)}, u32[]{:S(2)}, u32[]{:S(2)}) async-start(f32[8,4,24,512]{3,2,1,0:T(8,128)} %bitcast.55), calls=%async_computation | async-start | bytes 3145728 | tf_op jit(solution)/shard_map/all_to_all | solution.py:306
  190.4 8.6 %all-to-all-start.1 = ((f32[8,1,480]{2,1,0:T(1,128)}), f32[8,1,480]{2,1,0:T(1,128)S(1)}, u32[]{:S(2)}, u32[]{:S(2)}) async-start(f32[8,1,480]{2,1,0:T(1,128)} %reshape.312), calls=%async_computation.1 | async-start | bytes 32768 | tf_op jit(solution)/shard_map/all_to_all | solution.py:313
  218.3 8.0 %collective-permute-start.2 = (f32[1,5,5,4]{2,3,1,0:T(4,128)S(1)}, f32[1,5,5,4]{2,3,1,0:T(4,128)S(1)}, u32[]{:S(2)}, u32[]{:S(2)}) collective-permute-start(f32[1,5,5,4]{2,3,1,0:T(4,128)S(1)} %get-tuple-element.13), channel_id=1, source_target_pairs={{0,8},{8,16},{16,24},{24,0},{32,40},{40,48},{48,56},{56,32},{64,72... | collective-permute-start | bytes 1208 | tf_op jit(solution)/shard_map/ppermute | solution.py:263
  219.8 6.6 %collective-permute-start.3 = (f32[1,5,5,4]{2,3,1,0:T(4,128)S(1)}, f32[1,5,5,4]{2,3,1,0:T(4,128)S(1)}, u32[]{:S(2)}, u32[]{:S(2)}) collective-permute-start(f32[1,5,5,4]{2,3,1,0:T(4,128)S(1)} %get-tuple-element.13), channel_id=1, source_target_pairs={{0,16},{8,24},{16,0},{24,8},{32,48},{40,56},{48,32},{56,40},{64,80... | collective-permute-start | bytes 1208 | tf_op jit(solution)/shard_map/ppermute | solution.py:263
  222.5 3.9 %collective-permute-start.4 = (f32[1,5,5,4]{2,3,1,0:T(4,128)S(1)}, f32[1,5,5,4]{2,3,1,0:T(4,128)S(1)}, u32[]{:S(2)}, u32[]{:S(2)}) collective-permute-start(f32[1,5,5,4]{2,3,1,0:T(4,128)S(1)} %get-tuple-element.13), channel_id=1, source_target_pairs={{0,24},{8,0},{16,8},{24,16},{32,56},{40,32},{48,40},{56,48},{64,88... | collective-permute-start | bytes 1208 | tf_op jit(solution)/shard_map/ppermute | solution.py:263
  226.4 5.3 %collective-permute-start.5 = (f32[4,5,5,4]{2,3,1,0:T(4,128)S(1)}, f32[4,5,5,4]{2,3,1,0:T(4,128)S(1)}, u32[]{:S(2)}, u32[]{:S(2)}) collective-permute-start(f32[4,5,5,4]{2,3,1,0:T(4,128)S(1)} %pad_maximum_fusion.1), channel_id=1, source_target_pairs={{0,32},{8,40},{16,48},{24,56},{32,64},{40,72},{48,80},{56,88},{64,... | collective-permute-start | bytes 4808 | tf_op jit(solution)/shard_map/ppermute | solution.py:263
  226.7 5.5 %collective-permute-start.6 = (f32[4,5,5,4]{2,3,1,0:T(4,128)S(1)}, f32[4,5,5,4]{2,3,1,0:T(4,128)S(1)}, u32[]{:S(2)}, u32[]{:S(2)}) collective-permute-start(f32[4,5,5,4]{2,3,1,0:T(4,128)S(1)} %pad_maximum_fusion.1), channel_id=1, source_target_pairs={{0,64},{8,72},{16,80},{24,88},{32,96},{40,104},{48,112},{56,120},{... | collective-permute-start | bytes 4808 | tf_op jit(solution)/shard_map/ppermute | solution.py:263
  229.1 4.0 %collective-permute-start.7 = (f32[4,5,5,4]{2,3,1,0:T(4,128)S(1)}, f32[4,5,5,4]{2,3,1,0:T(4,128)S(1)}, u32[]{:S(2)}, u32[]{:S(2)}) collective-permute-start(f32[4,5,5,4]{2,3,1,0:T(4,128)S(1)} %pad_maximum_fusion.1), channel_id=1, source_target_pairs={{0,96},{8,104},{16,112},{24,120},{32,0},{40,8},{48,16},{56,24},{64... | collective-permute-start | bytes 4808 | tf_op jit(solution)/shard_map/ppermute | solution.py:263
Sparse Core Ops, SparseCore 0:
  10.2 59.0 all-gather.4
  71.4 55.9 all-gather.6

commit v12 on v11

--- a/solution.py
+++ b/solution.py
@@ -15,6 +15,7 @@
 EPSILON = 1e-05
 NEGATIVE = -1e30
 MESH_SIDE = 4
+SUBSHARDS = 4
 HALO = 8
 
 
@@ -81,11 +82,22 @@
 
 def crf_forward(emission, cross, valid, trans_within, trans_between, initial, rec_index):
     recordings, patches, _ = emission.shape
-    width = STATES * recordings
-    emit_in = lanes_padded(jnp.tile(jnp.transpose(emission, (1, 2, 0)), (1, 1, STATES)))
-    cross_in = lanes_padded(jnp.tile(cross.T.astype(jnp.float32), (1, STATES)))[:, None, :]
-    valid_in = lanes_padded(jnp.tile(valid.T.astype(jnp.float32), (1, STATES)))[:, None, :]
-    lane_start = jnp.arange(width, dtype=jnp.int32) // recordings
+    pieces = SUBSHARDS
+    steps = patches // pieces
+    block = STATES * recordings
+    width = pieces * block
+
+    def to_lanes(values):
+        split = values.reshape((recordings, pieces, steps) + values.shape[2:])
+        order = (2,) + tuple(range(3, split.ndim)) + (1, 0)
+        moved = jnp.transpose(split, order)
+        moved = jnp.broadcast_to(moved[..., None, :], moved.shape[:-1] + (STATES, recordings))
+        return lanes_padded(moved.reshape(moved.shape[:-3] + (width,)))
+
+    emit_in = to_lanes(emission)
+    cross_in = to_lanes(cross.astype(jnp.float32))[:, None, :]
+    valid_in = to_lanes(valid.astype(jnp.float32))[:, None, :]
+    lane_start = (jnp.arange(width, dtype=jnp.int32) // recordings) % STATES
     basis = jnp.arange(STATES, dtype=jnp.int32)[:, None] == lane_start[None, :]
     start = lanes_padded(jnp.where(basis, 0.0, NEGATIVE).astype(jnp.float32))
     within_in = jnp.broadcast_to(trans_within[:, :, None], (STATES, STATES, LANES))
@@ -93,37 +105,38 @@
     prefix, offset = pl.pallas_call(
         prefix_kernel,
         out_shape=(
-            jax.ShapeDtypeStruct((patches, STATES, LANES), jnp.float32),
-            jax.ShapeDtypeStruct((patches, 1, LANES), jnp.float32),
+            jax.ShapeDtypeStruct((steps, STATES, LANES), jnp.float32),
+            jax.ShapeDtypeStruct((steps, 1, LANES), jnp.float32),
         ),
         cost_estimate=pl.CostEstimate(
-            flops=patches * 80 * LANES * 8, transcendentals=patches * 8 * LANES * 8,
-            bytes_accessed=patches * 14 * LANES * 4,
+            flops=steps * 80 * LANES * 8, transcendentals=steps * 8 * LANES * 8,
+            bytes_accessed=steps * 14 * LANES * 4,
         ),
     )(within_in, between_in, start, emit_in, cross_in, valid_in)
-    prefix_sj = prefix[:, :, :width].reshape(patches, STATES, STATES, recordings)
-    offset_j = offset[:, 0, :width].reshape(patches, STATES, recordings)
-    transfer = prefix_sj[patches - 1] + offset_j[patches - 1][None]
-    transfer = jnp.transpose(transfer, (1, 0, 2))
+    prefix_sj = prefix[:, :, :width].reshape(steps, STATES, pieces, STATES, recordings)
+    offset_j = offset[:, 0, :width].reshape(steps, pieces, STATES, recordings)
+    transfer = prefix_sj[steps - 1] + offset_j[steps - 1][None]
+    transfer = jnp.transpose(transfer, (1, 2, 0, 3))
     gathered = torus_gather(transfer[None], rec_index, MESH_SIDE)
+    gathered = gathered.reshape((-1,) + gathered.shape[2:])
     mats = lanes_padded(gathered)
     prior = initial - log_sum_exp(initial, 0)
     prior_in = lanes_padded(jnp.broadcast_to(prior[:, None], (STATES, recordings)))
-    groups = gathered.shape[0]
+    count = gathered.shape[0]
     incoming, total = pl.pallas_call(
         chain_kernel,
         out_shape=(
-            jax.ShapeDtypeStruct((groups, STATES, LANES), jnp.float32),
+            jax.ShapeDtypeStruct((count, STATES, LANES), jnp.float32),
             jax.ShapeDtypeStruct((1, LANES), jnp.float32),
         ),
     )(prior_in, mats)
-    here = lax.dynamic_index_in_dim(incoming, rec_index, 0, keepdims=False)[:, :recordings]
+    here = lax.dynamic_slice_in_dim(incoming, rec_index * pieces, pieces, 0)[:, :, :recordings]
     weights = here[None, None] + offset_j[:, None] + prefix_sj
-    reached = log_sum_exp(weights, 2)
+    reached = log_sum_exp(weights, 3)
     totals = log_sum_exp(reached, 1)
-    filtered = jnp.transpose(reached - totals[:, None], (2, 1, 0))
+    normalized = reached - totals[:, None]
+    filtered = jnp.transpose(normalized, (3, 1, 2, 0)).reshape(recordings, STATES, patches)
     return filtered, total[0, :recordings]
-
 
 def neighbour_shift(block, axis, distance):
     devices = range(lax.axis_size(axis))

time: 249 us -> 250 us (level)
  Pallas kernels: 65.7 us -> 59.9 us
  waiting for transfers between devices: 81.4 us -> 85.7 us
    pallas_call x2, Pallas kernels: 16 us -> 10.3 us  [the longest x1 5.77 us: crf_forward(): pl.pallas_call(chain_kernel, out_shape=(jax.ShapeDtypeStruct((count, STAT...]
    ppermute x6, waiting for transfers between devices: 2.5 us -> 6.13 us  [shifted(): return lax.ppermute(values, 'rec', route)]
  transfers between devices with their start and end apart: 12 -> 12, of which waited for: 9 -> 8; matrix products, arithmetic and copies ran while one was open for 19% -> 19% of each run, Pallas kernels for 7% -> 7%
where the time goes in v12:
time: 250 us; the launch traced here: 248 us
  waiting for transfers between devices  85.7 us (34%)
  Pallas kernels  59.9 us (24%)
  local copies, waits for them, and re-layouts  46.9 us (19%)
  starting transfers between devices  22.9 us (9%)
  between operations  15.8 us (6%)
  other arithmetic  12.1 us (5%)
  matrix products  4.54 us (2%)
    pallas_call x3, Pallas kernels, per_type_call(): pl.pallas_call(kernel, grid=(types,), in_specs=[pl.BlockSpec((1,) + rows....  49.7 us
    all_gather x1, waiting for transfers between devices, local(): lax.all_gather(jnp.swapaxes(conv_hid[:, 0], 0, 1), 'rec', axis=1, tiled=T...  39.7 us
    reshape x1, local copies, waits for them, and re-layouts, local(): patch_rows = rows.reshape(groups, recordings, patches, SAMP)  20.3 us
    all_to_all x1, waiting for transfers between devices, local(): lax.all_to_all(jnp.swapaxes(pieces, 0, 1), 'chan', 0, 0, tiled=True)  18.2 us
    ppermute x2, waiting for transfers between devices, neighbour_shift(): return lax.ppermute(block, axis, route)  14.8 us
    ppermute x6, starting transfers between devices, shifted(): return lax.ppermute(values, 'rec', route)  9.84 us
    concatenate x1, other arithmetic, halo_rows(): return jnp.concatenate([from_left, patch_rows, from_right], axis=2)  6.4 us
    ppermute x6, waiting for transfers between devices, shifted(): return lax.ppermute(values, 'rec', route)  6.13 us
  transfers between devices with their start and end apart: 12, of which 8 were waited for; matrix products, arithmetic and copies ran while one was open for 19% of the time, Pallas kernels for 7%

profile of v12, /device:TPU:0, one launch (start us, length us, event | category | flops | bytes accessed | tf_op | source)
XLA Modules:
  0.0 247.8 jit_solution(6137431546043546365)
XLA Ops:
  7.2 0.7 all-gather.5.cloned.1.call-update
  8.0 0.7 all-gather.7.cloned.1.call-update
  8.7 0.7 broadcast_compare_fusion
  9.4 3.8 %fusion = bf16[16,4,38400]{2,0,1:T(8,128)(2,1)S(1)} fusion(bf16[4,16,38400]{2,1,0:T(8,128)(2,1)} %param.13, s32[4,16]{1,0:T(4,128)} %bitcast.66, pred[4,16]{1,0:T(4,128)(4,1)S(1)} %broadcast_compare_fusion), kind=kOutput, calls=%fused_computation.2 | convolution fusion | flops 81102848 | bytes 9830720 | tf_op jit(solution)/shard_map/bms,bst->mbt/dot_general | solution.py:309
  13.2 6.0 %copy.75 = bf16[16,4,38400]{2,1,0:T(4,128)(2,1)} copy(bf16[16,4,38400]{2,0,1:T(8,128)(2,1)S(1)} %fusion) | data formatting | bytes 9830400 | tf_op jit(solution)/shard_map/convert_element_type | solution.py:311
  19.2 20.3 %reshape.289 = bf16[16,4,192,200]{3,2,1,0:T(8,128)(2,1)} reshape(bf16[16,4,38400]{2,1,0:T(4,128)(2,1)} %copy.75) | data formatting | bytes 9830400 | tf_op jit(solution)/shard_map/reshape | solution.py:312
  39.5 1.1 fusion.44
  40.5 3.6 %collective-permute-start = (bf16[16,4,8,200]{3,2,1,0:T(8,128)(2,1)S(1)}, bf16[16,4,8,200]{3,2,1,0:T(8,128)(2,1)S(1)}, u32[]{:S(2)}, u32[]{:S(2)}) collective-permute-start(bf16[16,4,8,200]{3,2,1,0:T(8,128)(2,1)S(1)} %get-tuple-element.14), channel_id=1, source_target_pairs={{0,8},{8,16},{16,24},{24,32},{32,40},{40,48},{48,56},{56,64},{64,7... | collective-permute-start | bytes 614408 | tf_op jit(solution)/shard_map/ppermute | solution.py:144
  44.1 1.3 collective-permute-start.1
  45.5 10.3 %collective-permute-done = bf16[16,4,8,200]{3,2,1,0:T(8,128)(2,1)S(1)} collective-permute-done((bf16[16,4,8,200]{3,2,1,0:T(8,128)(2,1)S(1)}, bf16[16,4,8,200]{3,2,1,0:T(8,128)(2,1)S(1)}, u32[]{:S(2)}, u32[]{:S(2)}) %collective-permute-start) | collective-permute-done | bytes 204832 | tf_op jit(solution)/shard_map/ppermute | solution.py:144
  55.8 4.5 %collective-permute-done.1 = bf16[16,4,8,200]{3,2,1,0:T(8,128)(2,1)S(1)} collective-permute-done((bf16[16,4,8,200]{3,2,1,0:T(8,128)(2,1)S(1)}, bf16[16,4,8,200]{3,2,1,0:T(8,128)(2,1)S(1)}, u32[]{:S(2)}, u32[]{:S(2)}) %collective-permute-start.1) | collective-permute-done | bytes 204832 | tf_op jit(solution)/shard_map/ppermute | solution.py:144
  60.3 6.4 %pad_maximum_fusion.rows_ref = bf16[16,4,208,200]{3,2,1,0:T(8,128)(2,1)} fusion(bf16[16,4,8,200]{3,2,1,0:T(8,128)(2,1)S(1)} %collective-permute-done.1, bf16[16,4,192,200]{3,2,1,0:T(8,128)(2,1)} %reshape.289, bf16[16,4,8,200]{3,2,1,0:T(8,128)(2,1)S(1)} %collective-permute-done), kind=kLoop, calls=%fused_computation.3 | loop fusion | flops 15974400 | bytes 10649600 | tf_op jit(solution)/shard_map/concatenate | solution.py:151
  66.7 2.6 %all-gather.5.cloned.1.call-done = bf16[16,1,5,200,128]{4,3,2,1,0:T(8,128)(2,1)} async-done(((bf16[1,1,5,200,128]{4,3,2,1,0:T(8,128)(2,1)}), bf16[16,1,5,200,128]{4,3,2,1,0:T(8,128)(2,1)}) %all-gather.5.cloned.1.call-update) | async-done | bytes 4096016 | tf_op jit(solution)/shard_map/all_gather | solution.py:313
  69.3 0.9 tile.13.keep_ref
  70.2 17.5 %shard_map.140.rows_ref = bf16[16,4,208,128]{3,2,1,0:T(8,128)(2,1)} custom-call(bf16[16,4,208,200]{3,2,1,0:T(8,128)(2,1)} %pad_maximum_fusion.rows_ref, bf16[16,5,200,128]{3,2,1,0:T(8,128)(2,1)} %bitcast.55, f32[832,128]{1,0:T(8,128)} %tile.13.keep_ref), custom_call_target="tpu_custom_call" | custom-call | flops 3407872000 | bytes 16449536 | tf_op jit(solution)/shard_map/pallas_call | solution.py:217
  87.7 39.7 %all-gather.7.cloned.1.call-done = bf16[1,1,2,80,128,128]{5,4,3,2,1,0:T(8,128)(2,1)} async-done(((bf16[1,1,2,5,128,128]{5,4,3,2,1,0:T(8,128)(2,1)}), bf16[1,1,2,80,128,128]{5,4,3,2,1,0:T(8,128)(2,1)}) %all-gather.7.cloned.1.call-update) | async-done | bytes 5242896 | tf_op jit(solution)/shard_map/all_gather | solution.py:314
  127.4 15.4 %shard_map.141.rows_ref = bf16[16,4,208,128]{3,2,1,0:T(8,128)(2,1)} custom-call(bf16[16,4,208,128]{3,2,1,0:T(8,128)(2,1)} %shard_map.140.rows_ref, bf16[2,16,5,128,128]{4,3,2,1,0:T(8,128)(2,1)} %bitcast.53, f32[832,128]{1,0:T(8,128)} %tile.13.keep_ref), custom_call_target="tpu_custom_call" | custom-call | flops 2181038080 | bytes 13058048 | tf_op jit(solution)/shard_map/pallas_call | solution.py:217
  142.8 16.8 %shard_map.142 = f32[4,192,512]{2,1,0:T(8,128)} custom-call(bf16[16,4,208,128]{3,2,1,0:T(8,128)(2,1)} %shard_map.141.rows_ref, bf16[2,16,5,128,128]{4,3,2,1,0:T(8,128)(2,1)} %bitcast.54, bf16[16,128,512]{2,1,0:T(8,128)(2,1)} %bitcast.71), custom_call_target="tpu_custom_call" | custom-call | flops 3925868544 | bytes 9699328 | tf_op jit(solution)/shard_map/pallas_call | solution.py:217
  159.6 2.7 %copy.90 = f32[4,8,24,512]{3,2,0,1:T(8,128)} copy(f32[4,8,24,512]{3,2,1,0:T(8,128)} %bitcast.58) | data formatting | bytes 3145728 | tf_op jit(solution)/shard_map/reshape | solution.py:318
  162.4 4.6 %all-to-all-start = ((f32[8,4,24,512]{3,2,1,0:T(8,128)}), f32[8,4,24,512]{3,2,1,0:T(8,128)S(1)}, u32[]{:S(2)}, u32[]{:S(2)}) async-start(f32[8,4,24,512]{3,2,1,0:T(8,128)} %bitcast.50), calls=%async_computation | async-start | bytes 3145728 | tf_op jit(solution)/shard_map/all_to_all | solution.py:319
  167.6 1.2 exponential_reduce_fusion.2
  170.4 18.2 %all-to-all-done = f32[8,4,24,512]{3,2,1,0:T(8,128)S(1)} async-done(((f32[8,4,24,512]{3,2,1,0:T(8,128)}), f32[8,4,24,512]{3,2,1,0:T(8,128)S(1)}, u32[]{:S(2)}, u32[]{:S(2)}) %all-to-all-start) | async-done | bytes 1572896 | tf_op jit(solution)/shard_map/all_to_all | solution.py:319
  188.9 0.7 fusion.8
  189.7 0.7 reshape.316
  190.5 3.5 %all-to-all-start.1 = ((f32[8,1,480]{2,1,0:T(1,128)}), f32[8,1,480]{2,1,0:T(1,128)S(1)}, u32[]{:S(2)}, u32[]{:S(2)}) async-start(f32[8,1,480]{2,1,0:T(1,128)} %reshape.316), calls=%async_computation.1 | async-start | bytes 32768 | tf_op jit(solution)/shard_map/all_to_all | solution.py:326
  196.1 3.0 %all-to-all-done.1 = f32[8,1,480]{2,1,0:T(1,128)S(1)} async-done(((f32[8,1,480]{2,1,0:T(1,128)}), f32[8,1,480]{2,1,0:T(1,128)S(1)}, u32[]{:S(2)}, u32[]{:S(2)}) %all-to-all-start.1) | async-done | bytes 15392 | tf_op jit(solution)/shard_map/all_to_all | solution.py:326
  199.6 0.7 reduce.5
  200.7 0.7 pad.25.emit_ref
  201.4 0.7 broadcast_in_dim.43.within_ref
  202.1 0.7 broadcast_in_dim.44.between_ref
  202.8 4.5 %shard_map.143 = (f32[48,5,128]{2,1,0:T(8,128)}, f32[48,1,128]{2,1,0:T(1,128)}) custom-call(f32[5,5,128]{2,1,0:T(8,128)} %broadcast_in_dim.43.within_ref, f32[5,5,128]{2,1,0:T(8,128)} %broadcast_in_dim.44.between_ref, f32[5,128]{1,0:T(8,128)} %pad.24.start_ref, f32[48,5,128]{2,1,0:T(8,128)} %pad.25.emit_ref, f32[48,1,128]{2,1,0:T(1,128)} %bitcast.69, ...), custom_call_target="tpu_custom_call" | custom-call | flops 3932160 | bytes 344064 | tf_op jit(solution)/shard_map/pallas_call | solution.py:105
  207.3 0.7 slice.30
  208.0 0.7 slice_reduce_fusion
  208.9 1.5 collective-permute-start.2
  210.4 2.7 %collective-permute-start.3 = (f32[1,4,5,5,4]{3,4,2,1,0:T(4,128)S(1)}, f32[1,4,5,5,4]{3,4,2,1,0:T(4,128)S(1)}, u32[]{:S(2)}, u32[]{:S(2)}) collective-permute-start(f32[1,4,5,5,4]{3,4,2,1,0:T(4,128)S(1)} %get-tuple-element.13), channel_id=1, source_target_pairs={{0,16},{8,24},{16,0},{24,8},{32,48},{40,56},{48,32},{56,40},{64,80... | collective-permute-start | bytes 4808 | tf_op jit(solution)/shard_map/ppermute | solution.py:276
  213.1 1.4 collective-permute-start.4
  215.4 0.8 copy.86
  216.2 1.1 copy.87
  217.7 2.4 collective-permute-start.6
  220.1 1.5 collective-permute-start.7
  221.6 5.6 %collective-permute-done.5 = f32[4,4,5,5,4]{3,4,2,1,0:T(4,128)S(1)} collective-permute-done((f32[4,4,5,5,4]{3,4,2,1,0:T(4,128)S(1)}, f32[4,4,5,5,4]{3,4,2,1,0:T(4,128)S(1)}, u32[]{:S(2)}, u32[]{:S(2)}) %collective-permute-start.5) | collective-permute-done | bytes 6432 | tf_op jit(solution)/shard_map/ppermute | solution.py:276
  227.8 0.9 gather_fusion
  228.8 2.1 copy.85
  231.0 1.2 pad.28.mats_ref
  232.2 5.8 %shard_map.144 = (f32[64,5,128]{2,1,0:T(8,128)}, f32[1,128]{1,0:T(1,128)}) custom-call(f32[5,128]{1,0:T(8,128)} %pad.23.prior_ref, f32[64,5,5,128]{3,2,1,0:T(8,128)} %pad.28.mats_ref), custom_call_target="tpu_custom_call" | custom-call | tf_op jit(solution)/shard_map/pallas_call | solution.py:126
  238.0 0.7 constant_dynamic-slice_fusion
  239.1 0.7 reshape.296
  239.8 1.1 bitcast_divide_fusion
  (82 shorter events, 7.0 us)
Async XLA Ops:
  7.2 181.8 %copy-start = (f32[512,5]{0,1:T(8,128)S(1)}, f32[512,5]{0,1:T(8,128)}, u32[]{:S(2)}) copy-start(f32[512,5]{0,1:T(8,128)} %param.22) | copy-start | bytes 30724
  7.2 62.1 %all-gather.5.cloned.1.call-start = ((), (), s32[]{:S(2)}) async-start(), calls=%async_computation.2 | async-start | bytes 4352000 | tf_op jit(solution)/shard_map/all_gather | solution.py:313
  7.9 119.5 %all-gather.7.cloned.1.call-start = ((), (), s32[]{:S(2)}) async-start(), calls=%async_computation.3 | async-start | bytes 5570560 | tf_op jit(solution)/shard_map/all_gather | solution.py:314
  40.5 15.3 %collective-permute-start = (bf16[16,4,8,200]{3,2,1,0:T(8,128)(2,1)S(1)}, bf16[16,4,8,200]{3,2,1,0:T(8,128)(2,1)S(1)}, u32[]{:S(2)}, u32[]{:S(2)}) collective-permute-start(bf16[16,4,8,200]{3,2,1,0:T(8,128)(2,1)S(1)} %get-tuple-element.14), channel_id=1, source_target_pairs={{0,8},{8,16},{16,24},{24,32},{32,40},{40,48},{48,56},{56,64},{64,7... | collective-permute-start | bytes 614408 | tf_op jit(solution)/shard_map/ppermute | solution.py:144
  44.1 16.2 %collective-permute-start.1 = (bf16[16,4,8,200]{3,2,1,0:T(8,128)(2,1)S(1)}, bf16[16,4,8,200]{3,2,1,0:T(8,128)(2,1)S(1)}, u32[]{:S(2)}, u32[]{:S(2)}) collective-permute-start(bf16[16,4,8,200]{3,2,1,0:T(8,128)(2,1)S(1)} %get-tuple-element.15), channel_id=1, source_target_pairs={{8,0},{16,8},{24,16},{32,24},{40,32},{48,40},{56,48},{64,56},{72,6... | collective-permute-start | bytes 614408 | tf_op jit(solution)/shard_map/ppermute | solution.py:144
  159.6 7.3 %copy-start.6 = (f32[5]{0:T(128)S(1)}, f32[5]{0:T(128)}, u32[]{:S(2)}) copy-start(f32[5]{0:T(128)} %param.25) | copy-start | bytes 64
  159.6 10.6 %copy-start.1 = (s32[4,192]{1,0:T(4,128)S(1)}, s32[4,192]{1,0:T(4,128)}, u32[]{:S(2)}) copy-start(s32[4,192]{1,0:T(4,128)} %param.17) | copy-start | bytes 9220
  159.6 10.7 %copy-start.4 = (s32[4]{0:T(128)S(1)}, s32[4]{0:T(128)}, u32[]{:S(2)}) copy-start(s32[4]{0:T(128)} %param.16) | copy-start | bytes 52
  159.6 29.3 %copy-start.5 = (f32[512]{0:T(512)S(1)}, f32[512]{0:T(512)}, u32[]{:S(2)}) copy-start(f32[512]{0:T(512)} %param.21) | copy-start | bytes 6148
  162.4 39.0 %copy-start.2 = (f32[5,5]{1,0:T(8,128)S(1)}, f32[5,5]{1,0:T(8,128)}, u32[]{:S(2)}) copy-start(f32[5,5]{1,0:T(8,128)} %param.23) | copy-start | bytes 304
  162.4 39.7 %copy-start.3 = (f32[5,5]{1,0:T(8,128)S(1)}, f32[5,5]{1,0:T(8,128)}, u32[]{:S(2)}) copy-start(f32[5,5]{1,0:T(8,128)} %param.24) | copy-start | bytes 304
  162.4 26.1 %all-to-all-start = ((f32[8,4,24,512]{3,2,1,0:T(8,128)}), f32[8,4,24,512]{3,2,1,0:T(8,128)S(1)}, u32[]{:S(2)}, u32[]{:S(2)}) async-start(f32[8,4,24,512]{3,2,1,0:T(8,128)} %bitcast.50), calls=%async_computation | async-start | bytes 3145728 | tf_op jit(solution)/shard_map/all_to_all | solution.py:319
  190.5 8.6 %all-to-all-start.1 = ((f32[8,1,480]{2,1,0:T(1,128)}), f32[8,1,480]{2,1,0:T(1,128)S(1)}, u32[]{:S(2)}, u32[]{:S(2)}) async-start(f32[8,1,480]{2,1,0:T(1,128)} %reshape.316), calls=%async_computation.1 | async-start | bytes 32768 | tf_op jit(solution)/shard_map/all_to_all | solution.py:326
  208.9 8.4 %collective-permute-start.2 = (f32[1,4,5,5,4]{3,4,2,1,0:T(4,128)S(1)}, f32[1,4,5,5,4]{3,4,2,1,0:T(4,128)S(1)}, u32[]{:S(2)}, u32[]{:S(2)}) collective-permute-start(f32[1,4,5,5,4]{3,4,2,1,0:T(4,128)S(1)} %get-tuple-element.13), channel_id=1, source_target_pairs={{0,8},{8,16},{16,24},{24,0},{32,40},{40,48},{48,56},{56,32},{64,72... | collective-permute-start | bytes 4808 | tf_op jit(solution)/shard_map/ppermute | solution.py:276
  210.4 6.9 %collective-permute-start.3 = (f32[1,4,5,5,4]{3,4,2,1,0:T(4,128)S(1)}, f32[1,4,5,5,4]{3,4,2,1,0:T(4,128)S(1)}, u32[]{:S(2)}, u32[]{:S(2)}) collective-permute-start(f32[1,4,5,5,4]{3,4,2,1,0:T(4,128)S(1)} %get-tuple-element.13), channel_id=1, source_target_pairs={{0,16},{8,24},{16,0},{24,8},{32,48},{40,56},{48,32},{56,40},{64,80... | collective-permute-start | bytes 4808 | tf_op jit(solution)/shard_map/ppermute | solution.py:276
  213.1 4.2 %collective-permute-start.4 = (f32[1,4,5,5,4]{3,4,2,1,0:T(4,128)S(1)}, f32[1,4,5,5,4]{3,4,2,1,0:T(4,128)S(1)}, u32[]{:S(2)}, u32[]{:S(2)}) collective-permute-start(f32[1,4,5,5,4]{3,4,2,1,0:T(4,128)S(1)} %get-tuple-element.13), channel_id=1, source_target_pairs={{0,24},{8,0},{16,8},{24,16},{32,56},{40,32},{48,40},{56,48},{64,88... | collective-permute-start | bytes 4808 | tf_op jit(solution)/shard_map/ppermute | solution.py:276
  217.4 9.9 %collective-permute-start.5 = (f32[4,4,5,5,4]{3,4,2,1,0:T(4,128)S(1)}, f32[4,4,5,5,4]{3,4,2,1,0:T(4,128)S(1)}, u32[]{:S(2)}, u32[]{:S(2)}) collective-permute-start(f32[4,4,5,5,4]{3,4,2,1,0:T(4,128)S(1)} %pad_maximum_fusion.1), channel_id=1, source_target_pairs={{0,32},{8,40},{16,48},{24,56},{32,64},{40,72},{48,80},{56,88},{64,... | collective-permute-start | bytes 19208 | tf_op jit(solution)/shard_map/ppermute | solution.py:276
  217.7 9.6 %collective-permute-start.6 = (f32[4,4,5,5,4]{3,4,2,1,0:T(4,128)S(1)}, f32[4,4,5,5,4]{3,4,2,1,0:T(4,128)S(1)}, u32[]{:S(2)}, u32[]{:S(2)}) collective-permute-start(f32[4,4,5,5,4]{3,4,2,1,0:T(4,128)S(1)} %pad_maximum_fusion.1), channel_id=1, source_target_pairs={{0,64},{8,72},{16,80},{24,88},{32,96},{40,104},{48,112},{56,120},{... | collective-permute-start | bytes 19208 | tf_op jit(solution)/shard_map/ppermute | solution.py:276
  220.1 7.7 %collective-permute-start.7 = (f32[4,4,5,5,4]{3,4,2,1,0:T(4,128)S(1)}, f32[4,4,5,5,4]{3,4,2,1,0:T(4,128)S(1)}, u32[]{:S(2)}, u32[]{:S(2)}) collective-permute-start(f32[4,4,5,5,4]{3,4,2,1,0:T(4,128)S(1)} %pad_maximum_fusion.1), channel_id=1, source_target_pairs={{0,96},{8,104},{16,112},{24,120},{32,0},{40,8},{48,16},{56,24},{64... | collective-permute-start | bytes 19208 | tf_op jit(solution)/shard_map/ppermute | solution.py:276
Sparse Core Ops, SparseCore 0:
  10.2 59.0 all-gather.4
  71.4 55.9 all-gather.6

commit v13 on v12

--- a/solution.py
+++ b/solution.py
@@ -117,7 +117,7 @@
     offset_j = offset[:, 0, :width].reshape(steps, pieces, STATES, recordings)
     transfer = prefix_sj[steps - 1] + offset_j[steps - 1][None]
     transfer = jnp.transpose(transfer, (1, 2, 0, 3))
-    gathered = torus_gather(transfer[None], rec_index, MESH_SIDE)
+    gathered = ring_gather(transfer[None], rec_index)
     gathered = gathered.reshape((-1,) + gathered.shape[2:])
     mats = lanes_padded(gathered)
     prior = initial - log_sum_exp(initial, 0)
@@ -257,6 +257,17 @@
         (recordings, patches, mix_width), jax.ShapeDtypeStruct((recordings, patches, mix_width), jnp.float32),
         lambda m: (0, 0, 0), 2 * types * recordings * span * EMB * (EMB * taps + mix_width), layers - 1,
     )
+
+
+def ring_gather(block, rec_index):
+    devices = lax.axis_size("rec")
+    parts = [block]
+    for step in range(1, devices):
+        route = [(source, (source + step) % devices) for source in range(devices)]
+        parts.append(lax.ppermute(block, "rec", route))
+    whole = jnp.concatenate(parts, axis=0)
+    position = (rec_index - jnp.arange(devices, dtype=jnp.int32)) % devices
+    return jnp.take(whole, position, axis=0)
 
 
 def torus_gather(block, rec_index, side):

time: 250 us -> 267 us (1.068)
  starting transfers between devices: 22.9 us -> 44.2 us
  waiting for transfers between devices: 85.7 us -> 81.2 us
    ppermute x6 -> x15, starting transfers between devices: 9.84 us -> 31.1 us  [ring_gather(): parts.append(lax.ppermute(block, 'rec', route))]
    ppermute x6 -> x15, waiting for transfers between devices: 6.13 us -> 1.6 us  [ring_gather(): parts.append(lax.ppermute(block, 'rec', route))]
  transfers between devices with their start and end apart: 12 -> 21, of which waited for: 8 -> 8; matrix products, arithmetic and copies ran while one was open for 19% -> 17% of each run, Pallas kernels for 7% -> 7%
where the time goes in v13:
time: 267 us; the launch traced here: 265 us
  waiting for transfers between devices  81.2 us (30%)
  Pallas kernels  59.9 us (22%)
  local copies, waits for them, and re-layouts  46.9 us (18%)
  starting transfers between devices  44.2 us (17%)
  between operations  15.9 us (6%)
  other arithmetic  12.1 us (5%)
  matrix products  4.54 us (2%)
    pallas_call x3, Pallas kernels, per_type_call(): pl.pallas_call(kernel, grid=(types,), in_specs=[pl.BlockSpec((1,) + rows....  49.7 us
    all_gather x1, waiting for transfers between devices, local(): lax.all_gather(jnp.swapaxes(conv_hid[:, 0], 0, 1), 'rec', axis=1, tiled=T...  39.7 us
    ppermute x15, starting transfers between devices, ring_gather(): parts.append(lax.ppermute(block, 'rec', route))  31.1 us
    reshape x1, local copies, waits for them, and re-layouts, local(): patch_rows = rows.reshape(groups, recordings, patches, SAMP)  20.3 us
    all_to_all x1, waiting for transfers between devices, local(): lax.all_to_all(jnp.swapaxes(pieces, 0, 1), 'chan', 0, 0, tiled=True)  18.2 us
    ppermute x2, waiting for transfers between devices, neighbour_shift(): return lax.ppermute(block, axis, route)  14.8 us
    concatenate x1, other arithmetic, halo_rows(): return jnp.concatenate([from_left, patch_rows, from_right], axis=2)  6.4 us
    convert_element_type x1, local copies, waits for them, and re-layouts, local(): rows = jnp.einsum('bms,bst->mbt', pick.astype(jnp.bfloat16), signal, pref...  5.97 us
  transfers between devices with their start and end apart: 21, of which 8 were waited for; matrix products, arithmetic and copies ran while one was open for 17% of the time, Pallas kernels for 7%

profile of v13, /device:TPU:0, one launch (start us, length us, event | category | flops | bytes accessed | tf_op | source)
XLA Modules:
  0.0 264.7 jit_solution(1281991629381701301)
XLA Ops:
  8.0 0.7 all-gather.7.cloned.1.call-update
  8.7 0.7 broadcast_compare_fusion
  9.4 3.8 %fusion = bf16[16,4,38400]{2,0,1:T(8,128)(2,1)S(1)} fusion(bf16[4,16,38400]{2,1,0:T(8,128)(2,1)} %param.13, s32[4,16]{1,0:T(4,128)} %bitcast.66, pred[4,16]{1,0:T(4,128)(4,1)S(1)} %broadcast_compare_fusion), kind=kOutput, calls=%fused_computation.2 | convolution fusion | flops 81102848 | bytes 9830720 | tf_op jit(solution)/shard_map/bms,bst->mbt/dot_general | solution.py:320
  13.2 6.0 %copy.93 = bf16[16,4,38400]{2,1,0:T(4,128)(2,1)} copy(bf16[16,4,38400]{2,0,1:T(8,128)(2,1)S(1)} %fusion) | data formatting | bytes 9830400 | tf_op jit(solution)/shard_map/convert_element_type | solution.py:322
  19.2 20.3 %reshape.202 = bf16[16,4,192,200]{3,2,1,0:T(8,128)(2,1)} reshape(bf16[16,4,38400]{2,1,0:T(4,128)(2,1)} %copy.93) | data formatting | bytes 9830400 | tf_op jit(solution)/shard_map/reshape | solution.py:323
  39.5 1.1 fusion.34
  40.5 3.6 %collective-permute-start = (bf16[16,4,8,200]{3,2,1,0:T(8,128)(2,1)S(1)}, bf16[16,4,8,200]{3,2,1,0:T(8,128)(2,1)S(1)}, u32[]{:S(2)}, u32[]{:S(2)}) collective-permute-start(bf16[16,4,8,200]{3,2,1,0:T(8,128)(2,1)S(1)} %get-tuple-element.14), channel_id=1, source_target_pairs={{0,8},{8,16},{16,24},{24,32},{32,40},{40,48},{48,56},{56,64},{64,7... | collective-permute-start | bytes 614408 | tf_op jit(solution)/shard_map/ppermute | solution.py:144
  44.1 1.3 collective-permute-start.1
  45.5 10.3 %collective-permute-done = bf16[16,4,8,200]{3,2,1,0:T(8,128)(2,1)S(1)} collective-permute-done((bf16[16,4,8,200]{3,2,1,0:T(8,128)(2,1)S(1)}, bf16[16,4,8,200]{3,2,1,0:T(8,128)(2,1)S(1)}, u32[]{:S(2)}, u32[]{:S(2)}) %collective-permute-start) | collective-permute-done | bytes 204832 | tf_op jit(solution)/shard_map/ppermute | solution.py:144
  55.8 4.5 %collective-permute-done.1 = bf16[16,4,8,200]{3,2,1,0:T(8,128)(2,1)S(1)} collective-permute-done((bf16[16,4,8,200]{3,2,1,0:T(8,128)(2,1)S(1)}, bf16[16,4,8,200]{3,2,1,0:T(8,128)(2,1)S(1)}, u32[]{:S(2)}, u32[]{:S(2)}) %collective-permute-start.1) | collective-permute-done | bytes 204832 | tf_op jit(solution)/shard_map/ppermute | solution.py:144
  60.3 6.4 %pad_maximum_fusion.rows_ref = bf16[16,4,208,200]{3,2,1,0:T(8,128)(2,1)} fusion(bf16[16,4,8,200]{3,2,1,0:T(8,128)(2,1)S(1)} %collective-permute-done.1, bf16[16,4,192,200]{3,2,1,0:T(8,128)(2,1)} %reshape.202, bf16[16,4,8,200]{3,2,1,0:T(8,128)(2,1)S(1)} %collective-permute-done), kind=kLoop, calls=%fused_computation.3 | loop fusion | flops 15974400 | bytes 10649600 | tf_op jit(solution)/shard_map/concatenate | solution.py:151
  66.7 2.5 all-gather.5.cloned.1.call-done
  69.3 1.0 tile.13.keep_ref
  70.2 17.5 %shard_map.140.rows_ref = bf16[16,4,208,128]{3,2,1,0:T(8,128)(2,1)} custom-call(bf16[16,4,208,200]{3,2,1,0:T(8,128)(2,1)} %pad_maximum_fusion.rows_ref, bf16[16,5,200,128]{3,2,1,0:T(8,128)(2,1)} %bitcast.55, f32[832,128]{1,0:T(8,128)} %tile.13.keep_ref), custom_call_target="tpu_custom_call" | custom-call | flops 3407872000 | bytes 16449536 | tf_op jit(solution)/shard_map/pallas_call | solution.py:217
  87.7 39.7 %all-gather.7.cloned.1.call-done = bf16[1,1,2,80,128,128]{5,4,3,2,1,0:T(8,128)(2,1)} async-done(((bf16[1,1,2,5,128,128]{5,4,3,2,1,0:T(8,128)(2,1)}), bf16[1,1,2,80,128,128]{5,4,3,2,1,0:T(8,128)(2,1)}) %all-gather.7.cloned.1.call-update) | async-done | bytes 5242896 | tf_op jit(solution)/shard_map/all_gather | solution.py:325
  127.4 15.4 %shard_map.141.rows_ref = bf16[16,4,208,128]{3,2,1,0:T(8,128)(2,1)} custom-call(bf16[16,4,208,128]{3,2,1,0:T(8,128)(2,1)} %shard_map.140.rows_ref, bf16[2,16,5,128,128]{4,3,2,1,0:T(8,128)(2,1)} %bitcast.53, f32[832,128]{1,0:T(8,128)} %tile.13.keep_ref), custom_call_target="tpu_custom_call" | custom-call | flops 2181038080 | bytes 13058048 | tf_op jit(solution)/shard_map/pallas_call | solution.py:217
  142.8 16.8 %shard_map.142 = f32[4,192,512]{2,1,0:T(8,128)} custom-call(bf16[16,4,208,128]{3,2,1,0:T(8,128)(2,1)} %shard_map.141.rows_ref, bf16[2,16,5,128,128]{4,3,2,1,0:T(8,128)(2,1)} %bitcast.54, bf16[16,128,512]{2,1,0:T(8,128)(2,1)} %bitcast.71), custom_call_target="tpu_custom_call" | custom-call | flops 3925868544 | bytes 9699328 | tf_op jit(solution)/shard_map/pallas_call | solution.py:217
  159.7 2.7 %copy.108 = f32[4,8,24,512]{3,2,0,1:T(8,128)} copy(f32[4,8,24,512]{3,2,1,0:T(8,128)} %bitcast.58) | data formatting | bytes 3145728 | tf_op jit(solution)/shard_map/reshape | solution.py:329
  162.4 4.6 %all-to-all-start = ((f32[8,4,24,512]{3,2,1,0:T(8,128)}), f32[8,4,24,512]{3,2,1,0:T(8,128)S(1)}, u32[]{:S(2)}, u32[]{:S(2)}) async-start(f32[8,4,24,512]{3,2,1,0:T(8,128)} %bitcast.50), calls=%async_computation | async-start | bytes 3145728 | tf_op jit(solution)/shard_map/all_to_all | solution.py:330
  167.6 1.2 exponential_reduce_fusion.2
  170.3 18.2 %all-to-all-done = f32[8,4,24,512]{3,2,1,0:T(8,128)S(1)} async-done(((f32[8,4,24,512]{3,2,1,0:T(8,128)}), f32[8,4,24,512]{3,2,1,0:T(8,128)S(1)}, u32[]{:S(2)}, u32[]{:S(2)}) %all-to-all-start) | async-done | bytes 1572896 | tf_op jit(solution)/shard_map/all_to_all | solution.py:330
  189.0 0.7 fusion.8
  189.7 0.7 reshape.229
  190.5 3.5 %all-to-all-start.1 = ((f32[8,1,480]{2,1,0:T(1,128)}), f32[8,1,480]{2,1,0:T(1,128)S(1)}, u32[]{:S(2)}, u32[]{:S(2)}) async-start(f32[8,1,480]{2,1,0:T(1,128)} %reshape.229), calls=%async_computation.1 | async-start | bytes 32768 | tf_op jit(solution)/shard_map/all_to_all | solution.py:337
  196.1 3.0 %all-to-all-done.1 = f32[8,1,480]{2,1,0:T(1,128)S(1)} async-done(((f32[8,1,480]{2,1,0:T(1,128)}), f32[8,1,480]{2,1,0:T(1,128)S(1)}, u32[]{:S(2)}, u32[]{:S(2)}) %all-to-all-start.1) | async-done | bytes 15392 | tf_op jit(solution)/shard_map/all_to_all | solution.py:337
  202.8 4.5 %shard_map.143 = (f32[48,5,128]{2,1,0:T(8,128)}, f32[48,1,128]{2,1,0:T(1,128)}) custom-call(f32[5,5,128]{2,1,0:T(8,128)} %broadcast_in_dim.43.within_ref, f32[5,5,128]{2,1,0:T(8,128)} %broadcast_in_dim.44.between_ref, f32[5,128]{1,0:T(8,128)} %pad.24.start_ref, f32[48,5,128]{2,1,0:T(8,128)} %pad.25.emit_ref, f32[48,1,128]{2,1,0:T(1,128)} %bitcast.69, ...), custom_call_target="tpu_custom_call" | custom-call | flops 3932160 | bytes 344064 | tf_op jit(solution)/shard_map/pallas_call | solution.py:105
  208.9 1.5 collective-permute-start.2
  211.2 2.7 %collective-permute-start.3 = (f32[1,4,5,5,4]{3,4,2,1,0:T(4,128)S(1)}, f32[1,4,5,5,4]{3,4,2,1,0:T(4,128)S(1)}, u32[]{:S(2)}, u32[]{:S(2)}) collective-permute-start(f32[1,4,5,5,4]{3,4,2,1,0:T(4,128)S(1)} %get-tuple-element.13), channel_id=1, source_target_pairs={{0,16},{8,24},{16,32},{24,40},{32,48},{40,56},{48,64},{56,72},{64,... | collective-permute-start | bytes 4808 | tf_op jit(solution)/shard_map/ppermute | solution.py:267
  214.0 1.1 collective-permute-start.4
  215.1 1.2 collective-permute-start.5
  216.3 0.9 collective-permute-start.6
  217.1 0.8 copy.104
  218.0 1.1 copy.105
  219.0 2.8 %collective-permute-start.7 = (f32[1,4,5,5,4]{3,4,2,1,0:T(4,128)S(1)}, f32[1,4,5,5,4]{3,4,2,1,0:T(4,128)S(1)}, u32[]{:S(2)}, u32[]{:S(2)}) collective-permute-start(f32[1,4,5,5,4]{3,4,2,1,0:T(4,128)S(1)} %get-tuple-element.13), channel_id=1, source_target_pairs={{0,48},{8,56},{16,64},{24,72},{32,80},{40,88},{48,96},{56,104},{64... | collective-permute-start | bytes 4808 | tf_op jit(solution)/shard_map/ppermute | solution.py:267
  221.8 4.2 %collective-permute-start.8 = (f32[1,4,5,5,4]{3,4,2,1,0:T(4,128)S(1)}, f32[1,4,5,5,4]{3,4,2,1,0:T(4,128)S(1)}, u32[]{:S(2)}, u32[]{:S(2)}) collective-permute-start(f32[1,4,5,5,4]{3,4,2,1,0:T(4,128)S(1)} %get-tuple-element.13), channel_id=1, source_target_pairs={{0,56},{8,64},{16,72},{24,80},{32,88},{40,96},{48,104},{56,112},{6... | collective-permute-start | bytes 4808 | tf_op jit(solution)/shard_map/ppermute | solution.py:267
  226.1 2.1 collective-permute-start.9
  228.8 3.6 %collective-permute-start.11 = (f32[1,4,5,5,4]{3,4,2,1,0:T(4,128)S(1)}, f32[1,4,5,5,4]{3,4,2,1,0:T(4,128)S(1)}, u32[]{:S(2)}, u32[]{:S(2)}) collective-permute-start(f32[1,4,5,5,4]{3,4,2,1,0:T(4,128)S(1)} %get-tuple-element.13), channel_id=1, source_target_pairs={{0,80},{8,88},{16,96},{24,104},{32,112},{40,120},{48,0},{56,8},{64... | collective-permute-start | bytes 4808 | tf_op jit(solution)/shard_map/ppermute | solution.py:267
  232.5 4.5 %collective-permute-start.12 = (f32[1,4,5,5,4]{3,4,2,1,0:T(4,128)S(1)}, f32[1,4,5,5,4]{3,4,2,1,0:T(4,128)S(1)}, u32[]{:S(2)}, u32[]{:S(2)}) collective-permute-start(f32[1,4,5,5,4]{3,4,2,1,0:T(4,128)S(1)} %get-tuple-element.13), channel_id=1, source_target_pairs={{0,88},{8,96},{16,104},{24,112},{32,120},{40,0},{48,8},{56,16},{64... | collective-permute-start | bytes 4808 | tf_op jit(solution)/shard_map/ppermute | solution.py:267
  237.9 1.5 collective-permute-start.15
  239.4 3.6 %collective-permute-start.16 = (f32[1,4,5,5,4]{3,4,2,1,0:T(4,128)S(1)}, f32[1,4,5,5,4]{3,4,2,1,0:T(4,128)S(1)}, u32[]{:S(2)}, u32[]{:S(2)}) collective-permute-start(f32[1,4,5,5,4]{3,4,2,1,0:T(4,128)S(1)} %get-tuple-element.13), channel_id=1, source_target_pairs={{0,120},{8,0},{16,8},{24,16},{32,24},{40,32},{48,40},{56,48},{64,5... | collective-permute-start | bytes 4808 | tf_op jit(solution)/shard_map/ppermute | solution.py:267
  243.5 1.2 collective-permute-done.16
  244.7 0.9 gather_fusion
  245.6 2.1 copy.103
  247.9 1.2 pad.28.mats_ref
  249.1 5.7 %shard_map.144 = (f32[64,5,128]{2,1,0:T(8,128)}, f32[1,128]{1,0:T(1,128)}) custom-call(f32[5,128]{1,0:T(8,128)} %pad.23.prior_ref, f32[64,5,5,128]{3,2,1,0:T(8,128)} %pad.28.mats_ref), custom_call_target="tpu_custom_call" | custom-call | tf_op jit(solution)/shard_map/pallas_call | solution.py:126
  254.8 0.7 constant_dynamic-slice_fusion
  256.0 0.7 reshape.209
  256.7 1.2 bitcast_divide_fusion
  (108 shorter events, 12.7 us)
Async XLA Ops:
  7.2 181.8 %copy-start = (f32[512,5]{0,1:T(8,128)S(1)}, f32[512,5]{0,1:T(8,128)}, u32[]{:S(2)}) copy-start(f32[512,5]{0,1:T(8,128)} %param.22) | copy-start | bytes 30724
  7.2 62.1 %all-gather.5.cloned.1.call-start = ((), (), s32[]{:S(2)}) async-start(), calls=%async_computation.2 | async-start | bytes 4352000 | tf_op jit(solution)/shard_map/all_gather | solution.py:324
  7.9 119.5 %all-gather.7.cloned.1.call-start = ((), (), s32[]{:S(2)}) async-start(), calls=%async_computation.3 | async-start | bytes 5570560 | tf_op jit(solution)/shard_map/all_gather | solution.py:325
  40.5 15.3 %collective-permute-start = (bf16[16,4,8,200]{3,2,1,0:T(8,128)(2,1)S(1)}, bf16[16,4,8,200]{3,2,1,0:T(8,128)(2,1)S(1)}, u32[]{:S(2)}, u32[]{:S(2)}) collective-permute-start(bf16[16,4,8,200]{3,2,1,0:T(8,128)(2,1)S(1)} %get-tuple-element.14), channel_id=1, source_target_pairs={{0,8},{8,16},{16,24},{24,32},{32,40},{40,48},{48,56},{56,64},{64,7... | collective-permute-start | bytes 614408 | tf_op jit(solution)/shard_map/ppermute | solution.py:144
  44.1 16.2 %collective-permute-start.1 = (bf16[16,4,8,200]{3,2,1,0:T(8,128)(2,1)S(1)}, bf16[16,4,8,200]{3,2,1,0:T(8,128)(2,1)S(1)}, u32[]{:S(2)}, u32[]{:S(2)}) collective-permute-start(bf16[16,4,8,200]{3,2,1,0:T(8,128)(2,1)S(1)} %get-tuple-element.15), channel_id=1, source_target_pairs={{8,0},{16,8},{24,16},{32,24},{40,32},{48,40},{56,48},{64,56},{72,6... | collective-permute-start | bytes 614408 | tf_op jit(solution)/shard_map/ppermute | solution.py:144
  159.6 7.3 %copy-start.6 = (f32[5]{0:T(128)S(1)}, f32[5]{0:T(128)}, u32[]{:S(2)}) copy-start(f32[5]{0:T(128)} %param.25) | copy-start | bytes 64
  159.6 10.6 %copy-start.1 = (s32[4,192]{1,0:T(4,128)S(1)}, s32[4,192]{1,0:T(4,128)}, u32[]{:S(2)}) copy-start(s32[4,192]{1,0:T(4,128)} %param.17) | copy-start | bytes 9220
  159.6 10.6 %copy-start.4 = (s32[4]{0:T(128)S(1)}, s32[4]{0:T(128)}, u32[]{:S(2)}) copy-start(s32[4]{0:T(128)} %param.16) | copy-start | bytes 52
  159.6 29.3 %copy-start.5 = (f32[512]{0:T(512)S(1)}, f32[512]{0:T(512)}, u32[]{:S(2)}) copy-start(f32[512]{0:T(512)} %param.21) | copy-start | bytes 6148
  162.4 39.0 %copy-start.2 = (f32[5,5]{1,0:T(8,128)S(1)}, f32[5,5]{1,0:T(8,128)}, u32[]{:S(2)}) copy-start(f32[5,5]{1,0:T(8,128)} %param.23) | copy-start | bytes 304
  162.4 39.7 %copy-start.3 = (f32[5,5]{1,0:T(8,128)S(1)}, f32[5,5]{1,0:T(8,128)}, u32[]{:S(2)}) copy-start(f32[5,5]{1,0:T(8,128)} %param.24) | copy-start | bytes 304
  162.4 26.1 %all-to-all-start = ((f32[8,4,24,512]{3,2,1,0:T(8,128)}), f32[8,4,24,512]{3,2,1,0:T(8,128)S(1)}, u32[]{:S(2)}, u32[]{:S(2)}) async-start(f32[8,4,24,512]{3,2,1,0:T(8,128)} %bitcast.50), calls=%async_computation | async-start | bytes 3145728 | tf_op jit(solution)/shard_map/all_to_all | solution.py:330
  190.5 8.6 %all-to-all-start.1 = ((f32[8,1,480]{2,1,0:T(1,128)}), f32[8,1,480]{2,1,0:T(1,128)S(1)}, u32[]{:S(2)}, u32[]{:S(2)}) async-start(f32[8,1,480]{2,1,0:T(1,128)} %reshape.229), calls=%async_computation.1 | async-start | bytes 32768 | tf_op jit(solution)/shard_map/all_to_all | solution.py:337
  208.9 10.1 %collective-permute-start.2 = (f32[1,4,5,5,4]{3,4,2,1,0:T(4,128)S(1)}, f32[1,4,5,5,4]{3,4,2,1,0:T(4,128)S(1)}, u32[]{:S(2)}, u32[]{:S(2)}) collective-permute-start(f32[1,4,5,5,4]{3,4,2,1,0:T(4,128)S(1)} %get-tuple-element.13), channel_id=1, source_target_pairs={{0,8},{8,16},{16,24},{24,32},{32,40},{40,48},{48,56},{56,64},{64,7... | collective-permute-start | bytes 4808 | tf_op jit(solution)/shard_map/ppermute | solution.py:267
  211.2 10.6 %collective-permute-start.3 = (f32[1,4,5,5,4]{3,4,2,1,0:T(4,128)S(1)}, f32[1,4,5,5,4]{3,4,2,1,0:T(4,128)S(1)}, u32[]{:S(2)}, u32[]{:S(2)}) collective-permute-start(f32[1,4,5,5,4]{3,4,2,1,0:T(4,128)S(1)} %get-tuple-element.13), channel_id=1, source_target_pairs={{0,16},{8,24},{16,32},{24,40},{32,48},{40,56},{48,64},{56,72},{64,... | collective-permute-start | bytes 4808 | tf_op jit(solution)/shard_map/ppermute | solution.py:267
  214.0 12.1 %collective-permute-start.4 = (f32[1,4,5,5,4]{3,4,2,1,0:T(4,128)S(1)}, f32[1,4,5,5,4]{3,4,2,1,0:T(4,128)S(1)}, u32[]{:S(2)}, u32[]{:S(2)}) collective-permute-start(f32[1,4,5,5,4]{3,4,2,1,0:T(4,128)S(1)} %get-tuple-element.13), channel_id=1, source_target_pairs={{0,24},{8,32},{16,40},{24,48},{32,56},{40,64},{48,72},{56,80},{64,... | collective-permute-start | bytes 4808 | tf_op jit(solution)/shard_map/ppermute | solution.py:267
  215.1 13.1 %collective-permute-start.5 = (f32[1,4,5,5,4]{3,4,2,1,0:T(4,128)S(1)}, f32[1,4,5,5,4]{3,4,2,1,0:T(4,128)S(1)}, u32[]{:S(2)}, u32[]{:S(2)}) collective-permute-start(f32[1,4,5,5,4]{3,4,2,1,0:T(4,128)S(1)} %get-tuple-element.13), channel_id=1, source_target_pairs={{0,32},{8,40},{16,48},{24,56},{32,64},{40,72},{48,80},{56,88},{64,... | collective-permute-start | bytes 4808 | tf_op jit(solution)/shard_map/ppermute | solution.py:267
  216.3 12.6 %collective-permute-start.6 = (f32[1,4,5,5,4]{3,4,2,1,0:T(4,128)S(1)}, f32[1,4,5,5,4]{3,4,2,1,0:T(4,128)S(1)}, u32[]{:S(2)}, u32[]{:S(2)}) collective-permute-start(f32[1,4,5,5,4]{3,4,2,1,0:T(4,128)S(1)} %get-tuple-element.13), channel_id=1, source_target_pairs={{0,40},{8,48},{16,56},{24,64},{32,72},{40,80},{48,88},{56,96},{64,... | collective-permute-start | bytes 4808 | tf_op jit(solution)/shard_map/ppermute | solution.py:267
  219.0 13.5 %collective-permute-start.7 = (f32[1,4,5,5,4]{3,4,2,1,0:T(4,128)S(1)}, f32[1,4,5,5,4]{3,4,2,1,0:T(4,128)S(1)}, u32[]{:S(2)}, u32[]{:S(2)}) collective-permute-start(f32[1,4,5,5,4]{3,4,2,1,0:T(4,128)S(1)} %get-tuple-element.13), channel_id=1, source_target_pairs={{0,48},{8,56},{16,64},{24,72},{32,80},{40,88},{48,96},{56,104},{64... | collective-permute-start | bytes 4808 | tf_op jit(solution)/shard_map/ppermute | solution.py:267
  221.8 15.3 %collective-permute-start.8 = (f32[1,4,5,5,4]{3,4,2,1,0:T(4,128)S(1)}, f32[1,4,5,5,4]{3,4,2,1,0:T(4,128)S(1)}, u32[]{:S(2)}, u32[]{:S(2)}) collective-permute-start(f32[1,4,5,5,4]{3,4,2,1,0:T(4,128)S(1)} %get-tuple-element.13), channel_id=1, source_target_pairs={{0,56},{8,64},{16,72},{24,80},{32,88},{40,96},{48,104},{56,112},{6... | collective-permute-start | bytes 4808 | tf_op jit(solution)/shard_map/ppermute | solution.py:267
  226.1 11.7 %collective-permute-start.9 = (f32[1,4,5,5,4]{3,4,2,1,0:T(4,128)S(1)}, f32[1,4,5,5,4]{3,4,2,1,0:T(4,128)S(1)}, u32[]{:S(2)}, u32[]{:S(2)}) collective-permute-start(f32[1,4,5,5,4]{3,4,2,1,0:T(4,128)S(1)} %get-tuple-element.13), channel_id=1, source_target_pairs={{0,64},{8,72},{16,80},{24,88},{32,96},{40,104},{48,112},{56,120},{... | collective-permute-start | bytes 4808 | tf_op jit(solution)/shard_map/ppermute | solution.py:267
  228.2 9.6 %collective-permute-start.10 = (f32[1,4,5,5,4]{3,4,2,1,0:T(4,128)S(1)}, f32[1,4,5,5,4]{3,4,2,1,0:T(4,128)S(1)}, u32[]{:S(2)}, u32[]{:S(2)}) collective-permute-start(f32[1,4,5,5,4]{3,4,2,1,0:T(4,128)S(1)} %get-tuple-element.13), channel_id=1, source_target_pairs={{0,72},{8,80},{16,88},{24,96},{32,104},{40,112},{48,120},{56,0},{6... | collective-permute-start | bytes 4808 | tf_op jit(solution)/shard_map/ppermute | solution.py:267
  228.8 10.6 %collective-permute-start.11 = (f32[1,4,5,5,4]{3,4,2,1,0:T(4,128)S(1)}, f32[1,4,5,5,4]{3,4,2,1,0:T(4,128)S(1)}, u32[]{:S(2)}, u32[]{:S(2)}) collective-permute-start(f32[1,4,5,5,4]{3,4,2,1,0:T(4,128)S(1)} %get-tuple-element.13), channel_id=1, source_target_pairs={{0,80},{8,88},{16,96},{24,104},{32,112},{40,120},{48,0},{56,8},{64... | collective-permute-start | bytes 4808 | tf_op jit(solution)/shard_map/ppermute | solution.py:267
  232.5 10.5 %collective-permute-start.12 = (f32[1,4,5,5,4]{3,4,2,1,0:T(4,128)S(1)}, f32[1,4,5,5,4]{3,4,2,1,0:T(4,128)S(1)}, u32[]{:S(2)}, u32[]{:S(2)}) collective-permute-start(f32[1,4,5,5,4]{3,4,2,1,0:T(4,128)S(1)} %get-tuple-element.13), channel_id=1, source_target_pairs={{0,88},{8,96},{16,104},{24,112},{32,120},{40,0},{48,8},{56,16},{64... | collective-permute-start | bytes 4808 | tf_op jit(solution)/shard_map/ppermute | solution.py:267
  237.1 6.0 %collective-permute-start.13 = (f32[1,4,5,5,4]{3,4,2,1,0:T(4,128)S(1)}, f32[1,4,5,5,4]{3,4,2,1,0:T(4,128)S(1)}, u32[]{:S(2)}, u32[]{:S(2)}) collective-permute-start(f32[1,4,5,5,4]{3,4,2,1,0:T(4,128)S(1)} %get-tuple-element.13), channel_id=1, source_target_pairs={{0,96},{8,104},{16,112},{24,120},{32,0},{40,8},{48,16},{56,24},{64... | collective-permute-start | bytes 4808 | tf_op jit(solution)/shard_map/ppermute | solution.py:267
  237.8 5.3 %collective-permute-start.14 = (f32[1,4,5,5,4]{3,4,2,1,0:T(4,128)S(1)}, f32[1,4,5,5,4]{3,4,2,1,0:T(4,128)S(1)}, u32[]{:S(2)}, u32[]{:S(2)}) collective-permute-start(f32[1,4,5,5,4]{3,4,2,1,0:T(4,128)S(1)} %get-tuple-element.13), channel_id=1, source_target_pairs={{0,104},{8,112},{16,120},{24,0},{32,8},{40,16},{48,24},{56,32},{64... | collective-permute-start | bytes 4808 | tf_op jit(solution)/shard_map/ppermute | solution.py:267
  237.9 5.6 %collective-permute-start.15 = (f32[1,4,5,5,4]{3,4,2,1,0:T(4,128)S(1)}, f32[1,4,5,5,4]{3,4,2,1,0:T(4,128)S(1)}, u32[]{:S(2)}, u32[]{:S(2)}) collective-permute-start(f32[1,4,5,5,4]{3,4,2,1,0:T(4,128)S(1)} %get-tuple-element.13), channel_id=1, source_target_pairs={{0,112},{8,120},{16,0},{24,8},{32,16},{40,24},{48,32},{56,40},{64,... | collective-permute-start | bytes 4808 | tf_op jit(solution)/shard_map/ppermute | solution.py:267
  239.4 5.3 %collective-permute-start.16 = (f32[1,4,5,5,4]{3,4,2,1,0:T(4,128)S(1)}, f32[1,4,5,5,4]{3,4,2,1,0:T(4,128)S(1)}, u32[]{:S(2)}, u32[]{:S(2)}) collective-permute-start(f32[1,4,5,5,4]{3,4,2,1,0:T(4,128)S(1)} %get-tuple-element.13), channel_id=1, source_target_pairs={{0,120},{8,0},{16,8},{24,16},{32,24},{40,32},{48,40},{56,48},{64,5... | collective-permute-start | bytes 4808 | tf_op jit(solution)/shard_map/ppermute | solution.py:267
Sparse Core Ops, SparseCore 0:
  10.2 59.0 all-gather.4
  71.4 55.9 all-gather.6

commit v14 on v12

--- a/solution.py
+++ b/solution.py
@@ -71,7 +71,7 @@
         moved, level = forward_step(state, matrices, None)
         return moved, total + level
 
-    _, total = lax.fori_loop(0, count, body, (prior_ref[...], jnp.zeros((1, LANES), jnp.float32)))
+    _, total = lax.fori_loop(0, count, body, (prior_ref[...], jnp.zeros((1, prior_ref.shape[1]), jnp.float32)))
     total_ref[...] = total
 
 
@@ -119,15 +119,15 @@
     transfer = jnp.transpose(transfer, (1, 2, 0, 3))
     gathered = torus_gather(transfer[None], rec_index, MESH_SIDE)
     gathered = gathered.reshape((-1,) + gathered.shape[2:])
-    mats = lanes_padded(gathered)
+    mats = gathered
     prior = initial - log_sum_exp(initial, 0)
-    prior_in = lanes_padded(jnp.broadcast_to(prior[:, None], (STATES, recordings)))
+    prior_in = jnp.broadcast_to(prior[:, None], (STATES, recordings))
     count = gathered.shape[0]
     incoming, total = pl.pallas_call(
         chain_kernel,
         out_shape=(
-            jax.ShapeDtypeStruct((count, STATES, LANES), jnp.float32),
-            jax.ShapeDtypeStruct((1, LANES), jnp.float32),
+            jax.ShapeDtypeStruct((count, STATES, recordings), jnp.float32),
+            jax.ShapeDtypeStruct((1, recordings), jnp.float32),
         ),
     )(prior_in, mats)
     here = lax.dynamic_slice_in_dim(incoming, rec_index * pieces, pieces, 0)[:, :, :recordings]

time: 250 us -> 249 us (level)
  transfers between devices with their start and end apart: 12 -> 12, of which waited for: 8 -> 9; matrix products, arithmetic and copies ran while one was open for 19% -> 18% of each run, Pallas kernels for 7% -> 7%
where the time goes in v14:
time: 249 us; the launch traced here: 248 us
  waiting for transfers between devices  85.8 us (34%)
  Pallas kernels  59.9 us (24%)
  local copies, waits for them, and re-layouts  45.7 us (18%)
  starting transfers between devices  22.8 us (9%)
  between operations  15.8 us (6%)
  other arithmetic  13.1 us (5%)
  matrix products  4.54 us (2%)
    pallas_call x3, Pallas kernels, per_type_call(): pl.pallas_call(kernel, grid=(types,), in_specs=[pl.BlockSpec((1,) + rows....  49.7 us
    all_gather x1, waiting for transfers between devices, local(): lax.all_gather(jnp.swapaxes(conv_hid[:, 0], 0, 1), 'rec', axis=1, tiled=T...  39.7 us
    reshape x1, local copies, waits for them, and re-layouts, local(): patch_rows = rows.reshape(groups, recordings, patches, SAMP)  20.3 us
    all_to_all x1, waiting for transfers between devices, local(): lax.all_to_all(jnp.swapaxes(pieces, 0, 1), 'chan', 0, 0, tiled=True)  18.2 us
    ppermute x2, waiting for transfers between devices, neighbour_shift(): return lax.ppermute(block, axis, route)  14.8 us
    ppermute x6, starting transfers between devices, shifted(): return lax.ppermute(values, 'rec', route)  9.81 us
    concatenate x1, other arithmetic, halo_rows(): return jnp.concatenate([from_left, patch_rows, from_right], axis=2)  6.4 us
    ppermute x6, waiting for transfers between devices, shifted(): return lax.ppermute(values, 'rec', route)  6.17 us
  transfers between devices with their start and end apart: 12, of which 9 were waited for; matrix products, arithmetic and copies ran while one was open for 18% of the time, Pallas kernels for 7%

profile of v14, /device:TPU:0, one launch (start us, length us, event | category | flops | bytes accessed | tf_op | source)
XLA Modules:
  0.0 247.7 jit_solution(12756881994523328620)
XLA Ops:
  7.2 0.7 all-gather.5.cloned.1.call-update
  8.0 0.7 all-gather.7.cloned.1.call-update
  8.7 0.7 broadcast_compare_fusion
  9.4 3.8 %fusion = bf16[16,4,38400]{2,0,1:T(8,128)(2,1)S(1)} fusion(bf16[4,16,38400]{2,1,0:T(8,128)(2,1)} %param.13, s32[4,16]{1,0:T(4,128)} %bitcast.66, pred[4,16]{1,0:T(4,128)(4,1)S(1)} %broadcast_compare_fusion), kind=kOutput, calls=%fused_computation.2 | convolution fusion | flops 81102848 | bytes 9830720 | tf_op jit(solution)/shard_map/bms,bst->mbt/dot_general | solution.py:309
  13.2 6.0 %copy.75 = bf16[16,4,38400]{2,1,0:T(4,128)(2,1)} copy(bf16[16,4,38400]{2,0,1:T(8,128)(2,1)S(1)} %fusion) | data formatting | bytes 9830400 | tf_op jit(solution)/shard_map/convert_element_type | solution.py:311
  19.2 20.3 %reshape.289 = bf16[16,4,192,200]{3,2,1,0:T(8,128)(2,1)} reshape(bf16[16,4,38400]{2,1,0:T(4,128)(2,1)} %copy.75) | data formatting | bytes 9830400 | tf_op jit(solution)/shard_map/reshape | solution.py:312
  39.5 1.1 fusion.44
  40.5 3.6 %collective-permute-start = (bf16[16,4,8,200]{3,2,1,0:T(8,128)(2,1)S(1)}, bf16[16,4,8,200]{3,2,1,0:T(8,128)(2,1)S(1)}, u32[]{:S(2)}, u32[]{:S(2)}) collective-permute-start(bf16[16,4,8,200]{3,2,1,0:T(8,128)(2,1)S(1)} %get-tuple-element.14), channel_id=1, source_target_pairs={{0,8},{8,16},{16,24},{24,32},{32,40},{40,48},{48,56},{56,64},{64,7... | collective-permute-start | bytes 614408 | tf_op jit(solution)/shard_map/ppermute | solution.py:144
  44.1 1.3 collective-permute-start.1
  45.5 10.3 %collective-permute-done = bf16[16,4,8,200]{3,2,1,0:T(8,128)(2,1)S(1)} collective-permute-done((bf16[16,4,8,200]{3,2,1,0:T(8,128)(2,1)S(1)}, bf16[16,4,8,200]{3,2,1,0:T(8,128)(2,1)S(1)}, u32[]{:S(2)}, u32[]{:S(2)}) %collective-permute-start) | collective-permute-done | bytes 204832 | tf_op jit(solution)/shard_map/ppermute | solution.py:144
  55.8 4.5 %collective-permute-done.1 = bf16[16,4,8,200]{3,2,1,0:T(8,128)(2,1)S(1)} collective-permute-done((bf16[16,4,8,200]{3,2,1,0:T(8,128)(2,1)S(1)}, bf16[16,4,8,200]{3,2,1,0:T(8,128)(2,1)S(1)}, u32[]{:S(2)}, u32[]{:S(2)}) %collective-permute-start.1) | collective-permute-done | bytes 204832 | tf_op jit(solution)/shard_map/ppermute | solution.py:144
  60.3 6.4 %pad_maximum_fusion.rows_ref = bf16[16,4,208,200]{3,2,1,0:T(8,128)(2,1)} fusion(bf16[16,4,8,200]{3,2,1,0:T(8,128)(2,1)S(1)} %collective-permute-done.1, bf16[16,4,192,200]{3,2,1,0:T(8,128)(2,1)} %reshape.289, bf16[16,4,8,200]{3,2,1,0:T(8,128)(2,1)S(1)} %collective-permute-done), kind=kLoop, calls=%fused_computation.3 | loop fusion | flops 15974400 | bytes 10649600 | tf_op jit(solution)/shard_map/concatenate | solution.py:151
  66.7 2.6 %all-gather.5.cloned.1.call-done = bf16[16,1,5,200,128]{4,3,2,1,0:T(8,128)(2,1)} async-done(((bf16[1,1,5,200,128]{4,3,2,1,0:T(8,128)(2,1)}), bf16[16,1,5,200,128]{4,3,2,1,0:T(8,128)(2,1)}) %all-gather.5.cloned.1.call-update) | async-done | bytes 4096016 | tf_op jit(solution)/shard_map/all_gather | solution.py:313
  69.3 0.9 tile.13.keep_ref
  70.2 17.5 %shard_map.140.rows_ref = bf16[16,4,208,128]{3,2,1,0:T(8,128)(2,1)} custom-call(bf16[16,4,208,200]{3,2,1,0:T(8,128)(2,1)} %pad_maximum_fusion.rows_ref, bf16[16,5,200,128]{3,2,1,0:T(8,128)(2,1)} %bitcast.55, f32[832,128]{1,0:T(8,128)} %tile.13.keep_ref), custom_call_target="tpu_custom_call" | custom-call | flops 3407872000 | bytes 16449536 | tf_op jit(solution)/shard_map/pallas_call | solution.py:217
  87.7 39.7 %all-gather.7.cloned.1.call-done = bf16[1,1,2,80,128,128]{5,4,3,2,1,0:T(8,128)(2,1)} async-done(((bf16[1,1,2,5,128,128]{5,4,3,2,1,0:T(8,128)(2,1)}), bf16[1,1,2,80,128,128]{5,4,3,2,1,0:T(8,128)(2,1)}) %all-gather.7.cloned.1.call-update) | async-done | bytes 5242896 | tf_op jit(solution)/shard_map/all_gather | solution.py:314
  127.4 15.4 %shard_map.141.rows_ref = bf16[16,4,208,128]{3,2,1,0:T(8,128)(2,1)} custom-call(bf16[16,4,208,128]{3,2,1,0:T(8,128)(2,1)} %shard_map.140.rows_ref, bf16[2,16,5,128,128]{4,3,2,1,0:T(8,128)(2,1)} %bitcast.53, f32[832,128]{1,0:T(8,128)} %tile.13.keep_ref), custom_call_target="tpu_custom_call" | custom-call | flops 2181038080 | bytes 13058048 | tf_op jit(solution)/shard_map/pallas_call | solution.py:217
  142.8 16.8 %shard_map.142 = f32[4,192,512]{2,1,0:T(8,128)} custom-call(bf16[16,4,208,128]{3,2,1,0:T(8,128)(2,1)} %shard_map.141.rows_ref, bf16[2,16,5,128,128]{4,3,2,1,0:T(8,128)(2,1)} %bitcast.54, bf16[16,128,512]{2,1,0:T(8,128)(2,1)} %bitcast.71), custom_call_target="tpu_custom_call" | custom-call | flops 3925868544 | bytes 9699328 | tf_op jit(solution)/shard_map/pallas_call | solution.py:217
  159.6 2.7 %copy.90 = f32[4,8,24,512]{3,2,0,1:T(8,128)} copy(f32[4,8,24,512]{3,2,1,0:T(8,128)} %bitcast.58) | data formatting | bytes 3145728 | tf_op jit(solution)/shard_map/reshape | solution.py:318
  162.4 4.6 %all-to-all-start = ((f32[8,4,24,512]{3,2,1,0:T(8,128)}), f32[8,4,24,512]{3,2,1,0:T(8,128)S(1)}, u32[]{:S(2)}, u32[]{:S(2)}) async-start(f32[8,4,24,512]{3,2,1,0:T(8,128)} %bitcast.50), calls=%async_computation | async-start | bytes 3145728 | tf_op jit(solution)/shard_map/all_to_all | solution.py:319
  167.6 1.2 exponential_reduce_fusion.2
  170.4 18.2 %all-to-all-done = f32[8,4,24,512]{3,2,1,0:T(8,128)S(1)} async-done(((f32[8,4,24,512]{3,2,1,0:T(8,128)}), f32[8,4,24,512]{3,2,1,0:T(8,128)S(1)}, u32[]{:S(2)}, u32[]{:S(2)}) %all-to-all-start) | async-done | bytes 1572896 | tf_op jit(solution)/shard_map/all_to_all | solution.py:319
  188.9 0.7 fusion.8
  189.7 0.7 reshape.316
  190.5 3.5 %all-to-all-start.1 = ((f32[8,1,480]{2,1,0:T(1,128)}), f32[8,1,480]{2,1,0:T(1,128)S(1)}, u32[]{:S(2)}, u32[]{:S(2)}) async-start(f32[8,1,480]{2,1,0:T(1,128)} %reshape.316), calls=%async_computation.1 | async-start | bytes 32768 | tf_op jit(solution)/shard_map/all_to_all | solution.py:326
  196.1 3.0 %all-to-all-done.1 = f32[8,1,480]{2,1,0:T(1,128)S(1)} async-done(((f32[8,1,480]{2,1,0:T(1,128)}), f32[8,1,480]{2,1,0:T(1,128)S(1)}, u32[]{:S(2)}, u32[]{:S(2)}) %all-to-all-start.1) | async-done | bytes 15392 | tf_op jit(solution)/shard_map/all_to_all | solution.py:326
  199.6 0.7 reduce.5
  200.7 0.7 pad.16.emit_ref
  201.4 0.7 broadcast_in_dim.43.within_ref
  202.1 0.7 broadcast_in_dim.44.between_ref
  202.8 4.5 %shard_map.143 = (f32[48,5,128]{2,1,0:T(8,128)}, f32[48,1,128]{2,1,0:T(1,128)}) custom-call(f32[5,5,128]{2,1,0:T(8,128)} %broadcast_in_dim.43.within_ref, f32[5,5,128]{2,1,0:T(8,128)} %broadcast_in_dim.44.between_ref, f32[5,128]{1,0:T(8,128)} %pad.15.start_ref, f32[48,5,128]{2,1,0:T(8,128)} %pad.16.emit_ref, f32[48,1,128]{2,1,0:T(1,128)} %bitcast.69, ...), custom_call_target="tpu_custom_call" | custom-call | flops 3932160 | bytes 344064 | tf_op jit(solution)/shard_map/pallas_call | solution.py:105
  207.3 0.7 slice.24
  208.0 0.7 slice_reduce_fusion
  208.9 1.5 collective-permute-start.2
  210.4 2.7 %collective-permute-start.3 = (f32[1,4,5,5,4]{3,4,2,1,0:T(4,128)S(1)}, f32[1,4,5,5,4]{3,4,2,1,0:T(4,128)S(1)}, u32[]{:S(2)}, u32[]{:S(2)}) collective-permute-start(f32[1,4,5,5,4]{3,4,2,1,0:T(4,128)S(1)} %get-tuple-element.13), channel_id=1, source_target_pairs={{0,16},{8,24},{16,0},{24,8},{32,48},{40,56},{48,32},{56,40},{64,80... | collective-permute-start | bytes 4808 | tf_op jit(solution)/shard_map/ppermute | solution.py:276
  213.1 1.4 collective-permute-start.4
  214.7 0.8 copy.86
  215.6 1.1 copy.87
  217.5 2.3 collective-permute-start.6
  219.7 1.6 collective-permute-start.7
  221.4 5.2 %collective-permute-done.5 = f32[4,4,5,5,4]{3,4,2,1,0:T(4,128)S(1)} collective-permute-done((f32[4,4,5,5,4]{3,4,2,1,0:T(4,128)S(1)}, f32[4,4,5,5,4]{3,4,2,1,0:T(4,128)S(1)}, u32[]{:S(2)}, u32[]{:S(2)}) %collective-permute-start.5) | collective-permute-done | bytes 6432 | tf_op jit(solution)/shard_map/ppermute | solution.py:276
  227.2 0.9 gather_fusion
  228.1 2.1 copy.85
  230.2 1.3 bitcast_select_fusion.mats_ref
  232.1 5.8 %shard_map.144 = (f32[64,5,4]{2,1,0:T(8,128)}, f32[1,4]{1,0:T(1,128)}) custom-call(f32[5,4]{1,0:T(8,128)} %broadcast_in_dim.39.prior_ref, f32[64,5,5,4]{3,2,1,0:T(8,128)} %bitcast_select_fusion.mats_ref), custom_call_target="tpu_custom_call" | custom-call | tf_op jit(solution)/shard_map/pallas_call | solution.py:126
  237.9 0.7 constant_dynamic-slice_fusion
  239.0 0.7 reshape.296
  239.7 1.1 bitcast_divide_fusion
  (80 shorter events, 7.3 us)
Async XLA Ops:
  7.2 181.8 %copy-start = (f32[512,5]{0,1:T(8,128)S(1)}, f32[512,5]{0,1:T(8,128)}, u32[]{:S(2)}) copy-start(f32[512,5]{0,1:T(8,128)} %param.22) | copy-start | bytes 30724
  7.2 62.1 %all-gather.5.cloned.1.call-start = ((), (), s32[]{:S(2)}) async-start(), calls=%async_computation.2 | async-start | bytes 4352000 | tf_op jit(solution)/shard_map/all_gather | solution.py:313
  7.9 119.5 %all-gather.7.cloned.1.call-start = ((), (), s32[]{:S(2)}) async-start(), calls=%async_computation.3 | async-start | bytes 5570560 | tf_op jit(solution)/shard_map/all_gather | solution.py:314
  40.5 15.3 %collective-permute-start = (bf16[16,4,8,200]{3,2,1,0:T(8,128)(2,1)S(1)}, bf16[16,4,8,200]{3,2,1,0:T(8,128)(2,1)S(1)}, u32[]{:S(2)}, u32[]{:S(2)}) collective-permute-start(bf16[16,4,8,200]{3,2,1,0:T(8,128)(2,1)S(1)} %get-tuple-element.14), channel_id=1, source_target_pairs={{0,8},{8,16},{16,24},{24,32},{32,40},{40,48},{48,56},{56,64},{64,7... | collective-permute-start | bytes 614408 | tf_op jit(solution)/shard_map/ppermute | solution.py:144
  44.1 16.2 %collective-permute-start.1 = (bf16[16,4,8,200]{3,2,1,0:T(8,128)(2,1)S(1)}, bf16[16,4,8,200]{3,2,1,0:T(8,128)(2,1)S(1)}, u32[]{:S(2)}, u32[]{:S(2)}) collective-permute-start(bf16[16,4,8,200]{3,2,1,0:T(8,128)(2,1)S(1)} %get-tuple-element.15), channel_id=1, source_target_pairs={{8,0},{16,8},{24,16},{32,24},{40,32},{48,40},{56,48},{64,56},{72,6... | collective-permute-start | bytes 614408 | tf_op jit(solution)/shard_map/ppermute | solution.py:144
  159.6 7.3 %copy-start.6 = (f32[5]{0:T(128)S(1)}, f32[5]{0:T(128)}, u32[]{:S(2)}) copy-start(f32[5]{0:T(128)} %param.25) | copy-start | bytes 64
  159.6 10.6 %copy-start.1 = (s32[4,192]{1,0:T(4,128)S(1)}, s32[4,192]{1,0:T(4,128)}, u32[]{:S(2)}) copy-start(s32[4,192]{1,0:T(4,128)} %param.17) | copy-start | bytes 9220
  159.6 10.7 %copy-start.4 = (s32[4]{0:T(128)S(1)}, s32[4]{0:T(128)}, u32[]{:S(2)}) copy-start(s32[4]{0:T(128)} %param.16) | copy-start | bytes 52
  159.6 29.3 %copy-start.5 = (f32[512]{0:T(512)S(1)}, f32[512]{0:T(512)}, u32[]{:S(2)}) copy-start(f32[512]{0:T(512)} %param.21) | copy-start | bytes 6148
  162.4 39.0 %copy-start.2 = (f32[5,5]{1,0:T(8,128)S(1)}, f32[5,5]{1,0:T(8,128)}, u32[]{:S(2)}) copy-start(f32[5,5]{1,0:T(8,128)} %param.23) | copy-start | bytes 304
  162.4 39.7 %copy-start.3 = (f32[5,5]{1,0:T(8,128)S(1)}, f32[5,5]{1,0:T(8,128)}, u32[]{:S(2)}) copy-start(f32[5,5]{1,0:T(8,128)} %param.24) | copy-start | bytes 304
  162.4 26.1 %all-to-all-start = ((f32[8,4,24,512]{3,2,1,0:T(8,128)}), f32[8,4,24,512]{3,2,1,0:T(8,128)S(1)}, u32[]{:S(2)}, u32[]{:S(2)}) async-start(f32[8,4,24,512]{3,2,1,0:T(8,128)} %bitcast.50), calls=%async_computation | async-start | bytes 3145728 | tf_op jit(solution)/shard_map/all_to_all | solution.py:319
  190.5 8.6 %all-to-all-start.1 = ((f32[8,1,480]{2,1,0:T(1,128)}), f32[8,1,480]{2,1,0:T(1,128)S(1)}, u32[]{:S(2)}, u32[]{:S(2)}) async-start(f32[8,1,480]{2,1,0:T(1,128)} %reshape.316), calls=%async_computation.1 | async-start | bytes 32768 | tf_op jit(solution)/shard_map/all_to_all | solution.py:326
  208.9 7.7 %collective-permute-start.2 = (f32[1,4,5,5,4]{3,4,2,1,0:T(4,128)S(1)}, f32[1,4,5,5,4]{3,4,2,1,0:T(4,128)S(1)}, u32[]{:S(2)}, u32[]{:S(2)}) collective-permute-start(f32[1,4,5,5,4]{3,4,2,1,0:T(4,128)S(1)} %get-tuple-element.13), channel_id=1, source_target_pairs={{0,8},{8,16},{16,24},{24,0},{32,40},{40,48},{48,56},{56,32},{64,72... | collective-permute-start | bytes 4808 | tf_op jit(solution)/shard_map/ppermute | solution.py:276
  210.4 6.2 %collective-permute-start.3 = (f32[1,4,5,5,4]{3,4,2,1,0:T(4,128)S(1)}, f32[1,4,5,5,4]{3,4,2,1,0:T(4,128)S(1)}, u32[]{:S(2)}, u32[]{:S(2)}) collective-permute-start(f32[1,4,5,5,4]{3,4,2,1,0:T(4,128)S(1)} %get-tuple-element.13), channel_id=1, source_target_pairs={{0,16},{8,24},{16,0},{24,8},{32,48},{40,56},{48,32},{56,40},{64,80... | collective-permute-start | bytes 4808 | tf_op jit(solution)/shard_map/ppermute | solution.py:276
  213.1 4.0 %collective-permute-start.4 = (f32[1,4,5,5,4]{3,4,2,1,0:T(4,128)S(1)}, f32[1,4,5,5,4]{3,4,2,1,0:T(4,128)S(1)}, u32[]{:S(2)}, u32[]{:S(2)}) collective-permute-start(f32[1,4,5,5,4]{3,4,2,1,0:T(4,128)S(1)} %get-tuple-element.13), channel_id=1, source_target_pairs={{0,24},{8,0},{16,8},{24,16},{32,56},{40,32},{48,40},{56,48},{64,88... | collective-permute-start | bytes 4808 | tf_op jit(solution)/shard_map/ppermute | solution.py:276
  217.2 9.4 %collective-permute-start.5 = (f32[4,4,5,5,4]{3,4,2,1,0:T(4,128)S(1)}, f32[4,4,5,5,4]{3,4,2,1,0:T(4,128)S(1)}, u32[]{:S(2)}, u32[]{:S(2)}) collective-permute-start(f32[4,4,5,5,4]{3,4,2,1,0:T(4,128)S(1)} %pad_maximum_fusion.1), channel_id=1, source_target_pairs={{0,32},{8,40},{16,48},{24,56},{32,64},{40,72},{48,80},{56,88},{64,... | collective-permute-start | bytes 19208 | tf_op jit(solution)/shard_map/ppermute | solution.py:276
  217.5 9.1 %collective-permute-start.6 = (f32[4,4,5,5,4]{3,4,2,1,0:T(4,128)S(1)}, f32[4,4,5,5,4]{3,4,2,1,0:T(4,128)S(1)}, u32[]{:S(2)}, u32[]{:S(2)}) collective-permute-start(f32[4,4,5,5,4]{3,4,2,1,0:T(4,128)S(1)} %pad_maximum_fusion.1), channel_id=1, source_target_pairs={{0,64},{8,72},{16,80},{24,88},{32,96},{40,104},{48,112},{56,120},{... | collective-permute-start | bytes 19208 | tf_op jit(solution)/shard_map/ppermute | solution.py:276
  219.7 7.4 %collective-permute-start.7 = (f32[4,4,5,5,4]{3,4,2,1,0:T(4,128)S(1)}, f32[4,4,5,5,4]{3,4,2,1,0:T(4,128)S(1)}, u32[]{:S(2)}, u32[]{:S(2)}) collective-permute-start(f32[4,4,5,5,4]{3,4,2,1,0:T(4,128)S(1)} %pad_maximum_fusion.1), channel_id=1, source_target_pairs={{0,96},{8,104},{16,112},{24,120},{32,0},{40,8},{48,16},{56,24},{64... | collective-permute-start | bytes 19208 | tf_op jit(solution)/shard_map/ppermute | solution.py:276
Sparse Core Ops, SparseCore 0:
  10.2 59.0 all-gather.4
  71.4 55.9 all-gather.6

commit v15 on v14

--- a/solution.py
+++ b/solution.py
@@ -43,8 +43,9 @@
 
 def prefix_kernel(within_ref, between_ref, start_ref, emit_ref, cross_ref, valid_ref, prefix_ref, offset_ref):
     patches = emit_ref.shape[0]
-    within = [within_ref[i] for i in range(STATES)]
-    between = [between_ref[i] for i in range(STATES)]
+    lanes = start_ref.shape[1]
+    within = [jnp.broadcast_to(within_ref[i], (STATES, lanes)) for i in range(STATES)]
+    between = [jnp.broadcast_to(between_ref[i], (STATES, lanes)) for i in range(STATES)]
 
     def body(p, carry):
         state, offset = carry
@@ -100,8 +101,8 @@
     lane_start = (jnp.arange(width, dtype=jnp.int32) // recordings) % STATES
     basis = jnp.arange(STATES, dtype=jnp.int32)[:, None] == lane_start[None, :]
     start = lanes_padded(jnp.where(basis, 0.0, NEGATIVE).astype(jnp.float32))
-    within_in = jnp.broadcast_to(trans_within[:, :, None], (STATES, STATES, LANES))
-    between_in = jnp.broadcast_to(trans_between[:, :, None], (STATES, STATES, LANES))
+    within_in = trans_within[:, :, None]
+    between_in = trans_between[:, :, None]
     prefix, offset = pl.pallas_call(
         prefix_kernel,
         out_shape=(

time: 249 us -> 248 us (level)
  transfers between devices with their start and end apart: 12 -> 12, of which waited for: 9 -> 9; matrix products, arithmetic and copies ran while one was open for 18% -> 19% of each run, Pallas kernels for 7% -> 7%
where the time goes in v15:
time: 248 us; the launch traced here: 246 us
  waiting for transfers between devices  84.4 us (34%)
  Pallas kernels  60 us (24%)
  local copies, waits for them, and re-layouts  45.8 us (18%)
  starting transfers between devices  22.7 us (9%)
  between operations  15.8 us (6%)
  other arithmetic  13.1 us (5%)
  matrix products  4.54 us (2%)
    pallas_call x3, Pallas kernels, per_type_call(): pl.pallas_call(kernel, grid=(types,), in_specs=[pl.BlockSpec((1,) + rows....  49.7 us
    all_gather x1, waiting for transfers between devices, local(): lax.all_gather(jnp.swapaxes(conv_hid[:, 0], 0, 1), 'rec', axis=1, tiled=T...  39.7 us
    reshape x1, local copies, waits for them, and re-layouts, local(): patch_rows = rows.reshape(groups, recordings, patches, SAMP)  20.3 us
    all_to_all x1, waiting for transfers between devices, local(): lax.all_to_all(jnp.swapaxes(pieces, 0, 1), 'chan', 0, 0, tiled=True)  18.2 us
    ppermute x2, waiting for transfers between devices, neighbour_shift(): return lax.ppermute(block, axis, route)  14.8 us
    ppermute x6, starting transfers between devices, shifted(): return lax.ppermute(values, 'rec', route)  9.81 us
    concatenate x1, other arithmetic, halo_rows(): return jnp.concatenate([from_left, patch_rows, from_right], axis=2)  6.4 us
    ppermute x6, waiting for transfers between devices, shifted(): return lax.ppermute(values, 'rec', route)  6.17 us
  transfers between devices with their start and end apart: 12, of which 9 were waited for; matrix products, arithmetic and copies ran while one was open for 19% of the time, Pallas kernels for 7%

profile of v15, /device:TPU:0, one launch (start us, length us, event | category | flops | bytes accessed | tf_op | source)
XLA Modules:
  0.0 246.3 jit_solution(17815431201966580079)
XLA Ops:
  7.2 0.7 all-gather.5.cloned.1.call-update
  8.0 0.7 all-gather.7.cloned.1.call-update
  8.7 0.7 broadcast_compare_fusion
  9.4 3.8 %fusion = bf16[16,4,38400]{2,0,1:T(8,128)(2,1)S(1)} fusion(bf16[4,16,38400]{2,1,0:T(8,128)(2,1)} %param.13, s32[4,16]{1,0:T(4,128)} %bitcast.68, pred[4,16]{1,0:T(4,128)(4,1)S(1)} %broadcast_compare_fusion), kind=kOutput, calls=%fused_computation.2 | convolution fusion | flops 81102848 | bytes 9830720 | tf_op jit(solution)/shard_map/bms,bst->mbt/dot_general | solution.py:310
  13.2 6.0 %copy.83 = bf16[16,4,38400]{2,1,0:T(4,128)(2,1)} copy(bf16[16,4,38400]{2,0,1:T(8,128)(2,1)S(1)} %fusion) | data formatting | bytes 9830400 | tf_op jit(solution)/shard_map/convert_element_type | solution.py:312
  19.2 20.3 %reshape.287 = bf16[16,4,192,200]{3,2,1,0:T(8,128)(2,1)} reshape(bf16[16,4,38400]{2,1,0:T(4,128)(2,1)} %copy.83) | data formatting | bytes 9830400 | tf_op jit(solution)/shard_map/reshape | solution.py:313
  39.5 1.1 fusion.44
  40.5 3.6 %collective-permute-start = (bf16[16,4,8,200]{3,2,1,0:T(8,128)(2,1)S(1)}, bf16[16,4,8,200]{3,2,1,0:T(8,128)(2,1)S(1)}, u32[]{:S(2)}, u32[]{:S(2)}) collective-permute-start(bf16[16,4,8,200]{3,2,1,0:T(8,128)(2,1)S(1)} %get-tuple-element.14), channel_id=1, source_target_pairs={{0,8},{8,16},{16,24},{24,32},{32,40},{40,48},{48,56},{56,64},{64,7... | collective-permute-start | bytes 614408 | tf_op jit(solution)/shard_map/ppermute | solution.py:145
  44.1 1.3 collective-permute-start.1
  45.5 10.3 %collective-permute-done = bf16[16,4,8,200]{3,2,1,0:T(8,128)(2,1)S(1)} collective-permute-done((bf16[16,4,8,200]{3,2,1,0:T(8,128)(2,1)S(1)}, bf16[16,4,8,200]{3,2,1,0:T(8,128)(2,1)S(1)}, u32[]{:S(2)}, u32[]{:S(2)}) %collective-permute-start) | collective-permute-done | bytes 204832 | tf_op jit(solution)/shard_map/ppermute | solution.py:145
  55.8 4.5 %collective-permute-done.1 = bf16[16,4,8,200]{3,2,1,0:T(8,128)(2,1)S(1)} collective-permute-done((bf16[16,4,8,200]{3,2,1,0:T(8,128)(2,1)S(1)}, bf16[16,4,8,200]{3,2,1,0:T(8,128)(2,1)S(1)}, u32[]{:S(2)}, u32[]{:S(2)}) %collective-permute-start.1) | collective-permute-done | bytes 204832 | tf_op jit(solution)/shard_map/ppermute | solution.py:145
  60.3 6.4 %pad_maximum_fusion.rows_ref = bf16[16,4,208,200]{3,2,1,0:T(8,128)(2,1)} fusion(bf16[16,4,8,200]{3,2,1,0:T(8,128)(2,1)S(1)} %collective-permute-done.1, bf16[16,4,192,200]{3,2,1,0:T(8,128)(2,1)} %reshape.287, bf16[16,4,8,200]{3,2,1,0:T(8,128)(2,1)S(1)} %collective-permute-done), kind=kLoop, calls=%fused_computation.3 | loop fusion | flops 15974400 | bytes 10649600 | tf_op jit(solution)/shard_map/concatenate | solution.py:152
  66.7 2.6 %all-gather.5.cloned.1.call-done = bf16[16,1,5,200,128]{4,3,2,1,0:T(8,128)(2,1)} async-done(((bf16[1,1,5,200,128]{4,3,2,1,0:T(8,128)(2,1)}), bf16[16,1,5,200,128]{4,3,2,1,0:T(8,128)(2,1)}) %all-gather.5.cloned.1.call-update) | async-done | bytes 4096016 | tf_op jit(solution)/shard_map/all_gather | solution.py:314
  69.3 0.9 tile.13.keep_ref
  70.2 17.5 %shard_map.140.rows_ref = bf16[16,4,208,128]{3,2,1,0:T(8,128)(2,1)} custom-call(bf16[16,4,208,200]{3,2,1,0:T(8,128)(2,1)} %pad_maximum_fusion.rows_ref, bf16[16,5,200,128]{3,2,1,0:T(8,128)(2,1)} %bitcast.57, f32[832,128]{1,0:T(8,128)} %tile.13.keep_ref), custom_call_target="tpu_custom_call" | custom-call | flops 3407872000 | bytes 16449536 | tf_op jit(solution)/shard_map/pallas_call | solution.py:218
  87.7 39.7 %all-gather.7.cloned.1.call-done = bf16[1,1,2,80,128,128]{5,4,3,2,1,0:T(8,128)(2,1)} async-done(((bf16[1,1,2,5,128,128]{5,4,3,2,1,0:T(8,128)(2,1)}), bf16[1,1,2,80,128,128]{5,4,3,2,1,0:T(8,128)(2,1)}) %all-gather.7.cloned.1.call-update) | async-done | bytes 5242896 | tf_op jit(solution)/shard_map/all_gather | solution.py:315
  127.4 15.4 %shard_map.141.rows_ref = bf16[16,4,208,128]{3,2,1,0:T(8,128)(2,1)} custom-call(bf16[16,4,208,128]{3,2,1,0:T(8,128)(2,1)} %shard_map.140.rows_ref, bf16[2,16,5,128,128]{4,3,2,1,0:T(8,128)(2,1)} %bitcast.55, f32[832,128]{1,0:T(8,128)} %tile.13.keep_ref), custom_call_target="tpu_custom_call" | custom-call | flops 2181038080 | bytes 13058048 | tf_op jit(solution)/shard_map/pallas_call | solution.py:218
  142.8 16.8 %shard_map.142 = f32[4,192,512]{2,1,0:T(8,128)} custom-call(bf16[16,4,208,128]{3,2,1,0:T(8,128)(2,1)} %shard_map.141.rows_ref, bf16[2,16,5,128,128]{4,3,2,1,0:T(8,128)(2,1)} %bitcast.56, bf16[16,128,512]{2,1,0:T(8,128)(2,1)} %bitcast.75), custom_call_target="tpu_custom_call" | custom-call | flops 3925868544 | bytes 9699328 | tf_op jit(solution)/shard_map/pallas_call | solution.py:218
  159.7 2.8 %copy.100 = f32[4,8,24,512]{3,2,0,1:T(8,128)} copy(f32[4,8,24,512]{3,2,1,0:T(8,128)} %bitcast.60) | data formatting | bytes 3145728 | tf_op jit(solution)/shard_map/reshape | solution.py:319
  162.4 4.4 %all-to-all-start = ((f32[8,4,24,512]{3,2,1,0:T(8,128)}), f32[8,4,24,512]{3,2,1,0:T(8,128)S(1)}, u32[]{:S(2)}, u32[]{:S(2)}) async-start(f32[8,4,24,512]{3,2,1,0:T(8,128)} %bitcast.52), calls=%async_computation | async-start | bytes 3145728 | tf_op jit(solution)/shard_map/all_to_all | solution.py:320
  167.5 1.2 exponential_reduce_fusion.2
  170.3 18.2 %all-to-all-done = f32[8,4,24,512]{3,2,1,0:T(8,128)S(1)} async-done(((f32[8,4,24,512]{3,2,1,0:T(8,128)}), f32[8,4,24,512]{3,2,1,0:T(8,128)S(1)}, u32[]{:S(2)}, u32[]{:S(2)}) %all-to-all-start) | async-done | bytes 1572896 | tf_op jit(solution)/shard_map/all_to_all | solution.py:320
  188.9 0.7 fusion.8
  189.6 0.7 reshape.314
  190.4 3.5 %all-to-all-start.1 = ((f32[8,1,480]{2,1,0:T(1,128)}), f32[8,1,480]{2,1,0:T(1,128)S(1)}, u32[]{:S(2)}, u32[]{:S(2)}) async-start(f32[8,1,480]{2,1,0:T(1,128)} %reshape.314), calls=%async_computation.1 | async-start | bytes 32768 | tf_op jit(solution)/shard_map/all_to_all | solution.py:327
  195.4 0.7 copy.92.within_ref
  196.1 0.7 copy.93.between_ref
  197.4 1.6 all-to-all-done.1
  199.5 0.7 reduce.5
  200.6 0.7 pad.16.emit_ref
  201.3 4.6 %shard_map.143 = (f32[48,5,128]{2,1,0:T(8,128)}, f32[48,1,128]{2,1,0:T(1,128)}) custom-call(f32[5,5,1]{2,1,0:T(8,128)} %copy.92.within_ref, f32[5,5,1]{2,1,0:T(8,128)} %copy.93.between_ref, f32[5,128]{1,0:T(8,128)} %pad.15.start_ref, f32[48,5,128]{2,1,0:T(8,128)} %pad.16.emit_ref, f32[48,1,128]{2,1,0:T(1,128)} %bitcast.71, f32[48,1,128]{2,1,0:T(1,128)} %bitcast.70), custom_call_target="tpu_custom_call" | custom-call | flops 3932160 | bytes 344064 | tf_op jit(solution)/shard_map/pallas_call | solution.py:106
  205.9 0.7 slice.24
  206.6 0.7 slice_reduce_fusion
  207.5 1.5 collective-permute-start.2
  209.0 2.7 %collective-permute-start.3 = (f32[1,4,5,5,4]{3,4,2,1,0:T(4,128)S(1)}, f32[1,4,5,5,4]{3,4,2,1,0:T(4,128)S(1)}, u32[]{:S(2)}, u32[]{:S(2)}) collective-permute-start(f32[1,4,5,5,4]{3,4,2,1,0:T(4,128)S(1)} %get-tuple-element.13), channel_id=1, source_target_pairs={{0,16},{8,24},{16,0},{24,8},{32,48},{40,56},{48,32},{56,40},{64,80... | collective-permute-start | bytes 4808 | tf_op jit(solution)/shard_map/ppermute | solution.py:277
  211.7 1.4 collective-permute-start.4
  213.4 0.8 copy.96
  214.2 1.1 copy.97
  216.1 2.3 collective-permute-start.6
  218.4 1.6 collective-permute-start.7
  220.0 5.2 %collective-permute-done.5 = f32[4,4,5,5,4]{3,4,2,1,0:T(4,128)S(1)} collective-permute-done((f32[4,4,5,5,4]{3,4,2,1,0:T(4,128)S(1)}, f32[4,4,5,5,4]{3,4,2,1,0:T(4,128)S(1)}, u32[]{:S(2)}, u32[]{:S(2)}) %collective-permute-start.5) | collective-permute-done | bytes 6432 | tf_op jit(solution)/shard_map/ppermute | solution.py:277
  225.8 0.9 gather_fusion
  226.7 2.1 copy.95
  228.8 1.3 bitcast_select_fusion.mats_ref
  230.7 5.8 %shard_map.144 = (f32[64,5,4]{2,1,0:T(8,128)}, f32[1,4]{1,0:T(1,128)}) custom-call(f32[5,4]{1,0:T(8,128)} %broadcast_in_dim.39.prior_ref, f32[64,5,5,4]{3,2,1,0:T(8,128)} %bitcast_select_fusion.mats_ref), custom_call_target="tpu_custom_call" | custom-call | tf_op jit(solution)/shard_map/pallas_call | solution.py:127
  236.5 0.7 constant_dynamic-slice_fusion
  237.6 0.7 reshape.294
  238.3 1.1 bitcast_divide_fusion
  (80 shorter events, 7.3 us)
Async XLA Ops:
  7.2 181.7 %copy-start = (f32[512,5]{0,1:T(8,128)S(1)}, f32[512,5]{0,1:T(8,128)}, u32[]{:S(2)}) copy-start(f32[512,5]{0,1:T(8,128)} %param.22) | copy-start | bytes 30724
  7.2 62.1 %all-gather.5.cloned.1.call-start = ((), (), s32[]{:S(2)}) async-start(), calls=%async_computation.2 | async-start | bytes 4352000 | tf_op jit(solution)/shard_map/all_gather | solution.py:314
  7.9 119.5 %all-gather.7.cloned.1.call-start = ((), (), s32[]{:S(2)}) async-start(), calls=%async_computation.3 | async-start | bytes 5570560 | tf_op jit(solution)/shard_map/all_gather | solution.py:315
  40.5 15.3 %collective-permute-start = (bf16[16,4,8,200]{3,2,1,0:T(8,128)(2,1)S(1)}, bf16[16,4,8,200]{3,2,1,0:T(8,128)(2,1)S(1)}, u32[]{:S(2)}, u32[]{:S(2)}) collective-permute-start(bf16[16,4,8,200]{3,2,1,0:T(8,128)(2,1)S(1)} %get-tuple-element.14), channel_id=1, source_target_pairs={{0,8},{8,16},{16,24},{24,32},{32,40},{40,48},{48,56},{56,64},{64,7... | collective-permute-start | bytes 614408 | tf_op jit(solution)/shard_map/ppermute | solution.py:145
  44.1 16.2 %collective-permute-start.1 = (bf16[16,4,8,200]{3,2,1,0:T(8,128)(2,1)S(1)}, bf16[16,4,8,200]{3,2,1,0:T(8,128)(2,1)S(1)}, u32[]{:S(2)}, u32[]{:S(2)}) collective-permute-start(bf16[16,4,8,200]{3,2,1,0:T(8,128)(2,1)S(1)} %get-tuple-element.15), channel_id=1, source_target_pairs={{8,0},{16,8},{24,16},{32,24},{40,32},{48,40},{56,48},{64,56},{72,6... | collective-permute-start | bytes 614408 | tf_op jit(solution)/shard_map/ppermute | solution.py:145
  159.6 7.3 %copy-start.6 = (f32[5]{0:T(128)S(1)}, f32[5]{0:T(128)}, u32[]{:S(2)}) copy-start(f32[5]{0:T(128)} %param.25) | copy-start | bytes 64
  159.6 10.5 %copy-start.1 = (s32[4,192]{1,0:T(4,128)S(1)}, s32[4,192]{1,0:T(4,128)}, u32[]{:S(2)}) copy-start(s32[4,192]{1,0:T(4,128)} %param.17) | copy-start | bytes 9220
  159.6 10.6 %copy-start.4 = (s32[4]{0:T(128)S(1)}, s32[4]{0:T(128)}, u32[]{:S(2)}) copy-start(s32[4]{0:T(128)} %param.16) | copy-start | bytes 52
  159.6 29.2 %copy-start.5 = (f32[512]{0:T(512)S(1)}, f32[512]{0:T(512)}, u32[]{:S(2)}) copy-start(f32[512]{0:T(512)} %param.21) | copy-start | bytes 6148
  159.6 35.7 %copy-start.2 = (f32[5,5]{1,0:T(8,128)S(1)}, f32[5,5]{1,0:T(8,128)}, u32[]{:S(2)}) copy-start(f32[5,5]{1,0:T(8,128)} %param.23) | copy-start | bytes 304
  159.7 36.5 %copy-start.3 = (f32[5,5]{1,0:T(8,128)S(1)}, f32[5,5]{1,0:T(8,128)}, u32[]{:S(2)}) copy-start(f32[5,5]{1,0:T(8,128)} %param.24) | copy-start | bytes 304
  162.4 26.0 %all-to-all-start = ((f32[8,4,24,512]{3,2,1,0:T(8,128)}), f32[8,4,24,512]{3,2,1,0:T(8,128)S(1)}, u32[]{:S(2)}, u32[]{:S(2)}) async-start(f32[8,4,24,512]{3,2,1,0:T(8,128)} %bitcast.52), calls=%async_computation | async-start | bytes 3145728 | tf_op jit(solution)/shard_map/all_to_all | solution.py:320
  190.4 8.6 %all-to-all-start.1 = ((f32[8,1,480]{2,1,0:T(1,128)}), f32[8,1,480]{2,1,0:T(1,128)S(1)}, u32[]{:S(2)}, u32[]{:S(2)}) async-start(f32[8,1,480]{2,1,0:T(1,128)} %reshape.314), calls=%async_computation.1 | async-start | bytes 32768 | tf_op jit(solution)/shard_map/all_to_all | solution.py:327
  207.5 7.7 %collective-permute-start.2 = (f32[1,4,5,5,4]{3,4,2,1,0:T(4,128)S(1)}, f32[1,4,5,5,4]{3,4,2,1,0:T(4,128)S(1)}, u32[]{:S(2)}, u32[]{:S(2)}) collective-permute-start(f32[1,4,5,5,4]{3,4,2,1,0:T(4,128)S(1)} %get-tuple-element.13), channel_id=1, source_target_pairs={{0,8},{8,16},{16,24},{24,0},{32,40},{40,48},{48,56},{56,32},{64,72... | collective-permute-start | bytes 4808 | tf_op jit(solution)/shard_map/ppermute | solution.py:277
  209.0 6.2 %collective-permute-start.3 = (f32[1,4,5,5,4]{3,4,2,1,0:T(4,128)S(1)}, f32[1,4,5,5,4]{3,4,2,1,0:T(4,128)S(1)}, u32[]{:S(2)}, u32[]{:S(2)}) collective-permute-start(f32[1,4,5,5,4]{3,4,2,1,0:T(4,128)S(1)} %get-tuple-element.13), channel_id=1, source_target_pairs={{0,16},{8,24},{16,0},{24,8},{32,48},{40,56},{48,32},{56,40},{64,80... | collective-permute-start | bytes 4808 | tf_op jit(solution)/shard_map/ppermute | solution.py:277
  211.7 4.0 %collective-permute-start.4 = (f32[1,4,5,5,4]{3,4,2,1,0:T(4,128)S(1)}, f32[1,4,5,5,4]{3,4,2,1,0:T(4,128)S(1)}, u32[]{:S(2)}, u32[]{:S(2)}) collective-permute-start(f32[1,4,5,5,4]{3,4,2,1,0:T(4,128)S(1)} %get-tuple-element.13), channel_id=1, source_target_pairs={{0,24},{8,0},{16,8},{24,16},{32,56},{40,32},{48,40},{56,48},{64,88... | collective-permute-start | bytes 4808 | tf_op jit(solution)/shard_map/ppermute | solution.py:277
  215.8 9.4 %collective-permute-start.5 = (f32[4,4,5,5,4]{3,4,2,1,0:T(4,128)S(1)}, f32[4,4,5,5,4]{3,4,2,1,0:T(4,128)S(1)}, u32[]{:S(2)}, u32[]{:S(2)}) collective-permute-start(f32[4,4,5,5,4]{3,4,2,1,0:T(4,128)S(1)} %pad_maximum_fusion.1), channel_id=1, source_target_pairs={{0,32},{8,40},{16,48},{24,56},{32,64},{40,72},{48,80},{56,88},{64,... | collective-permute-start | bytes 19208 | tf_op jit(solution)/shard_map/ppermute | solution.py:277
  216.1 9.1 %collective-permute-start.6 = (f32[4,4,5,5,4]{3,4,2,1,0:T(4,128)S(1)}, f32[4,4,5,5,4]{3,4,2,1,0:T(4,128)S(1)}, u32[]{:S(2)}, u32[]{:S(2)}) collective-permute-start(f32[4,4,5,5,4]{3,4,2,1,0:T(4,128)S(1)} %pad_maximum_fusion.1), channel_id=1, source_target_pairs={{0,64},{8,72},{16,80},{24,88},{32,96},{40,104},{48,112},{56,120},{... | collective-permute-start | bytes 19208 | tf_op jit(solution)/shard_map/ppermute | solution.py:277
  218.4 7.4 %collective-permute-start.7 = (f32[4,4,5,5,4]{3,4,2,1,0:T(4,128)S(1)}, f32[4,4,5,5,4]{3,4,2,1,0:T(4,128)S(1)}, u32[]{:S(2)}, u32[]{:S(2)}) collective-permute-start(f32[4,4,5,5,4]{3,4,2,1,0:T(4,128)S(1)} %pad_maximum_fusion.1), channel_id=1, source_target_pairs={{0,96},{8,104},{16,112},{24,120},{32,0},{40,8},{48,16},{56,24},{64... | collective-permute-start | bytes 19208 | tf_op jit(solution)/shard_map/ppermute | solution.py:277
Sparse Core Ops, SparseCore 0:
  10.2 59.0 all-gather.4
  71.4 55.9 all-gather.6

commit v16 on v15

--- a/solution.py
+++ b/solution.py
@@ -186,7 +186,7 @@
     out_ref[0] = value.reshape(out_ref.shape[1:])
 
 
-def last_kernel(rows_ref, taps_ref, mix_ref, out_ref):
+def last_kernel(rows_ref, taps_ref, keep_ref, mix_ref, out_ref):
     @pl.when(pl.program_id(0) == 0)
     def _():
         out_ref[...] = jnp.zeros_like(out_ref)
@@ -194,7 +194,12 @@
     span = rows_ref.shape[2]
     recordings, patches = out_ref.shape[:2]
     margin = (span - patches) // 2
-    value = residual_layer(merged(rows_ref), taps_ref)
+    value = merged(rows_ref)
+    layers = taps_ref.shape[0]
+    for depth_index in range(layers):
+        value = residual_layer(value, taps_ref.at[depth_index : depth_index + 1])
+        if depth_index + 1 < layers:
+            value = jnp.where(keep_ref[...] > 0.5, value, jnp.zeros((), jnp.bfloat16))
     mixed = jnp.dot(value, mix_ref[0], preferred_element_type=jnp.float32)
     for item in range(recordings):
         start = item * span + margin
@@ -247,18 +252,25 @@
         first_kernel, extended, first_taps, keep, block, inner,
         lambda m: (m, 0, 0, 0), 2 * types * recordings * span * width * EMB * taps,
     )
-    for depth_index in range(layers - 1):
-        current = per_type_call(
-            hidden_kernel, current, hidden_taps, keep, block, inner,
-            lambda m: (m, 0, 0, 0), 2 * types * recordings * span * EMB * EMB * taps, depth_index,
-        )
     mix_width = mix.shape[-1]
-    return per_type_call(
-        last_kernel, current, hidden_taps, mix,
-        (recordings, patches, mix_width), jax.ShapeDtypeStruct((recordings, patches, mix_width), jnp.float32),
-        lambda m: (0, 0, 0), 2 * types * recordings * span * EMB * (EMB * taps + mix_width), layers - 1,
-    )
-
+    return pl.pallas_call(
+        last_kernel,
+        grid=(types,),
+        in_specs=[
+            pl.BlockSpec((1,) + current.shape[1:], lambda m: (m, 0, 0, 0)),
+            pl.BlockSpec((layers, 1) + hidden_taps.shape[2:], lambda m: (0, m, 0, 0, 0)),
+            pl.BlockSpec(keep.shape, lambda m: (0, 0)),
+            pl.BlockSpec((1,) + mix.shape[1:], lambda m: (m, 0, 0)),
+        ],
+        out_specs=pl.BlockSpec((recordings, patches, mix_width), lambda m: (0, 0, 0)),
+        out_shape=jax.ShapeDtypeStruct((recordings, patches, mix_width), jnp.float32),
+        compiler_params=pltpu.CompilerParams(dimension_semantics=("arbitrary",)),
+        cost_estimate=pl.CostEstimate(
+            flops=2 * types * recordings * span * EMB * (layers * EMB * taps + mix_width),
+            transcendentals=layers * types * recordings * span * EMB,
+            bytes_accessed=current.size * 2 + hidden_taps.size * 2 + mix.size * 2 + recordings * patches * mix_width * 4,
+        ),
+    )(current, hidden_taps, keep, mix)
 
 def torus_gather(block, rec_index, side):
     inner = rec_index % side

time: 248 us -> 239 us (0.964)
  Pallas kernels: 60 us -> 51.9 us
    pallas_call x3 -> x1, Pallas kernels: 49.7 us -> 17.5 us  [per_type_call(): pl.pallas_call(kernel, grid=(types,), in_specs=[pl.BlockSpec((1,) + rows....]
    pallas_call x0 -> x1, Pallas kernels: none -> 24 us  [conv_mix(): pl.pallas_call(last_kernel, grid=(types,), in_specs=[pl.BlockSpec((1,) +...]
  transfers between devices with their start and end apart: 12 -> 12, of which waited for: 9 -> 9; matrix products, arithmetic and copies ran while one was open for 19% -> 20% of each run, Pallas kernels for 7% -> 7%
where the time goes in v16:
time: 239 us; the launch traced here: 238 us
  waiting for transfers between devices  84.3 us (35%)
  Pallas kernels  51.9 us (22%)
  local copies, waits for them, and re-layouts  45.8 us (19%)
  starting transfers between devices  22.7 us (9%)
  between operations  15.8 us (7%)
  other arithmetic  13.1 us (5%)
  matrix products  4.54 us (2%)
    all_gather x1, waiting for transfers between devices, local(): lax.all_gather(jnp.swapaxes(conv_hid[:, 0], 0, 1), 'rec', axis=1, tiled=T...  39.7 us
    pallas_call x1, Pallas kernels, conv_mix(): pl.pallas_call(last_kernel, grid=(types,), in_specs=[pl.BlockSpec((1,) +...  24 us
    reshape x1, local copies, waits for them, and re-layouts, local(): patch_rows = rows.reshape(groups, recordings, patches, SAMP)  20.3 us
    all_to_all x1, waiting for transfers between devices, local(): lax.all_to_all(jnp.swapaxes(pieces, 0, 1), 'chan', 0, 0, tiled=True)  18.2 us
    pallas_call x1, Pallas kernels, per_type_call(): pl.pallas_call(kernel, grid=(types,), in_specs=[pl.BlockSpec((1,) + rows....  17.5 us
    ppermute x2, waiting for transfers between devices, neighbour_shift(): return lax.ppermute(block, axis, route)  14.8 us
    ppermute x6, starting transfers between devices, shifted(): return lax.ppermute(values, 'rec', route)  9.81 us
    concatenate x1, other arithmetic, halo_rows(): return jnp.concatenate([from_left, patch_rows, from_right], axis=2)  6.4 us
  transfers between devices with their start and end apart: 12, of which 9 were waited for; matrix products, arithmetic and copies ran while one was open for 20% of the time, Pallas kernels for 7%

profile of v16, /device:TPU:0, one launch (start us, length us, event | category | flops | bytes accessed | tf_op | source)
XLA Modules:
  0.0 238.2 jit_solution(8819355560842867883)
XLA Ops:
  7.2 0.7 all-gather.5.cloned.1.call-update
  8.0 0.7 all-gather.7.cloned.1.call-update
  8.7 0.7 broadcast_compare_fusion
  9.4 3.8 %fusion = bf16[16,4,38400]{2,0,1:T(8,128)(2,1)S(1)} fusion(bf16[4,16,38400]{2,1,0:T(8,128)(2,1)} %param.13, s32[4,16]{1,0:T(4,128)} %bitcast.66, pred[4,16]{1,0:T(4,128)(4,1)S(1)} %broadcast_compare_fusion), kind=kOutput, calls=%fused_computation.2 | convolution fusion | flops 81102848 | bytes 9830720 | tf_op jit(solution)/shard_map/bms,bst->mbt/dot_general | solution.py:322
  13.2 6.0 %copy.83 = bf16[16,4,38400]{2,1,0:T(4,128)(2,1)} copy(bf16[16,4,38400]{2,0,1:T(8,128)(2,1)S(1)} %fusion) | data formatting | bytes 9830400 | tf_op jit(solution)/shard_map/convert_element_type | solution.py:324
  19.2 20.3 %reshape.287 = bf16[16,4,192,200]{3,2,1,0:T(8,128)(2,1)} reshape(bf16[16,4,38400]{2,1,0:T(4,128)(2,1)} %copy.83) | data formatting | bytes 9830400 | tf_op jit(solution)/shard_map/reshape | solution.py:325
  39.5 1.1 fusion.44
  40.5 3.6 %collective-permute-start = (bf16[16,4,8,200]{3,2,1,0:T(8,128)(2,1)S(1)}, bf16[16,4,8,200]{3,2,1,0:T(8,128)(2,1)S(1)}, u32[]{:S(2)}, u32[]{:S(2)}) collective-permute-start(bf16[16,4,8,200]{3,2,1,0:T(8,128)(2,1)S(1)} %get-tuple-element.14), channel_id=1, source_target_pairs={{0,8},{8,16},{16,24},{24,32},{32,40},{40,48},{48,56},{56,64},{64,7... | collective-permute-start | bytes 614408 | tf_op jit(solution)/shard_map/ppermute | solution.py:145
  44.1 1.3 collective-permute-start.1
  45.5 10.3 %collective-permute-done = bf16[16,4,8,200]{3,2,1,0:T(8,128)(2,1)S(1)} collective-permute-done((bf16[16,4,8,200]{3,2,1,0:T(8,128)(2,1)S(1)}, bf16[16,4,8,200]{3,2,1,0:T(8,128)(2,1)S(1)}, u32[]{:S(2)}, u32[]{:S(2)}) %collective-permute-start) | collective-permute-done | bytes 204832 | tf_op jit(solution)/shard_map/ppermute | solution.py:145
  55.8 4.5 %collective-permute-done.1 = bf16[16,4,8,200]{3,2,1,0:T(8,128)(2,1)S(1)} collective-permute-done((bf16[16,4,8,200]{3,2,1,0:T(8,128)(2,1)S(1)}, bf16[16,4,8,200]{3,2,1,0:T(8,128)(2,1)S(1)}, u32[]{:S(2)}, u32[]{:S(2)}) %collective-permute-start.1) | collective-permute-done | bytes 204832 | tf_op jit(solution)/shard_map/ppermute | solution.py:145
  60.3 6.4 %pad_maximum_fusion.rows_ref = bf16[16,4,208,200]{3,2,1,0:T(8,128)(2,1)} fusion(bf16[16,4,8,200]{3,2,1,0:T(8,128)(2,1)S(1)} %collective-permute-done.1, bf16[16,4,192,200]{3,2,1,0:T(8,128)(2,1)} %reshape.287, bf16[16,4,8,200]{3,2,1,0:T(8,128)(2,1)S(1)} %collective-permute-done), kind=kLoop, calls=%fused_computation.3 | loop fusion | flops 15974400 | bytes 10649600 | tf_op jit(solution)/shard_map/concatenate | solution.py:152
  66.7 2.6 %all-gather.5.cloned.1.call-done = bf16[16,1,5,200,128]{4,3,2,1,0:T(8,128)(2,1)} async-done(((bf16[1,1,5,200,128]{4,3,2,1,0:T(8,128)(2,1)}), bf16[16,1,5,200,128]{4,3,2,1,0:T(8,128)(2,1)}) %all-gather.5.cloned.1.call-update) | async-done | bytes 4096016 | tf_op jit(solution)/shard_map/all_gather | solution.py:326
  69.3 0.9 tile.13.keep_ref
  70.2 17.5 %shard_map.140.rows_ref = bf16[16,4,208,128]{3,2,1,0:T(8,128)(2,1)} custom-call(bf16[16,4,208,200]{3,2,1,0:T(8,128)(2,1)} %pad_maximum_fusion.rows_ref, bf16[16,5,200,128]{3,2,1,0:T(8,128)(2,1)} %bitcast.55, f32[832,128]{1,0:T(8,128)} %tile.13.keep_ref), custom_call_target="tpu_custom_call" | custom-call | flops 3407872000 | bytes 16449536 | tf_op jit(solution)/shard_map/pallas_call | solution.py:223
  87.7 39.7 %all-gather.7.cloned.1.call-done = bf16[1,1,2,80,128,128]{5,4,3,2,1,0:T(8,128)(2,1)} async-done(((bf16[1,1,2,5,128,128]{5,4,3,2,1,0:T(8,128)(2,1)}), bf16[1,1,2,80,128,128]{5,4,3,2,1,0:T(8,128)(2,1)}) %all-gather.7.cloned.1.call-update) | async-done | bytes 5242896 | tf_op jit(solution)/shard_map/all_gather | solution.py:327
  127.4 24.0 %shard_map.141 = f32[4,192,512]{2,1,0:T(8,128)} custom-call(bf16[16,4,208,128]{3,2,1,0:T(8,128)(2,1)} %shard_map.140.rows_ref, bf16[2,16,5,128,128]{4,3,2,1,0:T(8,128)(2,1)} %bitcast.73, f32[832,128]{1,0:T(8,128)} %tile.13.keep_ref, bf16[16,128,512]{2,1,0:T(8,128)(2,1)} %bitcast.74), custom_call_target="tpu_custom_call" | custom-call | flops 6106906624 | bytes 12320768 | tf_op jit(solution)/shard_map/pallas_call | solution.py:256
  151.5 2.8 %copy.100 = f32[4,8,24,512]{3,2,0,1:T(8,128)} copy(f32[4,8,24,512]{3,2,1,0:T(8,128)} %bitcast.58) | data formatting | bytes 3145728 | tf_op jit(solution)/shard_map/reshape | solution.py:331
  154.3 4.4 %all-to-all-start = ((f32[8,4,24,512]{3,2,1,0:T(8,128)}), f32[8,4,24,512]{3,2,1,0:T(8,128)S(1)}, u32[]{:S(2)}, u32[]{:S(2)}) async-start(f32[8,4,24,512]{3,2,1,0:T(8,128)} %bitcast.52), calls=%async_computation | async-start | bytes 3145728 | tf_op jit(solution)/shard_map/all_to_all | solution.py:332
  159.3 1.2 exponential_reduce_fusion.2
  162.1 18.2 %all-to-all-done = f32[8,4,24,512]{3,2,1,0:T(8,128)S(1)} async-done(((f32[8,4,24,512]{3,2,1,0:T(8,128)}), f32[8,4,24,512]{3,2,1,0:T(8,128)S(1)}, u32[]{:S(2)}, u32[]{:S(2)}) %all-to-all-start) | async-done | bytes 1572896 | tf_op jit(solution)/shard_map/all_to_all | solution.py:332
  180.7 0.7 fusion.8
  181.4 0.7 reshape.314
  182.2 3.5 %all-to-all-start.1 = ((f32[8,1,480]{2,1,0:T(1,128)}), f32[8,1,480]{2,1,0:T(1,128)S(1)}, u32[]{:S(2)}, u32[]{:S(2)}) async-start(f32[8,1,480]{2,1,0:T(1,128)} %reshape.314), calls=%async_computation.1 | async-start | bytes 32768 | tf_op jit(solution)/shard_map/all_to_all | solution.py:339
  187.2 0.7 copy.92.within_ref
  187.9 0.7 copy.93.between_ref
  189.2 1.6 all-to-all-done.1
  191.3 0.7 reduce.5
  192.4 0.7 pad.16.emit_ref
  193.1 4.6 %shard_map.142 = (f32[48,5,128]{2,1,0:T(8,128)}, f32[48,1,128]{2,1,0:T(1,128)}) custom-call(f32[5,5,1]{2,1,0:T(8,128)} %copy.92.within_ref, f32[5,5,1]{2,1,0:T(8,128)} %copy.93.between_ref, f32[5,128]{1,0:T(8,128)} %pad.15.start_ref, f32[48,5,128]{2,1,0:T(8,128)} %pad.16.emit_ref, f32[48,1,128]{2,1,0:T(1,128)} %bitcast.69, f32[48,1,128]{2,1,0:T(1,128)} %bitcast.68), custom_call_target="tpu_custom_call" | custom-call | flops 3932160 | bytes 344064 | tf_op jit(solution)/shard_map/pallas_call | solution.py:106
  197.7 0.7 slice.24
  198.5 0.7 slice_reduce_fusion
  199.3 1.5 collective-permute-start.2
  200.8 2.7 %collective-permute-start.3 = (f32[1,4,5,5,4]{3,4,2,1,0:T(4,128)S(1)}, f32[1,4,5,5,4]{3,4,2,1,0:T(4,128)S(1)}, u32[]{:S(2)}, u32[]{:S(2)}) collective-permute-start(f32[1,4,5,5,4]{3,4,2,1,0:T(4,128)S(1)} %get-tuple-element.13), channel_id=1, source_target_pairs={{0,16},{8,24},{16,0},{24,8},{32,48},{40,56},{48,32},{56,40},{64,80... | collective-permute-start | bytes 4808 | tf_op jit(solution)/shard_map/ppermute | solution.py:289
  203.6 1.4 collective-permute-start.4
  205.2 0.8 copy.96
  206.0 1.1 copy.97
  207.9 2.3 collective-permute-start.6
  210.2 1.6 collective-permute-start.7
  211.8 5.2 %collective-permute-done.5 = f32[4,4,5,5,4]{3,4,2,1,0:T(4,128)S(1)} collective-permute-done((f32[4,4,5,5,4]{3,4,2,1,0:T(4,128)S(1)}, f32[4,4,5,5,4]{3,4,2,1,0:T(4,128)S(1)}, u32[]{:S(2)}, u32[]{:S(2)}) %collective-permute-start.5) | collective-permute-done | bytes 6432 | tf_op jit(solution)/shard_map/ppermute | solution.py:289
  217.6 0.9 gather_fusion
  218.6 2.1 copy.95
  220.6 1.3 bitcast_select_fusion.mats_ref
  221.9 0.7 broadcast_in_dim.39.prior_ref
  222.5 5.8 %shard_map.143 = (f32[64,5,4]{2,1,0:T(8,128)}, f32[1,4]{1,0:T(1,128)}) custom-call(f32[5,4]{1,0:T(8,128)} %broadcast_in_dim.39.prior_ref, f32[64,5,5,4]{3,2,1,0:T(8,128)} %bitcast_select_fusion.mats_ref), custom_call_target="tpu_custom_call" | custom-call | tf_op jit(solution)/shard_map/pallas_call | solution.py:127
  228.3 0.7 constant_dynamic-slice_fusion
  229.5 0.7 reshape.294
  230.2 1.1 bitcast_divide_fusion
  (79 shorter events, 6.6 us)
Async XLA Ops:
  7.2 173.5 %copy-start = (f32[512,5]{0,1:T(8,128)S(1)}, f32[512,5]{0,1:T(8,128)}, u32[]{:S(2)}) copy-start(f32[512,5]{0,1:T(8,128)} %param.22) | copy-start | bytes 30724
  7.2 62.1 %all-gather.5.cloned.1.call-start = ((), (), s32[]{:S(2)}) async-start(), calls=%async_computation.2 | async-start | bytes 4352000 | tf_op jit(solution)/shard_map/all_gather | solution.py:326
  7.9 119.5 %all-gather.7.cloned.1.call-start = ((), (), s32[]{:S(2)}) async-start(), calls=%async_computation.3 | async-start | bytes 5570560 | tf_op jit(solution)/shard_map/all_gather | solution.py:327
  40.5 15.3 %collective-permute-start = (bf16[16,4,8,200]{3,2,1,0:T(8,128)(2,1)S(1)}, bf16[16,4,8,200]{3,2,1,0:T(8,128)(2,1)S(1)}, u32[]{:S(2)}, u32[]{:S(2)}) collective-permute-start(bf16[16,4,8,200]{3,2,1,0:T(8,128)(2,1)S(1)} %get-tuple-element.14), channel_id=1, source_target_pairs={{0,8},{8,16},{16,24},{24,32},{32,40},{40,48},{48,56},{56,64},{64,7... | collective-permute-start | bytes 614408 | tf_op jit(solution)/shard_map/ppermute | solution.py:145
  44.1 16.2 %collective-permute-start.1 = (bf16[16,4,8,200]{3,2,1,0:T(8,128)(2,1)S(1)}, bf16[16,4,8,200]{3,2,1,0:T(8,128)(2,1)S(1)}, u32[]{:S(2)}, u32[]{:S(2)}) collective-permute-start(bf16[16,4,8,200]{3,2,1,0:T(8,128)(2,1)S(1)} %get-tuple-element.15), channel_id=1, source_target_pairs={{8,0},{16,8},{24,16},{32,24},{40,32},{48,40},{56,48},{64,56},{72,6... | collective-permute-start | bytes 614408 | tf_op jit(solution)/shard_map/ppermute | solution.py:145
  151.4 7.2 %copy-start.6 = (f32[5]{0:T(128)S(1)}, f32[5]{0:T(128)}, u32[]{:S(2)}) copy-start(f32[5]{0:T(128)} %param.25) | copy-start | bytes 64
  151.4 10.5 %copy-start.1 = (s32[4,192]{1,0:T(4,128)S(1)}, s32[4,192]{1,0:T(4,128)}, u32[]{:S(2)}) copy-start(s32[4,192]{1,0:T(4,128)} %param.17) | copy-start | bytes 9220
  151.5 10.6 %copy-start.4 = (s32[4]{0:T(128)S(1)}, s32[4]{0:T(128)}, u32[]{:S(2)}) copy-start(s32[4]{0:T(128)} %param.16) | copy-start | bytes 52
  151.5 29.2 %copy-start.5 = (f32[512]{0:T(512)S(1)}, f32[512]{0:T(512)}, u32[]{:S(2)}) copy-start(f32[512]{0:T(512)} %param.21) | copy-start | bytes 6148
  151.5 35.7 %copy-start.2 = (f32[5,5]{1,0:T(8,128)S(1)}, f32[5,5]{1,0:T(8,128)}, u32[]{:S(2)}) copy-start(f32[5,5]{1,0:T(8,128)} %param.23) | copy-start | bytes 304
  151.5 36.4 %copy-start.3 = (f32[5,5]{1,0:T(8,128)S(1)}, f32[5,5]{1,0:T(8,128)}, u32[]{:S(2)}) copy-start(f32[5,5]{1,0:T(8,128)} %param.24) | copy-start | bytes 304
  154.3 26.0 %all-to-all-start = ((f32[8,4,24,512]{3,2,1,0:T(8,128)}), f32[8,4,24,512]{3,2,1,0:T(8,128)S(1)}, u32[]{:S(2)}, u32[]{:S(2)}) async-start(f32[8,4,24,512]{3,2,1,0:T(8,128)} %bitcast.52), calls=%async_computation | async-start | bytes 3145728 | tf_op jit(solution)/shard_map/all_to_all | solution.py:332
  182.2 8.6 %all-to-all-start.1 = ((f32[8,1,480]{2,1,0:T(1,128)}), f32[8,1,480]{2,1,0:T(1,128)S(1)}, u32[]{:S(2)}, u32[]{:S(2)}) async-start(f32[8,1,480]{2,1,0:T(1,128)} %reshape.314), calls=%async_computation.1 | async-start | bytes 32768 | tf_op jit(solution)/shard_map/all_to_all | solution.py:339
  199.3 7.7 %collective-permute-start.2 = (f32[1,4,5,5,4]{3,4,2,1,0:T(4,128)S(1)}, f32[1,4,5,5,4]{3,4,2,1,0:T(4,128)S(1)}, u32[]{:S(2)}, u32[]{:S(2)}) collective-permute-start(f32[1,4,5,5,4]{3,4,2,1,0:T(4,128)S(1)} %get-tuple-element.13), channel_id=1, source_target_pairs={{0,8},{8,16},{16,24},{24,0},{32,40},{40,48},{48,56},{56,32},{64,72... | collective-permute-start | bytes 4808 | tf_op jit(solution)/shard_map/ppermute | solution.py:289
  200.8 6.2 %collective-permute-start.3 = (f32[1,4,5,5,4]{3,4,2,1,0:T(4,128)S(1)}, f32[1,4,5,5,4]{3,4,2,1,0:T(4,128)S(1)}, u32[]{:S(2)}, u32[]{:S(2)}) collective-permute-start(f32[1,4,5,5,4]{3,4,2,1,0:T(4,128)S(1)} %get-tuple-element.13), channel_id=1, source_target_pairs={{0,16},{8,24},{16,0},{24,8},{32,48},{40,56},{48,32},{56,40},{64,80... | collective-permute-start | bytes 4808 | tf_op jit(solution)/shard_map/ppermute | solution.py:289
  203.6 4.0 %collective-permute-start.4 = (f32[1,4,5,5,4]{3,4,2,1,0:T(4,128)S(1)}, f32[1,4,5,5,4]{3,4,2,1,0:T(4,128)S(1)}, u32[]{:S(2)}, u32[]{:S(2)}) collective-permute-start(f32[1,4,5,5,4]{3,4,2,1,0:T(4,128)S(1)} %get-tuple-element.13), channel_id=1, source_target_pairs={{0,24},{8,0},{16,8},{24,16},{32,56},{40,32},{48,40},{56,48},{64,88... | collective-permute-start | bytes 4808 | tf_op jit(solution)/shard_map/ppermute | solution.py:289
  207.6 9.4 %collective-permute-start.5 = (f32[4,4,5,5,4]{3,4,2,1,0:T(4,128)S(1)}, f32[4,4,5,5,4]{3,4,2,1,0:T(4,128)S(1)}, u32[]{:S(2)}, u32[]{:S(2)}) collective-permute-start(f32[4,4,5,5,4]{3,4,2,1,0:T(4,128)S(1)} %pad_maximum_fusion.1), channel_id=1, source_target_pairs={{0,32},{8,40},{16,48},{24,56},{32,64},{40,72},{48,80},{56,88},{64,... | collective-permute-start | bytes 19208 | tf_op jit(solution)/shard_map/ppermute | solution.py:289
  207.9 9.1 %collective-permute-start.6 = (f32[4,4,5,5,4]{3,4,2,1,0:T(4,128)S(1)}, f32[4,4,5,5,4]{3,4,2,1,0:T(4,128)S(1)}, u32[]{:S(2)}, u32[]{:S(2)}) collective-permute-start(f32[4,4,5,5,4]{3,4,2,1,0:T(4,128)S(1)} %pad_maximum_fusion.1), channel_id=1, source_target_pairs={{0,64},{8,72},{16,80},{24,88},{32,96},{40,104},{48,112},{56,120},{... | collective-permute-start | bytes 19208 | tf_op jit(solution)/shard_map/ppermute | solution.py:289
  210.2 7.4 %collective-permute-start.7 = (f32[4,4,5,5,4]{3,4,2,1,0:T(4,128)S(1)}, f32[4,4,5,5,4]{3,4,2,1,0:T(4,128)S(1)}, u32[]{:S(2)}, u32[]{:S(2)}) collective-permute-start(f32[4,4,5,5,4]{3,4,2,1,0:T(4,128)S(1)} %pad_maximum_fusion.1), channel_id=1, source_target_pairs={{0,96},{8,104},{16,112},{24,120},{32,0},{40,8},{48,16},{56,24},{64... | collective-permute-start | bytes 19208 | tf_op jit(solution)/shard_map/ppermute | solution.py:289
Sparse Core Ops, SparseCore 0:
  10.2 59.0 all-gather.4
  71.4 55.9 all-gather.6

commit v17 on v16

--- a/solution.py
+++ b/solution.py
@@ -192,7 +192,8 @@
         out_ref[...] = jnp.zeros_like(out_ref)
 
     span = rows_ref.shape[2]
-    recordings, patches = out_ref.shape[:2]
+    chunks, recordings, piece = out_ref.shape[:3]
+    patches = chunks * piece
     margin = (span - patches) // 2
     value = merged(rows_ref)
     layers = taps_ref.shape[0]
@@ -202,8 +203,9 @@
             value = jnp.where(keep_ref[...] > 0.5, value, jnp.zeros((), jnp.bfloat16))
     mixed = jnp.dot(value, mix_ref[0], preferred_element_type=jnp.float32)
     for item in range(recordings):
-        start = item * span + margin
-        out_ref[item] += mixed[start : start + patches]
+        for chunk in range(chunks):
+            start = item * span + margin + chunk * piece
+            out_ref[chunk, item] += mixed[start : start + piece]
 
 
 def edge_keep(span, margin, rec_index, patches, recordings):
@@ -253,6 +255,7 @@
         lambda m: (m, 0, 0, 0), 2 * types * recordings * span * width * EMB * taps,
     )
     mix_width = mix.shape[-1]
+    spread = lax.axis_size("chan")
     return pl.pallas_call(
         last_kernel,
         grid=(types,),
@@ -262,8 +265,8 @@
             pl.BlockSpec(keep.shape, lambda m: (0, 0)),
             pl.BlockSpec((1,) + mix.shape[1:], lambda m: (m, 0, 0)),
         ],
-        out_specs=pl.BlockSpec((recordings, patches, mix_width), lambda m: (0, 0, 0)),
-        out_shape=jax.ShapeDtypeStruct((recordings, patches, mix_width), jnp.float32),
+        out_specs=pl.BlockSpec((spread, recordings, patches // spread, mix_width), lambda m: (0, 0, 0, 0)),
+        out_shape=jax.ShapeDtypeStruct((spread, recordings, patches // spread, mix_width), jnp.float32),
         compiler_params=pltpu.CompilerParams(dimension_semantics=("arbitrary",)),
         cost_estimate=pl.CostEstimate(
             flops=2 * types * recordings * span * EMB * (layers * EMB * taps + mix_width),
@@ -328,8 +331,7 @@
     extended = halo_rows(patch_rows, HALO)
     partial_value = conv_mix(extended, first_taps, hidden_taps, mix_weight[:, 0], rec_index, patches)
     spread = lax.axis_size("chan")
-    pieces = partial_value.reshape(recordings, spread, patches // spread, partial_value.shape[-1])
-    pieces = lax.all_to_all(jnp.swapaxes(pieces, 0, 1), "chan", 0, 0, tiled=True)
+    pieces = lax.all_to_all(partial_value, "chan", 0, 0, tiled=True)
     summed = jnp.sum(pieces, axis=0)
     average = jnp.mean(summed, axis=-1, keepdims=True)
     centred = summed - average

time: 239 us -> 237 us (level)
  local copies, waits for them, and re-layouts: 45.8 us -> 43 us
    reshape x1 -> x0, local copies, waits for them, and re-layouts: 2.77 us -> none  [local(): partial_value.reshape(recordings, spread, patches // spread, partial_valu...]
where the time goes in v17:
time: 237 us; the launch traced here: 236 us
  waiting for transfers between devices  84.5 us (36%)
  Pallas kernels  51.9 us (22%)
  local copies, waits for them, and re-layouts  43 us (18%)
  starting transfers between devices  22.8 us (10%)
  between operations  15.8 us (7%)
  other arithmetic  13.1 us (6%)
  matrix products  4.54 us (2%)
    all_gather x1, waiting for transfers between devices, local(): lax.all_gather(jnp.swapaxes(conv_hid[:, 0], 0, 1), 'rec', axis=1, tiled=T...  39.7 us
    pallas_call x1, Pallas kernels, conv_mix(): pl.pallas_call(last_kernel, grid=(types,), in_specs=[pl.BlockSpec((1,) +...  24.1 us
    reshape x1, local copies, waits for them, and re-layouts, local(): patch_rows = rows.reshape(groups, recordings, patches, SAMP)  20.3 us
    all_to_all x1, waiting for transfers between devices, local(): pieces = lax.all_to_all(partial_value, 'chan', 0, 0, tiled=True)  18.2 us
    pallas_call x1, Pallas kernels, per_type_call(): pl.pallas_call(kernel, grid=(types,), in_specs=[pl.BlockSpec((1,) + rows....  17.5 us
    ppermute x2, waiting for transfers between devices, neighbour_shift(): return lax.ppermute(block, axis, route)  14.8 us
    ppermute x6, starting transfers between devices, shifted(): return lax.ppermute(values, 'rec', route)  9.99 us
    concatenate x1, other arithmetic, halo_rows(): return jnp.concatenate([from_left, patch_rows, from_right], axis=2)  6.4 us
  transfers between devices with their start and end apart: 12, of which 9 were waited for; matrix products, arithmetic and copies ran while one was open for 20% of the time, Pallas kernels for 7%

profile of v17, /device:TPU:0, one launch (start us, length us, event | category | flops | bytes accessed | tf_op | source)
XLA Modules:
  0.0 235.7 jit_solution(15241125148036455507)
XLA Ops:
  7.2 0.7 all-gather.5.cloned.1.call-update
  8.0 0.7 all-gather.7.cloned.1.call-update
  8.7 0.7 broadcast_compare_fusion
  9.4 3.8 %fusion = bf16[16,4,38400]{2,0,1:T(8,128)(2,1)S(1)} fusion(bf16[4,16,38400]{2,1,0:T(8,128)(2,1)} %param.13, s32[4,16]{1,0:T(4,128)} %bitcast.61, pred[4,16]{1,0:T(4,128)(4,1)S(1)} %broadcast_compare_fusion), kind=kOutput, calls=%fused_computation.2 | convolution fusion | flops 81102848 | bytes 9830720 | tf_op jit(solution)/shard_map/bms,bst->mbt/dot_general | solution.py:325
  13.2 6.0 %copy.81 = bf16[16,4,38400]{2,1,0:T(4,128)(2,1)} copy(bf16[16,4,38400]{2,0,1:T(8,128)(2,1)S(1)} %fusion) | data formatting | bytes 9830400 | tf_op jit(solution)/shard_map/convert_element_type | solution.py:327
  19.2 20.3 %reshape.284 = bf16[16,4,192,200]{3,2,1,0:T(8,128)(2,1)} reshape(bf16[16,4,38400]{2,1,0:T(4,128)(2,1)} %copy.81) | data formatting | bytes 9830400 | tf_op jit(solution)/shard_map/reshape | solution.py:328
  39.5 1.1 fusion.44
  40.5 3.6 %collective-permute-start = (bf16[16,4,8,200]{3,2,1,0:T(8,128)(2,1)S(1)}, bf16[16,4,8,200]{3,2,1,0:T(8,128)(2,1)S(1)}, u32[]{:S(2)}, u32[]{:S(2)}) collective-permute-start(bf16[16,4,8,200]{3,2,1,0:T(8,128)(2,1)S(1)} %get-tuple-element.14), channel_id=1, source_target_pairs={{0,8},{8,16},{16,24},{24,32},{32,40},{40,48},{48,56},{56,64},{64,7... | collective-permute-start | bytes 614408 | tf_op jit(solution)/shard_map/ppermute | solution.py:145
  44.1 1.3 collective-permute-start.1
  45.5 10.3 %collective-permute-done = bf16[16,4,8,200]{3,2,1,0:T(8,128)(2,1)S(1)} collective-permute-done((bf16[16,4,8,200]{3,2,1,0:T(8,128)(2,1)S(1)}, bf16[16,4,8,200]{3,2,1,0:T(8,128)(2,1)S(1)}, u32[]{:S(2)}, u32[]{:S(2)}) %collective-permute-start) | collective-permute-done | bytes 204832 | tf_op jit(solution)/shard_map/ppermute | solution.py:145
  55.8 4.5 %collective-permute-done.1 = bf16[16,4,8,200]{3,2,1,0:T(8,128)(2,1)S(1)} collective-permute-done((bf16[16,4,8,200]{3,2,1,0:T(8,128)(2,1)S(1)}, bf16[16,4,8,200]{3,2,1,0:T(8,128)(2,1)S(1)}, u32[]{:S(2)}, u32[]{:S(2)}) %collective-permute-start.1) | collective-permute-done | bytes 204832 | tf_op jit(solution)/shard_map/ppermute | solution.py:145
  60.3 6.4 %pad_maximum_fusion.rows_ref = bf16[16,4,208,200]{3,2,1,0:T(8,128)(2,1)} fusion(bf16[16,4,8,200]{3,2,1,0:T(8,128)(2,1)S(1)} %collective-permute-done.1, bf16[16,4,192,200]{3,2,1,0:T(8,128)(2,1)} %reshape.284, bf16[16,4,8,200]{3,2,1,0:T(8,128)(2,1)S(1)} %collective-permute-done), kind=kLoop, calls=%fused_computation.3 | loop fusion | flops 15974400 | bytes 10649600 | tf_op jit(solution)/shard_map/concatenate | solution.py:152
  66.7 2.6 %all-gather.5.cloned.1.call-done = bf16[16,1,5,200,128]{4,3,2,1,0:T(8,128)(2,1)} async-done(((bf16[1,1,5,200,128]{4,3,2,1,0:T(8,128)(2,1)}), bf16[16,1,5,200,128]{4,3,2,1,0:T(8,128)(2,1)}) %all-gather.5.cloned.1.call-update) | async-done | bytes 4096016 | tf_op jit(solution)/shard_map/all_gather | solution.py:329
  69.3 0.9 tile.13.keep_ref
  70.2 17.5 %shard_map.140.rows_ref = bf16[16,4,208,128]{3,2,1,0:T(8,128)(2,1)} custom-call(bf16[16,4,208,200]{3,2,1,0:T(8,128)(2,1)} %pad_maximum_fusion.rows_ref, bf16[16,5,200,128]{3,2,1,0:T(8,128)(2,1)} %bitcast.51, f32[832,128]{1,0:T(8,128)} %tile.13.keep_ref), custom_call_target="tpu_custom_call" | custom-call | flops 3407872000 | bytes 16449536 | tf_op jit(solution)/shard_map/pallas_call | solution.py:225
  87.7 39.7 %all-gather.7.cloned.1.call-done = bf16[1,1,2,80,128,128]{5,4,3,2,1,0:T(8,128)(2,1)} async-done(((bf16[1,1,2,5,128,128]{5,4,3,2,1,0:T(8,128)(2,1)}), bf16[1,1,2,80,128,128]{5,4,3,2,1,0:T(8,128)(2,1)}) %all-gather.7.cloned.1.call-update) | async-done | bytes 5242896 | tf_op jit(solution)/shard_map/all_gather | solution.py:330
  127.4 24.1 %shard_map.141 = f32[8,4,24,512]{3,2,1,0:T(8,128)} custom-call(bf16[16,4,208,128]{3,2,1,0:T(8,128)(2,1)} %shard_map.140.rows_ref, bf16[2,16,5,128,128]{4,3,2,1,0:T(8,128)(2,1)} %bitcast.68, f32[832,128]{1,0:T(8,128)} %tile.13.keep_ref, bf16[16,128,512]{2,1,0:T(8,128)(2,1)} %bitcast.69), custom_call_target="tpu_custom_call" | custom-call | flops 6106906624 | bytes 12320768 | tf_op jit(solution)/shard_map/pallas_call | solution.py:259
  151.5 4.6 %all-to-all-start = ((f32[8,4,24,512]{3,2,1,0:T(8,128)}), f32[8,4,24,512]{3,2,1,0:T(8,128)S(1)}, u32[]{:S(2)}, u32[]{:S(2)}) async-start(f32[8,4,24,512]{3,2,1,0:T(8,128)} %shard_map.141), calls=%async_computation | async-start | bytes 3145728 | tf_op jit(solution)/shard_map/all_to_all | solution.py:334
  156.7 1.2 exponential_reduce_fusion.2
  159.5 18.2 %all-to-all-done = f32[8,4,24,512]{3,2,1,0:T(8,128)S(1)} async-done(((f32[8,4,24,512]{3,2,1,0:T(8,128)}), f32[8,4,24,512]{3,2,1,0:T(8,128)S(1)}, u32[]{:S(2)}, u32[]{:S(2)}) %all-to-all-start) | async-done | bytes 1572896 | tf_op jit(solution)/shard_map/all_to_all | solution.py:334
  178.1 0.7 fusion.8
  178.8 0.7 reshape.310
  179.6 3.3 %all-to-all-start.1 = ((f32[8,1,480]{2,1,0:T(1,128)}), f32[8,1,480]{2,1,0:T(1,128)S(1)}, u32[]{:S(2)}, u32[]{:S(2)}) async-start(f32[8,1,480]{2,1,0:T(1,128)} %reshape.310), calls=%async_computation.1 | async-start | bytes 32768 | tf_op jit(solution)/shard_map/all_to_all | solution.py:341
  183.2 0.6 pad.18
  184.4 0.7 copy.89.within_ref
  185.1 0.7 copy.90.between_ref
  186.4 1.7 all-to-all-done.1
  188.7 0.7 reduce.5
  189.8 0.7 pad.16.emit_ref
  190.5 4.6 %shard_map.142 = (f32[48,5,128]{2,1,0:T(8,128)}, f32[48,1,128]{2,1,0:T(1,128)}) custom-call(f32[5,5,1]{2,1,0:T(8,128)} %copy.89.within_ref, f32[5,5,1]{2,1,0:T(8,128)} %copy.90.between_ref, f32[5,128]{1,0:T(8,128)} %pad.15.start_ref, f32[48,5,128]{2,1,0:T(8,128)} %pad.16.emit_ref, f32[48,1,128]{2,1,0:T(1,128)} %bitcast.64, f32[48,1,128]{2,1,0:T(1,128)} %bitcast.63), custom_call_target="tpu_custom_call" | custom-call | flops 3932160 | bytes 344064 | tf_op jit(solution)/shard_map/pallas_call | solution.py:106
  195.1 0.7 slice.24
  195.8 0.7 slice_reduce_fusion
  196.7 1.7 collective-permute-start.2
  198.4 2.7 %collective-permute-start.3 = (f32[1,4,5,5,4]{3,4,2,1,0:T(4,128)S(1)}, f32[1,4,5,5,4]{3,4,2,1,0:T(4,128)S(1)}, u32[]{:S(2)}, u32[]{:S(2)}) collective-permute-start(f32[1,4,5,5,4]{3,4,2,1,0:T(4,128)S(1)} %get-tuple-element.13), channel_id=1, source_target_pairs={{0,16},{8,24},{16,0},{24,8},{32,48},{40,56},{48,32},{56,40},{64,80... | collective-permute-start | bytes 4808 | tf_op jit(solution)/shard_map/ppermute | solution.py:292
  201.1 1.4 collective-permute-start.4
  202.7 0.8 copy.93
  203.6 1.1 copy.94
  205.5 2.3 collective-permute-start.6
  207.7 1.6 collective-permute-start.7
  209.4 5.2 %collective-permute-done.5 = f32[4,4,5,5,4]{3,4,2,1,0:T(4,128)S(1)} collective-permute-done((f32[4,4,5,5,4]{3,4,2,1,0:T(4,128)S(1)}, f32[4,4,5,5,4]{3,4,2,1,0:T(4,128)S(1)}, u32[]{:S(2)}, u32[]{:S(2)}) %collective-permute-start.5) | collective-permute-done | bytes 6432 | tf_op jit(solution)/shard_map/ppermute | solution.py:292
  215.2 0.9 gather_fusion
  216.1 2.1 copy.92
  218.2 1.3 bitcast_select_fusion.mats_ref
  219.5 0.7 broadcast_in_dim.39.prior_ref
  220.1 5.8 %shard_map.143 = (f32[64,5,4]{2,1,0:T(8,128)}, f32[1,4]{1,0:T(1,128)}) custom-call(f32[5,4]{1,0:T(8,128)} %broadcast_in_dim.39.prior_ref, f32[64,5,5,4]{3,2,1,0:T(8,128)} %bitcast_select_fusion.mats_ref), custom_call_target="tpu_custom_call" | custom-call | tf_op jit(solution)/shard_map/pallas_call | solution.py:127
  225.9 0.7 constant_dynamic-slice_fusion
  227.0 0.7 reshape.290
  227.7 1.1 bitcast_divide_fusion
  (78 shorter events, 6.0 us)
Async XLA Ops:
  7.2 170.9 %copy-start = (f32[512,5]{0,1:T(8,128)S(1)}, f32[512,5]{0,1:T(8,128)}, u32[]{:S(2)}) copy-start(f32[512,5]{0,1:T(8,128)} %param.22) | copy-start | bytes 30724
  7.2 62.1 %all-gather.5.cloned.1.call-start = ((), (), s32[]{:S(2)}) async-start(), calls=%async_computation.2 | async-start | bytes 4352000 | tf_op jit(solution)/shard_map/all_gather | solution.py:329
  7.9 119.5 %all-gather.7.cloned.1.call-start = ((), (), s32[]{:S(2)}) async-start(), calls=%async_computation.3 | async-start | bytes 5570560 | tf_op jit(solution)/shard_map/all_gather | solution.py:330
  40.5 15.3 %collective-permute-start = (bf16[16,4,8,200]{3,2,1,0:T(8,128)(2,1)S(1)}, bf16[16,4,8,200]{3,2,1,0:T(8,128)(2,1)S(1)}, u32[]{:S(2)}, u32[]{:S(2)}) collective-permute-start(bf16[16,4,8,200]{3,2,1,0:T(8,128)(2,1)S(1)} %get-tuple-element.14), channel_id=1, source_target_pairs={{0,8},{8,16},{16,24},{24,32},{32,40},{40,48},{48,56},{56,64},{64,7... | collective-permute-start | bytes 614408 | tf_op jit(solution)/shard_map/ppermute | solution.py:145
  44.1 16.2 %collective-permute-start.1 = (bf16[16,4,8,200]{3,2,1,0:T(8,128)(2,1)S(1)}, bf16[16,4,8,200]{3,2,1,0:T(8,128)(2,1)S(1)}, u32[]{:S(2)}, u32[]{:S(2)}) collective-permute-start(bf16[16,4,8,200]{3,2,1,0:T(8,128)(2,1)S(1)} %get-tuple-element.15), channel_id=1, source_target_pairs={{8,0},{16,8},{24,16},{32,24},{40,32},{48,40},{56,48},{64,56},{72,6... | collective-permute-start | bytes 614408 | tf_op jit(solution)/shard_map/ppermute | solution.py:145
  127.4 28.6 %copy-start.6 = (f32[5]{0:T(128)S(1)}, f32[5]{0:T(128)}, u32[]{:S(2)}) copy-start(f32[5]{0:T(128)} %param.25) | copy-start | bytes 64
  127.4 31.9 %copy-start.1 = (s32[4,192]{1,0:T(4,128)S(1)}, s32[4,192]{1,0:T(4,128)}, u32[]{:S(2)}) copy-start(s32[4,192]{1,0:T(4,128)} %param.17) | copy-start | bytes 9220
  127.4 32.0 %copy-start.4 = (s32[4]{0:T(128)S(1)}, s32[4]{0:T(128)}, u32[]{:S(2)}) copy-start(s32[4]{0:T(128)} %param.16) | copy-start | bytes 52
  151.5 26.6 %copy-start.5 = (f32[512]{0:T(512)S(1)}, f32[512]{0:T(512)}, u32[]{:S(2)}) copy-start(f32[512]{0:T(512)} %param.21) | copy-start | bytes 6148
  151.5 32.9 %copy-start.2 = (f32[5,5]{1,0:T(8,128)S(1)}, f32[5,5]{1,0:T(8,128)}, u32[]{:S(2)}) copy-start(f32[5,5]{1,0:T(8,128)} %param.23) | copy-start | bytes 304
  151.5 33.6 %copy-start.3 = (f32[5,5]{1,0:T(8,128)S(1)}, f32[5,5]{1,0:T(8,128)}, u32[]{:S(2)}) copy-start(f32[5,5]{1,0:T(8,128)} %param.24) | copy-start | bytes 304
  151.5 26.2 %all-to-all-start = ((f32[8,4,24,512]{3,2,1,0:T(8,128)}), f32[8,4,24,512]{3,2,1,0:T(8,128)S(1)}, u32[]{:S(2)}, u32[]{:S(2)}) async-start(f32[8,4,24,512]{3,2,1,0:T(8,128)} %shard_map.141), calls=%async_computation | async-start | bytes 3145728 | tf_op jit(solution)/shard_map/all_to_all | solution.py:334
  179.6 8.6 %all-to-all-start.1 = ((f32[8,1,480]{2,1,0:T(1,128)}), f32[8,1,480]{2,1,0:T(1,128)S(1)}, u32[]{:S(2)}, u32[]{:S(2)}) async-start(f32[8,1,480]{2,1,0:T(1,128)} %reshape.310), calls=%async_computation.1 | async-start | bytes 32768 | tf_op jit(solution)/shard_map/all_to_all | solution.py:341
  196.7 7.9 %collective-permute-start.2 = (f32[1,4,5,5,4]{3,4,2,1,0:T(4,128)S(1)}, f32[1,4,5,5,4]{3,4,2,1,0:T(4,128)S(1)}, u32[]{:S(2)}, u32[]{:S(2)}) collective-permute-start(f32[1,4,5,5,4]{3,4,2,1,0:T(4,128)S(1)} %get-tuple-element.13), channel_id=1, source_target_pairs={{0,8},{8,16},{16,24},{24,0},{32,40},{40,48},{48,56},{56,32},{64,72... | collective-permute-start | bytes 4808 | tf_op jit(solution)/shard_map/ppermute | solution.py:292
  198.4 6.2 %collective-permute-start.3 = (f32[1,4,5,5,4]{3,4,2,1,0:T(4,128)S(1)}, f32[1,4,5,5,4]{3,4,2,1,0:T(4,128)S(1)}, u32[]{:S(2)}, u32[]{:S(2)}) collective-permute-start(f32[1,4,5,5,4]{3,4,2,1,0:T(4,128)S(1)} %get-tuple-element.13), channel_id=1, source_target_pairs={{0,16},{8,24},{16,0},{24,8},{32,48},{40,56},{48,32},{56,40},{64,80... | collective-permute-start | bytes 4808 | tf_op jit(solution)/shard_map/ppermute | solution.py:292
  201.1 4.0 %collective-permute-start.4 = (f32[1,4,5,5,4]{3,4,2,1,0:T(4,128)S(1)}, f32[1,4,5,5,4]{3,4,2,1,0:T(4,128)S(1)}, u32[]{:S(2)}, u32[]{:S(2)}) collective-permute-start(f32[1,4,5,5,4]{3,4,2,1,0:T(4,128)S(1)} %get-tuple-element.13), channel_id=1, source_target_pairs={{0,24},{8,0},{16,8},{24,16},{32,56},{40,32},{48,40},{56,48},{64,88... | collective-permute-start | bytes 4808 | tf_op jit(solution)/shard_map/ppermute | solution.py:292
  205.2 9.4 %collective-permute-start.5 = (f32[4,4,5,5,4]{3,4,2,1,0:T(4,128)S(1)}, f32[4,4,5,5,4]{3,4,2,1,0:T(4,128)S(1)}, u32[]{:S(2)}, u32[]{:S(2)}) collective-permute-start(f32[4,4,5,5,4]{3,4,2,1,0:T(4,128)S(1)} %pad_maximum_fusion.1), channel_id=1, source_target_pairs={{0,32},{8,40},{16,48},{24,56},{32,64},{40,72},{48,80},{56,88},{64,... | collective-permute-start | bytes 19208 | tf_op jit(solution)/shard_map/ppermute | solution.py:292
  205.5 9.1 %collective-permute-start.6 = (f32[4,4,5,5,4]{3,4,2,1,0:T(4,128)S(1)}, f32[4,4,5,5,4]{3,4,2,1,0:T(4,128)S(1)}, u32[]{:S(2)}, u32[]{:S(2)}) collective-permute-start(f32[4,4,5,5,4]{3,4,2,1,0:T(4,128)S(1)} %pad_maximum_fusion.1), channel_id=1, source_target_pairs={{0,64},{8,72},{16,80},{24,88},{32,96},{40,104},{48,112},{56,120},{... | collective-permute-start | bytes 19208 | tf_op jit(solution)/shard_map/ppermute | solution.py:292
  207.7 7.4 %collective-permute-start.7 = (f32[4,4,5,5,4]{3,4,2,1,0:T(4,128)S(1)}, f32[4,4,5,5,4]{3,4,2,1,0:T(4,128)S(1)}, u32[]{:S(2)}, u32[]{:S(2)}) collective-permute-start(f32[4,4,5,5,4]{3,4,2,1,0:T(4,128)S(1)} %pad_maximum_fusion.1), channel_id=1, source_target_pairs={{0,96},{8,104},{16,112},{24,120},{32,0},{40,8},{48,16},{56,24},{64... | collective-permute-start | bytes 19208 | tf_op jit(solution)/shard_map/ppermute | solution.py:292
Sparse Core Ops, SparseCore 0:
  10.2 59.0 all-gather.4
  71.4 55.9 all-gather.6

commit v18 on v17

--- a/solution.py
+++ b/solution.py
@@ -72,7 +72,7 @@
         moved, level = forward_step(state, matrices, None)
         return moved, total + level
 
-    _, total = lax.fori_loop(0, count, body, (prior_ref[...], jnp.zeros((1, prior_ref.shape[1]), jnp.float32)))
+    _, total = lax.fori_loop(0, count, body, (prior_ref[...], jnp.zeros((1, prior_ref.shape[1]), jnp.float32)), unroll=8)
     total_ref[...] = total
 
 

time: 237 us -> 237 us (level)
  no operation moved by 1% of the time
where the time goes in v18:
time: 237 us; the launch traced here: 236 us
  waiting for transfers between devices  84.5 us (36%)
  Pallas kernels  51.8 us (22%)
  local copies, waits for them, and re-layouts  43 us (18%)
  starting transfers between devices  22.8 us (10%)
  between operations  15.8 us (7%)
  other arithmetic  13.1 us (6%)
  matrix products  4.54 us (2%)
    all_gather x1, waiting for transfers between devices, local(): lax.all_gather(jnp.swapaxes(conv_hid[:, 0], 0, 1), 'rec', axis=1, tiled=T...  39.7 us
    pallas_call x1, Pallas kernels, conv_mix(): pl.pallas_call(last_kernel, grid=(types,), in_specs=[pl.BlockSpec((1,) +...  24.1 us
    reshape x1, local copies, waits for them, and re-layouts, local(): patch_rows = rows.reshape(groups, recordings, patches, SAMP)  20.3 us
    all_to_all x1, waiting for transfers between devices, local(): pieces = lax.all_to_all(partial_value, 'chan', 0, 0, tiled=True)  18.2 us
    pallas_call x1, Pallas kernels, per_type_call(): pl.pallas_call(kernel, grid=(types,), in_specs=[pl.BlockSpec((1,) + rows....  17.5 us
    ppermute x2, waiting for transfers between devices, neighbour_shift(): return lax.ppermute(block, axis, route)  14.8 us
    ppermute x6, starting transfers between devices, shifted(): return lax.ppermute(values, 'rec', route)  9.99 us
    concatenate x1, other arithmetic, halo_rows(): return jnp.concatenate([from_left, patch_rows, from_right], axis=2)  6.4 us
  transfers between devices with their start and end apart: 12, of which 9 were waited for; matrix products, arithmetic and copies ran while one was open for 20% of the time, Pallas kernels for 7%

profile of v18, /device:TPU:0, one launch (start us, length us, event | category | flops | bytes accessed | tf_op | source)
XLA Modules:
  0.0 235.6 jit_solution(18265033757603092696)
XLA Ops:
  7.2 0.7 all-gather.5.cloned.1.call-update
  8.0 0.7 all-gather.7.cloned.1.call-update
  8.7 0.7 broadcast_compare_fusion
  9.4 3.8 %fusion = bf16[16,4,38400]{2,0,1:T(8,128)(2,1)S(1)} fusion(bf16[4,16,38400]{2,1,0:T(8,128)(2,1)} %param.13, s32[4,16]{1,0:T(4,128)} %bitcast.61, pred[4,16]{1,0:T(4,128)(4,1)S(1)} %broadcast_compare_fusion), kind=kOutput, calls=%fused_computation.2 | convolution fusion | flops 81102848 | bytes 9830720 | tf_op jit(solution)/shard_map/bms,bst->mbt/dot_general | solution.py:325
  13.2 6.0 %copy.81 = bf16[16,4,38400]{2,1,0:T(4,128)(2,1)} copy(bf16[16,4,38400]{2,0,1:T(8,128)(2,1)S(1)} %fusion) | data formatting | bytes 9830400 | tf_op jit(solution)/shard_map/convert_element_type | solution.py:327
  19.2 20.3 %reshape.284 = bf16[16,4,192,200]{3,2,1,0:T(8,128)(2,1)} reshape(bf16[16,4,38400]{2,1,0:T(4,128)(2,1)} %copy.81) | data formatting | bytes 9830400 | tf_op jit(solution)/shard_map/reshape | solution.py:328
  39.5 1.1 fusion.44
  40.5 3.6 %collective-permute-start = (bf16[16,4,8,200]{3,2,1,0:T(8,128)(2,1)S(1)}, bf16[16,4,8,200]{3,2,1,0:T(8,128)(2,1)S(1)}, u32[]{:S(2)}, u32[]{:S(2)}) collective-permute-start(bf16[16,4,8,200]{3,2,1,0:T(8,128)(2,1)S(1)} %get-tuple-element.14), channel_id=1, source_target_pairs={{0,8},{8,16},{16,24},{24,32},{32,40},{40,48},{48,56},{56,64},{64,7... | collective-permute-start | bytes 614408 | tf_op jit(solution)/shard_map/ppermute | solution.py:145
  44.1 1.3 collective-permute-start.1
  45.5 10.3 %collective-permute-done = bf16[16,4,8,200]{3,2,1,0:T(8,128)(2,1)S(1)} collective-permute-done((bf16[16,4,8,200]{3,2,1,0:T(8,128)(2,1)S(1)}, bf16[16,4,8,200]{3,2,1,0:T(8,128)(2,1)S(1)}, u32[]{:S(2)}, u32[]{:S(2)}) %collective-permute-start) | collective-permute-done | bytes 204832 | tf_op jit(solution)/shard_map/ppermute | solution.py:145
  55.8 4.5 %collective-permute-done.1 = bf16[16,4,8,200]{3,2,1,0:T(8,128)(2,1)S(1)} collective-permute-done((bf16[16,4,8,200]{3,2,1,0:T(8,128)(2,1)S(1)}, bf16[16,4,8,200]{3,2,1,0:T(8,128)(2,1)S(1)}, u32[]{:S(2)}, u32[]{:S(2)}) %collective-permute-start.1) | collective-permute-done | bytes 204832 | tf_op jit(solution)/shard_map/ppermute | solution.py:145
  60.3 6.4 %pad_maximum_fusion.rows_ref = bf16[16,4,208,200]{3,2,1,0:T(8,128)(2,1)} fusion(bf16[16,4,8,200]{3,2,1,0:T(8,128)(2,1)S(1)} %collective-permute-done.1, bf16[16,4,192,200]{3,2,1,0:T(8,128)(2,1)} %reshape.284, bf16[16,4,8,200]{3,2,1,0:T(8,128)(2,1)S(1)} %collective-permute-done), kind=kLoop, calls=%fused_computation.3 | loop fusion | flops 15974400 | bytes 10649600 | tf_op jit(solution)/shard_map/concatenate | solution.py:152
  66.7 2.6 %all-gather.5.cloned.1.call-done = bf16[16,1,5,200,128]{4,3,2,1,0:T(8,128)(2,1)} async-done(((bf16[1,1,5,200,128]{4,3,2,1,0:T(8,128)(2,1)}), bf16[16,1,5,200,128]{4,3,2,1,0:T(8,128)(2,1)}) %all-gather.5.cloned.1.call-update) | async-done | bytes 4096016 | tf_op jit(solution)/shard_map/all_gather | solution.py:329
  69.3 0.9 tile.13.keep_ref
  70.2 17.5 %shard_map.140.rows_ref = bf16[16,4,208,128]{3,2,1,0:T(8,128)(2,1)} custom-call(bf16[16,4,208,200]{3,2,1,0:T(8,128)(2,1)} %pad_maximum_fusion.rows_ref, bf16[16,5,200,128]{3,2,1,0:T(8,128)(2,1)} %bitcast.51, f32[832,128]{1,0:T(8,128)} %tile.13.keep_ref), custom_call_target="tpu_custom_call" | custom-call | flops 3407872000 | bytes 16449536 | tf_op jit(solution)/shard_map/pallas_call | solution.py:225
  87.7 39.7 %all-gather.7.cloned.1.call-done = bf16[1,1,2,80,128,128]{5,4,3,2,1,0:T(8,128)(2,1)} async-done(((bf16[1,1,2,5,128,128]{5,4,3,2,1,0:T(8,128)(2,1)}), bf16[1,1,2,80,128,128]{5,4,3,2,1,0:T(8,128)(2,1)}) %all-gather.7.cloned.1.call-update) | async-done | bytes 5242896 | tf_op jit(solution)/shard_map/all_gather | solution.py:330
  127.4 24.1 %shard_map.141 = f32[8,4,24,512]{3,2,1,0:T(8,128)} custom-call(bf16[16,4,208,128]{3,2,1,0:T(8,128)(2,1)} %shard_map.140.rows_ref, bf16[2,16,5,128,128]{4,3,2,1,0:T(8,128)(2,1)} %bitcast.68, f32[832,128]{1,0:T(8,128)} %tile.13.keep_ref, bf16[16,128,512]{2,1,0:T(8,128)(2,1)} %bitcast.69), custom_call_target="tpu_custom_call" | custom-call | flops 6106906624 | bytes 12320768 | tf_op jit(solution)/shard_map/pallas_call | solution.py:259
  151.5 4.6 %all-to-all-start = ((f32[8,4,24,512]{3,2,1,0:T(8,128)}), f32[8,4,24,512]{3,2,1,0:T(8,128)S(1)}, u32[]{:S(2)}, u32[]{:S(2)}) async-start(f32[8,4,24,512]{3,2,1,0:T(8,128)} %shard_map.141), calls=%async_computation | async-start | bytes 3145728 | tf_op jit(solution)/shard_map/all_to_all | solution.py:334
  156.7 1.2 exponential_reduce_fusion.2
  159.5 18.2 %all-to-all-done = f32[8,4,24,512]{3,2,1,0:T(8,128)S(1)} async-done(((f32[8,4,24,512]{3,2,1,0:T(8,128)}), f32[8,4,24,512]{3,2,1,0:T(8,128)S(1)}, u32[]{:S(2)}, u32[]{:S(2)}) %all-to-all-start) | async-done | bytes 1572896 | tf_op jit(solution)/shard_map/all_to_all | solution.py:334
  178.1 0.7 fusion.8
  178.8 0.7 reshape.310
  179.6 3.3 %all-to-all-start.1 = ((f32[8,1,480]{2,1,0:T(1,128)}), f32[8,1,480]{2,1,0:T(1,128)S(1)}, u32[]{:S(2)}, u32[]{:S(2)}) async-start(f32[8,1,480]{2,1,0:T(1,128)} %reshape.310), calls=%async_computation.1 | async-start | bytes 32768 | tf_op jit(solution)/shard_map/all_to_all | solution.py:341
  183.2 0.6 pad.18
  184.4 0.7 copy.89.within_ref
  185.1 0.7 copy.90.between_ref
  186.4 1.7 all-to-all-done.1
  188.7 0.7 reduce.5
  189.8 0.7 pad.16.emit_ref
  190.5 4.6 %shard_map.142 = (f32[48,5,128]{2,1,0:T(8,128)}, f32[48,1,128]{2,1,0:T(1,128)}) custom-call(f32[5,5,1]{2,1,0:T(8,128)} %copy.89.within_ref, f32[5,5,1]{2,1,0:T(8,128)} %copy.90.between_ref, f32[5,128]{1,0:T(8,128)} %pad.15.start_ref, f32[48,5,128]{2,1,0:T(8,128)} %pad.16.emit_ref, f32[48,1,128]{2,1,0:T(1,128)} %bitcast.64, f32[48,1,128]{2,1,0:T(1,128)} %bitcast.63), custom_call_target="tpu_custom_call" | custom-call | flops 3932160 | bytes 344064 | tf_op jit(solution)/shard_map/pallas_call | solution.py:106
  195.1 0.7 slice.24
  195.8 0.7 slice_reduce_fusion
  196.7 1.7 collective-permute-start.2
  198.4 2.7 %collective-permute-start.3 = (f32[1,4,5,5,4]{3,4,2,1,0:T(4,128)S(1)}, f32[1,4,5,5,4]{3,4,2,1,0:T(4,128)S(1)}, u32[]{:S(2)}, u32[]{:S(2)}) collective-permute-start(f32[1,4,5,5,4]{3,4,2,1,0:T(4,128)S(1)} %get-tuple-element.13), channel_id=1, source_target_pairs={{0,16},{8,24},{16,0},{24,8},{32,48},{40,56},{48,32},{56,40},{64,80... | collective-permute-start | bytes 4808 | tf_op jit(solution)/shard_map/ppermute | solution.py:292
  201.1 1.4 collective-permute-start.4
  202.7 0.8 copy.93
  203.6 1.1 copy.94
  205.5 2.3 collective-permute-start.6
  207.7 1.6 collective-permute-start.7
  209.4 5.2 %collective-permute-done.5 = f32[4,4,5,5,4]{3,4,2,1,0:T(4,128)S(1)} collective-permute-done((f32[4,4,5,5,4]{3,4,2,1,0:T(4,128)S(1)}, f32[4,4,5,5,4]{3,4,2,1,0:T(4,128)S(1)}, u32[]{:S(2)}, u32[]{:S(2)}) %collective-permute-start.5) | collective-permute-done | bytes 6432 | tf_op jit(solution)/shard_map/ppermute | solution.py:292
  215.2 0.9 gather_fusion
  216.1 2.1 copy.92
  218.2 1.3 bitcast_select_fusion.mats_ref
  219.5 0.7 broadcast_in_dim.39.prior_ref
  220.1 5.7 %shard_map.143 = (f32[64,5,4]{2,1,0:T(8,128)}, f32[1,4]{1,0:T(1,128)}) custom-call(f32[5,4]{1,0:T(8,128)} %broadcast_in_dim.39.prior_ref, f32[64,5,5,4]{3,2,1,0:T(8,128)} %bitcast_select_fusion.mats_ref), custom_call_target="tpu_custom_call" | custom-call | tf_op jit(solution)/shard_map/pallas_call | solution.py:127
  225.8 0.7 constant_dynamic-slice_fusion
  227.0 0.7 reshape.290
  227.7 1.1 bitcast_divide_fusion
  (78 shorter events, 6.0 us)
Async XLA Ops:
  7.2 170.9 %copy-start = (f32[512,5]{0,1:T(8,128)S(1)}, f32[512,5]{0,1:T(8,128)}, u32[]{:S(2)}) copy-start(f32[512,5]{0,1:T(8,128)} %param.22) | copy-start | bytes 30724
  7.2 62.1 %all-gather.5.cloned.1.call-start = ((), (), s32[]{:S(2)}) async-start(), calls=%async_computation.2 | async-start | bytes 4352000 | tf_op jit(solution)/shard_map/all_gather | solution.py:329
  7.9 119.5 %all-gather.7.cloned.1.call-start = ((), (), s32[]{:S(2)}) async-start(), calls=%async_computation.3 | async-start | bytes 5570560 | tf_op jit(solution)/shard_map/all_gather | solution.py:330
  40.5 15.3 %collective-permute-start = (bf16[16,4,8,200]{3,2,1,0:T(8,128)(2,1)S(1)}, bf16[16,4,8,200]{3,2,1,0:T(8,128)(2,1)S(1)}, u32[]{:S(2)}, u32[]{:S(2)}) collective-permute-start(bf16[16,4,8,200]{3,2,1,0:T(8,128)(2,1)S(1)} %get-tuple-element.14), channel_id=1, source_target_pairs={{0,8},{8,16},{16,24},{24,32},{32,40},{40,48},{48,56},{56,64},{64,7... | collective-permute-start | bytes 614408 | tf_op jit(solution)/shard_map/ppermute | solution.py:145
  44.1 16.2 %collective-permute-start.1 = (bf16[16,4,8,200]{3,2,1,0:T(8,128)(2,1)S(1)}, bf16[16,4,8,200]{3,2,1,0:T(8,128)(2,1)S(1)}, u32[]{:S(2)}, u32[]{:S(2)}) collective-permute-start(bf16[16,4,8,200]{3,2,1,0:T(8,128)(2,1)S(1)} %get-tuple-element.15), channel_id=1, source_target_pairs={{8,0},{16,8},{24,16},{32,24},{40,32},{48,40},{56,48},{64,56},{72,6... | collective-permute-start | bytes 614408 | tf_op jit(solution)/shard_map/ppermute | solution.py:145
  127.4 28.6 %copy-start.6 = (f32[5]{0:T(128)S(1)}, f32[5]{0:T(128)}, u32[]{:S(2)}) copy-start(f32[5]{0:T(128)} %param.25) | copy-start | bytes 64
  127.4 31.9 %copy-start.1 = (s32[4,192]{1,0:T(4,128)S(1)}, s32[4,192]{1,0:T(4,128)}, u32[]{:S(2)}) copy-start(s32[4,192]{1,0:T(4,128)} %param.17) | copy-start | bytes 9220
  127.4 32.0 %copy-start.4 = (s32[4]{0:T(128)S(1)}, s32[4]{0:T(128)}, u32[]{:S(2)}) copy-start(s32[4]{0:T(128)} %param.16) | copy-start | bytes 52
  151.5 26.6 %copy-start.5 = (f32[512]{0:T(512)S(1)}, f32[512]{0:T(512)}, u32[]{:S(2)}) copy-start(f32[512]{0:T(512)} %param.21) | copy-start | bytes 6148
  151.5 32.9 %copy-start.2 = (f32[5,5]{1,0:T(8,128)S(1)}, f32[5,5]{1,0:T(8,128)}, u32[]{:S(2)}) copy-start(f32[5,5]{1,0:T(8,128)} %param.23) | copy-start | bytes 304
  151.5 33.6 %copy-start.3 = (f32[5,5]{1,0:T(8,128)S(1)}, f32[5,5]{1,0:T(8,128)}, u32[]{:S(2)}) copy-start(f32[5,5]{1,0:T(8,128)} %param.24) | copy-start | bytes 304
  151.5 26.2 %all-to-all-start = ((f32[8,4,24,512]{3,2,1,0:T(8,128)}), f32[8,4,24,512]{3,2,1,0:T(8,128)S(1)}, u32[]{:S(2)}, u32[]{:S(2)}) async-start(f32[8,4,24,512]{3,2,1,0:T(8,128)} %shard_map.141), calls=%async_computation | async-start | bytes 3145728 | tf_op jit(solution)/shard_map/all_to_all | solution.py:334
  179.6 8.6 %all-to-all-start.1 = ((f32[8,1,480]{2,1,0:T(1,128)}), f32[8,1,480]{2,1,0:T(1,128)S(1)}, u32[]{:S(2)}, u32[]{:S(2)}) async-start(f32[8,1,480]{2,1,0:T(1,128)} %reshape.310), calls=%async_computation.1 | async-start | bytes 32768 | tf_op jit(solution)/shard_map/all_to_all | solution.py:341
  196.7 7.9 %collective-permute-start.2 = (f32[1,4,5,5,4]{3,4,2,1,0:T(4,128)S(1)}, f32[1,4,5,5,4]{3,4,2,1,0:T(4,128)S(1)}, u32[]{:S(2)}, u32[]{:S(2)}) collective-permute-start(f32[1,4,5,5,4]{3,4,2,1,0:T(4,128)S(1)} %get-tuple-element.13), channel_id=1, source_target_pairs={{0,8},{8,16},{16,24},{24,0},{32,40},{40,48},{48,56},{56,32},{64,72... | collective-permute-start | bytes 4808 | tf_op jit(solution)/shard_map/ppermute | solution.py:292
  198.4 6.2 %collective-permute-start.3 = (f32[1,4,5,5,4]{3,4,2,1,0:T(4,128)S(1)}, f32[1,4,5,5,4]{3,4,2,1,0:T(4,128)S(1)}, u32[]{:S(2)}, u32[]{:S(2)}) collective-permute-start(f32[1,4,5,5,4]{3,4,2,1,0:T(4,128)S(1)} %get-tuple-element.13), channel_id=1, source_target_pairs={{0,16},{8,24},{16,0},{24,8},{32,48},{40,56},{48,32},{56,40},{64,80... | collective-permute-start | bytes 4808 | tf_op jit(solution)/shard_map/ppermute | solution.py:292
  201.1 4.0 %collective-permute-start.4 = (f32[1,4,5,5,4]{3,4,2,1,0:T(4,128)S(1)}, f32[1,4,5,5,4]{3,4,2,1,0:T(4,128)S(1)}, u32[]{:S(2)}, u32[]{:S(2)}) collective-permute-start(f32[1,4,5,5,4]{3,4,2,1,0:T(4,128)S(1)} %get-tuple-element.13), channel_id=1, source_target_pairs={{0,24},{8,0},{16,8},{24,16},{32,56},{40,32},{48,40},{56,48},{64,88... | collective-permute-start | bytes 4808 | tf_op jit(solution)/shard_map/ppermute | solution.py:292
  205.2 9.4 %collective-permute-start.5 = (f32[4,4,5,5,4]{3,4,2,1,0:T(4,128)S(1)}, f32[4,4,5,5,4]{3,4,2,1,0:T(4,128)S(1)}, u32[]{:S(2)}, u32[]{:S(2)}) collective-permute-start(f32[4,4,5,5,4]{3,4,2,1,0:T(4,128)S(1)} %pad_maximum_fusion.1), channel_id=1, source_target_pairs={{0,32},{8,40},{16,48},{24,56},{32,64},{40,72},{48,80},{56,88},{64,... | collective-permute-start | bytes 19208 | tf_op jit(solution)/shard_map/ppermute | solution.py:292
  205.5 9.1 %collective-permute-start.6 = (f32[4,4,5,5,4]{3,4,2,1,0:T(4,128)S(1)}, f32[4,4,5,5,4]{3,4,2,1,0:T(4,128)S(1)}, u32[]{:S(2)}, u32[]{:S(2)}) collective-permute-start(f32[4,4,5,5,4]{3,4,2,1,0:T(4,128)S(1)} %pad_maximum_fusion.1), channel_id=1, source_target_pairs={{0,64},{8,72},{16,80},{24,88},{32,96},{40,104},{48,112},{56,120},{... | collective-permute-start | bytes 19208 | tf_op jit(solution)/shard_map/ppermute | solution.py:292
  207.7 7.4 %collective-permute-start.7 = (f32[4,4,5,5,4]{3,4,2,1,0:T(4,128)S(1)}, f32[4,4,5,5,4]{3,4,2,1,0:T(4,128)S(1)}, u32[]{:S(2)}, u32[]{:S(2)}) collective-permute-start(f32[4,4,5,5,4]{3,4,2,1,0:T(4,128)S(1)} %pad_maximum_fusion.1), channel_id=1, source_target_pairs={{0,96},{8,104},{16,112},{24,120},{32,0},{40,8},{48,16},{56,24},{64... | collective-permute-start | bytes 19208 | tf_op jit(solution)/shard_map/ppermute | solution.py:292
Sparse Core Ops, SparseCore 0:
  10.2 59.0 all-gather.4
  71.4 55.9 all-gather.6

commit v19 on v18

--- a/solution.py
+++ b/solution.py
@@ -59,7 +59,7 @@
         offset_ref[p] = offset
         return state, offset
 
-    lax.fori_loop(0, patches, body, (start_ref[...], jnp.zeros((1, LANES), jnp.float32)), unroll=8)
+    lax.fori_loop(0, patches, body, (start_ref[...], jnp.zeros((1, LANES), jnp.float32)), unroll=True)
 
 
 def chain_kernel(prior_ref, mats_ref, incoming_ref, total_ref):

time: 237 us -> 237 us (level)
  no operation moved by 1% of the time
where the time goes in v19:
time: 237 us; the launch traced here: 235 us
  waiting for transfers between devices  84.4 us (36%)
  Pallas kernels  51.8 us (22%)
  local copies, waits for them, and re-layouts  43 us (18%)
  starting transfers between devices  22.8 us (10%)
  between operations  15.8 us (7%)
  other arithmetic  13.1 us (6%)
  matrix products  4.54 us (2%)
    all_gather x1, waiting for transfers between devices, local(): lax.all_gather(jnp.swapaxes(conv_hid[:, 0], 0, 1), 'rec', axis=1, tiled=T...  39.7 us
    pallas_call x1, Pallas kernels, conv_mix(): pl.pallas_call(last_kernel, grid=(types,), in_specs=[pl.BlockSpec((1,) +...  24.1 us
    reshape x1, local copies, waits for them, and re-layouts, local(): patch_rows = rows.reshape(groups, recordings, patches, SAMP)  20.3 us
    all_to_all x1, waiting for transfers between devices, local(): pieces = lax.all_to_all(partial_value, 'chan', 0, 0, tiled=True)  18.2 us
    pallas_call x1, Pallas kernels, per_type_call(): pl.pallas_call(kernel, grid=(types,), in_specs=[pl.BlockSpec((1,) + rows....  17.5 us
    ppermute x2, waiting for transfers between devices, neighbour_shift(): return lax.ppermute(block, axis, route)  14.8 us
    ppermute x6, starting transfers between devices, shifted(): return lax.ppermute(values, 'rec', route)  9.81 us
    concatenate x1, other arithmetic, halo_rows(): return jnp.concatenate([from_left, patch_rows, from_right], axis=2)  6.4 us
  transfers between devices with their start and end apart: 12, of which 9 were waited for; matrix products, arithmetic and copies ran while one was open for 20% of the time, Pallas kernels for 7%

profile of v19, /device:TPU:0, one launch (start us, length us, event | category | flops | bytes accessed | tf_op | source)
XLA Modules:
  0.0 235.5 jit_solution(4689106442809303866)
XLA Ops:
  7.2 0.7 all-gather.5.cloned.1.call-update
  8.0 0.7 all-gather.7.cloned.1.call-update
  8.7 0.7 broadcast_compare_fusion
  9.4 3.8 %fusion = bf16[16,4,38400]{2,0,1:T(8,128)(2,1)S(1)} fusion(bf16[4,16,38400]{2,1,0:T(8,128)(2,1)} %param.13, s32[4,16]{1,0:T(4,128)} %bitcast.61, pred[4,16]{1,0:T(4,128)(4,1)S(1)} %broadcast_compare_fusion), kind=kOutput, calls=%fused_computation.2 | convolution fusion | flops 81102848 | bytes 9830720 | tf_op jit(solution)/shard_map/bms,bst->mbt/dot_general | solution.py:325
  13.2 6.0 %copy.81 = bf16[16,4,38400]{2,1,0:T(4,128)(2,1)} copy(bf16[16,4,38400]{2,0,1:T(8,128)(2,1)S(1)} %fusion) | data formatting | bytes 9830400 | tf_op jit(solution)/shard_map/convert_element_type | solution.py:327
  19.2 20.3 %reshape.284 = bf16[16,4,192,200]{3,2,1,0:T(8,128)(2,1)} reshape(bf16[16,4,38400]{2,1,0:T(4,128)(2,1)} %copy.81) | data formatting | bytes 9830400 | tf_op jit(solution)/shard_map/reshape | solution.py:328
  39.5 1.1 fusion.44
  40.5 3.6 %collective-permute-start = (bf16[16,4,8,200]{3,2,1,0:T(8,128)(2,1)S(1)}, bf16[16,4,8,200]{3,2,1,0:T(8,128)(2,1)S(1)}, u32[]{:S(2)}, u32[]{:S(2)}) collective-permute-start(bf16[16,4,8,200]{3,2,1,0:T(8,128)(2,1)S(1)} %get-tuple-element.14), channel_id=1, source_target_pairs={{0,8},{8,16},{16,24},{24,32},{32,40},{40,48},{48,56},{56,64},{64,7... | collective-permute-start | bytes 614408 | tf_op jit(solution)/shard_map/ppermute | solution.py:145
  44.1 1.3 collective-permute-start.1
  45.5 10.3 %collective-permute-done = bf16[16,4,8,200]{3,2,1,0:T(8,128)(2,1)S(1)} collective-permute-done((bf16[16,4,8,200]{3,2,1,0:T(8,128)(2,1)S(1)}, bf16[16,4,8,200]{3,2,1,0:T(8,128)(2,1)S(1)}, u32[]{:S(2)}, u32[]{:S(2)}) %collective-permute-start) | collective-permute-done | bytes 204832 | tf_op jit(solution)/shard_map/ppermute | solution.py:145
  55.8 4.5 %collective-permute-done.1 = bf16[16,4,8,200]{3,2,1,0:T(8,128)(2,1)S(1)} collective-permute-done((bf16[16,4,8,200]{3,2,1,0:T(8,128)(2,1)S(1)}, bf16[16,4,8,200]{3,2,1,0:T(8,128)(2,1)S(1)}, u32[]{:S(2)}, u32[]{:S(2)}) %collective-permute-start.1) | collective-permute-done | bytes 204832 | tf_op jit(solution)/shard_map/ppermute | solution.py:145
  60.3 6.4 %pad_maximum_fusion.rows_ref = bf16[16,4,208,200]{3,2,1,0:T(8,128)(2,1)} fusion(bf16[16,4,8,200]{3,2,1,0:T(8,128)(2,1)S(1)} %collective-permute-done.1, bf16[16,4,192,200]{3,2,1,0:T(8,128)(2,1)} %reshape.284, bf16[16,4,8,200]{3,2,1,0:T(8,128)(2,1)S(1)} %collective-permute-done), kind=kLoop, calls=%fused_computation.3 | loop fusion | flops 15974400 | bytes 10649600 | tf_op jit(solution)/shard_map/concatenate | solution.py:152
  66.7 2.6 %all-gather.5.cloned.1.call-done = bf16[16,1,5,200,128]{4,3,2,1,0:T(8,128)(2,1)} async-done(((bf16[1,1,5,200,128]{4,3,2,1,0:T(8,128)(2,1)}), bf16[16,1,5,200,128]{4,3,2,1,0:T(8,128)(2,1)}) %all-gather.5.cloned.1.call-update) | async-done | bytes 4096016 | tf_op jit(solution)/shard_map/all_gather | solution.py:329
  69.3 0.9 tile.13.keep_ref
  70.2 17.5 %shard_map.140.rows_ref = bf16[16,4,208,128]{3,2,1,0:T(8,128)(2,1)} custom-call(bf16[16,4,208,200]{3,2,1,0:T(8,128)(2,1)} %pad_maximum_fusion.rows_ref, bf16[16,5,200,128]{3,2,1,0:T(8,128)(2,1)} %bitcast.51, f32[832,128]{1,0:T(8,128)} %tile.13.keep_ref), custom_call_target="tpu_custom_call" | custom-call | flops 3407872000 | bytes 16449536 | tf_op jit(solution)/shard_map/pallas_call | solution.py:225
  87.7 39.7 %all-gather.7.cloned.1.call-done = bf16[1,1,2,80,128,128]{5,4,3,2,1,0:T(8,128)(2,1)} async-done(((bf16[1,1,2,5,128,128]{5,4,3,2,1,0:T(8,128)(2,1)}), bf16[1,1,2,80,128,128]{5,4,3,2,1,0:T(8,128)(2,1)}) %all-gather.7.cloned.1.call-update) | async-done | bytes 5242896 | tf_op jit(solution)/shard_map/all_gather | solution.py:330
  127.4 24.1 %shard_map.141 = f32[8,4,24,512]{3,2,1,0:T(8,128)} custom-call(bf16[16,4,208,128]{3,2,1,0:T(8,128)(2,1)} %shard_map.140.rows_ref, bf16[2,16,5,128,128]{4,3,2,1,0:T(8,128)(2,1)} %bitcast.68, f32[832,128]{1,0:T(8,128)} %tile.13.keep_ref, bf16[16,128,512]{2,1,0:T(8,128)(2,1)} %bitcast.69), custom_call_target="tpu_custom_call" | custom-call | flops 6106906624 | bytes 12320768 | tf_op jit(solution)/shard_map/pallas_call | solution.py:259
  151.5 4.6 %all-to-all-start = ((f32[8,4,24,512]{3,2,1,0:T(8,128)}), f32[8,4,24,512]{3,2,1,0:T(8,128)S(1)}, u32[]{:S(2)}, u32[]{:S(2)}) async-start(f32[8,4,24,512]{3,2,1,0:T(8,128)} %shard_map.141), calls=%async_computation | async-start | bytes 3145728 | tf_op jit(solution)/shard_map/all_to_all | solution.py:334
  156.7 1.2 exponential_reduce_fusion.2
  159.5 18.2 %all-to-all-done = f32[8,4,24,512]{3,2,1,0:T(8,128)S(1)} async-done(((f32[8,4,24,512]{3,2,1,0:T(8,128)}), f32[8,4,24,512]{3,2,1,0:T(8,128)S(1)}, u32[]{:S(2)}, u32[]{:S(2)}) %all-to-all-start) | async-done | bytes 1572896 | tf_op jit(solution)/shard_map/all_to_all | solution.py:334
  178.1 0.7 fusion.8
  178.8 0.7 reshape.310
  179.6 3.5 %all-to-all-start.1 = ((f32[8,1,480]{2,1,0:T(1,128)}), f32[8,1,480]{2,1,0:T(1,128)S(1)}, u32[]{:S(2)}, u32[]{:S(2)}) async-start(f32[8,1,480]{2,1,0:T(1,128)} %reshape.310), calls=%async_computation.1 | async-start | bytes 32768 | tf_op jit(solution)/shard_map/all_to_all | solution.py:341
  183.3 0.6 pad.18
  184.6 0.7 copy.89.within_ref
  185.3 0.7 copy.90.between_ref
  186.6 1.6 all-to-all-done.1
  188.7 0.7 reduce.5
  189.8 0.7 pad.16.emit_ref
  190.5 4.6 %shard_map.142 = (f32[48,5,128]{2,1,0:T(8,128)}, f32[48,1,128]{2,1,0:T(1,128)}) custom-call(f32[5,5,1]{2,1,0:T(8,128)} %copy.89.within_ref, f32[5,5,1]{2,1,0:T(8,128)} %copy.90.between_ref, f32[5,128]{1,0:T(8,128)} %pad.15.start_ref, f32[48,5,128]{2,1,0:T(8,128)} %pad.16.emit_ref, f32[48,1,128]{2,1,0:T(1,128)} %bitcast.64, f32[48,1,128]{2,1,0:T(1,128)} %bitcast.63), custom_call_target="tpu_custom_call" | custom-call | flops 3932160 | bytes 344064 | tf_op jit(solution)/shard_map/pallas_call | solution.py:106
  195.1 0.7 slice.24
  195.8 0.7 slice_reduce_fusion
  196.7 1.5 collective-permute-start.2
  198.2 2.7 %collective-permute-start.3 = (f32[1,4,5,5,4]{3,4,2,1,0:T(4,128)S(1)}, f32[1,4,5,5,4]{3,4,2,1,0:T(4,128)S(1)}, u32[]{:S(2)}, u32[]{:S(2)}) collective-permute-start(f32[1,4,5,5,4]{3,4,2,1,0:T(4,128)S(1)} %get-tuple-element.13), channel_id=1, source_target_pairs={{0,16},{8,24},{16,0},{24,8},{32,48},{40,56},{48,32},{56,40},{64,80... | collective-permute-start | bytes 4808 | tf_op jit(solution)/shard_map/ppermute | solution.py:292
  200.9 1.4 collective-permute-start.4
  202.6 0.8 copy.93
  203.4 1.1 copy.94
  205.3 2.3 collective-permute-start.6
  207.6 1.6 collective-permute-start.7
  209.2 5.2 %collective-permute-done.5 = f32[4,4,5,5,4]{3,4,2,1,0:T(4,128)S(1)} collective-permute-done((f32[4,4,5,5,4]{3,4,2,1,0:T(4,128)S(1)}, f32[4,4,5,5,4]{3,4,2,1,0:T(4,128)S(1)}, u32[]{:S(2)}, u32[]{:S(2)}) %collective-permute-start.5) | collective-permute-done | bytes 6432 | tf_op jit(solution)/shard_map/ppermute | solution.py:292
  215.0 0.9 gather_fusion
  215.9 2.1 copy.92
  218.0 1.3 bitcast_select_fusion.mats_ref
  219.3 0.7 broadcast_in_dim.39.prior_ref
  219.9 5.7 %shard_map.143 = (f32[64,5,4]{2,1,0:T(8,128)}, f32[1,4]{1,0:T(1,128)}) custom-call(f32[5,4]{1,0:T(8,128)} %broadcast_in_dim.39.prior_ref, f32[64,5,5,4]{3,2,1,0:T(8,128)} %bitcast_select_fusion.mats_ref), custom_call_target="tpu_custom_call" | custom-call | tf_op jit(solution)/shard_map/pallas_call | solution.py:127
  225.6 0.7 constant_dynamic-slice_fusion
  226.8 0.7 reshape.290
  227.5 1.1 bitcast_divide_fusion
  (78 shorter events, 6.0 us)
Async XLA Ops:
  7.2 170.9 %copy-start = (f32[512,5]{0,1:T(8,128)S(1)}, f32[512,5]{0,1:T(8,128)}, u32[]{:S(2)}) copy-start(f32[512,5]{0,1:T(8,128)} %param.22) | copy-start | bytes 30724
  7.2 62.1 %all-gather.5.cloned.1.call-start = ((), (), s32[]{:S(2)}) async-start(), calls=%async_computation.2 | async-start | bytes 4352000 | tf_op jit(solution)/shard_map/all_gather | solution.py:329
  7.9 119.5 %all-gather.7.cloned.1.call-start = ((), (), s32[]{:S(2)}) async-start(), calls=%async_computation.3 | async-start | bytes 5570560 | tf_op jit(solution)/shard_map/all_gather | solution.py:330
  40.5 15.3 %collective-permute-start = (bf16[16,4,8,200]{3,2,1,0:T(8,128)(2,1)S(1)}, bf16[16,4,8,200]{3,2,1,0:T(8,128)(2,1)S(1)}, u32[]{:S(2)}, u32[]{:S(2)}) collective-permute-start(bf16[16,4,8,200]{3,2,1,0:T(8,128)(2,1)S(1)} %get-tuple-element.14), channel_id=1, source_target_pairs={{0,8},{8,16},{16,24},{24,32},{32,40},{40,48},{48,56},{56,64},{64,7... | collective-permute-start | bytes 614408 | tf_op jit(solution)/shard_map/ppermute | solution.py:145
  44.1 16.2 %collective-permute-start.1 = (bf16[16,4,8,200]{3,2,1,0:T(8,128)(2,1)S(1)}, bf16[16,4,8,200]{3,2,1,0:T(8,128)(2,1)S(1)}, u32[]{:S(2)}, u32[]{:S(2)}) collective-permute-start(bf16[16,4,8,200]{3,2,1,0:T(8,128)(2,1)S(1)} %get-tuple-element.15), channel_id=1, source_target_pairs={{8,0},{16,8},{24,16},{32,24},{40,32},{48,40},{56,48},{64,56},{72,6... | collective-permute-start | bytes 614408 | tf_op jit(solution)/shard_map/ppermute | solution.py:145
  127.4 28.6 %copy-start.6 = (f32[5]{0:T(128)S(1)}, f32[5]{0:T(128)}, u32[]{:S(2)}) copy-start(f32[5]{0:T(128)} %param.25) | copy-start | bytes 64
  127.4 31.9 %copy-start.1 = (s32[4,192]{1,0:T(4,128)S(1)}, s32[4,192]{1,0:T(4,128)}, u32[]{:S(2)}) copy-start(s32[4,192]{1,0:T(4,128)} %param.17) | copy-start | bytes 9220
  127.4 32.0 %copy-start.4 = (s32[4]{0:T(128)S(1)}, s32[4]{0:T(128)}, u32[]{:S(2)}) copy-start(s32[4]{0:T(128)} %param.16) | copy-start | bytes 52
  151.5 26.6 %copy-start.5 = (f32[512]{0:T(512)S(1)}, f32[512]{0:T(512)}, u32[]{:S(2)}) copy-start(f32[512]{0:T(512)} %param.21) | copy-start | bytes 6148
  151.5 33.1 %copy-start.2 = (f32[5,5]{1,0:T(8,128)S(1)}, f32[5,5]{1,0:T(8,128)}, u32[]{:S(2)}) copy-start(f32[5,5]{1,0:T(8,128)} %param.23) | copy-start | bytes 304
  151.5 33.8 %copy-start.3 = (f32[5,5]{1,0:T(8,128)S(1)}, f32[5,5]{1,0:T(8,128)}, u32[]{:S(2)}) copy-start(f32[5,5]{1,0:T(8,128)} %param.24) | copy-start | bytes 304
  151.5 26.2 %all-to-all-start = ((f32[8,4,24,512]{3,2,1,0:T(8,128)}), f32[8,4,24,512]{3,2,1,0:T(8,128)S(1)}, u32[]{:S(2)}, u32[]{:S(2)}) async-start(f32[8,4,24,512]{3,2,1,0:T(8,128)} %shard_map.141), calls=%async_computation | async-start | bytes 3145728 | tf_op jit(solution)/shard_map/all_to_all | solution.py:334
  179.6 8.6 %all-to-all-start.1 = ((f32[8,1,480]{2,1,0:T(1,128)}), f32[8,1,480]{2,1,0:T(1,128)S(1)}, u32[]{:S(2)}, u32[]{:S(2)}) async-start(f32[8,1,480]{2,1,0:T(1,128)} %reshape.310), calls=%async_computation.1 | async-start | bytes 32768 | tf_op jit(solution)/shard_map/all_to_all | solution.py:341
  196.7 7.7 %collective-permute-start.2 = (f32[1,4,5,5,4]{3,4,2,1,0:T(4,128)S(1)}, f32[1,4,5,5,4]{3,4,2,1,0:T(4,128)S(1)}, u32[]{:S(2)}, u32[]{:S(2)}) collective-permute-start(f32[1,4,5,5,4]{3,4,2,1,0:T(4,128)S(1)} %get-tuple-element.13), channel_id=1, source_target_pairs={{0,8},{8,16},{16,24},{24,0},{32,40},{40,48},{48,56},{56,32},{64,72... | collective-permute-start | bytes 4808 | tf_op jit(solution)/shard_map/ppermute | solution.py:292
  198.2 6.2 %collective-permute-start.3 = (f32[1,4,5,5,4]{3,4,2,1,0:T(4,128)S(1)}, f32[1,4,5,5,4]{3,4,2,1,0:T(4,128)S(1)}, u32[]{:S(2)}, u32[]{:S(2)}) collective-permute-start(f32[1,4,5,5,4]{3,4,2,1,0:T(4,128)S(1)} %get-tuple-element.13), channel_id=1, source_target_pairs={{0,16},{8,24},{16,0},{24,8},{32,48},{40,56},{48,32},{56,40},{64,80... | collective-permute-start | bytes 4808 | tf_op jit(solution)/shard_map/ppermute | solution.py:292
  200.9 4.0 %collective-permute-start.4 = (f32[1,4,5,5,4]{3,4,2,1,0:T(4,128)S(1)}, f32[1,4,5,5,4]{3,4,2,1,0:T(4,128)S(1)}, u32[]{:S(2)}, u32[]{:S(2)}) collective-permute-start(f32[1,4,5,5,4]{3,4,2,1,0:T(4,128)S(1)} %get-tuple-element.13), channel_id=1, source_target_pairs={{0,24},{8,0},{16,8},{24,16},{32,56},{40,32},{48,40},{56,48},{64,88... | collective-permute-start | bytes 4808 | tf_op jit(solution)/shard_map/ppermute | solution.py:292
  205.0 9.4 %collective-permute-start.5 = (f32[4,4,5,5,4]{3,4,2,1,0:T(4,128)S(1)}, f32[4,4,5,5,4]{3,4,2,1,0:T(4,128)S(1)}, u32[]{:S(2)}, u32[]{:S(2)}) collective-permute-start(f32[4,4,5,5,4]{3,4,2,1,0:T(4,128)S(1)} %pad_maximum_fusion.1), channel_id=1, source_target_pairs={{0,32},{8,40},{16,48},{24,56},{32,64},{40,72},{48,80},{56,88},{64,... | collective-permute-start | bytes 19208 | tf_op jit(solution)/shard_map/ppermute | solution.py:292
  205.3 9.1 %collective-permute-start.6 = (f32[4,4,5,5,4]{3,4,2,1,0:T(4,128)S(1)}, f32[4,4,5,5,4]{3,4,2,1,0:T(4,128)S(1)}, u32[]{:S(2)}, u32[]{:S(2)}) collective-permute-start(f32[4,4,5,5,4]{3,4,2,1,0:T(4,128)S(1)} %pad_maximum_fusion.1), channel_id=1, source_target_pairs={{0,64},{8,72},{16,80},{24,88},{32,96},{40,104},{48,112},{56,120},{... | collective-permute-start | bytes 19208 | tf_op jit(solution)/shard_map/ppermute | solution.py:292
  207.6 7.4 %collective-permute-start.7 = (f32[4,4,5,5,4]{3,4,2,1,0:T(4,128)S(1)}, f32[4,4,5,5,4]{3,4,2,1,0:T(4,128)S(1)}, u32[]{:S(2)}, u32[]{:S(2)}) collective-permute-start(f32[4,4,5,5,4]{3,4,2,1,0:T(4,128)S(1)} %pad_maximum_fusion.1), channel_id=1, source_target_pairs={{0,96},{8,104},{16,112},{24,120},{32,0},{40,8},{48,16},{56,24},{64... | collective-permute-start | bytes 19208 | tf_op jit(solution)/shard_map/ppermute | solution.py:292
Sparse Core Ops, SparseCore 0:
  10.2 59.0 all-gather.4
  71.4 55.9 all-gather.6

commit v20 on v19

--- a/solution.py
+++ b/solution.py
@@ -72,7 +72,7 @@
         moved, level = forward_step(state, matrices, None)
         return moved, total + level
 
-    _, total = lax.fori_loop(0, count, body, (prior_ref[...], jnp.zeros((1, prior_ref.shape[1]), jnp.float32)), unroll=8)
+    _, total = lax.fori_loop(0, count, body, (prior_ref[...], jnp.zeros((1, prior_ref.shape[1]), jnp.float32)), unroll=True)
     total_ref[...] = total
 
 

time: 237 us -> 237 us (level)
  no operation moved by 1% of the time
where the time goes in v20:
time: 237 us; the launch traced here: 235 us
  waiting for transfers between devices  84.4 us (36%)
  Pallas kernels  51.8 us (22%)
  local copies, waits for them, and re-layouts  43 us (18%)
  starting transfers between devices  22.8 us (10%)
  between operations  15.8 us (7%)
  other arithmetic  13.1 us (6%)
  matrix products  4.54 us (2%)
    all_gather x1, waiting for transfers between devices, local(): lax.all_gather(jnp.swapaxes(conv_hid[:, 0], 0, 1), 'rec', axis=1, tiled=T...  39.7 us
    pallas_call x1, Pallas kernels, conv_mix(): pl.pallas_call(last_kernel, grid=(types,), in_specs=[pl.BlockSpec((1,) +...  24.1 us
    reshape x1, local copies, waits for them, and re-layouts, local(): patch_rows = rows.reshape(groups, recordings, patches, SAMP)  20.3 us
    all_to_all x1, waiting for transfers between devices, local(): pieces = lax.all_to_all(partial_value, 'chan', 0, 0, tiled=True)  18.2 us
    pallas_call x1, Pallas kernels, per_type_call(): pl.pallas_call(kernel, grid=(types,), in_specs=[pl.BlockSpec((1,) + rows....  17.5 us
    ppermute x2, waiting for transfers between devices, neighbour_shift(): return lax.ppermute(block, axis, route)  14.8 us
    ppermute x6, starting transfers between devices, shifted(): return lax.ppermute(values, 'rec', route)  9.81 us
    concatenate x1, other arithmetic, halo_rows(): return jnp.concatenate([from_left, patch_rows, from_right], axis=2)  6.4 us
  transfers between devices with their start and end apart: 12, of which 9 were waited for; matrix products, arithmetic and copies ran while one was open for 20% of the time, Pallas kernels for 7%

profile of v20, /device:TPU:0, one launch (start us, length us, event | category | flops | bytes accessed | tf_op | source)
XLA Modules:
  0.0 235.5 jit_solution(17955967814688967365)
XLA Ops:
  7.2 0.7 all-gather.5.cloned.1.call-update
  8.0 0.7 all-gather.7.cloned.1.call-update
  8.7 0.7 broadcast_compare_fusion
  9.4 3.8 %fusion = bf16[16,4,38400]{2,0,1:T(8,128)(2,1)S(1)} fusion(bf16[4,16,38400]{2,1,0:T(8,128)(2,1)} %param.13, s32[4,16]{1,0:T(4,128)} %bitcast.61, pred[4,16]{1,0:T(4,128)(4,1)S(1)} %broadcast_compare_fusion), kind=kOutput, calls=%fused_computation.2 | convolution fusion | flops 81102848 | bytes 9830720 | tf_op jit(solution)/shard_map/bms,bst->mbt/dot_general | solution.py:325
  13.2 6.0 %copy.81 = bf16[16,4,38400]{2,1,0:T(4,128)(2,1)} copy(bf16[16,4,38400]{2,0,1:T(8,128)(2,1)S(1)} %fusion) | data formatting | bytes 9830400 | tf_op jit(solution)/shard_map/convert_element_type | solution.py:327
  19.2 20.3 %reshape.284 = bf16[16,4,192,200]{3,2,1,0:T(8,128)(2,1)} reshape(bf16[16,4,38400]{2,1,0:T(4,128)(2,1)} %copy.81) | data formatting | bytes 9830400 | tf_op jit(solution)/shard_map/reshape | solution.py:328
  39.5 1.1 fusion.44
  40.5 3.6 %collective-permute-start = (bf16[16,4,8,200]{3,2,1,0:T(8,128)(2,1)S(1)}, bf16[16,4,8,200]{3,2,1,0:T(8,128)(2,1)S(1)}, u32[]{:S(2)}, u32[]{:S(2)}) collective-permute-start(bf16[16,4,8,200]{3,2,1,0:T(8,128)(2,1)S(1)} %get-tuple-element.14), channel_id=1, source_target_pairs={{0,8},{8,16},{16,24},{24,32},{32,40},{40,48},{48,56},{56,64},{64,7... | collective-permute-start | bytes 614408 | tf_op jit(solution)/shard_map/ppermute | solution.py:145
  44.1 1.3 collective-permute-start.1
  45.5 10.3 %collective-permute-done = bf16[16,4,8,200]{3,2,1,0:T(8,128)(2,1)S(1)} collective-permute-done((bf16[16,4,8,200]{3,2,1,0:T(8,128)(2,1)S(1)}, bf16[16,4,8,200]{3,2,1,0:T(8,128)(2,1)S(1)}, u32[]{:S(2)}, u32[]{:S(2)}) %collective-permute-start) | collective-permute-done | bytes 204832 | tf_op jit(solution)/shard_map/ppermute | solution.py:145
  55.8 4.5 %collective-permute-done.1 = bf16[16,4,8,200]{3,2,1,0:T(8,128)(2,1)S(1)} collective-permute-done((bf16[16,4,8,200]{3,2,1,0:T(8,128)(2,1)S(1)}, bf16[16,4,8,200]{3,2,1,0:T(8,128)(2,1)S(1)}, u32[]{:S(2)}, u32[]{:S(2)}) %collective-permute-start.1) | collective-permute-done | bytes 204832 | tf_op jit(solution)/shard_map/ppermute | solution.py:145
  60.3 6.4 %pad_maximum_fusion.rows_ref = bf16[16,4,208,200]{3,2,1,0:T(8,128)(2,1)} fusion(bf16[16,4,8,200]{3,2,1,0:T(8,128)(2,1)S(1)} %collective-permute-done.1, bf16[16,4,192,200]{3,2,1,0:T(8,128)(2,1)} %reshape.284, bf16[16,4,8,200]{3,2,1,0:T(8,128)(2,1)S(1)} %collective-permute-done), kind=kLoop, calls=%fused_computation.3 | loop fusion | flops 15974400 | bytes 10649600 | tf_op jit(solution)/shard_map/concatenate | solution.py:152
  66.7 2.6 %all-gather.5.cloned.1.call-done = bf16[16,1,5,200,128]{4,3,2,1,0:T(8,128)(2,1)} async-done(((bf16[1,1,5,200,128]{4,3,2,1,0:T(8,128)(2,1)}), bf16[16,1,5,200,128]{4,3,2,1,0:T(8,128)(2,1)}) %all-gather.5.cloned.1.call-update) | async-done | bytes 4096016 | tf_op jit(solution)/shard_map/all_gather | solution.py:329
  69.3 0.9 tile.13.keep_ref
  70.2 17.5 %shard_map.140.rows_ref = bf16[16,4,208,128]{3,2,1,0:T(8,128)(2,1)} custom-call(bf16[16,4,208,200]{3,2,1,0:T(8,128)(2,1)} %pad_maximum_fusion.rows_ref, bf16[16,5,200,128]{3,2,1,0:T(8,128)(2,1)} %bitcast.51, f32[832,128]{1,0:T(8,128)} %tile.13.keep_ref), custom_call_target="tpu_custom_call" | custom-call | flops 3407872000 | bytes 16449536 | tf_op jit(solution)/shard_map/pallas_call | solution.py:225
  87.7 39.7 %all-gather.7.cloned.1.call-done = bf16[1,1,2,80,128,128]{5,4,3,2,1,0:T(8,128)(2,1)} async-done(((bf16[1,1,2,5,128,128]{5,4,3,2,1,0:T(8,128)(2,1)}), bf16[1,1,2,80,128,128]{5,4,3,2,1,0:T(8,128)(2,1)}) %all-gather.7.cloned.1.call-update) | async-done | bytes 5242896 | tf_op jit(solution)/shard_map/all_gather | solution.py:330
  127.4 24.1 %shard_map.141 = f32[8,4,24,512]{3,2,1,0:T(8,128)} custom-call(bf16[16,4,208,128]{3,2,1,0:T(8,128)(2,1)} %shard_map.140.rows_ref, bf16[2,16,5,128,128]{4,3,2,1,0:T(8,128)(2,1)} %bitcast.68, f32[832,128]{1,0:T(8,128)} %tile.13.keep_ref, bf16[16,128,512]{2,1,0:T(8,128)(2,1)} %bitcast.69), custom_call_target="tpu_custom_call" | custom-call | flops 6106906624 | bytes 12320768 | tf_op jit(solution)/shard_map/pallas_call | solution.py:259
  151.5 4.6 %all-to-all-start = ((f32[8,4,24,512]{3,2,1,0:T(8,128)}), f32[8,4,24,512]{3,2,1,0:T(8,128)S(1)}, u32[]{:S(2)}, u32[]{:S(2)}) async-start(f32[8,4,24,512]{3,2,1,0:T(8,128)} %shard_map.141), calls=%async_computation | async-start | bytes 3145728 | tf_op jit(solution)/shard_map/all_to_all | solution.py:334
  156.7 1.2 exponential_reduce_fusion.2
  159.5 18.2 %all-to-all-done = f32[8,4,24,512]{3,2,1,0:T(8,128)S(1)} async-done(((f32[8,4,24,512]{3,2,1,0:T(8,128)}), f32[8,4,24,512]{3,2,1,0:T(8,128)S(1)}, u32[]{:S(2)}, u32[]{:S(2)}) %all-to-all-start) | async-done | bytes 1572896 | tf_op jit(solution)/shard_map/all_to_all | solution.py:334
  178.1 0.7 fusion.8
  178.8 0.7 reshape.310
  179.6 3.5 %all-to-all-start.1 = ((f32[8,1,480]{2,1,0:T(1,128)}), f32[8,1,480]{2,1,0:T(1,128)S(1)}, u32[]{:S(2)}, u32[]{:S(2)}) async-start(f32[8,1,480]{2,1,0:T(1,128)} %reshape.310), calls=%async_computation.1 | async-start | bytes 32768 | tf_op jit(solution)/shard_map/all_to_all | solution.py:341
  183.3 0.6 pad.18
  184.6 0.7 copy.89.within_ref
  185.3 0.7 copy.90.between_ref
  186.6 1.6 all-to-all-done.1
  188.7 0.7 reduce.5
  189.8 0.7 pad.16.emit_ref
  190.5 4.6 %shard_map.142 = (f32[48,5,128]{2,1,0:T(8,128)}, f32[48,1,128]{2,1,0:T(1,128)}) custom-call(f32[5,5,1]{2,1,0:T(8,128)} %copy.89.within_ref, f32[5,5,1]{2,1,0:T(8,128)} %copy.90.between_ref, f32[5,128]{1,0:T(8,128)} %pad.15.start_ref, f32[48,5,128]{2,1,0:T(8,128)} %pad.16.emit_ref, f32[48,1,128]{2,1,0:T(1,128)} %bitcast.64, f32[48,1,128]{2,1,0:T(1,128)} %bitcast.63), custom_call_target="tpu_custom_call" | custom-call | flops 3932160 | bytes 344064 | tf_op jit(solution)/shard_map/pallas_call | solution.py:106
  195.1 0.7 slice.24
  195.8 0.7 slice_reduce_fusion
  196.7 1.5 collective-permute-start.2
  198.2 2.7 %collective-permute-start.3 = (f32[1,4,5,5,4]{3,4,2,1,0:T(4,128)S(1)}, f32[1,4,5,5,4]{3,4,2,1,0:T(4,128)S(1)}, u32[]{:S(2)}, u32[]{:S(2)}) collective-permute-start(f32[1,4,5,5,4]{3,4,2,1,0:T(4,128)S(1)} %get-tuple-element.13), channel_id=1, source_target_pairs={{0,16},{8,24},{16,0},{24,8},{32,48},{40,56},{48,32},{56,40},{64,80... | collective-permute-start | bytes 4808 | tf_op jit(solution)/shard_map/ppermute | solution.py:292
  200.9 1.4 collective-permute-start.4
  202.6 0.8 copy.93
  203.4 1.1 copy.94
  205.3 2.3 collective-permute-start.6
  207.6 1.6 collective-permute-start.7
  209.2 5.2 %collective-permute-done.5 = f32[4,4,5,5,4]{3,4,2,1,0:T(4,128)S(1)} collective-permute-done((f32[4,4,5,5,4]{3,4,2,1,0:T(4,128)S(1)}, f32[4,4,5,5,4]{3,4,2,1,0:T(4,128)S(1)}, u32[]{:S(2)}, u32[]{:S(2)}) %collective-permute-start.5) | collective-permute-done | bytes 6432 | tf_op jit(solution)/shard_map/ppermute | solution.py:292
  215.0 0.9 gather_fusion
  215.9 2.1 copy.92
  218.0 1.3 bitcast_select_fusion.mats_ref
  219.3 0.7 broadcast_in_dim.39.prior_ref
  219.9 5.7 %shard_map.143 = (f32[64,5,4]{2,1,0:T(8,128)}, f32[1,4]{1,0:T(1,128)}) custom-call(f32[5,4]{1,0:T(8,128)} %broadcast_in_dim.39.prior_ref, f32[64,5,5,4]{3,2,1,0:T(8,128)} %bitcast_select_fusion.mats_ref), custom_call_target="tpu_custom_call" | custom-call | tf_op jit(solution)/shard_map/pallas_call | solution.py:127
  225.6 0.7 constant_dynamic-slice_fusion
  226.8 0.7 reshape.290
  227.5 1.1 bitcast_divide_fusion
  (78 shorter events, 6.0 us)
Async XLA Ops:
  7.2 170.9 %copy-start = (f32[512,5]{0,1:T(8,128)S(1)}, f32[512,5]{0,1:T(8,128)}, u32[]{:S(2)}) copy-start(f32[512,5]{0,1:T(8,128)} %param.22) | copy-start | bytes 30724
  7.2 62.1 %all-gather.5.cloned.1.call-start = ((), (), s32[]{:S(2)}) async-start(), calls=%async_computation.2 | async-start | bytes 4352000 | tf_op jit(solution)/shard_map/all_gather | solution.py:329
  7.9 119.5 %all-gather.7.cloned.1.call-start = ((), (), s32[]{:S(2)}) async-start(), calls=%async_computation.3 | async-start | bytes 5570560 | tf_op jit(solution)/shard_map/all_gather | solution.py:330
  40.5 15.3 %collective-permute-start = (bf16[16,4,8,200]{3,2,1,0:T(8,128)(2,1)S(1)}, bf16[16,4,8,200]{3,2,1,0:T(8,128)(2,1)S(1)}, u32[]{:S(2)}, u32[]{:S(2)}) collective-permute-start(bf16[16,4,8,200]{3,2,1,0:T(8,128)(2,1)S(1)} %get-tuple-element.14), channel_id=1, source_target_pairs={{0,8},{8,16},{16,24},{24,32},{32,40},{40,48},{48,56},{56,64},{64,7... | collective-permute-start | bytes 614408 | tf_op jit(solution)/shard_map/ppermute | solution.py:145
  44.1 16.2 %collective-permute-start.1 = (bf16[16,4,8,200]{3,2,1,0:T(8,128)(2,1)S(1)}, bf16[16,4,8,200]{3,2,1,0:T(8,128)(2,1)S(1)}, u32[]{:S(2)}, u32[]{:S(2)}) collective-permute-start(bf16[16,4,8,200]{3,2,1,0:T(8,128)(2,1)S(1)} %get-tuple-element.15), channel_id=1, source_target_pairs={{8,0},{16,8},{24,16},{32,24},{40,32},{48,40},{56,48},{64,56},{72,6... | collective-permute-start | bytes 614408 | tf_op jit(solution)/shard_map/ppermute | solution.py:145
  127.4 28.6 %copy-start.6 = (f32[5]{0:T(128)S(1)}, f32[5]{0:T(128)}, u32[]{:S(2)}) copy-start(f32[5]{0:T(128)} %param.25) | copy-start | bytes 64
  127.4 31.9 %copy-start.1 = (s32[4,192]{1,0:T(4,128)S(1)}, s32[4,192]{1,0:T(4,128)}, u32[]{:S(2)}) copy-start(s32[4,192]{1,0:T(4,128)} %param.17) | copy-start | bytes 9220
  127.4 32.0 %copy-start.4 = (s32[4]{0:T(128)S(1)}, s32[4]{0:T(128)}, u32[]{:S(2)}) copy-start(s32[4]{0:T(128)} %param.16) | copy-start | bytes 52
  151.5 26.6 %copy-start.5 = (f32[512]{0:T(512)S(1)}, f32[512]{0:T(512)}, u32[]{:S(2)}) copy-start(f32[512]{0:T(512)} %param.21) | copy-start | bytes 6148
  151.5 33.1 %copy-start.2 = (f32[5,5]{1,0:T(8,128)S(1)}, f32[5,5]{1,0:T(8,128)}, u32[]{:S(2)}) copy-start(f32[5,5]{1,0:T(8,128)} %param.23) | copy-start | bytes 304
  151.5 33.8 %copy-start.3 = (f32[5,5]{1,0:T(8,128)S(1)}, f32[5,5]{1,0:T(8,128)}, u32[]{:S(2)}) copy-start(f32[5,5]{1,0:T(8,128)} %param.24) | copy-start | bytes 304
  151.5 26.2 %all-to-all-start = ((f32[8,4,24,512]{3,2,1,0:T(8,128)}), f32[8,4,24,512]{3,2,1,0:T(8,128)S(1)}, u32[]{:S(2)}, u32[]{:S(2)}) async-start(f32[8,4,24,512]{3,2,1,0:T(8,128)} %shard_map.141), calls=%async_computation | async-start | bytes 3145728 | tf_op jit(solution)/shard_map/all_to_all | solution.py:334
  179.6 8.6 %all-to-all-start.1 = ((f32[8,1,480]{2,1,0:T(1,128)}), f32[8,1,480]{2,1,0:T(1,128)S(1)}, u32[]{:S(2)}, u32[]{:S(2)}) async-start(f32[8,1,480]{2,1,0:T(1,128)} %reshape.310), calls=%async_computation.1 | async-start | bytes 32768 | tf_op jit(solution)/shard_map/all_to_all | solution.py:341
  196.7 7.7 %collective-permute-start.2 = (f32[1,4,5,5,4]{3,4,2,1,0:T(4,128)S(1)}, f32[1,4,5,5,4]{3,4,2,1,0:T(4,128)S(1)}, u32[]{:S(2)}, u32[]{:S(2)}) collective-permute-start(f32[1,4,5,5,4]{3,4,2,1,0:T(4,128)S(1)} %get-tuple-element.13), channel_id=1, source_target_pairs={{0,8},{8,16},{16,24},{24,0},{32,40},{40,48},{48,56},{56,32},{64,72... | collective-permute-start | bytes 4808 | tf_op jit(solution)/shard_map/ppermute | solution.py:292
  198.2 6.2 %collective-permute-start.3 = (f32[1,4,5,5,4]{3,4,2,1,0:T(4,128)S(1)}, f32[1,4,5,5,4]{3,4,2,1,0:T(4,128)S(1)}, u32[]{:S(2)}, u32[]{:S(2)}) collective-permute-start(f32[1,4,5,5,4]{3,4,2,1,0:T(4,128)S(1)} %get-tuple-element.13), channel_id=1, source_target_pairs={{0,16},{8,24},{16,0},{24,8},{32,48},{40,56},{48,32},{56,40},{64,80... | collective-permute-start | bytes 4808 | tf_op jit(solution)/shard_map/ppermute | solution.py:292
  200.9 4.0 %collective-permute-start.4 = (f32[1,4,5,5,4]{3,4,2,1,0:T(4,128)S(1)}, f32[1,4,5,5,4]{3,4,2,1,0:T(4,128)S(1)}, u32[]{:S(2)}, u32[]{:S(2)}) collective-permute-start(f32[1,4,5,5,4]{3,4,2,1,0:T(4,128)S(1)} %get-tuple-element.13), channel_id=1, source_target_pairs={{0,24},{8,0},{16,8},{24,16},{32,56},{40,32},{48,40},{56,48},{64,88... | collective-permute-start | bytes 4808 | tf_op jit(solution)/shard_map/ppermute | solution.py:292
  205.0 9.4 %collective-permute-start.5 = (f32[4,4,5,5,4]{3,4,2,1,0:T(4,128)S(1)}, f32[4,4,5,5,4]{3,4,2,1,0:T(4,128)S(1)}, u32[]{:S(2)}, u32[]{:S(2)}) collective-permute-start(f32[4,4,5,5,4]{3,4,2,1,0:T(4,128)S(1)} %pad_maximum_fusion.1), channel_id=1, source_target_pairs={{0,32},{8,40},{16,48},{24,56},{32,64},{40,72},{48,80},{56,88},{64,... | collective-permute-start | bytes 19208 | tf_op jit(solution)/shard_map/ppermute | solution.py:292
  205.3 9.1 %collective-permute-start.6 = (f32[4,4,5,5,4]{3,4,2,1,0:T(4,128)S(1)}, f32[4,4,5,5,4]{3,4,2,1,0:T(4,128)S(1)}, u32[]{:S(2)}, u32[]{:S(2)}) collective-permute-start(f32[4,4,5,5,4]{3,4,2,1,0:T(4,128)S(1)} %pad_maximum_fusion.1), channel_id=1, source_target_pairs={{0,64},{8,72},{16,80},{24,88},{32,96},{40,104},{48,112},{56,120},{... | collective-permute-start | bytes 19208 | tf_op jit(solution)/shard_map/ppermute | solution.py:292
  207.6 7.4 %collective-permute-start.7 = (f32[4,4,5,5,4]{3,4,2,1,0:T(4,128)S(1)}, f32[4,4,5,5,4]{3,4,2,1,0:T(4,128)S(1)}, u32[]{:S(2)}, u32[]{:S(2)}) collective-permute-start(f32[4,4,5,5,4]{3,4,2,1,0:T(4,128)S(1)} %pad_maximum_fusion.1), channel_id=1, source_target_pairs={{0,96},{8,104},{16,112},{24,120},{32,0},{40,8},{48,16},{56,24},{64... | collective-permute-start | bytes 19208 | tf_op jit(solution)/shard_map/ppermute | solution.py:292
Sparse Core Ops, SparseCore 0:
  10.2 59.0 all-gather.4
  71.4 55.9 all-gather.6
